TPU v7x, 32 devices: a whole 2x2x4 slice. The times are simulated.
32 devices in a mesh: gx: 4 (over y, x), gy: 8 (over z, core).
Axes of the slice: x: 2, y: 2, z: 4, core: 2. Of those that a mesh axis runs over, the one named last changes fastest.
Arguments:
- populations: float32 [64, 128, 19, 128], P('gx', 'gy'), may hold values from 0.001 to 0.9, as said below
Outputs:
- relaxed_populations: float32 [64, 128, 19, 128], P('gx', 'gy')
- picture: float32 [4, 128, 128], P(None, 'gy', 'gx')
Inputs may be any that keep to these rules, and one draw needn't show every extreme that they name: `populations`: positive; near a local equilibrium of densities between 0.15 and 2.2 with drift of at most 0.08 a component.
All inputs are finite; a program needn't handle non-finite values.
Results may differ from a plain program's by a relative error of at most 0.0003.
Values sent between devices are 32-bit elements; how exact they have to be, the bound alone decides.
No kernel may reach another device: no remote copies, remote signals or barrier semaphores. Data moves between devices by JAX's collectives and lax.ppermute only.
A program may use at most 64 MiB of HBM per device.

v0:
```python
import jax
import jax.numpy as jnp
import numpy as np
from jax import lax
from jax.sharding import PartitionSpec as P

cohesion = -6.0
optical = 2.0


def extended(cells, sides, width):
    for axis, dim in sides:
        count = lax.axis_size(axis)
        head = lax.slice_in_dim(cells, 0, width, axis=dim)
        tail = lax.slice_in_dim(cells, cells.shape[dim] - width, cells.shape[dim], axis=dim)
        cells = jnp.concatenate(
            [
                lax.ppermute(tail, axis, [(i, (i + 1) % count) for i in range(count)]),
                cells,
                lax.ppermute(head, axis, [((i + 1) % count, i) for i in range(count)]),
            ],
            axis=dim,
        )
    return cells


def from_partner(x, axis, distance):
    return lax.ppermute(x, axis, [(i, i ^ 1 << distance) for i in range(lax.axis_size(axis))])


def lattice_tables():
    velocities = np.array(
        [
            [0, 0, 0],
            [1, 0, 0],
            [-1, 0, 0],
            [0, 1, 0],
            [0, -1, 0],
            [0, 0, 1],
            [0, 0, -1],
            [1, 1, 0],
            [-1, -1, 0],
            [1, -1, 0],
            [-1, 1, 0],
            [1, 0, 1],
            [-1, 0, -1],
            [1, 0, -1],
            [-1, 0, 1],
            [0, 1, 1],
            [0, -1, -1],
            [0, 1, -1],
            [0, -1, 1],
        ]
    )
    weights = np.array([1.0 / 3.0] + [1.0 / 18.0] * 6 + [1.0 / 36.0] * 12)
    along_x = velocities[:, 0] * 1.0
    along_y = velocities[:, 1] * 1.0
    along_z = velocities[:, 2] * 1.0
    squared = along_x * along_x + along_y * along_y + along_z * along_z
    moment_rows = [
        np.ones(19),
        19.0 * squared - 30.0,
        (21.0 * squared * squared - 53.0 * squared + 24.0) / 2.0,
        along_x,
        (5.0 * squared - 9.0) * along_x,
        along_y,
        (5.0 * squared - 9.0) * along_y,
        along_z,
        (5.0 * squared - 9.0) * along_z,
        3.0 * along_x * along_x - squared,
        (3.0 * squared - 5.0) * (3.0 * along_x * along_x - squared),
        along_y * along_y - along_z * along_z,
        (3.0 * squared - 5.0) * (along_y * along_y - along_z * along_z),
        along_x * along_y,
        along_y * along_z,
        along_x * along_z,
        (along_y * along_y - along_z * along_z) * along_x,
        (along_z * along_z - along_x * along_x) * along_y,
        (along_x * along_x - along_y * along_y) * along_z,
    ]
    moments = np.stack(moment_rows)
    inverse = moments.T / np.sum(moments * moments, axis=1)
    relax_rates = np.array(
        [
            0.0,
            1.19,
            1.4,
            0.0,
            1.2,
            0.0,
            1.2,
            0.0,
            1.2,
            1.0,
            1.4,
            1.0,
            1.4,
            1.0,
            1.0,
            1.0,
            1.98,
            1.98,
            1.98,
        ]
    )
    relaxing = inverse @ (relax_rates[:, None] * moments)
    forcing_map = inverse @ ((1.0 - 0.5 * relax_rates)[:, None] * moments)
    return (velocities, weights, relaxing, forcing_map)


def collide(populations, density, forcing, velocities, weights, relaxing, forcing_map):
    lattice = jnp.asarray(velocities, dtype=jnp.float32)
    spread = jnp.asarray(weights, dtype=jnp.float32)[None, None, :, None]
    relax_table = jnp.asarray(relaxing, dtype=jnp.float32)
    source_table = jnp.asarray(forcing_map, dtype=jnp.float32)
    momentum = jnp.einsum("qd,xyqz->dxyz", lattice, populations, precision=lax.Precision.HIGHEST)
    drift = (momentum + 0.5 * forcing) / density[None]
    along = jnp.einsum("qd,dxyz->xyqz", lattice, drift, precision=lax.Precision.HIGHEST)
    pushed = jnp.einsum("qd,dxyz->xyqz", lattice, forcing, precision=lax.Precision.HIGHEST)
    speed_squared = jnp.sum(drift * drift, axis=0)[:, :, None, :]
    work_done = jnp.sum(drift * forcing, axis=0)[:, :, None, :]
    balance = (
        spread
        * density[:, :, None, :]
        * (1.0 + 3.0 * along + 4.5 * along * along - 1.5 * speed_squared)
    )
    guo_term = spread * (3.0 * (pushed - work_done) + 9.0 * along * pushed)
    relaxed = jnp.einsum(
        "pq,xyqz->xypz", relax_table, populations - balance, precision=lax.Precision.HIGHEST
    )
    sourced = jnp.einsum("pq,xyqz->xypz", source_table, guo_term, precision=lax.Precision.HIGHEST)
    return populations - relaxed + sourced


def attraction(padded, offset, extent_x, extent_y, velocities, weights):
    centre = padded[offset : offset + extent_x, offset : offset + extent_y]
    totals = [jnp.zeros_like(centre), jnp.zeros_like(centre), jnp.zeros_like(centre)]
    for q in range(1, 19):
        steps = [int(v) for v in velocities[q]]
        start_x = offset + steps[0]
        start_y = offset + steps[1]
        neighbour = padded[start_x : start_x + extent_x, start_y : start_y + extent_y]
        neighbour = jnp.roll(neighbour, -steps[2], axis=2)
        for d in range(3):
            if steps[d] != 0:
                totals[d] = totals[d] + weights[q] * steps[d] * neighbour
    return jnp.stack([-cohesion * centre * totals[d] for d in range(3)])


def palette(density):
    reds = density / (1.0 + density)
    greens = jnp.exp(-density)
    blues = 0.5 * (1.0 + jnp.tanh(2.0 * (density - 1.0)))
    return (reds, greens, blues)


def body(populations):
    velocities, weights, relaxing, forcing_map = lattice_tables()
    extent_x = populations.shape[0]
    extent_y = populations.shape[1]
    read = []
    density = jnp.sum(populations, axis=2)
    potential = 1.0 - jnp.exp(-density)
    padded = extended(potential, (("gx", 0), ("gy", 1)), 1)
    forcing = attraction(padded, 1, extent_x, extent_y, velocities, weights)
    collided = collide(populations, density, forcing, velocities, weights, relaxing, forcing_map)
    moving = jnp.concatenate([collided[:, :, 1:5], collided[:, :, 7:]], axis=2)
    arriving = extended(moving, (("gx", 0), ("gy", 1)), 1)
    for q in range(19):
        steps = [int(v) for v in velocities[q]]
        if q in (0, 5, 6):
            column = collided[:, :, q]
        else:
            slot = q - 1 if q < 5 else q - 3
            column = arriving[
                1 - steps[0] : 1 - steps[0] + extent_x, 1 - steps[1] : 1 - steps[1] + extent_y, slot
            ]
        read.append(jnp.roll(column, steps[2], axis=2))
    fresh = jnp.stack(read, axis=2)
    groups = lax.axis_size("gx")
    length_x = extent_x * groups
    new_density = jnp.sum(fresh, axis=2)
    extinction = optical * new_density / length_x
    optical_depth = jnp.cumsum(extinction, axis=0) - extinction
    weight_map = jnp.exp(-optical_depth) * (1.0 - jnp.exp(-extinction))
    reds, greens, blues = palette(new_density)
    layered = jnp.stack(
        [
            jnp.sum(weight_map * reds, axis=0),
            jnp.sum(weight_map * greens, axis=0),
            jnp.sum(weight_map * blues, axis=0),
            1.0 - jnp.exp(-jnp.sum(extinction, axis=0)),
        ]
    )
    depth_z = layered.shape[2]
    block_len = depth_z // groups
    blocked = layered.reshape(4, extent_y, groups, block_len)
    position = lax.axis_index("gx")
    current = blocked
    for level in range(groups.bit_length() - 1):
        parity = position // (1 << level) % 2
        halves = current.shape[2] // 2
        paired = current.reshape(4, extent_y, halves, 2, block_len)
        lower = paired[:, :, :, 0]
        upper = paired[:, :, :, 1]
        kept = jnp.where(parity == 1, upper, lower)
        handed = jnp.where(parity == 1, lower, upper)
        partner = from_partner(handed, "gx", level)
        nearer = jnp.where(parity == 0, kept, partner)
        farther = jnp.where(parity == 0, partner, kept)
        current = nearer + (1.0 - nearer[3:4]) * farther
    picture = current.reshape(4, extent_y, block_len)
    return (fresh, picture)


def solution(mesh):
    placed = (P("gx", "gy", None, None),)
    return jax.shard_map(
        body,
        mesh=mesh,
        in_specs=placed,
        out_specs=(P("gx", "gy", None, None), P(None, "gy", "gx")),
        check_vma=False,
    )
```

profile of v0, /device:TPU:0, one launch (start us, length us, event | category | flops | bytes accessed | tf_op | source)
XLA Modules:
  0.0 74.6 jit_solution(1838713788385507313)
XLA Ops:
  0.7 2.0 %reduce_sum.135 = f32[16,16,128]{2,1,0:T(8,128)S(1)} reduce(f32[16,16,19,128]{3,1,2,0:T(8,128)} %param.5, f32[]{:T(128)} %constant.71.clone.1), dimensions={2}, to_apply=%region_0.0 | reduce | flops 589824 | bytes 2621444 | tf_op jit(solution)/shard_map/reduce_sum | solution.py:162
  2.7 3.0 %collective-permute-start.1 = (f32[1,16,128]{2,1,0:T(8,128)S(1)}, f32[1,16,128]{2,1,0:T(8,128)S(1)}, u32[]{:S(2)}, u32[]{:S(2)}) collective-permute-start(f32[1,16,128]{2,1,0:T(8,128)S(1)} %get-tuple-element.87), channel_id=1, source_target_pairs={{0,8},{8,16},{16,24},{24,0},{1,9},{9,17},{17,25},{25,1},{2,10},{10... | collective-permute-start | bytes 24584 | tf_op jit(solution)/shard_map/ppermute | solution.py:18
  5.7 1.0 %collective-permute-start = (f32[1,16,128]{2,1,0:T(8,128)S(1)}, f32[1,16,128]{2,1,0:T(8,128)S(1)}, u32[]{:S(2)}, u32[]{:S(2)}) collective-permute-start(f32[1,16,128]{2,1,0:T(8,128)S(1)} %get-tuple-element.88), channel_id=1, source_target_pairs={{8,0},{16,8},{24,16},{0,24},{9,1},{17,9},{25,17},{1,25},{10,2},{18... | collective-permute-start | bytes 24584 | tf_op jit(solution)/shard_map/ppermute | solution.py:20
  6.7 2.3 %fusion = f32[3,16,16,128]{3,0,2,1:T(4,128)S(1)} fusion(f32[19,3,1,1]{0,1,3,2:T(4,128)S(1)} %copy-done.2, f32[16,16,19,128]{3,1,2,0:T(8,128)S(1)} %copy-done), kind=kOutput, calls=%fused_computation.1 | convolution fusion | flops 22413312 | bytes 2883812 | tf_op jit(solution)/shard_map/qd,xyqz->dxyz/dot_general | solution.py:116
  9.1 0.3 collective-permute-done
  9.5 3.5 %collective-permute-start.2 = (f32[18,1,128]{2,1,0:T(1,128)S(1)}, f32[18,1,128]{2,1,0:T(1,128)S(1)}, u32[]{:S(2)}, u32[]{:S(2)}) collective-permute-start(f32[18,1,128]{2,1,0:T(1,128)S(1)} %get-tuple-element.67), channel_id=1, source_target_pairs={{1,0},{2,1},{3,2},{4,3},{5,4},{6,5},{7,6},{0,7},{9,8},{10,9},{11,1... | collective-permute-start | bytes 27656 | tf_op jit(solution)/shard_map/ppermute | solution.py:20
  13.0 0.2 pad_maximum_fusion.28
  13.2 0.2 fusion.35
  13.3 1.0 %collective-permute-done.3 = f32[18,1,128]{2,1,0:T(1,128)S(1)} collective-permute-done((f32[18,1,128]{2,1,0:T(1,128)S(1)}, f32[18,1,128]{2,1,0:T(1,128)S(1)}, u32[]{:S(2)}, u32[]{:S(2)}) %collective-permute-start.3) | collective-permute-done | bytes 9248 | tf_op jit(solution)/shard_map/ppermute | solution.py:18
  14.4 0.1 fusion.109
  14.5 0.1 fusion.108
  14.7 0.2 fusion.70
  14.9 0.4 fusion.80
  15.4 0.2 fusion.48
  15.6 0.1 multiply_reduce_fusion.1
  15.7 2.7 %fusion.29 = f32[16,16,128,19]{2,3,1,0:T(8,128)S(1)} fusion(f32[19,3,1,1]{0,1,3,2:T(4,128)S(1)} %copy-done.2, f32[3,16,16,128]{3,2,1,0:T(8,128)S(1)} %get-tuple-element.47), kind=kOutput, calls=%fused_computation.35 | convolution fusion | flops 22413312 | bytes 2883812 | tf_op jit(solution)/shard_map/qd,dxyz->xyqz/dot_general | solution.py:119
  18.5 2.7 %fusion.31 = f32[16,16,128,19]{2,3,1,0:T(8,128)S(1)} fusion(f32[19,3,1,1]{0,1,3,2:T(4,128)S(1)} %copy-done.2, f32[3,16,16,128]{3,2,1,0:T(8,128)S(1)} %get-tuple-element.29), kind=kOutput, calls=%fused_computation.37 | convolution fusion | flops 22413312 | bytes 2883812 | tf_op jit(solution)/shard_map/qd,dxyz->xyqz/dot_general | solution.py:118
  21.3 4.5 %fusion.2 = f32[16,16,128,19]{2,3,1,0:T(8,128)S(1)} fusion(f32[19,19,1,1]{1,0,3,2:T(8,128)S(1)} %copy-done.4, f32[16,16,19,128]{3,1,2,0:T(8,128)S(1)} %copy-done, f32[16,16,128,19]{2,3,1,0:T(8,128)S(1)} %fusion.31, f32[16,16,128]{2,1,0:T(8,128)S(1)} %broadcast_multiply_fusion, f32[16,16,128]{2,1,0:T(8,128)S(1)} %reduce_sum.135, f32[19]{0:T(128)S(1)} %copy-done.5), kind=kOutput, calls=%fused_computation.4 | convolution fusion | flops 147554304 | bytes 7734768 | tf_op jit(solution)/shard_map/pq,xyqz->xypz/dot_general | solution.py:128
  25.8 4.0 %fusion.10 = f32[16,16,128,19]{2,3,1,0:T(8,128)S(1)} fusion(f32[19,19,1,1]{1,0,3,2:T(8,128)S(1)} %copy-done.3, f32[16,16,128,19]{2,3,1,0:T(8,128)S(1)} %fusion.29, f32[16,16,128,19]{2,3,1,0:T(8,128)S(1)} %fusion.31, f32[16,16,128]{2,1,0:T(8,128)S(1)} %get-tuple-element.15, f32[19]{0:T(128)S(1)} %copy-done.5), kind=kOutput, calls=%fused_computation.13 | convolution fusion | flops 145686528 | bytes 7603696 | tf_op jit(solution)/shard_map/pq,xyqz->xypz/dot_general | solution.py:131
  29.8 0.9 %bitcast_add_fusion = f32[16,16,19,128]{3,1,0,2:T(8,128)S(1)} fusion(f32[16,16,128,19]{2,3,1,0:T(8,128)S(1)} %fusion.10, f32[16,16,19,128]{3,1,2,0:T(8,128)S(1)} %copy-done, f32[16,16,128,19]{2,3,1,0:T(8,128)S(1)} %fusion.2), kind=kLoop, calls=%fused_computation.19 | loop fusion | flops 1245184 | bytes 9961472 | tf_op jit(solution)/shard_map/add | solution.py:132
  30.7 0.2 slice.422
  31.0 1.2 %copy-done.1 = f32[16,16,19,128]{3,1,0,2:T(8,128)} copy-done((f32[16,16,19,128]{3,1,0,2:T(8,128)}, f32[16,16,19,128]{3,1,0,2:T(8,128)S(1)}, u32[]{:S(2)}) %copy-start.1) | copy-done | bytes 2490392
  32.2 2.4 %collective-permute-start.4 = (f32[1,16,16,128]{3,1,0,2:T(8,128)S(1)}, f32[1,16,16,128]{3,1,0,2:T(8,128)S(1)}, u32[]{:S(2)}, u32[]{:S(2)}) collective-permute-start(f32[1,16,16,128]{3,1,0,2:T(8,128)S(1)} %get-tuple-element.45), channel_id=1, source_target_pairs={{0,8},{8,16},{16,24},{24,0},{1,9},{9,17},{17,25},{25,1},{2,10},{10... | collective-permute-start | bytes 393224 | tf_op jit(solution)/shard_map/ppermute | solution.py:18
  34.6 0.5 collective-permute-start.5
  35.1 4.3 %collective-permute-done.4 = f32[1,16,16,128]{3,1,0,2:T(8,128)S(1)} collective-permute-done((f32[1,16,16,128]{3,1,0,2:T(8,128)S(1)}, f32[1,16,16,128]{3,1,0,2:T(8,128)S(1)}, u32[]{:S(2)}, u32[]{:S(2)}) %collective-permute-start.4) | collective-permute-done | bytes 131104 | tf_op jit(solution)/shard_map/ppermute | solution.py:18
  39.4 2.2 %collective-permute-done.5 = f32[1,16,16,128]{3,1,0,2:T(8,128)S(1)} collective-permute-done((f32[1,16,16,128]{3,1,0,2:T(8,128)S(1)}, f32[1,16,16,128]{3,1,0,2:T(8,128)S(1)}, u32[]{:S(2)}, u32[]{:S(2)}) %collective-permute-start.5) | collective-permute-done | bytes 131104 | tf_op jit(solution)/shard_map/ppermute | solution.py:20
  41.6 0.2 pad_maximum_fusion.5
  41.8 2.2 %collective-permute-start.7 = (f32[18,1,16,128]{3,1,0,2:T(1,128)S(1)}, f32[18,1,16,128]{3,1,0,2:T(1,128)S(1)}, u32[]{:S(2)}, u32[]{:S(2)}) collective-permute-start(f32[18,1,16,128]{3,1,0,2:T(1,128)S(1)} %get-tuple-element.38), channel_id=1, source_target_pairs={{1,0},{2,1},{3,2},{4,3},{5,4},{6,5},{7,6},{0,7},{9,8},{10,9},{11,1... | collective-permute-start | bytes 442376 | tf_op jit(solution)/shard_map/ppermute | solution.py:20
  44.0 1.7 %slice_bitcast_fusion.1 = (f32[16,16,128]{2,1,0:T(8,128)S(1)}, f32[16,16,128]{2,1,0:T(8,128)S(1)}, f32[16,16,19,128]{3,1,0,2:T(8,128)}) fusion(f32[16,16,19,128]{3,1,0,2:T(8,128)} %copy-done.1), kind=kLoop, calls=%fused_computation.106 | loop fusion | bytes 786432 | tf_op jit(solution)/shard_map/squeeze | solution.py:172
  45.8 0.1 slice.424
  45.9 0.8 %collective-permute-done.7 = f32[18,1,16,128]{3,1,0,2:T(1,128)S(1)} collective-permute-done((f32[18,1,16,128]{3,1,0,2:T(1,128)S(1)}, f32[18,1,16,128]{3,1,0,2:T(1,128)S(1)}, u32[]{:S(2)}, u32[]{:S(2)}) %collective-permute-start.7) | collective-permute-done | bytes 147488 | tf_op jit(solution)/shard_map/ppermute | solution.py:20
  46.8 3.5 %collective-permute-done.6 = f32[18,1,16,128]{3,1,0,2:T(1,128)S(1)} collective-permute-done((f32[18,1,16,128]{3,1,0,2:T(1,128)S(1)}, f32[18,1,16,128]{3,1,0,2:T(1,128)S(1)}, u32[]{:S(2)}, u32[]{:S(2)}) %collective-permute-start.6) | collective-permute-done | bytes 147488 | tf_op jit(solution)/shard_map/ppermute | solution.py:18
  50.5 0.1 slice.439
  50.6 0.1 slice.437
  50.7 0.1 slice.435
  50.8 0.1 slice.433
  50.9 0.1 slice.431
  51.0 0.1 slice.429
  51.1 1.5 %fusion.88 = (f32[16,16,128]{2,1,0:T(8,128)S(1)}, f32[16,16,1,128]{3,1,0,2:T(8,128)S(1)}, f32[16,16,1,128]{3,1,0,2:T(8,128)S(1)}, f32[16,16,1,128]{3,1,0,2:T(8,1...) fusion(f32[16,16,19,128]{3,1,0,2:T(8,128)} %copy-done.1, ...), kind=kLoop, calls=%fused_computation.180 | loop fusion | flops 1835008 | bytes 5275648 | tf_op jit(solution)/shard_map/reduce_sum | solution.py:182
  52.6 0.7 constant_dynamic-update-slice_fusion.7
  53.2 0.6 constant_dynamic-update-slice_fusion.6
  53.9 0.7 constant_dynamic-update-slice_fusion.5
  54.6 0.7 constant_dynamic-update-slice_fusion.4
  55.2 0.8 %bitcast_dynamic-update-slice_fusion.9 = f32[16,16,19,128]{3,1,0,2:T(8,128)} fusion(f32[16,16,19,128]{3,1,0,2:T(8,128)} %constant_dynamic-update-slice_fusion.4, f32[16,16,127]{2,1,0:T(8,128)S(1)} %bitcast.231, f32[16,16,1]{2,1,0:T(8,128)S(1)} %slice.424), kind=kLoop, calls=%fused_computation.195 | loop fusion | flops 32768 | bytes 262144
  56.0 0.8 %bitcast_dynamic-update-slice_fusion.8 = f32[16,16,19,128]{3,1,0,2:T(8,128)} fusion(f32[16,16,19,128]{3,1,0,2:T(8,128)} %bitcast_dynamic-update-slice_fusion.9, f32[16,16,1]{2,1,0:T(8,128)S(1)} %bitcast.229, f32[16,16,127]{2,1,0:T(8,128)S(1)} %slice.427), kind=kLoop, calls=%fused_computation.194 | loop fusion | flops 32768 | bytes 262144
  56.7 0.7 constant_dynamic-update-slice_fusion.3
  57.4 0.7 constant_dynamic-update-slice_fusion.2
  58.0 0.7 constant_dynamic-update-slice_fusion.1
  58.7 0.7 constant_dynamic-update-slice_fusion
  59.4 0.8 %bitcast_dynamic-update-slice_fusion.7 = f32[16,16,19,128]{3,1,0,2:T(8,128)} fusion(f32[16,16,19,128]{3,1,0,2:T(8,128)} %constant_dynamic-update-slice_fusion, f32[16,16,127]{2,1,0:T(8,128)S(1)} %bitcast.227, f32[16,16,1]{2,1,0:T(8,128)S(1)} %slice.429), kind=kLoop, calls=%fused_computation.193 | loop fusion | flops 32768 | bytes 262144
  60.1 0.8 %bitcast_dynamic-update-slice_fusion.6 = f32[16,16,19,128]{3,1,0,2:T(8,128)} fusion(f32[16,16,19,128]{3,1,0,2:T(8,128)} %bitcast_dynamic-update-slice_fusion.7, f32[16,16,1]{2,1,0:T(8,128)S(1)} %bitcast.223, f32[16,16,127]{2,1,0:T(8,128)S(1)} %slice.431), kind=kLoop, calls=%fused_computation.192 | loop fusion | flops 32768 | bytes 262144
  60.9 0.8 %bitcast_dynamic-update-slice_fusion.5 = f32[16,16,19,128]{3,1,0,2:T(8,128)} fusion(f32[16,16,19,128]{3,1,0,2:T(8,128)} %bitcast_dynamic-update-slice_fusion.6, f32[16,16,1]{2,1,0:T(8,128)S(1)} %bitcast.219, f32[16,16,127]{2,1,0:T(8,128)S(1)} %slice.433), kind=kLoop, calls=%fused_computation.191 | loop fusion | flops 32768 | bytes 262144
  61.6 0.7 bitcast_dynamic-update-slice_fusion.4
  62.4 0.8 %bitcast_dynamic-update-slice_fusion.3 = f32[16,16,19,128]{3,1,0,2:T(8,128)} fusion(f32[16,16,19,128]{3,1,0,2:T(8,128)} %bitcast_dynamic-update-slice_fusion.4, f32[16,16,127]{2,1,0:T(8,128)S(1)} %bitcast.221, f32[16,16,1]{2,1,0:T(8,128)S(1)} %slice.437), kind=kLoop, calls=%fused_computation.189 | loop fusion | flops 32768 | bytes 262144
  63.1 0.8 %bitcast_dynamic-update-slice_fusion.2 = f32[16,16,19,128]{3,1,0,2:T(8,128)} fusion(f32[16,16,19,128]{3,1,0,2:T(8,128)} %bitcast_dynamic-update-slice_fusion.3, f32[16,16,1]{2,1,0:T(8,128)S(1)} %bitcast.217, f32[16,16,127]{2,1,0:T(8,128)S(1)} %slice.439), kind=kLoop, calls=%fused_computation.188 | loop fusion | flops 32768 | bytes 262144
  63.9 0.1 multiply_reduce_fusion.2
  64.5 0.1 fusion.112
  64.6 1.3 %collective-permute-start.8 = (f32[4,16,2,32]{3,2,1,0:T(2,128)S(1)}, f32[4,16,2,32]{3,2,1,0:T(2,128)S(1)}, u32[]{:S(2)}, u32[]{:S(2)}) collective-permute-start(f32[4,16,2,32]{3,2,1,0:T(2,128)S(1)} %bitcast.248), channel_id=1, source_target_pairs={{0,8},{8,0},{16,24},{24,16},{1,9},{9,1},{17,25},{25,17},{2,10},{10... | collective-permute-start | bytes 49160 | tf_op jit(solution)/shard_map/ppermute | solution.py:28
  65.9 0.8 %bitcast_dynamic-update-slice_fusion.1 = f32[16,16,19,128]{3,1,0,2:T(8,128)} fusion(f32[16,16,19,128]{3,1,0,2:T(8,128)} %bitcast_dynamic-update-slice_fusion.2, f32[16,16,1]{2,1,0:T(8,128)S(1)} %bitcast.215, f32[16,16,127]{2,1,0:T(8,128)S(1)} %slice.441), kind=kLoop, calls=%fused_computation.187 | loop fusion | flops 32768 | bytes 262144
  66.6 2.3 %collective-permute-done.8 = f32[4,16,2,32]{3,2,1,0:T(2,128)S(1)} collective-permute-done((f32[4,16,2,32]{3,2,1,0:T(2,128)S(1)}, f32[4,16,2,32]{3,2,1,0:T(2,128)S(1)}, u32[]{:S(2)}, u32[]{:S(2)}) %collective-permute-start.8) | collective-permute-done | bytes 16416 | tf_op jit(solution)/shard_map/ppermute | solution.py:28
  69.1 0.8 %collective-permute-start.9 = (f32[4,16,1,32]{3,1,0,2:T(8,128)S(1)}, f32[4,16,1,32]{3,1,0,2:T(8,128)S(1)}, u32[]{:S(2)}, u32[]{:S(2)}) collective-permute-start(f32[4,16,1,32]{3,1,0,2:T(8,128)S(1)} %bitcast.249), channel_id=1, source_target_pairs={{0,16},{8,24},{16,0},{24,8},{1,17},{9,25},{17,1},{25,9},{2,18},{10... | collective-permute-start | bytes 24584 | tf_op jit(solution)/shard_map/ppermute | solution.py:28
  69.9 0.8 %bitcast_dynamic-update-slice_fusion = f32[16,16,19,128]{3,1,0,2:T(8,128)} fusion(f32[16,16,19,128]{3,1,0,2:T(8,128)} %bitcast_dynamic-update-slice_fusion.1, f32[16,16,127]{2,1,0:T(8,128)S(1)} %bitcast.213, f32[16,16,1]{2,1,0:T(8,128)S(1)} %slice.443), kind=kLoop, calls=%fused_computation.186 | loop fusion | flops 32768 | bytes 262144 | tf_op jit(solution)/shard_map/stack | solution.py:179
  70.7 3.3 %copy.267 = f32[16,16,19,128]{3,1,2,0:T(8,128)} copy(f32[16,16,19,128]{3,1,0,2:T(8,128)} %bitcast_dynamic-update-slice_fusion) | data formatting | bytes 4980736
  74.0 0.6 fusion.98
  (43 shorter events, 1.2 us)
Async XLA Ops:
  0.6 6.1 %copy-start.2 = (f32[19,3,1,1]{0,1,3,2:T(4,128)S(1)}, f32[19,3,1,1]{0,1,3,2:T(4,128)}, u32[]{:S(2)}) copy-start(f32[19,3,1,1]{0,1,3,2:T(4,128)} %constant.95) | copy-start | bytes 688
  0.6 6.1 %copy-start = (f32[16,16,19,128]{3,1,2,0:T(8,128)S(1)}, f32[16,16,19,128]{3,1,2,0:T(8,128)}, u32[]{:S(2)}) copy-start(f32[16,16,19,128]{3,1,2,0:T(8,128)} %param.5) | copy-start | bytes 7471108
  2.7 6.4 %collective-permute-start.1 = (f32[1,16,128]{2,1,0:T(8,128)S(1)}, f32[1,16,128]{2,1,0:T(8,128)S(1)}, u32[]{:S(2)}, u32[]{:S(2)}) collective-permute-start(f32[1,16,128]{2,1,0:T(8,128)S(1)} %get-tuple-element.87), channel_id=1, source_target_pairs={{0,8},{8,16},{16,24},{24,0},{1,9},{9,17},{17,25},{25,1},{2,10},{10... | collective-permute-start | bytes 24584 | tf_op jit(solution)/shard_map/ppermute | solution.py:18
  5.7 3.7 %collective-permute-start = (f32[1,16,128]{2,1,0:T(8,128)S(1)}, f32[1,16,128]{2,1,0:T(8,128)S(1)}, u32[]{:S(2)}, u32[]{:S(2)}) collective-permute-start(f32[1,16,128]{2,1,0:T(8,128)S(1)} %get-tuple-element.88), channel_id=1, source_target_pairs={{8,0},{16,8},{24,16},{0,24},{9,1},{17,9},{25,17},{1,25},{10,2},{18... | collective-permute-start | bytes 24584 | tf_op jit(solution)/shard_map/ppermute | solution.py:20
  9.4 4.9 %collective-permute-start.3 = (f32[18,1,128]{2,1,0:T(1,128)S(1)}, f32[18,1,128]{2,1,0:T(1,128)S(1)}, u32[]{:S(2)}, u32[]{:S(2)}) collective-permute-start(f32[18,1,128]{2,1,0:T(1,128)S(1)} %get-tuple-element.66), channel_id=1, source_target_pairs={{0,1},{1,2},{2,3},{3,4},{4,5},{5,6},{6,7},{7,0},{8,9},{9,10},{10,1... | collective-permute-start | bytes 27656 | tf_op jit(solution)/shard_map/ppermute | solution.py:18
  9.5 4.9 %collective-permute-start.2 = (f32[18,1,128]{2,1,0:T(1,128)S(1)}, f32[18,1,128]{2,1,0:T(1,128)S(1)}, u32[]{:S(2)}, u32[]{:S(2)}) collective-permute-start(f32[18,1,128]{2,1,0:T(1,128)S(1)} %get-tuple-element.67), channel_id=1, source_target_pairs={{1,0},{2,1},{3,2},{4,3},{5,4},{6,5},{7,6},{0,7},{9,8},{10,9},{11,1... | collective-permute-start | bytes 27656 | tf_op jit(solution)/shard_map/ppermute | solution.py:20
  18.4 2.8 %copy-start.4 = (f32[19,19,1,1]{1,0,3,2:T(8,128)S(1)}, f32[19,19,1,1]{1,0,3,2:T(8,128)}, u32[]{:S(2)}) copy-start(f32[19,19,1,1]{1,0,3,2:T(8,128)} %constant.96) | copy-start | bytes 4336
  18.5 2.8 %copy-start.5 = (f32[19]{0:T(128)S(1)}, f32[19]{0:T(128)}, u32[]{:S(2)}) copy-start(f32[19]{0:T(128)} %constant.92.clone) | copy-start | bytes 232
  21.2 4.6 %copy-start.3 = (f32[19,19,1,1]{1,0,3,2:T(8,128)S(1)}, f32[19,19,1,1]{1,0,3,2:T(8,128)}, u32[]{:S(2)}) copy-start(f32[19,19,1,1]{1,0,3,2:T(8,128)} %constant.97) | copy-start | bytes 4336
  30.7 1.5 %copy-start.1 = (f32[16,16,19,128]{3,1,0,2:T(8,128)}, f32[16,16,19,128]{3,1,0,2:T(8,128)S(1)}, u32[]{:S(2)}) copy-start(f32[16,16,19,128]{3,1,0,2:T(8,128)S(1)} %bitcast_add_fusion) | copy-start | bytes 7471108
  32.2 7.3 %collective-permute-start.4 = (f32[1,16,16,128]{3,1,0,2:T(8,128)S(1)}, f32[1,16,16,128]{3,1,0,2:T(8,128)S(1)}, u32[]{:S(2)}, u32[]{:S(2)}) collective-permute-start(f32[1,16,16,128]{3,1,0,2:T(8,128)S(1)} %get-tuple-element.45), channel_id=1, source_target_pairs={{0,8},{8,16},{16,24},{24,0},{1,9},{9,17},{17,25},{25,1},{2,10},{10... | collective-permute-start | bytes 393224 | tf_op jit(solution)/shard_map/ppermute | solution.py:18
  34.6 7.0 %collective-permute-start.5 = (f32[1,16,16,128]{3,1,0,2:T(8,128)S(1)}, f32[1,16,16,128]{3,1,0,2:T(8,128)S(1)}, u32[]{:S(2)}, u32[]{:S(2)}) collective-permute-start(f32[1,16,16,128]{3,1,0,2:T(8,128)S(1)} %get-tuple-element.46), channel_id=1, source_target_pairs={{8,0},{16,8},{24,16},{0,24},{9,1},{17,9},{25,17},{1,25},{10,2},{18... | collective-permute-start | bytes 393224 | tf_op jit(solution)/shard_map/ppermute | solution.py:20
  41.8 4.8 %collective-permute-start.7 = (f32[18,1,16,128]{3,1,0,2:T(1,128)S(1)}, f32[18,1,16,128]{3,1,0,2:T(1,128)S(1)}, u32[]{:S(2)}, u32[]{:S(2)}) collective-permute-start(f32[18,1,16,128]{3,1,0,2:T(1,128)S(1)} %get-tuple-element.38), channel_id=1, source_target_pairs={{1,0},{2,1},{3,2},{4,3},{5,4},{6,5},{7,6},{0,7},{9,8},{10,9},{11,1... | collective-permute-start | bytes 442376 | tf_op jit(solution)/shard_map/ppermute | solution.py:20
  44.0 6.4 %collective-permute-start.6 = (f32[18,1,16,128]{3,1,0,2:T(1,128)S(1)}, f32[18,1,16,128]{3,1,0,2:T(1,128)S(1)}, u32[]{:S(2)}, u32[]{:S(2)}) collective-permute-start(f32[18,1,16,128]{3,1,0,2:T(1,128)S(1)} %get-tuple-element.37), channel_id=1, source_target_pairs={{0,1},{1,2},{2,3},{3,4},{4,5},{5,6},{6,7},{7,0},{8,9},{9,10},{10,1... | collective-permute-start | bytes 442376 | tf_op jit(solution)/shard_map/ppermute | solution.py:18
  64.6 4.3 %collective-permute-start.8 = (f32[4,16,2,32]{3,2,1,0:T(2,128)S(1)}, f32[4,16,2,32]{3,2,1,0:T(2,128)S(1)}, u32[]{:S(2)}, u32[]{:S(2)}) collective-permute-start(f32[4,16,2,32]{3,2,1,0:T(2,128)S(1)} %bitcast.248), channel_id=1, source_target_pairs={{0,8},{8,0},{16,24},{24,16},{1,9},{9,1},{17,25},{25,17},{2,10},{10... | collective-permute-start | bytes 49160 | tf_op jit(solution)/shard_map/ppermute | solution.py:28
  69.1 4.9 %collective-permute-start.9 = (f32[4,16,1,32]{3,1,0,2:T(8,128)S(1)}, f32[4,16,1,32]{3,1,0,2:T(8,128)S(1)}, u32[]{:S(2)}, u32[]{:S(2)}) collective-permute-start(f32[4,16,1,32]{3,1,0,2:T(8,128)S(1)} %bitcast.249), channel_id=1, source_target_pairs={{0,16},{8,24},{16,0},{24,8},{1,17},{9,25},{17,1},{25,9},{2,18},{10... | collective-permute-start | bytes 24584 | tf_op jit(solution)/shard_map/ppermute | solution.py:28
where the time goes:
time: 74.8 us; the launch traced here: 74.6 us
  matrix products  16.3 us (22%)
  other arithmetic  14.8 us (20%)
  starting transfers between devices  14.7 us (20%)
  waiting for transfers between devices  14.4 us (19%)
  local copies, waits for them, and re-layouts  13.3 us (18%)
  between operations  1.09 us (1%)
    unnamed x24, local copies, waits for them, and re-layouts  9.83 us
    ppermute x4, waiting for transfers between devices, extended(): lax.ppermute(tail, axis, [(i, (i + 1) % count) for i in range(count)])  8.85 us
    ppermute x4, starting transfers between devices, extended(): lax.ppermute(head, axis, [((i + 1) % count, i) for i in range(count)])  7.25 us
    unnamed x9, other arithmetic  6.8 us
    ppermute x4, starting transfers between devices, extended(): lax.ppermute(tail, axis, [(i, (i + 1) % count) for i in range(count)])  5.44 us
    dot_general x1, matrix products, collide(): jnp.einsum('pq,xyqz->xypz', relax_table, populations - balance, precision...  4.54 us
    dot_general x1, matrix products, collide(): jnp.einsum('pq,xyqz->xypz', source_table, guo_term, precision=lax.Precisi...  3.95 us
    ppermute x4, waiting for transfers between devices, extended(): lax.ppermute(head, axis, [((i + 1) % count, i) for i in range(count)])  3.25 us
  transfers between devices with their start and end apart: 10, of which 7 were waited for; matrix products, arithmetic and copies ran while one was open for 13% of the time, Pallas kernels for 0%

commit v1 on v0

--- a/solution.py
+++ b/solution.py
@@ -154,28 +154,90 @@
     return (reds, greens, blues)
 
 
+SIDES = [(-1, -1), (-1, 0), (-1, 1), (0, -1), (0, 1), (1, -1), (1, 0), (1, 1)]
+
+
+def from_side(slab, side):
+    sx, sy = side
+    nx = lax.axis_size("gx")
+    ny = lax.axis_size("gy")
+    if sx == 0:
+        return lax.ppermute(slab, "gy", [(j, (j - sy) % ny) for j in range(ny)])
+    if sy == 0:
+        return lax.ppermute(slab, "gx", [(i, (i - sx) % nx) for i in range(nx)])
+    pairs = []
+    for i in range(nx):
+        for j in range(ny):
+            pairs.append((i * ny + j, ((i - sx) % nx) * ny + (j - sy) % ny))
+    return lax.ppermute(slab, ("gx", "gy"), pairs)
+
+
+def side_range(s, n):
+    if s == -1:
+        return slice(n - 1, n)
+    if s == 1:
+        return slice(0, 1)
+    return slice(0, n)
+
+
+def exchange(cells, extent_x, extent_y):
+    got = {}
+    for side in SIDES:
+        slab = cells[side_range(side[0], extent_x), side_range(side[1], extent_y)]
+        got[side] = from_side(slab, side)
+    return got
+
+
+def padded_from(centre, got):
+    rows = []
+    for sx in (-1, 0, 1):
+        parts = []
+        for sy in (-1, 0, 1):
+            parts.append(centre if (sx, sy) == (0, 0) else got[(sx, sy)])
+        rows.append(jnp.concatenate(parts, axis=1))
+    return jnp.concatenate(rows, axis=0)
+
+
 def body(populations):
     velocities, weights, relaxing, forcing_map = lattice_tables()
     extent_x = populations.shape[0]
     extent_y = populations.shape[1]
-    read = []
     density = jnp.sum(populations, axis=2)
     potential = 1.0 - jnp.exp(-density)
-    padded = extended(potential, (("gx", 0), ("gy", 1)), 1)
+    padded = padded_from(potential, exchange(potential, extent_x, extent_y))
     forcing = attraction(padded, 1, extent_x, extent_y, velocities, weights)
     collided = collide(populations, density, forcing, velocities, weights, relaxing, forcing_map)
-    moving = jnp.concatenate([collided[:, :, 1:5], collided[:, :, 7:]], axis=2)
-    arriving = extended(moving, (("gx", 0), ("gy", 1)), 1)
+    wanted = {}
+    got = {}
+    for side in SIDES:
+        sx, sy = side
+        qs = [
+            q
+            for q in range(19)
+            if (sx == 0 or velocities[q][0] == -sx) and (sy == 0 or velocities[q][1] == -sy)
+        ]
+        wanted[side] = qs
+        slab = collided[side_range(sx, extent_x), side_range(sy, extent_y)][:, :, np.array(qs)]
+        got[side] = from_side(slab, side)
+    read = []
     for q in range(19):
-        steps = [int(v) for v in velocities[q]]
-        if q in (0, 5, 6):
-            column = collided[:, :, q]
-        else:
-            slot = q - 1 if q < 5 else q - 3
-            column = arriving[
-                1 - steps[0] : 1 - steps[0] + extent_x, 1 - steps[1] : 1 - steps[1] + extent_y, slot
-            ]
-        read.append(jnp.roll(column, steps[2], axis=2))
+        cx, cy, cz = [int(v) for v in velocities[q]]
+        column = collided[:, :, q]
+        if (cx, cy) != (0, 0):
+            pieces = {}
+            for side in SIDES:
+                if q in wanted[side]:
+                    pieces[side] = got[side][:, :, wanted[side].index(q)]
+                else:
+                    shape = (
+                        1 if side[0] else extent_x,
+                        1 if side[1] else extent_y,
+                        column.shape[2],
+                    )
+                    pieces[side] = jnp.zeros(shape, column.dtype)
+            whole = padded_from(column, pieces)
+            column = whole[1 - cx : 1 - cx + extent_x, 1 - cy : 1 - cy + extent_y]
+        read.append(jnp.roll(column, cz, axis=2))
     fresh = jnp.stack(read, axis=2)
     groups = lax.axis_size("gx")
     length_x = extent_x * groups
@@ -196,20 +258,23 @@
     block_len = depth_z // groups
     blocked = layered.reshape(4, extent_y, groups, block_len)
     position = lax.axis_index("gx")
-    current = blocked
-    for level in range(groups.bit_length() - 1):
-        parity = position // (1 << level) % 2
-        halves = current.shape[2] // 2
-        paired = current.reshape(4, extent_y, halves, 2, block_len)
-        lower = paired[:, :, :, 0]
-        upper = paired[:, :, :, 1]
-        kept = jnp.where(parity == 1, upper, lower)
-        handed = jnp.where(parity == 1, lower, upper)
-        partner = from_partner(handed, "gx", level)
-        nearer = jnp.where(parity == 0, kept, partner)
-        farther = jnp.where(parity == 0, partner, kept)
-        current = nearer + (1.0 - nearer[3:4]) * farther
-    picture = current.reshape(4, extent_y, block_len)
+    own = lax.dynamic_index_in_dim(blocked, position, 2, keepdims=False)
+    parts = [None] * groups
+    for shift in range(groups):
+        if shift == 0:
+            continue
+        target = (position + shift) % groups
+        outgoing = lax.dynamic_index_in_dim(blocked, target, 2, keepdims=False)
+        incoming = lax.ppermute(outgoing, "gx", [(i, (i + shift) % groups) for i in range(groups)])
+        parts[shift] = incoming
+    total = None
+    for source in range(groups):
+        shift = (position - source) % groups
+        piece = own
+        for s in range(1, groups):
+            piece = jnp.where(shift == s, parts[s], piece)
+        total = piece if total is None else total + (1.0 - total[3:4]) * piece
+    picture = total
     return (fresh, picture)
 
 

time: 74.8 us -> 110 us (1.47)
  starting transfers between devices: 14.7 us -> 30.4 us
  other arithmetic: 14.8 us -> 23.7 us
  waiting for transfers between devices: 14.4 us -> 19.6 us
  local copies, waits for them, and re-layouts: 13.3 us -> 17.8 us
    ppermute x10 -> x19, starting transfers between devices: 14.7 us -> 30.4 us  [the longest x8 11.6 us: from_side(): return lax.ppermute(slab, ('gx', 'gy'), pairs)]
    another operation x1, other arithmetic: 0.12 us -> 10.6 us  [body(): optical_depth = jnp.cumsum(extinction, axis=0) - extinction]
    gather x0 -> x5, local copies, waits for them, and re-layouts: none -> 8.95 us  [body(): collided[side_range(sx, extent_x), side_range(sy, extent_y)]]
    unnamed x24 -> x52, local copies, waits for them, and re-layouts: 9.83 us -> 1.77 us
    ppermute x10 -> x19, waiting for transfers between devices: 14.4 us -> 19.6 us  [the longest x8 10.6 us: from_side(): return lax.ppermute(slab, ('gx', 'gy'), pairs)]
    slice x13 -> x17, local copies, waits for them, and re-layouts: 1.15 us -> 3.73 us  [the longest x10 1.96 us: body(): read.append(jnp.roll(column, cz, axis=2))]
    concatenate x4 -> x9, other arithmetic: 0.38 us -> 1.93 us  [the longest x3 1.06 us: padded_from(): return jnp.concatenate(rows, axis=0)]
    reduce_sum x1 -> x0, other arithmetic: 1.46 us -> none  [body(): new_density = jnp.sum(fresh, axis=2)]
  transfers between devices with their start and end apart: 10 -> 19, of which waited for: 7 -> 8; matrix products, arithmetic and copies ran while one was open for 13% -> 19% of each run, Pallas kernels for 0% -> 0%
where the time goes in v1:
time: 110 us; the launch traced here: 109 us
  starting transfers between devices  30.4 us (28%)
  other arithmetic  23.7 us (22%)
  waiting for transfers between devices  19.6 us (18%)
  local copies, waits for them, and re-layouts  17.8 us (16%)
  matrix products  16.3 us (15%)
  between operations  1.56 us (1%)
    ppermute x8, starting transfers between devices, from_side(): return lax.ppermute(slab, ('gx', 'gy'), pairs)  11.6 us
    ppermute x8, waiting for transfers between devices, from_side(): return lax.ppermute(slab, ('gx', 'gy'), pairs)  10.6 us
    another operation x1, other arithmetic, body(): optical_depth = jnp.cumsum(extinction, axis=0) - extinction  10.6 us
    gather x5, local copies, waits for them, and re-layouts, body(): collided[side_range(sx, extent_x), side_range(sy, extent_y)]  8.95 us
    ppermute x4, starting transfers between devices, from_side(): return lax.ppermute(slab, 'gx', [(i, (i - sx) % nx) for i in range(nx)])  8.09 us
    ppermute x4, starting transfers between devices, from_side(): return lax.ppermute(slab, 'gy', [(j, (j - sy) % ny) for j in range(ny)])  7.07 us
    unnamed x17, other arithmetic  6.32 us
    dot_general x1, matrix products, collide(): jnp.einsum('pq,xyqz->xypz', relax_table, populations - balance, precision...  4.54 us
  transfers between devices with their start and end apart: 19, of which 8 were waited for; matrix products, arithmetic and copies ran while one was open for 19% of the time, Pallas kernels for 0%

profile of v1, /device:TPU:0, one launch (start us, length us, event | category | flops | bytes accessed | tf_op | source)
XLA Modules:
  0.0 109.3 jit_solution(15123521208263215735)
XLA Ops:
  0.7 2.0 %reduce_sum.123 = f32[16,16,128]{2,1,0:T(8,128)S(1)} reduce(f32[16,16,19,128]{3,1,2,0:T(8,128)} %param.21, f32[]{:T(128)} %constant.110.clone.1), dimensions={2}, to_apply=%region_0.0 | reduce | flops 589824 | bytes 2621444 | tf_op jit(solution)/shard_map/reduce_sum | solution.py:205
  2.8 2.4 %collective-permute-start.5 = (f32[1,1,128]{2,1,0:T(1,128)S(1)}, f32[1,1,128]{2,1,0:T(1,128)S(1)}, u32[]{:S(2)}, u32[]{:S(2)}) collective-permute-start(f32[1,1,128]{2,1,0:T(1,128)S(1)} %get-tuple-element.131), channel_id=1, source_target_pairs={{0,9},{1,10},{2,11},{3,12},{4,13},{5,14},{6,15},{7,8},{8,17},{9,18... | collective-permute-start | bytes 1544 | tf_op jit(solution)/shard_map/ppermute | solution.py:172
  5.2 1.7 %collective-permute-start = (f32[16,1,128]{2,1,0:T(1,128)S(1)}, f32[16,1,128]{2,1,0:T(1,128)S(1)}, u32[]{:S(2)}, u32[]{:S(2)}) collective-permute-start(f32[16,1,128]{2,1,0:T(1,128)S(1)} %get-tuple-element.137), channel_id=1, source_target_pairs={{0,1},{1,2},{2,3},{3,4},{4,5},{5,6},{6,7},{7,0},{8,9},{9,10},{10,1... | collective-permute-start | bytes 24584 | tf_op jit(solution)/shard_map/ppermute | solution.py:165
  7.0 1.9 %collective-permute-start.1 = (f32[16,1,128]{2,1,0:T(1,128)S(1)}, f32[16,1,128]{2,1,0:T(1,128)S(1)}, u32[]{:S(2)}, u32[]{:S(2)}) collective-permute-start(f32[16,1,128]{2,1,0:T(1,128)S(1)} %get-tuple-element.138), channel_id=1, source_target_pairs={{0,7},{1,0},{2,1},{3,2},{4,3},{5,4},{6,5},{7,6},{8,15},{9,8},{10,9... | collective-permute-start | bytes 24584 | tf_op jit(solution)/shard_map/ppermute | solution.py:165
  8.9 1.5 %collective-permute-start.6 = (f32[1,16,128]{2,1,0:T(8,128)S(1)}, f32[1,16,128]{2,1,0:T(8,128)S(1)}, u32[]{:S(2)}, u32[]{:S(2)}) collective-permute-start(f32[1,16,128]{2,1,0:T(8,128)S(1)} %get-tuple-element.135), channel_id=1, source_target_pairs={{0,8},{8,16},{16,24},{24,0},{1,9},{9,17},{17,25},{25,1},{2,10},{10... | collective-permute-start | bytes 24584 | tf_op jit(solution)/shard_map/ppermute | solution.py:167
  10.4 1.4 %collective-permute-start.3 = (f32[1,16,128]{2,1,0:T(8,128)S(1)}, f32[1,16,128]{2,1,0:T(8,128)S(1)}, u32[]{:S(2)}, u32[]{:S(2)}) collective-permute-start(f32[1,16,128]{2,1,0:T(8,128)S(1)} %get-tuple-element.136), channel_id=1, source_target_pairs={{0,24},{8,0},{16,8},{24,16},{1,25},{9,1},{17,9},{25,17},{2,26},{10... | collective-permute-start | bytes 24584 | tf_op jit(solution)/shard_map/ppermute | solution.py:167
  11.8 2.3 %fusion = f32[3,16,16,128]{3,0,2,1:T(4,128)S(1)} fusion(f32[19,3,1,1]{0,1,3,2:T(4,128)S(1)} %copy-done.14, f32[16,16,19,128]{3,1,2,0:T(8,128)S(1)} %copy-done), kind=kOutput, calls=%fused_computation.5 | convolution fusion | flops 22413312 | bytes 2883812 | tf_op jit(solution)/shard_map/qd,xyqz->dxyz/dot_general | solution.py:116
  14.4 3.8 %collective-permute-done.7 = f32[1,1,128]{2,1,0:T(1,128)S(1)} collective-permute-done((f32[1,1,128]{2,1,0:T(1,128)S(1)}, f32[1,1,128]{2,1,0:T(1,128)S(1)}, u32[]{:S(2)}, u32[]{:S(2)}) %collective-permute-start.7) | collective-permute-done | bytes 544 | tf_op jit(solution)/shard_map/ppermute | solution.py:172
  18.3 2.8 %collective-permute-start.4 = (f32[1,1,128]{2,1,0:T(1,128)S(1)}, f32[1,1,128]{2,1,0:T(1,128)S(1)}, u32[]{:S(2)}, u32[]{:S(2)}) collective-permute-start(f32[1,1,128]{2,1,0:T(1,128)S(1)} %get-tuple-element.133), channel_id=1, source_target_pairs={{0,31},{1,24},{2,25},{3,26},{4,27},{5,28},{6,29},{7,30},{8,7},{9,0... | collective-permute-start | bytes 1544 | tf_op jit(solution)/shard_map/ppermute | solution.py:172
  21.0 1.3 %collective-permute-done.4 = f32[1,1,128]{2,1,0:T(1,128)S(1)} collective-permute-done((f32[1,1,128]{2,1,0:T(1,128)S(1)}, f32[1,1,128]{2,1,0:T(1,128)S(1)}, u32[]{:S(2)}, u32[]{:S(2)}) %collective-permute-start.4) | collective-permute-done | bytes 544 | tf_op jit(solution)/shard_map/ppermute | solution.py:172
  22.3 0.2 collective-permute-start.2
  22.5 5.5 %collective-permute-done.2 = f32[1,1,128]{2,1,0:T(1,128)S(1)} collective-permute-done((f32[1,1,128]{2,1,0:T(1,128)S(1)}, f32[1,1,128]{2,1,0:T(1,128)S(1)}, u32[]{:S(2)}, u32[]{:S(2)}) %collective-permute-start.2) | collective-permute-done | bytes 544 | tf_op jit(solution)/shard_map/ppermute | solution.py:172
  28.1 0.1 fusion.127
  28.2 0.1 fusion.128
  28.4 0.2 fusion.84
  28.6 0.2 fusion.43
  28.8 0.2 pad_maximum_fusion.47
  29.0 0.4 fusion.94
  29.4 0.3 fusion.56
  29.8 2.7 %fusion.31 = f32[16,16,128,19]{2,3,1,0:T(8,128)S(1)} fusion(f32[19,3,1,1]{0,1,3,2:T(4,128)S(1)} %copy-done.14, f32[3,16,16,128]{3,2,1,0:T(8,128)S(1)} %get-tuple-element.64), kind=kOutput, calls=%fused_computation.41 | convolution fusion | flops 22413312 | bytes 2883812 | tf_op jit(solution)/shard_map/qd,dxyz->xyqz/dot_general | solution.py:118
  32.6 2.7 %fusion.29 = f32[16,16,128,19]{2,3,1,0:T(8,128)S(1)} fusion(f32[19,3,1,1]{0,1,3,2:T(4,128)S(1)} %copy-done.14, f32[3,16,16,128]{3,2,1,0:T(8,128)S(1)} %get-tuple-element.92), kind=kOutput, calls=%fused_computation.39 | convolution fusion | flops 22413312 | bytes 2883812 | tf_op jit(solution)/shard_map/qd,dxyz->xyqz/dot_general | solution.py:119
  35.4 4.5 %fusion.2 = f32[16,16,128,19]{2,3,1,0:T(8,128)S(1)} fusion(f32[19,19,1,1]{1,0,3,2:T(8,128)S(1)} %copy-done.16, f32[16,16,19,128]{3,1,2,0:T(8,128)S(1)} %copy-done, f32[16,16,128,19]{2,3,1,0:T(8,128)S(1)} %fusion.31, f32[16,16,128]{2,1,0:T(8,128)S(1)} %broadcast_multiply_fusion, f32[16,16,128]{2,1,0:T(8,128)S(1)} %reduce_sum.123, f32[19]{0:T(128)S(1)} %copy-done.19), kind=kOutput, calls=%fused_computation.8 | convolution fusion | flops 147554304 | bytes 7734768 | tf_op jit(solution)/shard_map/pq,xyqz->xypz/dot_general | solution.py:128
  39.9 3.9 %fusion.10 = f32[16,16,128,19]{2,3,1,0:T(8,128)S(1)} fusion(f32[19,19,1,1]{1,0,3,2:T(8,128)S(1)} %copy-done.15, f32[16,16,128,19]{2,3,1,0:T(8,128)S(1)} %fusion.29, f32[16,16,128,19]{2,3,1,0:T(8,128)S(1)} %fusion.31, f32[16,16,128]{2,1,0:T(8,128)S(1)} %get-tuple-element.59, f32[19]{0:T(128)S(1)} %copy-done.19), kind=kOutput, calls=%fused_computation.17 | convolution fusion | flops 145686528 | bytes 7603696 | tf_op jit(solution)/shard_map/pq,xyqz->xypz/dot_general | solution.py:131
  43.9 0.9 bitcast_add_fusion
  44.8 0.8 slice_bitcast_fusion
  45.6 0.9 fusion.126
  46.6 1.2 %slice_bitcast_fusion.2 = (f32[16,16,128]{2,1,0:T(8,128)S(1)}, f32[16,16,128]{2,1,0:T(8,128)S(1)}, f32[16,16,128]{2,1,0:T(8,128)S(1)}, f32[16,16,128]{2,1,0:T(8,...) fusion(f32[16,16,19,128]{3,1,0,2:T(8,128)S(1)} %bitcast_add_fusion), kind=kLoop, calls=%fused_computation.125 | loop fusion | bytes 4980736 | tf_op jit(solution)/shard_map/squeeze | solution.py:225
  47.7 1.5 %gather_fusion.3 = f32[5,16,128]{2,1,0:T(8,128)S(1)} fusion(f32[16,19,128]{2,0,1:T(8,128)} %bitcast.297, s32[1024]{0:T(1024)S(1)} %get-tuple-element.170), kind=kCustom, calls=%fused_computation.3 | custom fusion | bytes 81940 | tf_op jit(solution)/shard_map/gather | solution.py:220
  49.2 1.5 %collective-permute-start.11 = (f32[16,1,5,128]{3,0,2,1:T(8,128)S(1)}, f32[16,1,5,128]{3,0,2,1:T(8,128)S(1)}, u32[]{:S(2)}, u32[]{:S(2)}) collective-permute-start(f32[16,1,5,128]{3,0,2,1:T(8,128)S(1)} %bitcast.323), channel_id=1, source_target_pairs={{0,7},{1,0},{2,1},{3,2},{4,3},{5,4},{6,5},{7,6},{8,15},{9,8},{10,9... | collective-permute-start | bytes 122888 | tf_op jit(solution)/shard_map/ppermute | solution.py:165
  50.8 1.3 %fusion.125 = (f32[1,1,1,128]{3,1,0,2:T(1,128)}, f32[1,1,1,128]{3,1,0,2:T(1,128)}, f32[1,1,1,128]{3,1,0,2:T(1,128)}, f32[1,1,1,128]{3,1,0,2:T(1,128)}) fusion(f32[16,16,19,128]{3,1,0,2:T(8,128)} %copy-done.1), kind=kLoop, calls=%fused_computation.328 | loop fusion | bytes 4096 | tf_op jit(solution)/shard_map/gather | solution.py:220
  52.0 1.8 %collective-permute-start.15 = (f32[1,1,1,128]{3,1,0,2:T(1,128)}, f32[1,1,1,128]{3,1,0,2:T(1,128)S(1)}, u32[]{:S(2)}, u32[]{:S(2)}) collective-permute-start(f32[1,1,1,128]{3,1,0,2:T(1,128)} %get-tuple-element.84), channel_id=1, source_target_pairs={{0,25},{1,26},{2,27},{3,28},{4,29},{5,30},{6,31},{7,24},{8,1},{9,2... | collective-permute-start | bytes 1544 | tf_op jit(solution)/shard_map/ppermute | solution.py:172
  53.8 2.7 %collective-permute-start.14 = (f32[1,1,1,128]{3,1,0,2:T(1,128)}, f32[1,1,1,128]{3,1,0,2:T(1,128)S(1)}, u32[]{:S(2)}, u32[]{:S(2)}) collective-permute-start(f32[1,1,1,128]{3,1,0,2:T(1,128)} %get-tuple-element.85), channel_id=1, source_target_pairs={{0,15},{1,8},{2,9},{3,10},{4,11},{5,12},{6,13},{7,14},{8,23},{9,16... | collective-permute-start | bytes 1544 | tf_op jit(solution)/shard_map/ppermute | solution.py:172
  56.5 1.0 collective-permute-start.13
  57.4 0.8 collective-permute-start.12
  58.2 0.8 slice.635
  59.0 0.8 slice.632
  59.7 2.1 %gather_fusion.1 = f32[5,16,128]{2,1,0:T(8,128)} fusion(f32[16,19,128]{2,0,1:T(8,128)} %get-tuple-element.90, s32[1024]{0:T(1024)S(1)} %get-tuple-element.172), kind=kCustom, calls=%fused_computation.1 | custom fusion | bytes 81940 | tf_op jit(solution)/shard_map/gather | solution.py:220
  61.8 2.1 %gather_fusion = f32[5,16,128]{2,1,0:T(8,128)} fusion(f32[16,19,128]{2,0,1:T(8,128)} %get-tuple-element.91, s32[1024]{0:T(1024)S(1)} %get-tuple-element.173), kind=kCustom, calls=%fused_computation | custom fusion | bytes 81940 | tf_op jit(solution)/shard_map/gather | solution.py:220
  63.9 2.1 %gather_fusion.2 = f32[5,16,128]{2,1,0:T(8,128)} fusion(f32[16,19,128]{2,0,1:T(8,128)} %bitcast.296, s32[1024]{0:T(1024)S(1)} %get-tuple-element.171), kind=kCustom, calls=%fused_computation.2 | custom fusion | bytes 81940 | tf_op jit(solution)/shard_map/gather | solution.py:220
  66.0 1.9 %collective-permute-start.10 = (f32[16,1,5,128]{3,0,2,1:T(8,128)}, f32[16,1,5,128]{3,0,2,1:T(8,128)S(1)}, u32[]{:S(2)}, u32[]{:S(2)}) collective-permute-start(f32[16,1,5,128]{3,0,2,1:T(8,128)} %bitcast.48), channel_id=1, source_target_pairs={{0,1},{1,2},{2,3},{3,4},{4,5},{5,6},{6,7},{7,0},{8,9},{9,10},{10,1... | collective-permute-start | bytes 122888 | tf_op jit(solution)/shard_map/ppermute | solution.py:165
  68.0 3.7 %collective-permute-done.10 = f32[16,1,5,128]{3,0,2,1:T(8,128)S(1)} collective-permute-done((f32[16,1,5,128]{3,0,2,1:T(8,128)}, f32[16,1,5,128]{3,0,2,1:T(8,128)S(1)}, u32[]{:S(2)}, u32[]{:S(2)}) %collective-permute-start.10) | collective-permute-done | bytes 40992 | tf_op jit(solution)/shard_map/ppermute | solution.py:165
  71.7 3.1 %collective-permute-start.8 = (f32[1,16,5,128]{3,1,2,0:T(8,128)}, f32[1,16,5,128]{3,1,2,0:T(8,128)S(1)}, u32[]{:S(2)}, u32[]{:S(2)}) collective-permute-start(f32[1,16,5,128]{3,1,2,0:T(8,128)} %bitcast.324), channel_id=1, source_target_pairs={{0,8},{8,16},{16,24},{24,0},{1,9},{9,17},{17,25},{25,1},{2,10},{10... | collective-permute-start | bytes 122888 | tf_op jit(solution)/shard_map/ppermute | solution.py:167
  75.0 0.1 fusion.41
  75.2 2.8 %collective-permute-done.8 = f32[1,16,5,128]{3,1,2,0:T(8,128)S(1)} collective-permute-done((f32[1,16,5,128]{3,1,2,0:T(8,128)}, f32[1,16,5,128]{3,1,2,0:T(8,128)S(1)}, u32[]{:S(2)}, u32[]{:S(2)}) %collective-permute-start.8) | collective-permute-done | bytes 40992 | tf_op jit(solution)/shard_map/ppermute | solution.py:167
  78.0 2.0 %collective-permute-start.9 = (f32[1,16,5,128]{3,1,2,0:T(8,128)}, f32[1,16,5,128]{3,1,2,0:T(8,128)S(1)}, u32[]{:S(2)}, u32[]{:S(2)}) collective-permute-start(f32[1,16,5,128]{3,1,2,0:T(8,128)} %bitcast.322), channel_id=1, source_target_pairs={{0,24},{8,0},{16,8},{24,16},{1,25},{9,1},{17,9},{25,17},{2,26},{10... | collective-permute-start | bytes 122888 | tf_op jit(solution)/shard_map/ppermute | solution.py:167
  80.1 0.9 fusion.36
  81.0 0.9 bitcast_dynamic-update-slice_fusion.17
  81.9 0.3 collective-permute-done.9
  82.2 0.9 bitcast_dynamic-update-slice_fusion.16
  83.2 0.9 bitcast_dynamic-update-slice_fusion.15
  84.4 0.7 bitcast_dynamic-update-slice_fusion.11
  85.1 0.9 bitcast_dynamic-update-slice_fusion.10
  86.0 0.9 bitcast_dynamic-update-slice_fusion.9
  88.3 0.1 bitcast_dynamic-update-slice_fusion.2
  88.4 10.6 %multiply_reduce_fusion.2 = (f32[16,128]{1,0:T(8,128)}, f32[16,128]{1,0:T(8,128)}, f32[16,128]{1,0:T(8,128)S(1)}, f32[16,128]{1,0:T(8,128)S(1)}) fusion(f32[16,1,128]{2,1,0:T(1,128)S(1)} %bitcast.299, f32[16,16,128]{2,1,0:T(8,128)S(1)} %get-tuple-element.65, f32[16,16,1]{2,1,0:T(8,128)S(1)} %fusion.39, f32[16,16,128]{2,1,0:T(8,128)S(1)} %get-tuple-element.66, ...), kind=kOutput, calls=%fused_computation.272 | output fusion | flops 5365760 | bytes 7918592 | tf_op jit(solution)/shard_map/jit(cumsum)/reduce_window_sum | solution.py:246
  99.2 0.8 stack.105
  100.0 0.8 stack.104
  100.9 0.1 constant_dynamic-slice_fusion
  101.1 2.0 %collective-permute-start.18 = (f32[4,16,32]{2,1,0:T(8,128)S(1)}, f32[4,16,32]{2,1,0:T(8,128)S(1)}, u32[]{:S(2)}, u32[]{:S(2)}) collective-permute-start(f32[4,16,32]{2,1,0:T(8,128)S(1)} %bitcast.327), channel_id=1, source_target_pairs={{0,8},{8,16},{16,24},{24,0},{1,9},{9,17},{17,25},{25,1},{2,10},{10... | collective-permute-start | bytes 24584 | tf_op jit(solution)/shard_map/ppermute | solution.py:268
  103.1 1.5 %collective-permute-start.17 = (f32[4,16,32]{2,1,0:T(8,128)S(1)}, f32[4,16,32]{2,1,0:T(8,128)S(1)}, u32[]{:S(2)}, u32[]{:S(2)}) collective-permute-start(f32[4,16,32]{2,1,0:T(8,128)S(1)} %bitcast.326), channel_id=1, source_target_pairs={{0,16},{8,24},{16,0},{24,8},{1,17},{9,25},{17,1},{25,9},{2,18},{10... | collective-permute-start | bytes 24584 | tf_op jit(solution)/shard_map/ppermute | solution.py:268
  104.7 1.6 %copy.394 = f32[16,16,19,128]{3,1,2,0:T(8,128)} copy(f32[16,16,19,128]{3,1,0,2:T(8,128)S(1)} %bitcast_dynamic-update-slice_fusion) | data formatting | bytes 4980736
  106.4 0.6 collective-permute-done.17
  107.0 1.5 %collective-permute-done.16 = f32[4,16,32]{2,1,0:T(8,128)S(1)} collective-permute-done((f32[4,16,32]{2,1,0:T(8,128)S(1)}, f32[4,16,32]{2,1,0:T(8,128)S(1)}, u32[]{:S(2)}, u32[]{:S(2)}) %collective-permute-start.16) | collective-permute-done | bytes 8224 | tf_op jit(solution)/shard_map/ppermute | solution.py:268
  108.6 0.6 multiply_add_fusion
  (112 shorter events, 2.6 us)
Async XLA Ops:
  0.6 11.2 %copy-start.14 = (f32[19,3,1,1]{0,1,3,2:T(4,128)S(1)}, f32[19,3,1,1]{0,1,3,2:T(4,128)}, u32[]{:S(2)}) copy-start(f32[19,3,1,1]{0,1,3,2:T(4,128)} %constant.242) | copy-start | bytes 688
  0.6 11.2 %copy-start = (f32[16,16,19,128]{3,1,2,0:T(8,128)S(1)}, f32[16,16,19,128]{3,1,2,0:T(8,128)}, u32[]{:S(2)}) copy-start(f32[16,16,19,128]{3,1,2,0:T(8,128)} %param.21) | copy-start | bytes 7471108
  2.7 11.5 %copy-start.22 = (s32[5]{0:T(128)S(1)}, s32[5]{0:T(128)}, u32[]{:S(2)}) copy-start(s32[5]{0:T(128)} %constant.239) | copy-start | bytes 64
  2.7 11.5 %copy-start.23 = (s32[5]{0:T(128)S(1)}, s32[5]{0:T(128)}, u32[]{:S(2)}) copy-start(s32[5]{0:T(128)} %constant.238) | copy-start | bytes 64
  2.7 11.5 %copy-start.20 = (s32[5]{0:T(128)S(1)}, s32[5]{0:T(128)}, u32[]{:S(2)}) copy-start(s32[5]{0:T(128)} %constant.241) | copy-start | bytes 64
  2.7 11.5 %copy-start.21 = (s32[5]{0:T(128)S(1)}, s32[5]{0:T(128)}, u32[]{:S(2)}) copy-start(s32[5]{0:T(128)} %constant.240) | copy-start | bytes 64
  2.8 11.6 %collective-permute-start.5 = (f32[1,1,128]{2,1,0:T(1,128)S(1)}, f32[1,1,128]{2,1,0:T(1,128)S(1)}, u32[]{:S(2)}, u32[]{:S(2)}) collective-permute-start(f32[1,1,128]{2,1,0:T(1,128)S(1)} %get-tuple-element.131), channel_id=1, source_target_pairs={{0,9},{1,10},{2,11},{3,12},{4,13},{5,14},{6,15},{7,8},{8,17},{9,18... | collective-permute-start | bytes 1544 | tf_op jit(solution)/shard_map/ppermute | solution.py:172
  5.2 22.8 %collective-permute-start = (f32[16,1,128]{2,1,0:T(1,128)S(1)}, f32[16,1,128]{2,1,0:T(1,128)S(1)}, u32[]{:S(2)}, u32[]{:S(2)}) collective-permute-start(f32[16,1,128]{2,1,0:T(1,128)S(1)} %get-tuple-element.137), channel_id=1, source_target_pairs={{0,1},{1,2},{2,3},{3,4},{4,5},{5,6},{6,7},{7,0},{8,9},{9,10},{10,1... | collective-permute-start | bytes 24584 | tf_op jit(solution)/shard_map/ppermute | solution.py:165
  7.0 21.0 %collective-permute-start.1 = (f32[16,1,128]{2,1,0:T(1,128)S(1)}, f32[16,1,128]{2,1,0:T(1,128)S(1)}, u32[]{:S(2)}, u32[]{:S(2)}) collective-permute-start(f32[16,1,128]{2,1,0:T(1,128)S(1)} %get-tuple-element.138), channel_id=1, source_target_pairs={{0,7},{1,0},{2,1},{3,2},{4,3},{5,4},{6,5},{7,6},{8,15},{9,8},{10,9... | collective-permute-start | bytes 24584 | tf_op jit(solution)/shard_map/ppermute | solution.py:165
  8.9 19.1 %collective-permute-start.6 = (f32[1,16,128]{2,1,0:T(8,128)S(1)}, f32[1,16,128]{2,1,0:T(8,128)S(1)}, u32[]{:S(2)}, u32[]{:S(2)}) collective-permute-start(f32[1,16,128]{2,1,0:T(8,128)S(1)} %get-tuple-element.135), channel_id=1, source_target_pairs={{0,8},{8,16},{16,24},{24,0},{1,9},{9,17},{17,25},{25,1},{2,10},{10... | collective-permute-start | bytes 24584 | tf_op jit(solution)/shard_map/ppermute | solution.py:167
  10.4 17.6 %collective-permute-start.3 = (f32[1,16,128]{2,1,0:T(8,128)S(1)}, f32[1,16,128]{2,1,0:T(8,128)S(1)}, u32[]{:S(2)}, u32[]{:S(2)}) collective-permute-start(f32[1,16,128]{2,1,0:T(8,128)S(1)} %get-tuple-element.136), channel_id=1, source_target_pairs={{0,24},{8,0},{16,8},{24,16},{1,25},{9,1},{17,9},{25,17},{2,26},{10... | collective-permute-start | bytes 24584 | tf_op jit(solution)/shard_map/ppermute | solution.py:167
  14.3 3.9 %collective-permute-start.7 = (f32[1,1,128]{2,1,0:T(1,128)S(1)}, f32[1,1,128]{2,1,0:T(1,128)S(1)}, u32[]{:S(2)}, u32[]{:S(2)}) collective-permute-start(f32[1,1,128]{2,1,0:T(1,128)S(1)} %get-tuple-element.132), channel_id=1, source_target_pairs={{0,15},{1,8},{2,9},{3,10},{4,11},{5,12},{6,13},{7,14},{8,23},{9,16... | collective-permute-start | bytes 1544 | tf_op jit(solution)/shard_map/ppermute | solution.py:172
  18.3 4.1 %collective-permute-start.4 = (f32[1,1,128]{2,1,0:T(1,128)S(1)}, f32[1,1,128]{2,1,0:T(1,128)S(1)}, u32[]{:S(2)}, u32[]{:S(2)}) collective-permute-start(f32[1,1,128]{2,1,0:T(1,128)S(1)} %get-tuple-element.133), channel_id=1, source_target_pairs={{0,31},{1,24},{2,25},{3,26},{4,27},{5,28},{6,29},{7,30},{8,7},{9,0... | collective-permute-start | bytes 1544 | tf_op jit(solution)/shard_map/ppermute | solution.py:172
  22.3 5.7 %collective-permute-start.2 = (f32[1,1,128]{2,1,0:T(1,128)S(1)}, f32[1,1,128]{2,1,0:T(1,128)S(1)}, u32[]{:S(2)}, u32[]{:S(2)}) collective-permute-start(f32[1,1,128]{2,1,0:T(1,128)S(1)} %get-tuple-element.134), channel_id=1, source_target_pairs={{0,25},{1,26},{2,27},{3,28},{4,29},{5,30},{6,31},{7,24},{8,1},{9,2... | collective-permute-start | bytes 1544 | tf_op jit(solution)/shard_map/ppermute | solution.py:172
  32.6 2.8 %copy-start.16 = (f32[19,19,1,1]{1,0,3,2:T(8,128)S(1)}, f32[19,19,1,1]{1,0,3,2:T(8,128)}, u32[]{:S(2)}) copy-start(f32[19,19,1,1]{1,0,3,2:T(8,128)} %constant.243) | copy-start | bytes 4336
  32.6 2.8 %copy-start.19 = (f32[19]{0:T(128)S(1)}, f32[19]{0:T(128)}, u32[]{:S(2)}) copy-start(f32[19]{0:T(128)} %constant.137.clone) | copy-start | bytes 232
  35.3 4.6 %copy-start.15 = (f32[19,19,1,1]{1,0,3,2:T(8,128)S(1)}, f32[19,19,1,1]{1,0,3,2:T(8,128)}, u32[]{:S(2)}) copy-start(f32[19,19,1,1]{1,0,3,2:T(8,128)} %constant.244) | copy-start | bytes 4336
  44.8 2.9 %copy-start.1 = (f32[16,16,19,128]{3,1,0,2:T(8,128)}, f32[16,16,19,128]{3,1,0,2:T(8,128)S(1)}, u32[]{:S(2)}) copy-start(f32[16,16,19,128]{3,1,0,2:T(8,128)S(1)} %bitcast_add_fusion) | copy-start | bytes 7471108
  49.2 16.8 %collective-permute-start.11 = (f32[16,1,5,128]{3,0,2,1:T(8,128)S(1)}, f32[16,1,5,128]{3,0,2,1:T(8,128)S(1)}, u32[]{:S(2)}, u32[]{:S(2)}) collective-permute-start(f32[16,1,5,128]{3,0,2,1:T(8,128)S(1)} %bitcast.323), channel_id=1, source_target_pairs={{0,7},{1,0},{2,1},{3,2},{4,3},{5,4},{6,5},{7,6},{8,15},{9,8},{10,9... | collective-permute-start | bytes 122888 | tf_op jit(solution)/shard_map/ppermute | solution.py:165
  52.0 35.6 %collective-permute-start.15 = (f32[1,1,1,128]{3,1,0,2:T(1,128)}, f32[1,1,1,128]{3,1,0,2:T(1,128)S(1)}, u32[]{:S(2)}, u32[]{:S(2)}) collective-permute-start(f32[1,1,1,128]{3,1,0,2:T(1,128)} %get-tuple-element.84), channel_id=1, source_target_pairs={{0,25},{1,26},{2,27},{3,28},{4,29},{5,30},{6,31},{7,24},{8,1},{9,2... | collective-permute-start | bytes 1544 | tf_op jit(solution)/shard_map/ppermute | solution.py:172
  53.8 32.2 %collective-permute-start.14 = (f32[1,1,1,128]{3,1,0,2:T(1,128)}, f32[1,1,1,128]{3,1,0,2:T(1,128)S(1)}, u32[]{:S(2)}, u32[]{:S(2)}) collective-permute-start(f32[1,1,1,128]{3,1,0,2:T(1,128)} %get-tuple-element.85), channel_id=1, source_target_pairs={{0,15},{1,8},{2,9},{3,10},{4,11},{5,12},{6,13},{7,14},{8,23},{9,16... | collective-permute-start | bytes 1544 | tf_op jit(solution)/shard_map/ppermute | solution.py:172
  56.5 28.6 %collective-permute-start.13 = (f32[1,1,1,128]{3,1,0,2:T(1,128)}, f32[1,1,1,128]{3,1,0,2:T(1,128)}, u32[]{:S(2)}, u32[]{:S(2)}) collective-permute-start(f32[1,1,1,128]{3,1,0,2:T(1,128)} %get-tuple-element.86), channel_id=1, source_target_pairs={{0,31},{1,24},{2,25},{3,26},{4,27},{5,28},{6,29},{7,30},{8,7},{9,0... | collective-permute-start | bytes 1544 | tf_op jit(solution)/shard_map/ppermute | solution.py:172
  57.4 26.9 %collective-permute-start.12 = (f32[1,1,1,128]{3,1,0,2:T(1,128)}, f32[1,1,1,128]{3,1,0,2:T(1,128)}, u32[]{:S(2)}, u32[]{:S(2)}) collective-permute-start(f32[1,1,1,128]{3,1,0,2:T(1,128)} %get-tuple-element.87), channel_id=1, source_target_pairs={{0,9},{1,10},{2,11},{3,12},{4,13},{5,14},{6,15},{7,8},{8,17},{9,18... | collective-permute-start | bytes 1544 | tf_op jit(solution)/shard_map/ppermute | solution.py:172
  66.0 18.1 %copy-start.5 = (f32[16,16,128]{2,1,0:T(8,128)S(1)}, f32[16,16,128]{2,1,0:T(8,128)}, u32[]{:S(2)}) copy-start(f32[16,16,128]{2,1,0:T(8,128)} %get-tuple-element.79) | copy-start | bytes 393220
  66.0 18.2 %copy-start.10 = (f32[16,16,1]{2,1,0:T(8,128)S(1)}, f32[16,16,1]{2,1,0:T(8,128)}, u32[]{:S(2)}) copy-start(f32[16,16,1]{2,1,0:T(8,128)} %slice.632) | copy-start | bytes 3076
  66.0 18.3 %copy-start.9 = (f32[16,16,127]{2,1,0:T(8,128)S(1)}, f32[16,16,127]{2,1,0:T(8,128)}, u32[]{:S(2)}) copy-start(f32[16,16,127]{2,1,0:T(8,128)} %slice.635) | copy-start | bytes 390148
  66.0 18.4 %copy-start.4 = (f32[16,16,128]{2,1,0:T(8,128)S(1)}, f32[16,16,128]{2,1,0:T(8,128)}, u32[]{:S(2)}) copy-start(f32[16,16,128]{2,1,0:T(8,128)} %get-tuple-element.76) | copy-start | bytes 393220
  66.0 21.0 %copy-start.11 = (f32[16,16,128]{2,1,0:T(8,128)S(1)}, f32[16,16,128]{2,1,0:T(8,128)}, u32[]{:S(2)}) copy-start(f32[16,16,128]{2,1,0:T(8,128)} %get-tuple-element.69) | copy-start | bytes 393220
  66.0 21.0 %copy-start.12 = (f32[16,16,128]{2,1,0:T(8,128)S(1)}, f32[16,16,128]{2,1,0:T(8,128)}, u32[]{:S(2)}) copy-start(f32[16,16,128]{2,1,0:T(8,128)} %get-tuple-element.71) | copy-start | bytes 393220
  66.0 21.0 %copy-start.13 = (f32[16,16,128]{2,1,0:T(8,128)S(1)}, f32[16,16,128]{2,1,0:T(8,128)}, u32[]{:S(2)}) copy-start(f32[16,16,128]{2,1,0:T(8,128)} %get-tuple-element.72) | copy-start | bytes 393220
  66.0 5.7 %collective-permute-start.10 = (f32[16,1,5,128]{3,0,2,1:T(8,128)}, f32[16,1,5,128]{3,0,2,1:T(8,128)S(1)}, u32[]{:S(2)}, u32[]{:S(2)}) collective-permute-start(f32[16,1,5,128]{3,0,2,1:T(8,128)} %bitcast.48), channel_id=1, source_target_pairs={{0,1},{1,2},{2,3},{3,4},{4,5},{5,6},{6,7},{7,0},{8,9},{9,10},{10,1... | collective-permute-start | bytes 122888 | tf_op jit(solution)/shard_map/ppermute | solution.py:165
  71.7 6.3 %collective-permute-start.8 = (f32[1,16,5,128]{3,1,2,0:T(8,128)}, f32[1,16,5,128]{3,1,2,0:T(8,128)S(1)}, u32[]{:S(2)}, u32[]{:S(2)}) collective-permute-start(f32[1,16,5,128]{3,1,2,0:T(8,128)} %bitcast.324), channel_id=1, source_target_pairs={{0,8},{8,16},{16,24},{24,0},{1,9},{9,17},{17,25},{25,1},{2,10},{10... | collective-permute-start | bytes 122888 | tf_op jit(solution)/shard_map/ppermute | solution.py:167
  78.0 4.2 %collective-permute-start.9 = (f32[1,16,5,128]{3,1,2,0:T(8,128)}, f32[1,16,5,128]{3,1,2,0:T(8,128)S(1)}, u32[]{:S(2)}, u32[]{:S(2)}) collective-permute-start(f32[1,16,5,128]{3,1,2,0:T(8,128)} %bitcast.322), channel_id=1, source_target_pairs={{0,24},{8,0},{16,8},{24,16},{1,25},{9,1},{17,9},{25,17},{2,26},{10... | collective-permute-start | bytes 122888 | tf_op jit(solution)/shard_map/ppermute | solution.py:167
  86.0 2.1 %copy-start.18 = (f32[1,1,1,128]{3,1,0,2:T(1,128)}, f32[1,1,1,128]{3,1,0,2:T(1,128)S(1)}, u32[]{:S(2)}) copy-start(f32[1,1,1,128]{3,1,0,2:T(1,128)S(1)} %collective-permute-done.14) | copy-start | bytes 1540
  87.1 1.3 %copy-start.2 = (f32[16,16,128]{2,1,0:T(8,128)S(1)}, f32[16,16,128]{2,1,0:T(8,128)}, u32[]{:S(2)}) copy-start(f32[16,16,128]{2,1,0:T(8,128)} %get-tuple-element.74) | copy-start | bytes 393220
  87.1 1.3 %copy-start.3 = (f32[16,16,128]{2,1,0:T(8,128)S(1)}, f32[16,16,128]{2,1,0:T(8,128)}, u32[]{:S(2)}) copy-start(f32[16,16,128]{2,1,0:T(8,128)} %get-tuple-element.75) | copy-start | bytes 393220
  87.1 1.3 %copy-start.6 = (f32[16,16,128]{2,1,0:T(8,128)S(1)}, f32[16,16,128]{2,1,0:T(8,128)}, u32[]{:S(2)}) copy-start(f32[16,16,128]{2,1,0:T(8,128)} %get-tuple-element.80) | copy-start | bytes 393220
  87.1 1.3 %copy-start.7 = (f32[16,16,128]{2,1,0:T(8,128)S(1)}, f32[16,16,128]{2,1,0:T(8,128)}, u32[]{:S(2)}) copy-start(f32[16,16,128]{2,1,0:T(8,128)} %get-tuple-element.81) | copy-start | bytes 393220
  87.1 1.3 %copy-start.8 = (f32[16,16,128]{2,1,0:T(8,128)S(1)}, f32[16,16,128]{2,1,0:T(8,128)}, u32[]{:S(2)}) copy-start(f32[16,16,128]{2,1,0:T(8,128)} %get-tuple-element.82) | copy-start | bytes 393220
  87.6 0.6 copy-start.17
  101.1 5.3 %collective-permute-start.18 = (f32[4,16,32]{2,1,0:T(8,128)S(1)}, f32[4,16,32]{2,1,0:T(8,128)S(1)}, u32[]{:S(2)}, u32[]{:S(2)}) collective-permute-start(f32[4,16,32]{2,1,0:T(8,128)S(1)} %bitcast.327), channel_id=1, source_target_pairs={{0,8},{8,16},{16,24},{24,0},{1,9},{9,17},{17,25},{25,1},{2,10},{10... | collective-permute-start | bytes 24584 | tf_op jit(solution)/shard_map/ppermute | solution.py:268
  103.1 3.9 %collective-permute-start.17 = (f32[4,16,32]{2,1,0:T(8,128)S(1)}, f32[4,16,32]{2,1,0:T(8,128)S(1)}, u32[]{:S(2)}, u32[]{:S(2)}) collective-permute-start(f32[4,16,32]{2,1,0:T(8,128)S(1)} %bitcast.326), channel_id=1, source_target_pairs={{0,16},{8,24},{16,0},{24,8},{1,17},{9,25},{17,1},{25,9},{2,18},{10... | collective-permute-start | bytes 24584 | tf_op jit(solution)/shard_map/ppermute | solution.py:268
  104.6 3.9 %collective-permute-start.16 = (f32[4,16,32]{2,1,0:T(8,128)S(1)}, f32[4,16,32]{2,1,0:T(8,128)S(1)}, u32[]{:S(2)}, u32[]{:S(2)}) collective-permute-start(f32[4,16,32]{2,1,0:T(8,128)S(1)} %bitcast.325), channel_id=1, source_target_pairs={{0,24},{8,0},{16,8},{24,16},{1,25},{9,1},{17,9},{25,17},{2,26},{10... | collective-permute-start | bytes 24584 | tf_op jit(solution)/shard_map/ppermute | solution.py:268

commit v2 on v0

--- a/solution.py
+++ b/solution.py
@@ -154,32 +154,87 @@
     return (reds, greens, blues)
 
 
+def shift_ring(x, axis, step):
+    count = lax.axis_size(axis)
+    return lax.ppermute(x, axis, [(i, (i - step) % count) for i in range(count)])
+
+
+def collide_major(f, rho, force, velocities, weights, relaxing, forcing_map):
+    lattice = velocities.astype(np.float32)
+    extra = (1,) * rho.ndim
+    cx = jnp.asarray(lattice[:, 0]).reshape((19,) + extra)
+    cy = jnp.asarray(lattice[:, 1]).reshape((19,) + extra)
+    cz = jnp.asarray(lattice[:, 2]).reshape((19,) + extra)
+    spread = jnp.asarray(weights.astype(np.float32)).reshape((19,) + extra)
+    momentum = [
+        sum(f[q] * float(velocities[q][d]) for q in range(19) if velocities[q][d] != 0)
+        for d in range(3)
+    ]
+    drift = [(momentum[d] + 0.5 * force[d]) / rho for d in range(3)]
+    along = cx * drift[0] + cy * drift[1] + cz * drift[2]
+    pushed = cx * force[0] + cy * force[1] + cz * force[2]
+    speed_squared = drift[0] * drift[0] + drift[1] * drift[1] + drift[2] * drift[2]
+    work_done = drift[0] * force[0] + drift[1] * force[1] + drift[2] * force[2]
+    balance = spread * rho * (1.0 + 3.0 * along + 4.5 * along * along - 1.5 * speed_squared)
+    guo_term = spread * (3.0 * (pushed - work_done) + 9.0 * along * pushed)
+    relax_table = jnp.asarray(relaxing, dtype=jnp.float32)
+    source_table = jnp.asarray(forcing_map, dtype=jnp.float32)
+    relaxed = jnp.einsum("pq,q...->p...", relax_table, f - balance, precision=lax.Precision.HIGHEST)
+    sourced = jnp.einsum("pq,q...->p...", source_table, guo_term, precision=lax.Precision.HIGHEST)
+    return f - relaxed + sourced
+
+
 def body(populations):
     velocities, weights, relaxing, forcing_map = lattice_tables()
     extent_x = populations.shape[0]
     extent_y = populations.shape[1]
+    f = jnp.transpose(populations, (2, 0, 1, 3))
+    potential = 1.0 - jnp.exp(-jnp.sum(f, axis=0))
+    to_next = jnp.concatenate([f[:, extent_x - 1], potential[extent_x - 1 : extent_x], potential[extent_x - 2 : extent_x - 1]])
+    to_prev = jnp.concatenate([f[:, 0], potential[0:1], potential[1:2]])
+    from_prev = shift_ring(to_next, "gx", -1)
+    from_next = shift_ring(to_prev, "gx", 1)
+    fx = jnp.concatenate([from_prev[None, :19].transpose(1, 0, 2, 3), f, from_next[None, :19].transpose(1, 0, 2, 3)], axis=1)
+    px = jnp.concatenate([from_prev[20:21], from_prev[19:20], potential, from_next[19:20], from_next[20:21]], axis=0)
+    zero_x = jnp.zeros((19, 1, fx.shape[3]), f.dtype)
+
+    def y_message(row_pop, row_near, row_far):
+        pops = jnp.concatenate([zero_x, fx[:, :, row_pop], zero_x], axis=1)
+        return jnp.concatenate([pops, px[None, :, row_near], px[None, :, row_far]], axis=0)
+
+    from_below = shift_ring(y_message(extent_y - 1, extent_y - 1, extent_y - 2), "gy", -1)
+    from_above = shift_ring(y_message(0, 0, 1), "gy", 1)
+    fxy = jnp.concatenate(
+        [from_below[:19, 1:-1, None], fx, from_above[:19, 1:-1, None]], axis=2
+    )
+    pxy = jnp.concatenate(
+        [from_below[20][:, None], from_below[19][:, None], px, from_above[19][:, None], from_above[20][:, None]],
+        axis=1,
+    )
+    ext_x = extent_x + 2
+    ext_y = extent_y + 2
+    centre = pxy[1 : 1 + ext_x, 1 : 1 + ext_y]
+    totals = [jnp.zeros_like(centre), jnp.zeros_like(centre), jnp.zeros_like(centre)]
+    for q in range(1, 19):
+        steps = [int(v) for v in velocities[q]]
+        neighbour = pxy[1 + steps[0] : 1 + steps[0] + ext_x, 1 + steps[1] : 1 + steps[1] + ext_y]
+        neighbour = jnp.roll(neighbour, -steps[2], axis=2)
+        for d in range(3):
+            if steps[d] != 0:
+                totals[d] = totals[d] + weights[q] * steps[d] * neighbour
+    force = [-cohesion * centre * totals[d] for d in range(3)]
+    rho = jnp.sum(fxy, axis=0)
+    collided = collide_major(fxy, rho, force, velocities, weights, relaxing, forcing_map)
     read = []
-    density = jnp.sum(populations, axis=2)
-    potential = 1.0 - jnp.exp(-density)
-    padded = extended(potential, (("gx", 0), ("gy", 1)), 1)
-    forcing = attraction(padded, 1, extent_x, extent_y, velocities, weights)
-    collided = collide(populations, density, forcing, velocities, weights, relaxing, forcing_map)
-    moving = jnp.concatenate([collided[:, :, 1:5], collided[:, :, 7:]], axis=2)
-    arriving = extended(moving, (("gx", 0), ("gy", 1)), 1)
     for q in range(19):
-        steps = [int(v) for v in velocities[q]]
-        if q in (0, 5, 6):
-            column = collided[:, :, q]
-        else:
-            slot = q - 1 if q < 5 else q - 3
-            column = arriving[
-                1 - steps[0] : 1 - steps[0] + extent_x, 1 - steps[1] : 1 - steps[1] + extent_y, slot
-            ]
-        read.append(jnp.roll(column, steps[2], axis=2))
-    fresh = jnp.stack(read, axis=2)
+        cx, cy, cz = [int(v) for v in velocities[q]]
+        column = collided[q, 1 - cx : 1 - cx + extent_x, 1 - cy : 1 - cy + extent_y]
+        read.append(jnp.roll(column, cz, axis=2))
+    fresh_major = jnp.stack(read, axis=0)
+    fresh = jnp.transpose(fresh_major, (1, 2, 0, 3))
     groups = lax.axis_size("gx")
     length_x = extent_x * groups
-    new_density = jnp.sum(fresh, axis=2)
+    new_density = jnp.sum(fresh_major, axis=0)
     extinction = optical * new_density / length_x
     optical_depth = jnp.cumsum(extinction, axis=0) - extinction
     weight_map = jnp.exp(-optical_depth) * (1.0 - jnp.exp(-extinction))

time: 74.8 us -> 83.3 us (1.11)
  local copies, waits for them, and re-layouts: 13.3 us -> 27.9 us
  other arithmetic: 14.8 us -> 22.1 us
  matrix products: 16.3 us -> 9.15 us
  starting transfers between devices: 14.7 us -> 9.7 us
  waiting for transfers between devices: 14.4 us -> 12.7 us
    dot_general x5 -> x2, matrix products: 16.3 us -> 9.15 us  [the longest x1 5.08 us: collide_major(): jnp.einsum('pq,q...->p...', relax_table, f - balance, precision=lax.Preci...]
    unnamed x24 -> x30, local copies, waits for them, and re-layouts: 9.83 us -> 15.9 us
    sub x1 -> x2, other arithmetic: 0.03 us -> 5.52 us  [the longest x1 5.49 us: collide_major(): f - balance]
    ppermute x8 -> x4, starting transfers between devices: 12.7 us -> 7.57 us  [shift_ring(): lax.ppermute(x, axis, [(i, (i - step) % count) for i in range(count)])]
    another operation x4, local copies, waits for them, and re-layouts: 0.27 us -> 4.17 us  [body(): jnp.stack([jnp.sum(weight_map * reds, axis=0), jnp.sum(weight_map * green...]
    reduce_sum x3 -> x1, other arithmetic: 3.6 us -> 0.16 us  [body(): potential = 1.0 - jnp.exp(-jnp.sum(f, axis=0))]
    slice x15 -> x21, local copies, waits for them, and re-layouts: 1.43 us -> 4.74 us  [the longest x1 2.82 us: body(): column = collided[q, 1 - cx:1 - cx + extent_x, 1 - cy:1 - cy + extent_y]]
    ppermute x2, waiting for transfers between devices: 2.3 us -> 0.01 us  [from_partner(): lax.ppermute(x, axis, [(i, i ^ 1 << distance) for i in range(lax.axis_siz...]
  transfers between devices with their start and end apart: 10 -> 6, of which waited for: 7 -> 3; matrix products, arithmetic and copies ran while one was open for 13% -> 22% of each run, Pallas kernels for 0% -> 0%
where the time goes in v2:
time: 83.3 us; the launch traced here: 82.7 us
  local copies, waits for them, and re-layouts  27.9 us (33%)
  other arithmetic  22.1 us (27%)
  waiting for transfers between devices  12.7 us (15%)
  starting transfers between devices  9.7 us (12%)
  matrix products  9.15 us (11%)
  between operations  1.16 us (1%)
    unnamed x30, local copies, waits for them, and re-layouts  15.9 us
    ppermute x4, waiting for transfers between devices, shift_ring(): lax.ppermute(x, axis, [(i, (i - step) % count) for i in range(count)])  12.6 us
    unnamed x9, other arithmetic  7.75 us
    ppermute x4, starting transfers between devices, shift_ring(): lax.ppermute(x, axis, [(i, (i - step) % count) for i in range(count)])  7.57 us
    sub x1, other arithmetic, collide_major(): f - balance  5.49 us
    dot_general x1, matrix products, collide_major(): jnp.einsum('pq,q...->p...', relax_table, f - balance, precision=lax.Preci...  5.08 us
    another operation x4, local copies, waits for them, and re-layouts, body(): jnp.stack([jnp.sum(weight_map * reds, axis=0), jnp.sum(weight_map * green...  4.17 us
    dot_general x1, matrix products, collide_major(): jnp.einsum('pq,q...->p...', source_table, guo_term, precision=lax.Precisi...  4.06 us
  transfers between devices with their start and end apart: 6, of which 3 were waited for; matrix products, arithmetic and copies ran while one was open for 22% of the time, Pallas kernels for 0%

profile of v2, /device:TPU:0, one launch (start us, length us, event | category | flops | bytes accessed | tf_op | source)
XLA Modules:
  0.0 82.7 jit_solution(15387035514542343466)
XLA Ops:
  0.6 2.1 %copy.215 = f32[16,16,19,128]{3,1,0,2:T(8,128)S(1)} copy(f32[16,16,19,128]{3,1,2,0:T(8,128)} %param.7) | data formatting | bytes 4980736 | tf_op args[0]
  2.8 0.3 copy-done
  3.1 0.2 fusion.111
  3.3 3.0 %collective-permute-start = (f32[21,16,128]{2,1,0:T(8,128)S(1)}, f32[21,16,128]{2,1,0:T(8,128)S(1)}, u32[]{:S(2)}, u32[]{:S(2)}) collective-permute-start(f32[21,16,128]{2,1,0:T(8,128)S(1)} %pad_maximum_fusion.14), channel_id=1, source_target_pairs={{0,8},{8,16},{16,24},{24,0},{1,9},{9,17},{17,25},{25,1},{2,10},{10... | collective-permute-start | bytes 516104 | tf_op jit(solution)/shard_map/ppermute | solution.py:159
  6.4 1.0 %collective-permute-start.1 = (f32[21,16,128]{2,1,0:T(8,128)S(1)}, f32[21,16,128]{2,1,0:T(8,128)S(1)}, u32[]{:S(2)}, u32[]{:S(2)}) collective-permute-start(f32[21,16,128]{2,1,0:T(8,128)S(1)} %pad_maximum_fusion.15), channel_id=1, source_target_pairs={{0,24},{8,0},{16,8},{24,16},{1,25},{9,1},{17,9},{25,17},{2,26},{10... | collective-permute-start | bytes 516104 | tf_op jit(solution)/shard_map/ppermute | solution.py:159
  7.4 5.1 %collective-permute-done = f32[21,16,128]{2,1,0:T(8,128)S(1)} collective-permute-done((f32[21,16,128]{2,1,0:T(8,128)S(1)}, f32[21,16,128]{2,1,0:T(8,128)S(1)}, u32[]{:S(2)}, u32[]{:S(2)}) %collective-permute-start) | collective-permute-done | bytes 172064 | tf_op jit(solution)/shard_map/ppermute | solution.py:159
  12.5 3.1 %collective-permute-done.1 = f32[21,16,128]{2,1,0:T(8,128)S(1)} collective-permute-done((f32[21,16,128]{2,1,0:T(8,128)S(1)}, f32[21,16,128]{2,1,0:T(8,128)S(1)}, u32[]{:S(2)}, u32[]{:S(2)}) %collective-permute-start.1) | collective-permute-done | bytes 172064 | tf_op jit(solution)/shard_map/ppermute | solution.py:159
  15.6 0.2 pad_maximum_fusion.13
  16.2 3.5 %collective-permute-start.3 = (f32[21,20,128]{2,0,1:T(8,128)S(1)}, f32[21,20,128]{2,0,1:T(8,128)S(1)}, u32[]{:S(2)}, u32[]{:S(2)}) collective-permute-start(f32[21,20,128]{2,0,1:T(8,128)S(1)} %get-tuple-element.90), channel_id=1, source_target_pairs={{0,7},{1,0},{2,1},{3,2},{4,3},{5,4},{6,5},{7,6},{8,15},{9,8},{10,9... | collective-permute-start | bytes 645128 | tf_op jit(solution)/shard_map/ppermute | solution.py:159
  19.7 4.4 %collective-permute-done.2 = f32[21,20,128]{2,0,1:T(8,128)} collective-permute-done((f32[21,20,128]{2,0,1:T(8,128)S(1)}, f32[21,20,128]{2,0,1:T(8,128)}, u32[]{:S(2)}, u32[]{:S(2)}) %collective-permute-start.2) | collective-permute-done | bytes 215072 | tf_op jit(solution)/shard_map/ppermute | solution.py:159
  24.1 1.0 %slice_bitcast_fusion.7 = (f32[20,1,128]{2,1,0:T(1,128)S(1)}, f32[20,1,128]{2,1,0:T(1,128)S(1)}) fusion(f32[21,20,128]{2,0,1:T(8,128)} %collective-permute-done.2), kind=kLoop, calls=%fused_computation.207 | loop fusion | bytes 40960 | tf_op jit(solution)/shard_map/broadcast_in_dim;squeeze | solution.py:211
  25.2 0.2 fusion.120
  25.5 0.2 fusion.121
  25.7 0.1 fusion.122
  25.8 0.1 fusion.123
  26.0 0.1 fusion.124
  26.1 0.1 fusion.125
  26.2 1.0 %slice_bitcast_fusion.2 = f32[19,18,1,128]{3,0,2,1:T(8,128)S(1)} fusion(f32[21,20,128]{2,0,1:T(8,128)} %collective-permute-done.2), kind=kLoop, calls=%fused_computation.101 | loop fusion | bytes 350208 | tf_op jit(solution)/shard_map/broadcast_in_dim | solution.py:208
  27.2 0.2 copy.147
  27.4 0.2 copy.148
  27.6 1.7 %pad_maximum_fusion = (f32[19,18,18,128]{3,2,1,0:T(8,128)S(1)}, f32[18,18,128]{2,1,0:T(8,128)S(1)}) fusion(f32[19,18,1,128]{3,2,1,0:T(1,128)S(1)} %copy.148, f32[19,1,16,128]{3,2,1,0:T(8,128)S(1)} %slice_bitcast_fusion.3, f32[19,16,16,128]{3,2,1,0:T(8,128)S(1)} %bitcast.239, f32[19,1,16,128]{3,2,1,0:T(8,128)S(1)} %slice_bitcast_fusion.5, ...), kind=kLoop, calls=%fused_computation.5 | loop fusion | flops 3898368 | bytes 6469632 | tf_op jit(solution)/shard_map/concatenate | solution.py:207
  29.3 1.4 %add_multiply_fusion.1 = (f32[18,18,128]{2,1,0:T(8,128)S(1)}, f32[18,18,128]{2,1,0:T(8,128)S(1)}, f32[18,18,128]{2,1,0:T(8,128)S(1)}, f32[18,18,128]{2,1,0:T(8,1...) fusion(f32[18,18,128]{2,1,0:T(8,128)S(1)} %get-tuple-element.41, ...), kind=kLoop, calls=%fused_computation.125 | loop fusion | flops 4935168 | bytes 7464960 | tf_op jit(solution)/shard_map/mul | solution.py:178
  30.8 5.5 %fusion.3 = (f32[19,18,18,128]{3,2,1,0:T(8,128)S(1)}, f32[19,18,18,128]{3,2,1,0:T(8,128)S(1)}) fusion(f32[18,18,128]{2,1,0:T(8,128)S(1)} %get-tuple-element.14, f32[18,18,128]{2,1,0:T(8,128)S(1)} %get-tuple-element.19, f32[19]{0:T(128)S(1)} %copy-done.7, f32[18,18,128]{2,1,0:T(8,128)S(1)} %get-tuple-element.17, f32[19]{0:T(128)S(1)} %copy-done.6, ...), kind=kLoop, calls=%fused_computation.4 | loop fusion | flops 22851072 | bytes 10948912 | tf_op jit(solution)/shard_map/sub | solution.py:182
  36.3 4.1 %fusion.4 = f32[19,18,18,128]{3,0,2,1:T(8,128)S(1)} fusion(f32[19,19,1,1]{1,0,3,2:T(8,128)S(1)} %copy-done.3, f32[19,18,18,128]{3,2,1,0:T(8,128)S(1)} %get-tuple-element.47), kind=kOutput, calls=%fused_computation.8 | convolution fusion | flops 179656704 | bytes 6305188 | tf_op jit(solution)/shard_map/pq,q...->p.../dot_general | solution.py:183
  40.4 5.1 %fusion.6 = f32[19,18,18,128]{3,0,2,1:T(8,128)S(1)} fusion(f32[19,18,18,128]{3,0,2,1:T(8,128)S(1)} %fusion.4, f32[19,18,18,128]{3,2,1,0:T(8,128)S(1)} %get-tuple-element.40, f32[19,19,1,1]{1,0,3,2:T(8,128)S(1)} %copy-done.2, f32[19,18,18,128]{3,2,1,0:T(8,128)S(1)} %get-tuple-element.46), kind=kOutput, calls=%fused_computation.11 | convolution fusion | flops 181232640 | bytes 12608932 | tf_op jit(solution)/shard_map/pq,q...->p.../dot_general | solution.py:182
  45.5 2.8 %fusion.119 = (f32[1,16,16,128]{3,0,2,1:T(1,128)S(1)}, f32[1,16,16,128]{3,0,2,1:T(1,128)S(1)}, f32[1,16,16,128]{3,0,2,1:T(1,128)S(1)}, f32[1,16,16,128]{3,0,2,1:...) fusion(f32[19,18,18,128]{3,0,2,1:T(8,128)S(1)} %fusion.6), kind=kLoop, calls=%fused_computation.224 | loop fusion | bytes 4980736 | tf_op jit(solution)/shard_map/slice | solution.py:231
  48.5 0.1 slice.598
  48.6 0.1 slice.601
  48.7 0.1 slice.604
  49.1 0.1 slice.613
  49.4 0.7 constant_dynamic-update-slice_fusion.8
  50.0 1.7 %multiply_reduce_fusion = (f32[16,128]{1,0:T(8,128)S(1)}, f32[16,128]{1,0:T(8,128)S(1)}, f32[16,128]{1,0:T(8,128)}, f32[16,128]{1,0:T(8,128)}) fusion(f32[16,16,127]{2,1,0:T(8,128)S(1)} %bitcast.242, f32[16,16,1]{2,1,0:T(8,128)S(1)} %slice.619, f32[16,16,1]{2,1,0:T(8,128)S(1)} %bitcast.245, f32[16,16,127]{2,1,0:T(8,128)S(1)} %slice.616, ...), kind=kOutput, calls=%fused_computation.171 | output fusion | flops 3006464 | bytes 2523136 | tf_op jit(solution)/shard_map/jit(cumsum)/reduce_window_sum | solution.py:239
  51.8 1.4 %stack.66 = f32[1,16,2,2,32]{4,3,2,1,0:T(2,128)} reshape(f32[16,128]{1,0:T(8,128)} %get-tuple-element.12) | data formatting | bytes 16384 | tf_op jit(solution)/shard_map/stack | solution.py:242
  53.2 1.4 %constant_dynamic-update-slice_fusion.12 = f32[4,16,2,2,32]{4,3,2,1,0:T(2,128)} fusion(f32[1,16,2,2,32]{4,3,2,1,0:T(2,128)} %stack.66), kind=kLoop, calls=%fused_computation.198 | loop fusion | bytes 40960
  54.5 0.7 stack.67
  55.2 0.7 stack.68
  55.9 0.7 exponential_subtract_fusion.1
  56.6 0.7 sub.81
  57.3 1.4 %constant_dynamic-update-slice_fusion.11 = f32[4,16,2,2,32]{4,3,2,1,0:T(2,128)} fusion(f32[4,16,2,2,32]{4,3,2,1,0:T(2,128)} %constant_dynamic-update-slice_fusion.12, f32[1,16,2,2,32]{4,3,2,1,0:T(2,128)} %stack.67), kind=kLoop, calls=%fused_computation.197 | loop fusion | bytes 65536
  58.7 1.4 %constant_dynamic-update-slice_fusion.10 = f32[4,16,2,2,32]{4,3,2,1,0:T(2,128)} fusion(f32[4,16,2,2,32]{4,3,2,1,0:T(2,128)} %constant_dynamic-update-slice_fusion.11, f32[1,16,2,2,32]{4,3,2,1,0:T(2,128)} %stack.68), kind=kLoop, calls=%fused_computation.196 | loop fusion | bytes 65536
  60.1 1.4 %constant_dynamic-update-slice_fusion.9 = f32[4,16,2,2,32]{4,3,2,1,0:T(2,128)} fusion(f32[4,16,2,2,32]{4,3,2,1,0:T(2,128)} %constant_dynamic-update-slice_fusion.10, f32[1,16,2,2,32]{4,3,2,1,0:T(2,128)} %sub.81), kind=kLoop, calls=%fused_computation.195 | loop fusion | bytes 65536 | tf_op jit(solution)/shard_map/stack | solution.py:242
  61.4 1.1 %fusion.127 = (f32[4,16,2,1,32]{4,3,2,1,0:T(1,128)S(1)}, f32[4,16,2,1,32]{4,3,2,1,0:T(1,128)S(1)}, f32[4,16,2,1,32]{4,3,2,1,0:T(1,128)S(1)}) fusion(f32[4,16,2,2,32]{4,3,2,1,0:T(2,128)} %constant_dynamic-update-slice_fusion.9, pred[]{:T(512)S(6)} %eq.22), kind=kLoop, calls=%fused_computation.232 | loop fusion | flops 4096 | bytes 81921 | tf_op jit(solution)/shard_map/slice | solution.py:259
  62.6 1.6 %collective-permute-start.4 = (f32[4,16,2,32]{3,2,1,0:T(2,128)S(1)}, f32[4,16,2,32]{3,2,1,0:T(2,128)S(1)}, u32[]{:S(2)}, u32[]{:S(2)}) collective-permute-start(f32[4,16,2,32]{3,2,1,0:T(2,128)S(1)} %bitcast.298), channel_id=1, source_target_pairs={{0,8},{8,0},{16,24},{24,16},{1,9},{9,1},{17,25},{25,17},{2,10},{10... | collective-permute-start | bytes 49160 | tf_op jit(solution)/shard_map/ppermute | solution.py:28
  64.1 0.6 constant_dynamic-update-slice_fusion.7
  64.8 0.7 constant_dynamic-update-slice_fusion.6
  65.4 0.7 constant_dynamic-update-slice_fusion.5
  66.1 0.7 constant_dynamic-update-slice_fusion.4
  66.8 1.7 %bitcast_dynamic-update-slice_fusion.9 = f32[19,16,16,128]{3,2,1,0:T(8,128)} fusion(f32[19,16,16,128]{3,2,1,0:T(8,128)} %constant_dynamic-update-slice_fusion.4, f32[16,16,127]{2,1,0:T(8,128)S(1)} %bitcast.270, f32[16,16,1]{2,1,0:T(8,128)} %copy-done.1), kind=kLoop, calls=%fused_computation.170 | loop fusion | flops 32768 | bytes 392192
  68.4 0.8 bitcast_dynamic-update-slice_fusion.8
  69.2 0.7 constant_dynamic-update-slice_fusion.3
  69.9 0.7 constant_dynamic-update-slice_fusion.2
  70.5 0.7 constant_dynamic-update-slice_fusion.1
  71.2 0.7 constant_dynamic-update-slice_fusion
  71.9 0.8 bitcast_dynamic-update-slice_fusion.7
  72.6 0.8 bitcast_dynamic-update-slice_fusion.6
  73.4 0.8 bitcast_dynamic-update-slice_fusion.5
  74.1 0.8 bitcast_dynamic-update-slice_fusion.4
  74.9 0.8 bitcast_dynamic-update-slice_fusion.3
  75.7 0.8 bitcast_dynamic-update-slice_fusion.2
  76.4 0.8 bitcast_dynamic-update-slice_fusion.1
  77.4 0.6 collective-permute-start.5
  78.0 0.8 bitcast_dynamic-update-slice_fusion
  78.7 3.3 %copy.178 = f32[16,16,19,128]{3,1,2,0:T(8,128)} copy(f32[16,16,19,128]{3,1,0,2:T(8,128)} %bitcast.271) | data formatting | bytes 4980736
  82.1 0.6 fusion.106
  (49 shorter events, 1.3 us)
Async XLA Ops:
  0.6 2.5 %copy-start = (f32[16,16,19,128]{3,1,2,0:T(8,128)S(1)}, f32[16,16,19,128]{3,1,2,0:T(8,128)}, u32[]{:S(2)}) copy-start(f32[16,16,19,128]{3,1,2,0:T(8,128)} %param.7) | copy-start | bytes 7471108
  3.3 9.1 %collective-permute-start = (f32[21,16,128]{2,1,0:T(8,128)S(1)}, f32[21,16,128]{2,1,0:T(8,128)S(1)}, u32[]{:S(2)}, u32[]{:S(2)}) collective-permute-start(f32[21,16,128]{2,1,0:T(8,128)S(1)} %pad_maximum_fusion.14), channel_id=1, source_target_pairs={{0,8},{8,16},{16,24},{24,0},{1,9},{9,17},{17,25},{25,1},{2,10},{10... | collective-permute-start | bytes 516104 | tf_op jit(solution)/shard_map/ppermute | solution.py:159
  6.4 9.2 %collective-permute-start.1 = (f32[21,16,128]{2,1,0:T(8,128)S(1)}, f32[21,16,128]{2,1,0:T(8,128)S(1)}, u32[]{:S(2)}, u32[]{:S(2)}) collective-permute-start(f32[21,16,128]{2,1,0:T(8,128)S(1)} %pad_maximum_fusion.15), channel_id=1, source_target_pairs={{0,24},{8,0},{16,8},{24,16},{1,25},{9,1},{17,9},{25,17},{2,26},{10... | collective-permute-start | bytes 516104 | tf_op jit(solution)/shard_map/ppermute | solution.py:159
  16.1 8.0 %collective-permute-start.2 = (f32[21,20,128]{2,0,1:T(8,128)S(1)}, f32[21,20,128]{2,0,1:T(8,128)}, u32[]{:S(2)}, u32[]{:S(2)}) collective-permute-start(f32[21,20,128]{2,0,1:T(8,128)S(1)} %get-tuple-element.89), channel_id=1, source_target_pairs={{0,1},{1,2},{2,3},{3,4},{4,5},{5,6},{6,7},{7,0},{8,9},{9,10},{10,1... | collective-permute-start | bytes 645128 | tf_op jit(solution)/shard_map/ppermute | solution.py:159
  16.2 8.9 %collective-permute-start.3 = (f32[21,20,128]{2,0,1:T(8,128)S(1)}, f32[21,20,128]{2,0,1:T(8,128)S(1)}, u32[]{:S(2)}, u32[]{:S(2)}) collective-permute-start(f32[21,20,128]{2,0,1:T(8,128)S(1)} %get-tuple-element.90), channel_id=1, source_target_pairs={{0,7},{1,0},{2,1},{3,2},{4,3},{5,4},{6,5},{7,6},{8,15},{9,8},{10,9... | collective-permute-start | bytes 645128 | tf_op jit(solution)/shard_map/ppermute | solution.py:159
  29.3 1.5 %copy-start.4 = (f32[19]{0:T(128)S(1)}, f32[19]{0:T(128)}, u32[]{:S(2)}) copy-start(f32[19]{0:T(128)} %constant.100.clone) | copy-start | bytes 232
  29.3 1.5 %copy-start.5 = (f32[19]{0:T(128)S(1)}, f32[19]{0:T(128)}, u32[]{:S(2)}) copy-start(f32[19]{0:T(128)} %constant.97.clone) | copy-start | bytes 232
  29.3 1.5 %copy-start.6 = (f32[19]{0:T(128)S(1)}, f32[19]{0:T(128)}, u32[]{:S(2)}) copy-start(f32[19]{0:T(128)} %constant.98.clone) | copy-start | bytes 232
  29.3 1.5 %copy-start.7 = (f32[19]{0:T(128)S(1)}, f32[19]{0:T(128)}, u32[]{:S(2)}) copy-start(f32[19]{0:T(128)} %constant.99.clone) | copy-start | bytes 232
  30.8 5.5 %copy-start.3 = (f32[19,19,1,1]{1,0,3,2:T(8,128)S(1)}, f32[19,19,1,1]{1,0,3,2:T(8,128)}, u32[]{:S(2)}) copy-start(f32[19,19,1,1]{1,0,3,2:T(8,128)} %constant.104) | copy-start | bytes 4336
  36.3 4.1 %copy-start.2 = (f32[19,19,1,1]{1,0,3,2:T(8,128)S(1)}, f32[19,19,1,1]{1,0,3,2:T(8,128)}, u32[]{:S(2)}) copy-start(f32[19,19,1,1]{1,0,3,2:T(8,128)} %constant.103) | copy-start | bytes 4336
  48.4 3.3 %copy-start.1 = (f32[16,16,1]{2,1,0:T(8,128)}, f32[16,16,1]{2,1,0:T(8,128)S(1)}, u32[]{:S(2)}) copy-start(f32[16,16,1]{2,1,0:T(8,128)S(1)} %slice.588) | copy-start | bytes 3076
  62.6 14.6 %collective-permute-start.4 = (f32[4,16,2,32]{3,2,1,0:T(2,128)S(1)}, f32[4,16,2,32]{3,2,1,0:T(2,128)S(1)}, u32[]{:S(2)}, u32[]{:S(2)}) collective-permute-start(f32[4,16,2,32]{3,2,1,0:T(2,128)S(1)} %bitcast.298), channel_id=1, source_target_pairs={{0,8},{8,0},{16,24},{24,16},{1,9},{9,1},{17,25},{25,17},{2,10},{10... | collective-permute-start | bytes 49160 | tf_op jit(solution)/shard_map/ppermute | solution.py:28
  77.4 4.6 %collective-permute-start.5 = (f32[4,16,1,32]{3,1,0,2:T(8,128)S(1)}, f32[4,16,1,32]{3,1,0,2:T(8,128)S(1)}, u32[]{:S(2)}, u32[]{:S(2)}) collective-permute-start(f32[4,16,1,32]{3,1,0,2:T(8,128)S(1)} %bitcast.299), channel_id=1, source_target_pairs={{0,16},{8,24},{16,0},{24,8},{1,17},{9,25},{17,1},{25,9},{2,18},{10... | collective-permute-start | bytes 24584 | tf_op jit(solution)/shard_map/ppermute | solution.py:28

commit v3 on v2

--- a/solution.py
+++ b/solution.py
@@ -3,6 +3,8 @@
 import numpy as np
 from jax import lax
 from jax.sharding import PartitionSpec as P
+from jax.experimental import pallas as pl
+from jax.experimental.pallas import tpu as pltpu
 
 cohesion = -6.0
 optical = 2.0
@@ -184,6 +186,53 @@
     return f - relaxed + sourced
 
 
+def stream_and_render(collided, velocities, extent_x, extent_y, length_x):
+    depth_z = collided.shape[3]
+    steps = [[int(v) for v in velocities[q]] for q in range(19)]
+
+    def kernel(c_ref, o_ref, pic_ref):
+        for q in range(19):
+            cx, cy, cz = steps[q]
+
+            def move(x, carry):
+                v = c_ref[q, x + 1 - cx, pl.ds(1 - cy, extent_y), :]
+                if cz != 0:
+                    v = pltpu.roll(v, shift=cz % depth_z, axis=1)
+                o_ref[q, x] = v
+                return carry
+
+            lax.fori_loop(0, extent_x, move, 0)
+
+        def render(x, carry):
+            depth, red, green, blue = carry
+            fresh_density = o_ref[0, x]
+            for q in range(1, 19):
+                fresh_density = fresh_density + o_ref[q, x]
+            extinction = optical * fresh_density / length_x
+            weight = jnp.exp(-depth) * (1.0 - jnp.exp(-extinction))
+            red = red + weight * (fresh_density / (1.0 + fresh_density))
+            green = green + weight * jnp.exp(-fresh_density)
+            blue = blue + weight * (0.5 * (1.0 + jnp.tanh(2.0 * (fresh_density - 1.0))))
+            return (depth + extinction, red, green, blue)
+
+        zero = jnp.zeros((extent_y, depth_z), jnp.float32)
+        depth, red, green, blue = lax.fori_loop(0, extent_x, render, (zero, zero, zero, zero))
+        pic_ref[0] = red
+        pic_ref[1] = green
+        pic_ref[2] = blue
+        pic_ref[3] = 1.0 - jnp.exp(-depth)
+
+    return pl.pallas_call(
+        kernel,
+        out_shape=(
+            jax.ShapeDtypeStruct((19, extent_x, extent_y, depth_z), jnp.float32),
+            jax.ShapeDtypeStruct((4, extent_y, depth_z), jnp.float32),
+        ),
+        in_specs=[pl.BlockSpec(memory_space=pltpu.VMEM)],
+        out_specs=(pl.BlockSpec(memory_space=pltpu.VMEM), pl.BlockSpec(memory_space=pltpu.VMEM)),
+    )(collided)
+
+
 def body(populations):
     velocities, weights, relaxing, forcing_map = lattice_tables()
     extent_x = populations.shape[0]
@@ -225,28 +274,10 @@
     force = [-cohesion * centre * totals[d] for d in range(3)]
     rho = jnp.sum(fxy, axis=0)
     collided = collide_major(fxy, rho, force, velocities, weights, relaxing, forcing_map)
-    read = []
-    for q in range(19):
-        cx, cy, cz = [int(v) for v in velocities[q]]
-        column = collided[q, 1 - cx : 1 - cx + extent_x, 1 - cy : 1 - cy + extent_y]
-        read.append(jnp.roll(column, cz, axis=2))
-    fresh_major = jnp.stack(read, axis=0)
-    fresh = jnp.transpose(fresh_major, (1, 2, 0, 3))
     groups = lax.axis_size("gx")
     length_x = extent_x * groups
-    new_density = jnp.sum(fresh_major, axis=0)
-    extinction = optical * new_density / length_x
-    optical_depth = jnp.cumsum(extinction, axis=0) - extinction
-    weight_map = jnp.exp(-optical_depth) * (1.0 - jnp.exp(-extinction))
-    reds, greens, blues = palette(new_density)
-    layered = jnp.stack(
-        [
-            jnp.sum(weight_map * reds, axis=0),
-            jnp.sum(weight_map * greens, axis=0),
-            jnp.sum(weight_map * blues, axis=0),
-            1.0 - jnp.exp(-jnp.sum(extinction, axis=0)),
-        ]
-    )
+    fresh_major, layered = stream_and_render(collided, velocities, extent_x, extent_y, length_x)
+    fresh = jnp.transpose(fresh_major, (1, 2, 0, 3))
     depth_z = layered.shape[2]
     block_len = depth_z // groups
     blocked = layered.reshape(4, extent_y, groups, block_len)

time: 83.3 us -> 76.8 us (0.922)
  Pallas kernels: 0 us -> 16.3 us
  local copies, waits for them, and re-layouts: 27.9 us -> 11.7 us
  other arithmetic: 22.1 us -> 10 us
  waiting for transfers between devices: 12.7 us -> 17.5 us
  matrix products: 9.15 us -> 11.5 us
  starting transfers between devices: 9.7 us -> 8.42 us
    pallas_call x0 -> x1, Pallas kernels: none -> 16.3 us  [stream_and_render(): pl.pallas_call(kernel, out_shape=(jax.ShapeDtypeStruct((19, extent_x, ext...]
    unnamed x30 -> x16, local copies, waits for them, and re-layouts: 15.9 us -> 3.4 us
    unnamed x9 -> x0, other arithmetic: 7.75 us -> none
    sub x2 -> x0, other arithmetic: 6.19 us -> none  [the longest x1 5.49 us: collide_major(): f - balance]
    add x0 -> x2, other arithmetic: none -> 3.91 us  [the longest x1 3.11 us: collide_major(): return f - relaxed + sourced]
    ppermute x2, waiting for transfers between devices: 0.01 us -> 2.85 us  [from_partner(): lax.ppermute(x, axis, [(i, i ^ 1 << distance) for i in range(lax.axis_siz...]
    another operation x2 -> x0, other arithmetic: 2.46 us -> none  [the longest x1 1.7 us: body(): optical_depth = jnp.cumsum(extinction, axis=0) - extinction]
    another operation x5 -> x2, local copies, waits for them, and re-layouts: 4.18 us -> 1.89 us  [the longest x1 0.98 us: body(): from_above[19][:, None]]
  transfers between devices with their start and end apart: 6 -> 6, of which waited for: 3 -> 6; matrix products, arithmetic and copies ran while one was open for 22% -> 7% of each run, Pallas kernels for 0% -> 0%
where the time goes in v3:
time: 76.8 us; the launch traced here: 76.4 us
  waiting for transfers between devices  17.5 us (23%)
  Pallas kernels  16.3 us (21%)
  local copies, waits for them, and re-layouts  11.7 us (15%)
  matrix products  11.5 us (15%)
  other arithmetic  10 us (13%)
  starting transfers between devices  8.42 us (11%)
  between operations  1.03 us (1%)
    pallas_call x1, Pallas kernels, stream_and_render(): pl.pallas_call(kernel, out_shape=(jax.ShapeDtypeStruct((19, extent_x, ext...  16.3 us
    ppermute x4, waiting for transfers between devices, shift_ring(): lax.ppermute(x, axis, [(i, (i - step) % count) for i in range(count)])  14.6 us
    ppermute x4, starting transfers between devices, shift_ring(): lax.ppermute(x, axis, [(i, (i - step) % count) for i in range(count)])  6.28 us
    dot_general x1, matrix products, collide_major(): jnp.einsum('pq,q...->p...', relax_table, f - balance, precision=lax.Preci...  5.92 us
    dot_general x1, matrix products, collide_major(): jnp.einsum('pq,q...->p...', source_table, guo_term, precision=lax.Precisi...  5.62 us
    unnamed x16, local copies, waits for them, and re-layouts  3.4 us
    add x1, other arithmetic, collide_major(): return f - relaxed + sourced  3.11 us
    ppermute x2, waiting for transfers between devices, from_partner(): lax.ppermute(x, axis, [(i, i ^ 1 << distance) for i in range(lax.axis_siz...  2.85 us
  transfers between devices with their start and end apart: 6, of which 6 were waited for; matrix products, arithmetic and copies ran while one was open for 7% of the time, Pallas kernels for 0%

profile of v3, /device:TPU:0, one launch (start us, length us, event | category | flops | bytes accessed | tf_op | source)
XLA Modules:
  0.0 76.4 jit_solution(4090440802842017968)
XLA Ops:
  0.6 0.0 copy-start
  0.6 2.0 %bitcast_reduce_fusion = f32[16,16,128]{2,1,0:T(8,128)S(1)} fusion(f32[16,16,19,128]{3,1,2,0:T(8,128)} %param.7), kind=kLoop, calls=%fused_computation.200 | loop fusion | flops 589824 | bytes 2621440 | tf_op jit(solution)/shard_map/reduce_sum | solution.py:241
  2.7 1.0 %slice_bitcast_fusion.5 = (f32[19,16,128]{2,1,0:T(8,128)S(1)}, f32[19,16,128]{2,1,0:T(8,128)S(1)}) fusion(f32[19,16,16,128]{3,2,0,1:T(8,128)} %bitcast.118), kind=kLoop, calls=%fused_computation.169 | loop fusion | bytes 622592 | tf_op jit(solution)/shard_map/squeeze | solution.py:242
  3.8 3.9 %collective-permute-start.1 = (f32[21,16,128]{2,1,0:T(8,128)S(1)}, f32[21,16,128]{2,1,0:T(8,128)S(1)}, u32[]{:S(2)}, u32[]{:S(2)}) collective-permute-start(f32[21,16,128]{2,1,0:T(8,128)S(1)} %pad_maximum_fusion.13), channel_id=1, source_target_pairs={{0,24},{8,0},{16,8},{24,16},{1,25},{9,1},{17,9},{25,17},{2,26},{10... | collective-permute-start | bytes 516104 | tf_op jit(solution)/shard_map/ppermute | solution.py:161
  7.7 0.1 collective-permute-start
  7.8 4.7 %collective-permute-done.1 = f32[21,16,128]{2,1,0:T(8,128)S(1)} collective-permute-done((f32[21,16,128]{2,1,0:T(8,128)S(1)}, f32[21,16,128]{2,1,0:T(8,128)S(1)}, u32[]{:S(2)}, u32[]{:S(2)}) %collective-permute-start.1) | collective-permute-done | bytes 172064 | tf_op jit(solution)/shard_map/ppermute | solution.py:161
  12.5 3.5 %collective-permute-done = f32[21,16,128]{2,1,0:T(8,128)S(1)} collective-permute-done((f32[21,16,128]{2,1,0:T(8,128)S(1)}, f32[21,16,128]{2,1,0:T(8,128)S(1)}, u32[]{:S(2)}, u32[]{:S(2)}) %collective-permute-start) | collective-permute-done | bytes 172064 | tf_op jit(solution)/shard_map/ppermute | solution.py:161
  16.0 0.0 copy-done
  16.0 0.2 pad_maximum_fusion.1
  16.3 0.2 fusion.132
  16.6 0.1 fusion.50
  16.7 2.2 %collective-permute-start.3 = (f32[21,20,128]{2,0,1:T(8,128)S(1)}, f32[21,20,128]{2,0,1:T(8,128)}, u32[]{:S(2)}, u32[]{:S(2)}) collective-permute-start(f32[21,20,128]{2,0,1:T(8,128)S(1)} %get-tuple-element.77), channel_id=1, source_target_pairs={{0,7},{1,0},{2,1},{3,2},{4,3},{5,4},{6,5},{7,6},{8,15},{9,8},{10,9... | collective-permute-start | bytes 645128 | tf_op jit(solution)/shard_map/ppermute | solution.py:161
  18.9 1.0 %copy.20 = f32[19,18,16,128]{3,0,2,1:T(8,128)S(1)} copy(f32[19,18,16,128]{3,2,0,1:T(8,128)S(1)} %pad_maximum_fusion.1) | data formatting | bytes 5603328 | tf_op jit(solution)/shard_map/concatenate | solution.py:246
  19.9 0.1 collective-permute-start.2
  20.0 5.2 %collective-permute-done.3 = f32[21,20,128]{2,0,1:T(8,128)} collective-permute-done((f32[21,20,128]{2,0,1:T(8,128)S(1)}, f32[21,20,128]{2,0,1:T(8,128)}, u32[]{:S(2)}, u32[]{:S(2)}) %collective-permute-start.3) | collective-permute-done | bytes 215072 | tf_op jit(solution)/shard_map/ppermute | solution.py:161
  25.2 1.0 %slice_bitcast_fusion.8 = (f32[20,1,128]{2,1,0:T(1,128)S(1)}, f32[20,1,128]{2,1,0:T(1,128)S(1)}) fusion(f32[21,20,128]{2,0,1:T(8,128)} %collective-permute-done.3), kind=kLoop, calls=%fused_computation.189 | loop fusion | bytes 40960 | tf_op jit(solution)/shard_map/broadcast_in_dim;squeeze | solution.py:260
  26.2 1.2 %collective-permute-done.2 = f32[21,20,128]{2,0,1:T(8,128)S(1)} collective-permute-done((f32[21,20,128]{2,0,1:T(8,128)S(1)}, f32[21,20,128]{2,0,1:T(8,128)S(1)}, u32[]{:S(2)}, u32[]{:S(2)}) %collective-permute-start.2) | collective-permute-done | bytes 215072 | tf_op jit(solution)/shard_map/ppermute | solution.py:161
  27.4 0.1 pad_maximum_fusion.6
  27.5 0.1 fusion.137
  27.7 0.1 fusion.138
  27.8 0.1 fusion.135
  27.9 0.1 fusion.136
  28.0 0.2 fusion.134
  28.3 0.2 fusion.133
  28.5 1.0 %slice_bitcast_fusion = f32[19,18,1,128]{3,0,2,1:T(8,128)S(1)} fusion(f32[21,20,128]{2,0,1:T(8,128)} %collective-permute-done.3), kind=kLoop, calls=%fused_computation.120 | loop fusion | bytes 350208 | tf_op jit(solution)/shard_map/broadcast_in_dim | solution.py:257
  29.5 0.9 %pad_maximum_fusion = (f32[19,18,18,128]{3,0,2,1:T(8,128)S(1)}, f32[18,18,128]{2,1,0:T(8,128)S(1)}) fusion(f32[19,18,1,128]{3,0,2,1:T(8,128)S(1)} %slice_bitcast_fusion, f32[19,18,16,128]{3,0,2,1:T(8,128)S(1)} %copy.20, f32[19,18,1,128]{3,0,2,1:T(8,128)S(1)} %slice_bitcast_fusion.1), kind=kLoop, calls=%fused_computation.7 | loop fusion | flops 2322432 | bytes 6469632 | tf_op jit(solution)/shard_map/concatenate | solution.py:256
  30.5 2.0 %fusion.131 = (f32[1,18,18,128]{3,0,2,1:T(1,128)S(1)}, f32[1,18,18,128]{3,0,2,1:T(1,128)S(1)}, f32[1,18,18,128]{3,0,2,1:T(1,128)S(1)}, f32[1,18,18,128]{3,0,2,1:...) fusion(f32[19,18,18,128]{3,0,2,1:T(8,128)S(1)} %get-tuple-eleme, ...), kind=kLoop, calls=%fused_computation.207 | loop fusion | bytes 5308416 | tf_op jit(solution)/shard_map/slice | solution.py:172
  32.6 0.8 %copy_add_fusion.7 = f32[1,18,18,128]{3,0,2,1:T(1,128)S(1)} fusion(f32[1,18,18,128]{3,2,1,0:T(8,128)S(1)} %copy_multiply_fusion.7, f32[1,18,18,128]{3,2,1,0:T(8,128)S(1)} %copy_multiply_fusion.3, f32[1,18,18,128]{3,2,1,0:T(8,128)S(1)} %copy_multiply_fusion.9, f32[19,18,18,128]{3,0,2,1:T(8,128)S(1)} %get-tuple-element.33), kind=kLoop, calls=%fused_computation.161 | loop fusion | flops 331776 | bytes 1492992 | tf_op jit(solution)/shard_map/add | solution.py:172
  33.4 0.7 fusion.69
  34.1 0.0 copy-start.2
  34.1 0.0 copy-start.3
  34.1 0.0 copy-start.4
  34.1 0.0 copy-start.5
  34.2 0.0 copy-start.6
  34.2 1.1 %add_multiply_fusion = (f32[18,18,128]{2,1,0:T(8,128)S(1)}, f32[18,18,128]{2,1,0:T(8,128)S(1)}, f32[18,18,128]{2,1,0:T(8,128)S(1)}, f32[18,18,128]{2,1,0:T(8,128)S(1)}, f32[18,18,128]{2,1,0:T(8,128)S(1)}) fusion(f32[18,18,128]{2,1,0:T(8,128)S(1)} %get-tuple-element.15, f32[18,18,128]{2,1,0:T(8,128)S(1)} %get-tuple-element.34, ...), kind=kLoop, calls=%fused_computation.155 | loop fusion | flops 3566592 | bytes 6635520 | tf_op jit(solution)/shard_map/mul | solution.py:180
  35.2 0.1 multiply_add_fusion.3
  35.3 0.0 copy-done.2
  35.4 0.0 copy-done.3
  35.4 0.0 copy-done.4
  35.4 0.0 copy-done.5
  35.4 0.0 copy-done.6
  35.4 0.0 copy-start.1
  35.4 5.6 %fusion.6 = f32[19,18,18,128]{3,0,2,1:T(8,128)S(1)} fusion(f32[19,19,1,1]{1,0,3,2:T(8,128)S(1)} %copy-done.2, f32[18,18,128]{2,1,0:T(8,128)S(1)} %multiply_add_fusion.3, f32[18,18,128]{2,1,0:T(8,128)S(1)} %get-tuple-element.16, f32[18,18,128]{2,1,0:T(8,128)S(1)} %get-tuple-element.14, f32[18,18,128]{2,1,0:T(8,128)S(1)} %get-tuple-element.12, ...), kind=kOutput, calls=%fused_computation.8 | convolution fusion | flops 192264192 | bytes 4314836 | tf_op jit(solution)/shard_map/pq,q...->p.../dot_general | solution.py:185
  41.0 0.0 copy-done.1
  41.0 5.9 %fusion.21 = f32[19,18,18,128]{3,0,2,1:T(8,128)S(1)} fusion(f32[19,19,1,1]{1,0,3,2:T(8,128)S(1)} %copy-done.1, f32[18,18,128]{2,1,0:T(8,128)S(1)} %get-tuple-element.10, f32[18,18,128]{2,1,0:T(8,128)S(1)} %get-tuple-element.15, f32[19]{0:T(128)S(1)} %copy-done.3, f32[18,18,128]{2,1,0:T(8,128)S(1)} %get-tuple-element.13, f32[19]{0:T(128)S(1)} %copy-done.4, ...), kind=kOutput, calls=%fused_computation.25 | convolution fusion | flops 194628096 | bytes 7134932 | tf_op jit(solution)/shard_map/pq,q...->p.../dot_general | solution.py:184
  47.0 3.1 %copy_add_fusion.c_ref = f32[19,18,18,128]{3,2,1,0:T(8,128)} fusion(f32[19,18,18,128]{3,0,2,1:T(8,128)S(1)} %fusion.6, f32[19,18,18,128]{3,0,2,1:T(8,128)S(1)} %fusion.21), kind=kLoop, calls=%fused_computation.1 | loop fusion | flops 787968 | bytes 9455616 | tf_op jit(solution)/shard_map/add | solution.py:186
  50.1 16.3 %shard_map.86 = (f32[19,16,16,128]{3,2,1,0:T(8,128)}, f32[4,16,128]{2,1,0:T(8,128)}) custom-call(f32[19,18,18,128]{3,2,1,0:T(8,128)} %copy_add_fusion.c_ref), custom_call_target="tpu_custom_call" | custom-call | tf_op jit(solution)/shard_map/pallas_call | solution.py:225
  66.3 0.9 %reshape_reshape.3 = f32[4,16,2,2,32]{4,3,2,1,0:T(2,128)S(1)} reshape(f32[4,16,128]{2,1,0:T(8,128)} %get-tuple-element.5) | data formatting | bytes 65536 | tf_op jit(solution)/shard_map/reshape;reshape | solution.py:289
  67.3 0.1 fusion.140
  67.4 1.6 %collective-permute-start.4 = (f32[4,16,2,32]{3,1,0,2:T(8,128)S(1)}, f32[4,16,2,32]{3,1,0,2:T(8,128)S(1)}, u32[]{:S(2)}, u32[]{:S(2)}) collective-permute-start(f32[4,16,2,32]{3,1,0,2:T(8,128)S(1)} %select_bitcast_fusion), channel_id=1, source_target_pairs={{0,8},{8,0},{16,24},{24,16},{1,9},{9,1},{17,25},{25,17},{2,10},{10... | collective-permute-start | bytes 49160 | tf_op jit(solution)/shard_map/ppermute | solution.py:30
  69.0 2.8 %collective-permute-done.4 = f32[4,16,2,32]{3,1,0,2:T(8,128)S(1)} collective-permute-done((f32[4,16,2,32]{3,1,0,2:T(8,128)S(1)}, f32[4,16,2,32]{3,1,0,2:T(8,128)S(1)}, u32[]{:S(2)}, u32[]{:S(2)}) %collective-permute-start.4) | collective-permute-done | bytes 16416 | tf_op jit(solution)/shard_map/ppermute | solution.py:30
  71.8 0.6 collective-permute-start.5
  72.4 3.3 %copy.49 = f32[16,16,19,128]{3,1,2,0:T(8,128)} copy(f32[16,16,19,128]{3,1,0,2:T(8,128)} %bitcast.120) | data formatting | bytes 4980736
  75.7 0.1 collective-permute-done.5
  75.8 0.6 fusion.116
  (24 shorter events, 0.3 us)
Async XLA Ops:
  0.6 15.4 %copy-start = (f32[16,16,19,128]{3,1,2,0:T(8,128)S(1)}, f32[16,16,19,128]{3,1,2,0:T(8,128)}, u32[]{:S(2)}) copy-start(f32[16,16,19,128]{3,1,2,0:T(8,128)} %param.7) | copy-start | bytes 7471108
  3.8 8.7 %collective-permute-start.1 = (f32[21,16,128]{2,1,0:T(8,128)S(1)}, f32[21,16,128]{2,1,0:T(8,128)S(1)}, u32[]{:S(2)}, u32[]{:S(2)}) collective-permute-start(f32[21,16,128]{2,1,0:T(8,128)S(1)} %pad_maximum_fusion.13), channel_id=1, source_target_pairs={{0,24},{8,0},{16,8},{24,16},{1,25},{9,1},{17,9},{25,17},{2,26},{10... | collective-permute-start | bytes 516104 | tf_op jit(solution)/shard_map/ppermute | solution.py:161
  7.7 8.3 %collective-permute-start = (f32[21,16,128]{2,1,0:T(8,128)S(1)}, f32[21,16,128]{2,1,0:T(8,128)S(1)}, u32[]{:S(2)}, u32[]{:S(2)}) collective-permute-start(f32[21,16,128]{2,1,0:T(8,128)S(1)} %pad_maximum_fusion.12), channel_id=1, source_target_pairs={{0,8},{8,16},{16,24},{24,0},{1,9},{9,17},{17,25},{25,1},{2,10},{10... | collective-permute-start | bytes 516104 | tf_op jit(solution)/shard_map/ppermute | solution.py:161
  16.7 8.5 %collective-permute-start.3 = (f32[21,20,128]{2,0,1:T(8,128)S(1)}, f32[21,20,128]{2,0,1:T(8,128)}, u32[]{:S(2)}, u32[]{:S(2)}) collective-permute-start(f32[21,20,128]{2,0,1:T(8,128)S(1)} %get-tuple-element.77), channel_id=1, source_target_pairs={{0,7},{1,0},{2,1},{3,2},{4,3},{5,4},{6,5},{7,6},{8,15},{9,8},{10,9... | collective-permute-start | bytes 645128 | tf_op jit(solution)/shard_map/ppermute | solution.py:161
  19.9 7.5 %collective-permute-start.2 = (f32[21,20,128]{2,0,1:T(8,128)S(1)}, f32[21,20,128]{2,0,1:T(8,128)S(1)}, u32[]{:S(2)}, u32[]{:S(2)}) collective-permute-start(f32[21,20,128]{2,0,1:T(8,128)S(1)} %get-tuple-element.76), channel_id=1, source_target_pairs={{0,1},{1,2},{2,3},{3,4},{4,5},{5,6},{6,7},{7,0},{8,9},{9,10},{10,1... | collective-permute-start | bytes 645128 | tf_op jit(solution)/shard_map/ppermute | solution.py:161
  34.1 1.2 %copy-start.2 = (f32[19,19,1,1]{1,0,3,2:T(8,128)S(1)}, f32[19,19,1,1]{1,0,3,2:T(8,128)}, u32[]{:S(2)}) copy-start(f32[19,19,1,1]{1,0,3,2:T(8,128)} %constant.92) | copy-start | bytes 4336
  34.1 1.2 %copy-start.3 = (f32[19]{0:T(128)S(1)}, f32[19]{0:T(128)}, u32[]{:S(2)}) copy-start(f32[19]{0:T(128)} %constant.87.clone) | copy-start | bytes 232
  34.1 1.2 %copy-start.4 = (f32[19]{0:T(128)S(1)}, f32[19]{0:T(128)}, u32[]{:S(2)}) copy-start(f32[19]{0:T(128)} %constant.86.clone) | copy-start | bytes 232
  34.1 1.2 %copy-start.5 = (f32[19]{0:T(128)S(1)}, f32[19]{0:T(128)}, u32[]{:S(2)}) copy-start(f32[19]{0:T(128)} %constant.85.clone) | copy-start | bytes 232
  34.2 1.2 %copy-start.6 = (f32[19]{0:T(128)S(1)}, f32[19]{0:T(128)}, u32[]{:S(2)}) copy-start(f32[19]{0:T(128)} %constant.88.clone) | copy-start | bytes 232
  35.4 5.6 %copy-start.1 = (f32[19,19,1,1]{1,0,3,2:T(8,128)S(1)}, f32[19,19,1,1]{1,0,3,2:T(8,128)}, u32[]{:S(2)}) copy-start(f32[19,19,1,1]{1,0,3,2:T(8,128)} %constant.91) | copy-start | bytes 4336
  67.4 4.3 %collective-permute-start.4 = (f32[4,16,2,32]{3,1,0,2:T(8,128)S(1)}, f32[4,16,2,32]{3,1,0,2:T(8,128)S(1)}, u32[]{:S(2)}, u32[]{:S(2)}) collective-permute-start(f32[4,16,2,32]{3,1,0,2:T(8,128)S(1)} %select_bitcast_fusion), channel_id=1, source_target_pairs={{0,8},{8,0},{16,24},{24,16},{1,9},{9,1},{17,25},{25,17},{2,10},{10... | collective-permute-start | bytes 49160 | tf_op jit(solution)/shard_map/ppermute | solution.py:30
  71.8 4.0 %collective-permute-start.5 = (f32[4,16,1,32]{3,1,0,2:T(8,128)S(1)}, f32[4,16,1,32]{3,1,0,2:T(8,128)S(1)}, u32[]{:S(2)}, u32[]{:S(2)}) collective-permute-start(f32[4,16,1,32]{3,1,0,2:T(8,128)S(1)} %select_bitcast_fusion.1), channel_id=1, source_target_pairs={{0,16},{8,24},{16,0},{24,8},{1,17},{9,25},{17,1},{25,9},{2,18},{10... | collective-permute-start | bytes 24584 | tf_op jit(solution)/shard_map/ppermute | solution.py:30

commit v4 on v3

--- a/solution.py
+++ b/solution.py
@@ -201,7 +201,7 @@
                 o_ref[q, x] = v
                 return carry
 
-            lax.fori_loop(0, extent_x, move, 0)
+            lax.fori_loop(0, extent_x, move, 0, unroll=True)
 
         def render(x, carry):
             depth, red, green, blue = carry
@@ -216,7 +216,7 @@
             return (depth + extinction, red, green, blue)
 
         zero = jnp.zeros((extent_y, depth_z), jnp.float32)
-        depth, red, green, blue = lax.fori_loop(0, extent_x, render, (zero, zero, zero, zero))
+        depth, red, green, blue = lax.fori_loop(0, extent_x, render, (zero, zero, zero, zero), unroll=True)
         pic_ref[0] = red
         pic_ref[1] = green
         pic_ref[2] = blue

time: 76.8 us -> 64.6 us (0.84)
  Pallas kernels: 16.3 us -> 4.09 us
    pallas_call x1, Pallas kernels: 16.3 us -> 4.09 us  [stream_and_render(): pl.pallas_call(kernel, out_shape=(jax.ShapeDtypeStruct((19, extent_x, ext...]
  transfers between devices with their start and end apart: 6 -> 6, of which waited for: 6 -> 6; matrix products, arithmetic and copies ran while one was open for 7% -> 8% of each run, Pallas kernels for 0% -> 0%
where the time goes in v4:
time: 64.6 us; the launch traced here: 64.2 us
  waiting for transfers between devices  17.5 us (27%)
  local copies, waits for them, and re-layouts  11.7 us (18%)
  matrix products  11.5 us (18%)
  other arithmetic  10 us (15%)
  starting transfers between devices  8.42 us (13%)
  Pallas kernels  4.09 us (6%)
  between operations  1.03 us (2%)
    ppermute x4, waiting for transfers between devices, shift_ring(): lax.ppermute(x, axis, [(i, (i - step) % count) for i in range(count)])  14.6 us
    ppermute x4, starting transfers between devices, shift_ring(): lax.ppermute(x, axis, [(i, (i - step) % count) for i in range(count)])  6.28 us
    dot_general x1, matrix products, collide_major(): jnp.einsum('pq,q...->p...', relax_table, f - balance, precision=lax.Preci...  5.92 us
    dot_general x1, matrix products, collide_major(): jnp.einsum('pq,q...->p...', source_table, guo_term, precision=lax.Precisi...  5.62 us
    pallas_call x1, Pallas kernels, stream_and_render(): pl.pallas_call(kernel, out_shape=(jax.ShapeDtypeStruct((19, extent_x, ext...  4.09 us
    unnamed x16, local copies, waits for them, and re-layouts  3.4 us
    add x1, other arithmetic, collide_major(): return f - relaxed + sourced  3.11 us
    ppermute x2, waiting for transfers between devices, from_partner(): lax.ppermute(x, axis, [(i, i ^ 1 << distance) for i in range(lax.axis_siz...  2.85 us
  transfers between devices with their start and end apart: 6, of which 6 were waited for; matrix products, arithmetic and copies ran while one was open for 8% of the time, Pallas kernels for 0%

profile of v4, /device:TPU:0, one launch (start us, length us, event | category | flops | bytes accessed | tf_op | source)
XLA Modules:
  0.0 64.2 jit_solution(12925544611785698078)
XLA Ops:
  0.6 0.0 copy-start
  0.6 2.0 %bitcast_reduce_fusion = f32[16,16,128]{2,1,0:T(8,128)S(1)} fusion(f32[16,16,19,128]{3,1,2,0:T(8,128)} %param.7), kind=kLoop, calls=%fused_computation.200 | loop fusion | flops 589824 | bytes 2621440 | tf_op jit(solution)/shard_map/reduce_sum | solution.py:241
  2.7 1.0 %slice_bitcast_fusion.5 = (f32[19,16,128]{2,1,0:T(8,128)S(1)}, f32[19,16,128]{2,1,0:T(8,128)S(1)}) fusion(f32[19,16,16,128]{3,2,0,1:T(8,128)} %bitcast.118), kind=kLoop, calls=%fused_computation.169 | loop fusion | bytes 622592 | tf_op jit(solution)/shard_map/squeeze | solution.py:242
  3.8 3.9 %collective-permute-start.1 = (f32[21,16,128]{2,1,0:T(8,128)S(1)}, f32[21,16,128]{2,1,0:T(8,128)S(1)}, u32[]{:S(2)}, u32[]{:S(2)}) collective-permute-start(f32[21,16,128]{2,1,0:T(8,128)S(1)} %pad_maximum_fusion.13), channel_id=1, source_target_pairs={{0,24},{8,0},{16,8},{24,16},{1,25},{9,1},{17,9},{25,17},{2,26},{10... | collective-permute-start | bytes 516104 | tf_op jit(solution)/shard_map/ppermute | solution.py:161
  7.7 0.1 collective-permute-start
  7.8 4.7 %collective-permute-done.1 = f32[21,16,128]{2,1,0:T(8,128)S(1)} collective-permute-done((f32[21,16,128]{2,1,0:T(8,128)S(1)}, f32[21,16,128]{2,1,0:T(8,128)S(1)}, u32[]{:S(2)}, u32[]{:S(2)}) %collective-permute-start.1) | collective-permute-done | bytes 172064 | tf_op jit(solution)/shard_map/ppermute | solution.py:161
  12.5 3.5 %collective-permute-done = f32[21,16,128]{2,1,0:T(8,128)S(1)} collective-permute-done((f32[21,16,128]{2,1,0:T(8,128)S(1)}, f32[21,16,128]{2,1,0:T(8,128)S(1)}, u32[]{:S(2)}, u32[]{:S(2)}) %collective-permute-start) | collective-permute-done | bytes 172064 | tf_op jit(solution)/shard_map/ppermute | solution.py:161
  16.0 0.0 copy-done
  16.0 0.2 pad_maximum_fusion.1
  16.3 0.2 fusion.132
  16.6 0.1 fusion.50
  16.7 2.2 %collective-permute-start.3 = (f32[21,20,128]{2,0,1:T(8,128)S(1)}, f32[21,20,128]{2,0,1:T(8,128)}, u32[]{:S(2)}, u32[]{:S(2)}) collective-permute-start(f32[21,20,128]{2,0,1:T(8,128)S(1)} %get-tuple-element.77), channel_id=1, source_target_pairs={{0,7},{1,0},{2,1},{3,2},{4,3},{5,4},{6,5},{7,6},{8,15},{9,8},{10,9... | collective-permute-start | bytes 645128 | tf_op jit(solution)/shard_map/ppermute | solution.py:161
  18.9 1.0 %copy.20 = f32[19,18,16,128]{3,0,2,1:T(8,128)S(1)} copy(f32[19,18,16,128]{3,2,0,1:T(8,128)S(1)} %pad_maximum_fusion.1) | data formatting | bytes 5603328 | tf_op jit(solution)/shard_map/concatenate | solution.py:246
  19.9 0.1 collective-permute-start.2
  20.0 5.2 %collective-permute-done.3 = f32[21,20,128]{2,0,1:T(8,128)} collective-permute-done((f32[21,20,128]{2,0,1:T(8,128)S(1)}, f32[21,20,128]{2,0,1:T(8,128)}, u32[]{:S(2)}, u32[]{:S(2)}) %collective-permute-start.3) | collective-permute-done | bytes 215072 | tf_op jit(solution)/shard_map/ppermute | solution.py:161
  25.2 1.0 %slice_bitcast_fusion.8 = (f32[20,1,128]{2,1,0:T(1,128)S(1)}, f32[20,1,128]{2,1,0:T(1,128)S(1)}) fusion(f32[21,20,128]{2,0,1:T(8,128)} %collective-permute-done.3), kind=kLoop, calls=%fused_computation.189 | loop fusion | bytes 40960 | tf_op jit(solution)/shard_map/broadcast_in_dim;squeeze | solution.py:260
  26.2 1.2 %collective-permute-done.2 = f32[21,20,128]{2,0,1:T(8,128)S(1)} collective-permute-done((f32[21,20,128]{2,0,1:T(8,128)S(1)}, f32[21,20,128]{2,0,1:T(8,128)S(1)}, u32[]{:S(2)}, u32[]{:S(2)}) %collective-permute-start.2) | collective-permute-done | bytes 215072 | tf_op jit(solution)/shard_map/ppermute | solution.py:161
  27.4 0.1 pad_maximum_fusion.6
  27.5 0.1 fusion.137
  27.7 0.1 fusion.138
  27.8 0.1 fusion.135
  27.9 0.1 fusion.136
  28.0 0.2 fusion.134
  28.3 0.2 fusion.133
  28.5 1.0 %slice_bitcast_fusion = f32[19,18,1,128]{3,0,2,1:T(8,128)S(1)} fusion(f32[21,20,128]{2,0,1:T(8,128)} %collective-permute-done.3), kind=kLoop, calls=%fused_computation.120 | loop fusion | bytes 350208 | tf_op jit(solution)/shard_map/broadcast_in_dim | solution.py:257
  29.5 0.9 %pad_maximum_fusion = (f32[19,18,18,128]{3,0,2,1:T(8,128)S(1)}, f32[18,18,128]{2,1,0:T(8,128)S(1)}) fusion(f32[19,18,1,128]{3,0,2,1:T(8,128)S(1)} %slice_bitcast_fusion, f32[19,18,16,128]{3,0,2,1:T(8,128)S(1)} %copy.20, f32[19,18,1,128]{3,0,2,1:T(8,128)S(1)} %slice_bitcast_fusion.1), kind=kLoop, calls=%fused_computation.7 | loop fusion | flops 2322432 | bytes 6469632 | tf_op jit(solution)/shard_map/concatenate | solution.py:256
  30.5 2.0 %fusion.131 = (f32[1,18,18,128]{3,0,2,1:T(1,128)S(1)}, f32[1,18,18,128]{3,0,2,1:T(1,128)S(1)}, f32[1,18,18,128]{3,0,2,1:T(1,128)S(1)}, f32[1,18,18,128]{3,0,2,1:...) fusion(f32[19,18,18,128]{3,0,2,1:T(8,128)S(1)} %get-tuple-eleme, ...), kind=kLoop, calls=%fused_computation.207 | loop fusion | bytes 5308416 | tf_op jit(solution)/shard_map/slice | solution.py:172
  32.6 0.8 %copy_add_fusion.7 = f32[1,18,18,128]{3,0,2,1:T(1,128)S(1)} fusion(f32[1,18,18,128]{3,2,1,0:T(8,128)S(1)} %copy_multiply_fusion.7, f32[1,18,18,128]{3,2,1,0:T(8,128)S(1)} %copy_multiply_fusion.3, f32[1,18,18,128]{3,2,1,0:T(8,128)S(1)} %copy_multiply_fusion.9, f32[19,18,18,128]{3,0,2,1:T(8,128)S(1)} %get-tuple-element.33), kind=kLoop, calls=%fused_computation.161 | loop fusion | flops 331776 | bytes 1492992 | tf_op jit(solution)/shard_map/add | solution.py:172
  33.4 0.7 %fusion.69 = (f32[18,18,128]{2,1,0:T(8,128)S(1)}, f32[18,18,128]{2,1,0:T(8,128)S(1)}) fusion(f32[18,18,128]{2,1,0:T(8,128)S(1)} %get-tuple-element.34, f32[1,18,18,128]{3,0,2,1:T(1,128)S(1)} %get-tuple-element.30, f32[1,18,18,128]{3,0,2,1:T(1,128)S(1)} %get-tuple-element.31, f32[1,18,18,128]{3,0,2,1:T(1,128)S(1)} %copy_add_fusion.7, ...), kind=kLoop, calls=%fused_computation.88 | loop fusion | flops 1534464 | bytes 2820096 | tf_op jit(solution)/shard_map/div | solution.py:175
  34.1 0.0 copy-start.2
  34.1 0.0 copy-start.3
  34.1 0.0 copy-start.4
  34.1 0.0 copy-start.5
  34.2 0.0 copy-start.6
  34.2 1.1 %add_multiply_fusion = (f32[18,18,128]{2,1,0:T(8,128)S(1)}, f32[18,18,128]{2,1,0:T(8,128)S(1)}, f32[18,18,128]{2,1,0:T(8,128)S(1)}, f32[18,18,128]{2,1,0:T(8,128)S(1)}, f32[18,18,128]{2,1,0:T(8,128)S(1)}) fusion(f32[18,18,128]{2,1,0:T(8,128)S(1)} %get-tuple-element.15, f32[18,18,128]{2,1,0:T(8,128)S(1)} %get-tuple-element.34, ...), kind=kLoop, calls=%fused_computation.155 | loop fusion | flops 3566592 | bytes 6635520 | tf_op jit(solution)/shard_map/mul | solution.py:180
  35.2 0.1 multiply_add_fusion.3
  35.3 0.0 copy-done.2
  35.4 0.0 copy-done.3
  35.4 0.0 copy-done.4
  35.4 0.0 copy-done.5
  35.4 0.0 copy-done.6
  35.4 0.0 copy-start.1
  35.4 5.6 %fusion.6 = f32[19,18,18,128]{3,0,2,1:T(8,128)S(1)} fusion(f32[19,19,1,1]{1,0,3,2:T(8,128)S(1)} %copy-done.2, f32[18,18,128]{2,1,0:T(8,128)S(1)} %multiply_add_fusion.3, f32[18,18,128]{2,1,0:T(8,128)S(1)} %get-tuple-element.16, f32[18,18,128]{2,1,0:T(8,128)S(1)} %get-tuple-element.14, f32[18,18,128]{2,1,0:T(8,128)S(1)} %get-tuple-element.12, ...), kind=kOutput, calls=%fused_computation.8 | convolution fusion | flops 192264192 | bytes 4314836 | tf_op jit(solution)/shard_map/pq,q...->p.../dot_general | solution.py:185
  41.0 0.0 copy-done.1
  41.0 5.9 %fusion.21 = f32[19,18,18,128]{3,0,2,1:T(8,128)S(1)} fusion(f32[19,19,1,1]{1,0,3,2:T(8,128)S(1)} %copy-done.1, f32[18,18,128]{2,1,0:T(8,128)S(1)} %get-tuple-element.10, f32[18,18,128]{2,1,0:T(8,128)S(1)} %get-tuple-element.15, f32[19]{0:T(128)S(1)} %copy-done.3, f32[18,18,128]{2,1,0:T(8,128)S(1)} %get-tuple-element.13, f32[19]{0:T(128)S(1)} %copy-done.4, ...), kind=kOutput, calls=%fused_computation.25 | convolution fusion | flops 194628096 | bytes 7134932 | tf_op jit(solution)/shard_map/pq,q...->p.../dot_general | solution.py:184
  47.0 3.1 %copy_add_fusion.c_ref = f32[19,18,18,128]{3,2,1,0:T(8,128)} fusion(f32[19,18,18,128]{3,0,2,1:T(8,128)S(1)} %fusion.6, f32[19,18,18,128]{3,0,2,1:T(8,128)S(1)} %fusion.21), kind=kLoop, calls=%fused_computation.1 | loop fusion | flops 787968 | bytes 9455616 | tf_op jit(solution)/shard_map/add | solution.py:186
  50.1 4.1 %shard_map.86 = (f32[19,16,16,128]{3,2,1,0:T(8,128)}, f32[4,16,128]{2,1,0:T(8,128)}) custom-call(f32[19,18,18,128]{3,2,1,0:T(8,128)} %copy_add_fusion.c_ref), custom_call_target="tpu_custom_call" | custom-call | tf_op jit(solution)/shard_map/pallas_call | solution.py:225
  54.2 0.9 %reshape_reshape.3 = f32[4,16,2,2,32]{4,3,2,1,0:T(2,128)S(1)} reshape(f32[4,16,128]{2,1,0:T(8,128)} %get-tuple-element.5) | data formatting | bytes 65536 | tf_op jit(solution)/shard_map/reshape;reshape | solution.py:289
  55.1 0.1 fusion.140
  55.2 1.6 %collective-permute-start.4 = (f32[4,16,2,32]{3,1,0,2:T(8,128)S(1)}, f32[4,16,2,32]{3,1,0,2:T(8,128)S(1)}, u32[]{:S(2)}, u32[]{:S(2)}) collective-permute-start(f32[4,16,2,32]{3,1,0,2:T(8,128)S(1)} %select_bitcast_fusion), channel_id=1, source_target_pairs={{0,8},{8,0},{16,24},{24,16},{1,9},{9,1},{17,25},{25,17},{2,10},{10... | collective-permute-start | bytes 49160 | tf_op jit(solution)/shard_map/ppermute | solution.py:30
  56.8 2.8 %collective-permute-done.4 = f32[4,16,2,32]{3,1,0,2:T(8,128)S(1)} collective-permute-done((f32[4,16,2,32]{3,1,0,2:T(8,128)S(1)}, f32[4,16,2,32]{3,1,0,2:T(8,128)S(1)}, u32[]{:S(2)}, u32[]{:S(2)}) %collective-permute-start.4) | collective-permute-done | bytes 16416 | tf_op jit(solution)/shard_map/ppermute | solution.py:30
  59.6 0.6 collective-permute-start.5
  60.2 3.3 %copy.49 = f32[16,16,19,128]{3,1,2,0:T(8,128)} copy(f32[16,16,19,128]{3,1,0,2:T(8,128)} %bitcast.120) | data formatting | bytes 4980736
  63.5 0.1 collective-permute-done.5
  63.6 0.6 fusion.116
  (24 shorter events, 0.3 us)
Async XLA Ops:
  0.6 15.4 %copy-start = (f32[16,16,19,128]{3,1,2,0:T(8,128)S(1)}, f32[16,16,19,128]{3,1,2,0:T(8,128)}, u32[]{:S(2)}) copy-start(f32[16,16,19,128]{3,1,2,0:T(8,128)} %param.7) | copy-start | bytes 7471108
  3.8 8.7 %collective-permute-start.1 = (f32[21,16,128]{2,1,0:T(8,128)S(1)}, f32[21,16,128]{2,1,0:T(8,128)S(1)}, u32[]{:S(2)}, u32[]{:S(2)}) collective-permute-start(f32[21,16,128]{2,1,0:T(8,128)S(1)} %pad_maximum_fusion.13), channel_id=1, source_target_pairs={{0,24},{8,0},{16,8},{24,16},{1,25},{9,1},{17,9},{25,17},{2,26},{10... | collective-permute-start | bytes 516104 | tf_op jit(solution)/shard_map/ppermute | solution.py:161
  7.7 8.3 %collective-permute-start = (f32[21,16,128]{2,1,0:T(8,128)S(1)}, f32[21,16,128]{2,1,0:T(8,128)S(1)}, u32[]{:S(2)}, u32[]{:S(2)}) collective-permute-start(f32[21,16,128]{2,1,0:T(8,128)S(1)} %pad_maximum_fusion.12), channel_id=1, source_target_pairs={{0,8},{8,16},{16,24},{24,0},{1,9},{9,17},{17,25},{25,1},{2,10},{10... | collective-permute-start | bytes 516104 | tf_op jit(solution)/shard_map/ppermute | solution.py:161
  16.7 8.5 %collective-permute-start.3 = (f32[21,20,128]{2,0,1:T(8,128)S(1)}, f32[21,20,128]{2,0,1:T(8,128)}, u32[]{:S(2)}, u32[]{:S(2)}) collective-permute-start(f32[21,20,128]{2,0,1:T(8,128)S(1)} %get-tuple-element.77), channel_id=1, source_target_pairs={{0,7},{1,0},{2,1},{3,2},{4,3},{5,4},{6,5},{7,6},{8,15},{9,8},{10,9... | collective-permute-start | bytes 645128 | tf_op jit(solution)/shard_map/ppermute | solution.py:161
  19.9 7.5 %collective-permute-start.2 = (f32[21,20,128]{2,0,1:T(8,128)S(1)}, f32[21,20,128]{2,0,1:T(8,128)S(1)}, u32[]{:S(2)}, u32[]{:S(2)}) collective-permute-start(f32[21,20,128]{2,0,1:T(8,128)S(1)} %get-tuple-element.76), channel_id=1, source_target_pairs={{0,1},{1,2},{2,3},{3,4},{4,5},{5,6},{6,7},{7,0},{8,9},{9,10},{10,1... | collective-permute-start | bytes 645128 | tf_op jit(solution)/shard_map/ppermute | solution.py:161
  34.1 1.2 %copy-start.2 = (f32[19,19,1,1]{1,0,3,2:T(8,128)S(1)}, f32[19,19,1,1]{1,0,3,2:T(8,128)}, u32[]{:S(2)}) copy-start(f32[19,19,1,1]{1,0,3,2:T(8,128)} %constant.92) | copy-start | bytes 4336
  34.1 1.2 %copy-start.3 = (f32[19]{0:T(128)S(1)}, f32[19]{0:T(128)}, u32[]{:S(2)}) copy-start(f32[19]{0:T(128)} %constant.87.clone) | copy-start | bytes 232
  34.1 1.2 %copy-start.4 = (f32[19]{0:T(128)S(1)}, f32[19]{0:T(128)}, u32[]{:S(2)}) copy-start(f32[19]{0:T(128)} %constant.86.clone) | copy-start | bytes 232
  34.1 1.2 %copy-start.5 = (f32[19]{0:T(128)S(1)}, f32[19]{0:T(128)}, u32[]{:S(2)}) copy-start(f32[19]{0:T(128)} %constant.85.clone) | copy-start | bytes 232
  34.2 1.2 %copy-start.6 = (f32[19]{0:T(128)S(1)}, f32[19]{0:T(128)}, u32[]{:S(2)}) copy-start(f32[19]{0:T(128)} %constant.88.clone) | copy-start | bytes 232
  35.4 5.6 %copy-start.1 = (f32[19,19,1,1]{1,0,3,2:T(8,128)S(1)}, f32[19,19,1,1]{1,0,3,2:T(8,128)}, u32[]{:S(2)}) copy-start(f32[19,19,1,1]{1,0,3,2:T(8,128)} %constant.91) | copy-start | bytes 4336
  55.2 4.3 %collective-permute-start.4 = (f32[4,16,2,32]{3,1,0,2:T(8,128)S(1)}, f32[4,16,2,32]{3,1,0,2:T(8,128)S(1)}, u32[]{:S(2)}, u32[]{:S(2)}) collective-permute-start(f32[4,16,2,32]{3,1,0,2:T(8,128)S(1)} %select_bitcast_fusion), channel_id=1, source_target_pairs={{0,8},{8,0},{16,24},{24,16},{1,9},{9,1},{17,25},{25,17},{2,10},{10... | collective-permute-start | bytes 49160 | tf_op jit(solution)/shard_map/ppermute | solution.py:30
  59.6 4.0 %collective-permute-start.5 = (f32[4,16,1,32]{3,1,0,2:T(8,128)S(1)}, f32[4,16,1,32]{3,1,0,2:T(8,128)S(1)}, u32[]{:S(2)}, u32[]{:S(2)}) collective-permute-start(f32[4,16,1,32]{3,1,0,2:T(8,128)S(1)} %select_bitcast_fusion.1), channel_id=1, source_target_pairs={{0,16},{8,24},{16,0},{24,8},{1,17},{9,25},{17,1},{25,9},{2,18},{10... | collective-permute-start | bytes 24584 | tf_op jit(solution)/shard_map/ppermute | solution.py:30

commit v5 on v4

--- a/solution.py
+++ b/solution.py
@@ -181,9 +181,9 @@
     guo_term = spread * (3.0 * (pushed - work_done) + 9.0 * along * pushed)
     relax_table = jnp.asarray(relaxing, dtype=jnp.float32)
     source_table = jnp.asarray(forcing_map, dtype=jnp.float32)
-    relaxed = jnp.einsum("pq,q...->p...", relax_table, f - balance, precision=lax.Precision.HIGHEST)
-    sourced = jnp.einsum("pq,q...->p...", source_table, guo_term, precision=lax.Precision.HIGHEST)
-    return f - relaxed + sourced
+    table = jnp.concatenate([relax_table, -source_table], axis=1)
+    stacked = jnp.concatenate([f - balance, guo_term], axis=0)
+    return f - jnp.einsum("pq,q...->p...", table, stacked, precision=lax.Precision.HIGH)
 
 
 def stream_and_render(collided, velocities, extent_x, extent_y, length_x):

time: 64.6 us -> 62.8 us (0.972)
  other arithmetic: 10 us -> 18.8 us
  matrix products: 11.5 us -> 3.79 us
  local copies, waits for them, and re-layouts: 11.7 us -> 8.98 us
  waiting for transfers between devices: 17.5 us -> 16.5 us
  starting transfers between devices: 8.42 us -> 9.32 us
    sub x0 -> x2, other arithmetic: none -> 9.33 us  [the longest x1 6.51 us: collide_major(): stacked = jnp.concatenate([f - balance, guo_term], axis=0)]
    dot_general x2 -> x1, matrix products: 11.5 us -> 3.79 us  [collide_major(): jnp.einsum('pq,q...->p...', table, stacked, precision=lax.Precision.HIGH)]
    concatenate x0 -> x1, other arithmetic: none -> 4.02 us  [collide_major(): stacked = jnp.concatenate([f - balance, guo_term], axis=0)]
    add x2 -> x0, other arithmetic: 3.91 us -> none  [the longest x1 3.11 us: collide_major(): return f - relaxed + sourced]
    slice x1 -> x0, local copies, waits for them, and re-layouts: 2.04 us -> none  [collide_major(): f[q] * float(velocities[q][d])]
    ppermute x4, waiting for transfers between devices: 14.6 us -> 12.6 us  [shift_ring(): lax.ppermute(x, axis, [(i, (i - step) % count) for i in range(count)])]
    ppermute x4, starting transfers between devices: 6.28 us -> 7.6 us  [shift_ring(): lax.ppermute(x, axis, [(i, (i - step) % count) for i in range(count)])]
    broadcast_in_dim x1 -> x2, local copies, waits for them, and re-layouts: 0.02 us -> 1.13 us  [body(): from_below[:19, 1:-1, None]]
  transfers between devices with their start and end apart: 6 -> 6, of which waited for: 6 -> 5; matrix products, arithmetic and copies ran while one was open for 8% -> 7% of each run, Pallas kernels for 0% -> 0%
where the time goes in v5:
time: 62.8 us; the launch traced here: 62.5 us
  other arithmetic  18.8 us (30%)
  waiting for transfers between devices  16.5 us (26%)
  starting transfers between devices  9.32 us (15%)
  local copies, waits for them, and re-layouts  8.98 us (14%)
  Pallas kernels  4.1 us (7%)
  matrix products  3.79 us (6%)
  between operations  1 us (2%)
    ppermute x4, waiting for transfers between devices, shift_ring(): lax.ppermute(x, axis, [(i, (i - step) % count) for i in range(count)])  12.6 us
    ppermute x4, starting transfers between devices, shift_ring(): lax.ppermute(x, axis, [(i, (i - step) % count) for i in range(count)])  7.6 us
    sub x1, other arithmetic, collide_major(): stacked = jnp.concatenate([f - balance, guo_term], axis=0)  6.51 us
    pallas_call x1, Pallas kernels, stream_and_render(): pl.pallas_call(kernel, out_shape=(jax.ShapeDtypeStruct((19, extent_x, ext...  4.1 us
    concatenate x1, other arithmetic, collide_major(): stacked = jnp.concatenate([f - balance, guo_term], axis=0)  4.02 us
    ppermute x2, waiting for transfers between devices, from_partner(): lax.ppermute(x, axis, [(i, i ^ 1 << distance) for i in range(lax.axis_siz...  3.88 us
    dot_general x1, matrix products, collide_major(): jnp.einsum('pq,q...->p...', table, stacked, precision=lax.Precision.HIGH)  3.79 us
    unnamed x14, local copies, waits for them, and re-layouts  3.39 us
  transfers between devices with their start and end apart: 6, of which 5 were waited for; matrix products, arithmetic and copies ran while one was open for 7% of the time, Pallas kernels for 0%

profile of v5, /device:TPU:0, one launch (start us, length us, event | category | flops | bytes accessed | tf_op | source)
XLA Modules:
  0.0 62.5 jit_solution(1251105059336457435)
XLA Ops:
  0.6 0.0 copy-start
  0.6 2.0 %bitcast_reduce_fusion = f32[16,16,128]{2,1,0:T(8,128)S(1)} fusion(f32[16,16,19,128]{3,1,2,0:T(8,128)} %param.7), kind=kLoop, calls=%fused_computation.156 | loop fusion | flops 589824 | bytes 2621440 | tf_op jit(solution)/shard_map/reduce_sum | solution.py:241
  2.7 1.0 %slice_bitcast_fusion.6 = (f32[19,16,128]{2,1,0:T(8,128)S(1)}, f32[19,16,128]{2,1,0:T(8,128)S(1)}) fusion(f32[19,16,16,128]{3,2,0,1:T(8,128)} %bitcast.111), kind=kLoop, calls=%fused_computation.125 | loop fusion | bytes 622592 | tf_op jit(solution)/shard_map/squeeze | solution.py:242
  3.8 3.0 %collective-permute-start = (f32[21,16,128]{2,1,0:T(8,128)S(1)}, f32[21,16,128]{2,1,0:T(8,128)S(1)}, u32[]{:S(2)}, u32[]{:S(2)}) collective-permute-start(f32[21,16,128]{2,1,0:T(8,128)S(1)} %pad_maximum_fusion.13), channel_id=1, source_target_pairs={{0,8},{8,16},{16,24},{24,0},{1,9},{9,17},{17,25},{25,1},{2,10},{10... | collective-permute-start | bytes 516104 | tf_op jit(solution)/shard_map/ppermute | solution.py:161
  6.8 1.0 %collective-permute-start.1 = (f32[21,16,128]{2,1,0:T(8,128)S(1)}, f32[21,16,128]{2,1,0:T(8,128)S(1)}, u32[]{:S(2)}, u32[]{:S(2)}) collective-permute-start(f32[21,16,128]{2,1,0:T(8,128)S(1)} %pad_maximum_fusion.14), channel_id=1, source_target_pairs={{0,24},{8,0},{16,8},{24,16},{1,25},{9,1},{17,9},{25,17},{2,26},{10... | collective-permute-start | bytes 516104 | tf_op jit(solution)/shard_map/ppermute | solution.py:161
  7.8 5.1 %collective-permute-done = f32[21,16,128]{2,1,0:T(8,128)S(1)} collective-permute-done((f32[21,16,128]{2,1,0:T(8,128)S(1)}, f32[21,16,128]{2,1,0:T(8,128)S(1)}, u32[]{:S(2)}, u32[]{:S(2)}) %collective-permute-start) | collective-permute-done | bytes 172064 | tf_op jit(solution)/shard_map/ppermute | solution.py:161
  12.9 3.1 %collective-permute-done.1 = f32[21,16,128]{2,1,0:T(8,128)S(1)} collective-permute-done((f32[21,16,128]{2,1,0:T(8,128)S(1)}, f32[21,16,128]{2,1,0:T(8,128)S(1)}, u32[]{:S(2)}, u32[]{:S(2)}) %collective-permute-start.1) | collective-permute-done | bytes 172064 | tf_op jit(solution)/shard_map/ppermute | solution.py:161
  16.0 0.0 copy-done
  16.0 0.2 pad_maximum_fusion.2
  16.3 0.2 fusion.92
  16.6 0.1 fusion.7
  16.7 0.1 collective-permute-start.2
  16.8 3.5 %collective-permute-start.3 = (f32[21,20,128]{2,0,1:T(8,128)S(1)}, f32[21,20,128]{2,0,1:T(8,128)S(1)}, u32[]{:S(2)}, u32[]{:S(2)}) collective-permute-start(f32[21,20,128]{2,0,1:T(8,128)S(1)} %get-tuple-element.61), channel_id=1, source_target_pairs={{0,7},{1,0},{2,1},{3,2},{4,3},{5,4},{6,5},{7,6},{8,15},{9,8},{10,9... | collective-permute-start | bytes 645128 | tf_op jit(solution)/shard_map/ppermute | solution.py:161
  20.3 4.4 %collective-permute-done.2 = f32[21,20,128]{2,0,1:T(8,128)} collective-permute-done((f32[21,20,128]{2,0,1:T(8,128)S(1)}, f32[21,20,128]{2,0,1:T(8,128)}, u32[]{:S(2)}, u32[]{:S(2)}) %collective-permute-start.2) | collective-permute-done | bytes 215072 | tf_op jit(solution)/shard_map/ppermute | solution.py:161
  24.8 1.0 %slice_bitcast_fusion.7 = (f32[20,1,128]{2,1,0:T(1,128)S(1)}, f32[20,1,128]{2,1,0:T(1,128)S(1)}) fusion(f32[21,20,128]{2,0,1:T(8,128)} %collective-permute-done.2), kind=kLoop, calls=%fused_computation.143 | loop fusion | bytes 40960 | tf_op jit(solution)/shard_map/broadcast_in_dim;squeeze | solution.py:260
  25.7 0.0 collective-permute-done.3
  25.8 0.1 maximum_maximum_fusion
  25.9 0.2 fusion.93
  26.1 0.2 fusion.94
  26.4 0.1 fusion.95
  26.5 0.1 fusion.96
  26.6 0.1 fusion.97
  26.7 0.1 fusion.98
  26.9 0.2 copy.11
  27.1 1.0 %slice_bitcast_fusion.2 = f32[19,18,1,128]{3,0,1,2:T(8,128)S(1)} fusion(f32[21,20,128]{2,0,1:T(8,128)} %collective-permute-done.2), kind=kLoop, calls=%fused_computation.95 | loop fusion | bytes 350208 | tf_op jit(solution)/shard_map/broadcast_in_dim | solution.py:257
  28.0 0.2 copy.9
  28.2 0.8 %pad_maximum_fusion.1 = (f32[19,18,18,128]{3,2,1,0:T(8,128)S(1)}, f32[18,18,128]{2,1,0:T(8,128)S(1)}) fusion(f32[19,18,1,128]{3,2,1,0:T(1,128)S(1)} %copy.11, f32[19,18,1,128]{3,2,1,0:T(1,128)S(1)} %copy.9, f32[19,1,16,128]{3,2,0,1:T(8,128)S(1)} %slice_bitcast_fusion.3, f32[19,16,16,128]{3,2,0,1:T(8,128)S(1)} %bitcast.113, ...), kind=kLoop, calls=%fused_computation.8 | loop fusion | flops 3723264 | bytes 6469632 | tf_op jit(solution)/shard_map/concatenate | solution.py:256
  29.0 0.0 copy-start.2
  29.0 0.0 copy-start.3
  29.0 0.0 copy-start.4
  29.0 0.0 copy-start.5
  29.1 1.4 %add_multiply_fusion.1 = (f32[18,18,128]{2,1,0:T(8,128)S(1)}, f32[18,18,128]{2,1,0:T(8,128)S(1)}, f32[18,18,128]{2,1,0:T(8,128)S(1)}, f32[18,18,128]{2,1,0:T(8,1...) fusion(f32[18,18,128]{2,1,0:T(8,128)S(1)} %get-tuple-element.16, ...), kind=kLoop, calls=%fused_computation.119 | loop fusion | flops 4935168 | bytes 7464960 | tf_op jit(solution)/shard_map/mul | solution.py:180
  30.4 0.1 multiply_add_fusion.1
  30.5 0.0 copy-done.2
  30.5 0.0 copy-done.3
  30.5 0.0 copy-done.4
  30.5 0.0 copy-done.5
  30.5 6.5 %fusion.5 = (f32[19,18,18,128]{3,2,1,0:T(8,128)}, f32[19,18,18,128]{3,2,1,0:T(8,128)}) fusion(f32[18,18,128]{2,1,0:T(8,128)S(1)} %get-tuple-element.8, f32[18,18,128]{2,1,0:T(8,128)S(1)} %get-tuple-element.13, f32[19]{0:T(128)S(1)} %copy-done.4, f32[18,18,128]{2,1,0:T(8,128)S(1)} %get-tuple-element.11, f32[19]{0:T(128)S(1)} %copy-done.3, ...), kind=kLoop, calls=%fused_computation.7 | loop fusion | flops 22675968 | bytes 10948912 | tf_op jit(solution)/shard_map/sub | solution.py:185
  37.0 0.0 copy-start.1
  37.0 4.0 %pad_maximum_fusion = f32[38,18,18,128]{3,2,1,0:T(8,128)S(1)} fusion(f32[19,18,18,128]{3,2,1,0:T(8,128)} %get-tuple-element.22, f32[19,18,18,128]{3,2,1,0:T(8,128)} %get-tuple-element.21), kind=kLoop, calls=%fused_computation | loop fusion | flops 1575936 | bytes 12607488 | tf_op jit(solution)/shard_map/concatenate | solution.py:185
  41.1 0.0 copy-done.1
  41.1 3.8 %fusion = f32[19,18,18,128]{3,0,2,1:T(8,128)S(1)} fusion(f32[19,38,1,1]{1,0,3,2:T(8,128)S(1)} %copy-done.1, f32[38,18,18,128]{3,2,1,0:T(8,128)S(1)} %pad_maximum_fusion), kind=kOutput, calls=%fused_computation.1 | convolution fusion | flops 179656704 | bytes 9458504 | tf_op jit(solution)/shard_map/pq,q...->p.../dot_general | solution.py:186
  44.9 2.8 %copy_subtract_fusion.c_ref = f32[19,18,18,128]{3,2,1,0:T(8,128)} fusion(f32[19,18,18,128]{3,0,2,1:T(8,128)S(1)} %fusion, f32[19,18,1,128]{3,2,1,0:T(1,128)S(1)} %copy.11, f32[19,18,1,128]{3,2,1,0:T(1,128)S(1)} %copy.9, f32[19,1,16,128]{3,2,0,1:T(8,128)S(1)} %slice_bitcast_fusion.3, f32[19,16,16,128]{3,2,0,1:T(8,128)S(1)} %bitcast.115, ...), kind=kLoop, calls=%fused_computation.9 | loop fusion | flops 3764736 | bytes 9455616 | tf_op jit(solution)/shard_map/sub | solution.py:186
  47.7 4.1 %shard_map.86 = (f32[19,16,16,128]{3,2,1,0:T(8,128)}, f32[4,16,128]{2,1,0:T(8,128)}) custom-call(f32[19,18,18,128]{3,2,1,0:T(8,128)} %copy_subtract_fusion.c_ref), custom_call_target="tpu_custom_call" | custom-call | tf_op jit(solution)/shard_map/pallas_call | solution.py:225
  51.8 0.9 %reshape_reshape.3 = f32[4,16,2,2,32]{4,3,2,1,0:T(2,128)S(1)} reshape(f32[4,16,128]{2,1,0:T(8,128)} %get-tuple-element.5) | data formatting | bytes 65536 | tf_op jit(solution)/shard_map/reshape;reshape | solution.py:289
  52.7 0.1 fusion.100
  52.8 1.6 %collective-permute-start.4 = (f32[4,16,2,32]{3,1,0,2:T(8,128)S(1)}, f32[4,16,2,32]{3,1,0,2:T(8,128)S(1)}, u32[]{:S(2)}, u32[]{:S(2)}) collective-permute-start(f32[4,16,2,32]{3,1,0,2:T(8,128)S(1)} %select_bitcast_fusion), channel_id=1, source_target_pairs={{0,8},{8,0},{16,24},{24,16},{1,9},{9,1},{17,25},{25,17},{2,10},{10... | collective-permute-start | bytes 49160 | tf_op jit(solution)/shard_map/ppermute | solution.py:30
  54.4 3.4 %collective-permute-done.4 = f32[4,16,2,32]{3,1,0,2:T(8,128)S(1)} collective-permute-done((f32[4,16,2,32]{3,1,0,2:T(8,128)S(1)}, f32[4,16,2,32]{3,1,0,2:T(8,128)S(1)}, u32[]{:S(2)}, u32[]{:S(2)}) %collective-permute-start.4) | collective-permute-done | bytes 16416 | tf_op jit(solution)/shard_map/ppermute | solution.py:30
  57.9 0.2 collective-permute-start.5
  58.0 3.3 %copy.16 = f32[16,16,19,128]{3,1,2,0:T(8,128)} copy(f32[16,16,19,128]{3,1,0,2:T(8,128)} %bitcast.116) | data formatting | bytes 4980736
  61.3 0.5 collective-permute-done.5
  61.9 0.6 %fusion.81 = f32[4,16,32]{2,1,0:T(8,128)} fusion(f32[4,16,1,32]{3,1,0,2:T(8,128)S(1)} %collective-permute-done.5, f32[16,32]{1,0:T(8,128)S(1)} %fusion.84, pred[]{:T(512)S(6)} %eq.19, f32[4,16,1,2,32]{4,1,0,3,2:T(8,128)S(1)} %fusion.78, pred[]{:T(512)S(6)} %eq.20), kind=kLoop, calls=%fused_computation.138 | loop fusion | flops 10240 | bytes 34818 | tf_op jit(solution)/shard_map/reshape | solution.py:298
  (21 shorter events, 0.3 us)
Async XLA Ops:
  0.6 15.4 %copy-start = (f32[16,16,19,128]{3,1,2,0:T(8,128)S(1)}, f32[16,16,19,128]{3,1,2,0:T(8,128)}, u32[]{:S(2)}) copy-start(f32[16,16,19,128]{3,1,2,0:T(8,128)} %param.7) | copy-start | bytes 7471108
  3.8 9.1 %collective-permute-start = (f32[21,16,128]{2,1,0:T(8,128)S(1)}, f32[21,16,128]{2,1,0:T(8,128)S(1)}, u32[]{:S(2)}, u32[]{:S(2)}) collective-permute-start(f32[21,16,128]{2,1,0:T(8,128)S(1)} %pad_maximum_fusion.13), channel_id=1, source_target_pairs={{0,8},{8,16},{16,24},{24,0},{1,9},{9,17},{17,25},{25,1},{2,10},{10... | collective-permute-start | bytes 516104 | tf_op jit(solution)/shard_map/ppermute | solution.py:161
  6.8 9.2 %collective-permute-start.1 = (f32[21,16,128]{2,1,0:T(8,128)S(1)}, f32[21,16,128]{2,1,0:T(8,128)S(1)}, u32[]{:S(2)}, u32[]{:S(2)}) collective-permute-start(f32[21,16,128]{2,1,0:T(8,128)S(1)} %pad_maximum_fusion.14), channel_id=1, source_target_pairs={{0,24},{8,0},{16,8},{24,16},{1,25},{9,1},{17,9},{25,17},{2,26},{10... | collective-permute-start | bytes 516104 | tf_op jit(solution)/shard_map/ppermute | solution.py:161
  16.7 8.0 %collective-permute-start.2 = (f32[21,20,128]{2,0,1:T(8,128)S(1)}, f32[21,20,128]{2,0,1:T(8,128)}, u32[]{:S(2)}, u32[]{:S(2)}) collective-permute-start(f32[21,20,128]{2,0,1:T(8,128)S(1)} %get-tuple-element.60), channel_id=1, source_target_pairs={{0,1},{1,2},{2,3},{3,4},{4,5},{5,6},{6,7},{7,0},{8,9},{9,10},{10,1... | collective-permute-start | bytes 645128 | tf_op jit(solution)/shard_map/ppermute | solution.py:161
  16.8 8.9 %collective-permute-start.3 = (f32[21,20,128]{2,0,1:T(8,128)S(1)}, f32[21,20,128]{2,0,1:T(8,128)S(1)}, u32[]{:S(2)}, u32[]{:S(2)}) collective-permute-start(f32[21,20,128]{2,0,1:T(8,128)S(1)} %get-tuple-element.61), channel_id=1, source_target_pairs={{0,7},{1,0},{2,1},{3,2},{4,3},{5,4},{6,5},{7,6},{8,15},{9,8},{10,9... | collective-permute-start | bytes 645128 | tf_op jit(solution)/shard_map/ppermute | solution.py:161
  29.0 1.5 %copy-start.2 = (f32[19]{0:T(128)S(1)}, f32[19]{0:T(128)}, u32[]{:S(2)}) copy-start(f32[19]{0:T(128)} %constant.85.clone) | copy-start | bytes 232
  29.0 1.5 %copy-start.3 = (f32[19]{0:T(128)S(1)}, f32[19]{0:T(128)}, u32[]{:S(2)}) copy-start(f32[19]{0:T(128)} %constant.86.clone) | copy-start | bytes 232
  29.0 1.5 %copy-start.4 = (f32[19]{0:T(128)S(1)}, f32[19]{0:T(128)}, u32[]{:S(2)}) copy-start(f32[19]{0:T(128)} %constant.87.clone) | copy-start | bytes 232
  29.0 1.5 %copy-start.5 = (f32[19]{0:T(128)S(1)}, f32[19]{0:T(128)}, u32[]{:S(2)}) copy-start(f32[19]{0:T(128)} %constant.88.clone) | copy-start | bytes 232
  37.0 4.0 %copy-start.1 = (f32[19,38,1,1]{1,0,3,2:T(8,128)S(1)}, f32[19,38,1,1]{1,0,3,2:T(8,128)}, u32[]{:S(2)}) copy-start(f32[19,38,1,1]{1,0,3,2:T(8,128)} %constant.93) | copy-start | bytes 8668
  52.8 4.9 %collective-permute-start.4 = (f32[4,16,2,32]{3,1,0,2:T(8,128)S(1)}, f32[4,16,2,32]{3,1,0,2:T(8,128)S(1)}, u32[]{:S(2)}, u32[]{:S(2)}) collective-permute-start(f32[4,16,2,32]{3,1,0,2:T(8,128)S(1)} %select_bitcast_fusion), channel_id=1, source_target_pairs={{0,8},{8,0},{16,24},{24,16},{1,9},{9,1},{17,25},{25,17},{2,10},{10... | collective-permute-start | bytes 49160 | tf_op jit(solution)/shard_map/ppermute | solution.py:30
  57.9 4.0 %collective-permute-start.5 = (f32[4,16,1,32]{3,1,0,2:T(8,128)S(1)}, f32[4,16,1,32]{3,1,0,2:T(8,128)S(1)}, u32[]{:S(2)}, u32[]{:S(2)}) collective-permute-start(f32[4,16,1,32]{3,1,0,2:T(8,128)S(1)} %select_bitcast_fusion.1), channel_id=1, source_target_pairs={{0,16},{8,24},{16,0},{24,8},{1,17},{9,25},{17,1},{25,9},{2,18},{10... | collective-permute-start | bytes 24584 | tf_op jit(solution)/shard_map/ppermute | solution.py:30

commit v6 on v5

--- a/solution.py
+++ b/solution.py
@@ -187,10 +187,19 @@
 
 
 def stream_and_render(collided, velocities, extent_x, extent_y, length_x):
-    depth_z = collided.shape[3]
+    near_y, band, far_y = collided
+    depth_z = band.shape[3]
+    edge = near_y.shape[2]
     steps = [[int(v) for v in velocities[q]] for q in range(19)]
 
-    def kernel(c_ref, o_ref, pic_ref):
+    def kernel(near_ref, band_ref, far_ref, o_ref, pic_ref, c_ref):
+        def gather(q, carry):
+            c_ref[q, :, 0:edge] = near_ref[q]
+            c_ref[q, :, edge : edge + extent_y - 2] = band_ref[q]
+            c_ref[q, :, edge + extent_y - 2 :] = far_ref[q]
+            return carry
+
+        lax.fori_loop(0, 19, gather, 0)
         for q in range(19):
             cx, cy, cz = steps[q]
 
@@ -228,9 +237,27 @@
             jax.ShapeDtypeStruct((19, extent_x, extent_y, depth_z), jnp.float32),
             jax.ShapeDtypeStruct((4, extent_y, depth_z), jnp.float32),
         ),
-        in_specs=[pl.BlockSpec(memory_space=pltpu.VMEM)],
+        in_specs=[pl.BlockSpec(memory_space=pltpu.VMEM)] * 3,
         out_specs=(pl.BlockSpec(memory_space=pltpu.VMEM), pl.BlockSpec(memory_space=pltpu.VMEM)),
-    )(collided)
+        scratch_shapes=[pltpu.VMEM((19, extent_x + 2, extent_y + 2, depth_z), jnp.float32)],
+    )(near_y, band, far_y)
+
+
+def collide_region(cells, pot, tables):
+    velocities, weights, relaxing, forcing_map = tables
+    nx, ny = cells.shape[1], cells.shape[2]
+    centre = pot[1 : 1 + nx, 1 : 1 + ny]
+    totals = [jnp.zeros_like(centre), jnp.zeros_like(centre), jnp.zeros_like(centre)]
+    for q in range(1, 19):
+        steps = [int(v) for v in velocities[q]]
+        neighbour = pot[1 + steps[0] : 1 + steps[0] + nx, 1 + steps[1] : 1 + steps[1] + ny]
+        neighbour = jnp.roll(neighbour, -steps[2], axis=2)
+        for d in range(3):
+            if steps[d] != 0:
+                totals[d] = totals[d] + weights[q] * steps[d] * neighbour
+    force = [-cohesion * centre * totals[d] for d in range(3)]
+    rho = jnp.sum(cells, axis=0)
+    return collide_major(cells, rho, force, velocities, weights, relaxing, forcing_map)
 
 
 def body(populations):
@@ -260,20 +287,14 @@
         [from_below[20][:, None], from_below[19][:, None], px, from_above[19][:, None], from_above[20][:, None]],
         axis=1,
     )
-    ext_x = extent_x + 2
-    ext_y = extent_y + 2
-    centre = pxy[1 : 1 + ext_x, 1 : 1 + ext_y]
-    totals = [jnp.zeros_like(centre), jnp.zeros_like(centre), jnp.zeros_like(centre)]
-    for q in range(1, 19):
-        steps = [int(v) for v in velocities[q]]
-        neighbour = pxy[1 + steps[0] : 1 + steps[0] + ext_x, 1 + steps[1] : 1 + steps[1] + ext_y]
-        neighbour = jnp.roll(neighbour, -steps[2], axis=2)
-        for d in range(3):
-            if steps[d] != 0:
-                totals[d] = totals[d] + weights[q] * steps[d] * neighbour
-    force = [-cohesion * centre * totals[d] for d in range(3)]
-    rho = jnp.sum(fxy, axis=0)
-    collided = collide_major(fxy, rho, force, velocities, weights, relaxing, forcing_map)
+    tables = (velocities, weights, relaxing, forcing_map)
+    inner = collide_region(f[:, 1 : extent_x - 1, 1 : extent_y - 1], potential, tables)
+    near_x = collide_region(fx[:, 0:2, 1 : extent_y - 1], px[0:4], tables)
+    far_x = collide_region(fx[:, extent_x : extent_x + 2, 1 : extent_y - 1], px[extent_x : extent_x + 4], tables)
+    band = jnp.concatenate([near_x, inner, far_x], axis=1)
+    near_y = collide_region(fxy[:, :, 0:2], pxy[:, 0:4], tables)
+    far_y = collide_region(fxy[:, :, extent_y : extent_y + 2], pxy[:, extent_y : extent_y + 4], tables)
+    collided = (near_y, band, far_y)
     groups = lax.axis_size("gx")
     length_x = extent_x * groups
     fresh_major, layered = stream_and_render(collided, velocities, extent_x, extent_y, length_x)

time: 62.8 us -> 54.1 us (0.86)
  waiting for transfers between devices: 16.5 us -> 4.6 us
  other arithmetic: 18.8 us -> 20.1 us
  starting transfers between devices: 9.32 us -> 10.4 us
    ppermute x4, waiting for transfers between devices: 12.6 us -> 2.28 us  [shift_ring(): lax.ppermute(x, axis, [(i, (i - step) % count) for i in range(count)])]
    concatenate x1 -> x5, other arithmetic: 4.02 us -> 1.13 us  [collide_major(): stacked = jnp.concatenate([f - balance, guo_term], axis=0)]
    concatenate x0 -> x1, local copies, waits for them, and re-layouts: none -> 1.86 us  [body(): band = jnp.concatenate([near_x, inner, far_x], axis=1)]
    ppermute x2, starting transfers between devices: 1.72 us -> 3.53 us  [from_partner(): lax.ppermute(x, axis, [(i, i ^ 1 << distance) for i in range(lax.axis_siz...]
    ppermute x2, waiting for transfers between devices: 3.88 us -> 2.32 us  [from_partner(): lax.ppermute(x, axis, [(i, i ^ 1 << distance) for i in range(lax.axis_siz...]
    sub x1 -> x4, other arithmetic: 2.82 us -> 4.12 us  [collide_major(): f - jnp.einsum('pq,q...->p...', table, stacked, precision=lax.Precision.H...]
    mul x1 -> x5, other arithmetic: 1.37 us -> 2.61 us  [collide_major(): 1.5 * speed_squared]
    unnamed x14 -> x15, local copies, waits for them, and re-layouts: 3.39 us -> 4.6 us
  transfers between devices with their start and end apart: 6 -> 6, of which waited for: 5 -> 2; matrix products, arithmetic and copies ran while one was open for 7% -> 31% of each run, Pallas kernels for 0% -> 0%
where the time goes in v6:
time: 54.1 us; the launch traced here: 53.8 us
  other arithmetic  20.1 us (37%)
  starting transfers between devices  10.4 us (19%)
  local copies, waits for them, and re-layouts  9.3 us (17%)
  waiting for transfers between devices  4.6 us (9%)
  Pallas kernels  4.34 us (8%)
  matrix products  3.79 us (7%)
  between operations  1.28 us (2%)
    ppermute x4, starting transfers between devices, shift_ring(): lax.ppermute(x, axis, [(i, (i - step) % count) for i in range(count)])  6.82 us
    sub x5, other arithmetic, collide_major(): stacked = jnp.concatenate([f - balance, guo_term], axis=0)  5.65 us
    unnamed x15, local copies, waits for them, and re-layouts  4.6 us
    pallas_call x1, Pallas kernels, stream_and_render(): pl.pallas_call(kernel, out_shape=(jax.ShapeDtypeStruct((19, extent_x, ext...  4.34 us
    sub x4, other arithmetic, collide_major(): f - jnp.einsum('pq,q...->p...', table, stacked, precision=lax.Precision.H...  4.12 us
    dot_general x5, matrix products, collide_major(): jnp.einsum('pq,q...->p...', table, stacked, precision=lax.Precision.HIGH)  3.79 us
    ppermute x2, starting transfers between devices, from_partner(): lax.ppermute(x, axis, [(i, i ^ 1 << distance) for i in range(lax.axis_siz...  3.53 us
    mul x5, other arithmetic, collide_major(): 1.5 * speed_squared  2.61 us
  transfers between devices with their start and end apart: 6, of which 2 were waited for; matrix products, arithmetic and copies ran while one was open for 31% of the time, Pallas kernels for 0%

profile of v6, /device:TPU:0, one launch (start us, length us, event | category | flops | bytes accessed | tf_op | source)
XLA Modules:
  0.0 53.8 jit_solution(11363396198964878025)
XLA Ops:
  0.6 2.0 %bitcast_reduce_fusion = f32[16,16,128]{2,1,0:T(8,128)S(1)} fusion(f32[16,16,19,128]{3,1,2,0:T(8,128)} %param.31), kind=kLoop, calls=%fused_computation.832 | loop fusion | flops 589824 | bytes 2621440 | tf_op jit(solution)/shard_map/reduce_sum | solution.py:268
  2.7 0.4 copy-done
  3.1 3.9 %collective-permute-start.1 = (f32[21,16,128]{2,1,0:T(8,128)S(1)}, f32[21,16,128]{2,1,0:T(8,128)S(1)}, u32[]{:S(2)}, u32[]{:S(2)}) collective-permute-start(f32[21,16,128]{2,1,0:T(8,128)S(1)} %pad_maximum_fusion.16), channel_id=1, source_target_pairs={{0,24},{8,0},{16,8},{24,16},{1,25},{9,1},{17,9},{25,17},{2,26},{10... | collective-permute-start | bytes 516104 | tf_op jit(solution)/shard_map/ppermute | solution.py:161
  7.2 0.2 slice_reduce_fusion
  7.4 0.2 fusion.452
  7.6 0.2 fusion.453
  7.9 0.9 %add_multiply_fusion.5 = (f32[14,14,128]{2,1,0:T(8,128)S(1)}, f32[14,14,128]{2,1,0:T(8,128)S(1)}, f32[14,14,128]{2,1,0:T(8,128)S(1)}, f32[14,14,128]{2,1,0:T(8,1...) fusion(f32[14,14,128]{2,1,0:T(8,128)S(1)} %slice_reduce_fusion, ...), kind=kLoop, calls=%fused_computation.316 | loop fusion | flops 2985472 | bytes 6207488 | tf_op jit(solution)/shard_map/mul | solution.py:180
  8.9 2.1 %fusion.5 = (f32[19,14,14,128]{3,2,0,1:T(8,128)S(1)}, f32[19,14,14,128]{3,2,0,1:T(8,128)S(1)}) fusion(f32[19,16,16,128]{3,2,0,1:T(8,128)S(1)} %bitcast.544, f32[14,14,128]{2,1,0:T(8,128)S(1)} %get-tuple-element.30, f32[14,14,128]{2,1,0:T(8,128)S(1)} %get-tuple-element.35, f32[19]{0:T(128)S(1)} %copy-done.4, f32[14,14,128]{2,1,0:T(8,128)S(1)} %get-tuple-element.33, ...), kind=kLoop, calls=%fused_computation.46 | loop fusion | flops 11916800 | bytes 6623536 | tf_op jit(solution)/shard_map/sub | solution.py:185
  11.0 0.4 pad_maximum_fusion
  11.5 0.3 copy-done.2
  11.7 2.2 %fusion = f32[19,14,14,128]{3,0,2,1:T(8,128)S(1)} fusion(f32[19,38,1,1]{1,0,3,2:T(8,128)S(1)} %copy-done.2, f32[38,14,14,128]{3,2,0,1:T(8,128)S(1)} %pad_maximum_fusion), kind=kOutput, calls=%fused_computation.39 | convolution fusion | flops 108681216 | bytes 5722952 | tf_op jit(solution)/shard_map/pq,q...->p.../dot_general | solution.py:186
  14.0 2.0 %copy_subtract_fusion = f32[19,14,14,128]{3,2,0,1:T(8,128)} fusion(f32[19,14,14,128]{3,0,2,1:T(8,128)S(1)} %fusion, f32[19,16,16,128]{3,2,0,1:T(8,128)S(1)} %bitcast.545), kind=kLoop, calls=%fused_computation.47 | loop fusion | flops 476672 | bytes 5720064 | tf_op jit(solution)/shard_map/sub | solution.py:186
  16.0 0.1 fusion.330
  16.1 0.1 fusion.329
  16.2 0.1 fusion.303
  16.3 0.1 fusion.302
  16.5 0.1 fusion.423
  16.6 0.1 fusion.449
  16.8 0.2 pad_maximum_fusion.12
  17.1 0.1 fusion.35
  17.1 2.8 %collective-permute-start.3 = (f32[21,20,128]{2,0,1:T(8,128)S(1)}, f32[21,20,128]{2,0,1:T(8,128)S(1)}, u32[]{:S(2)}, u32[]{:S(2)}) collective-permute-start(f32[21,20,128]{2,0,1:T(8,128)S(1)} %get-tuple-element.197), channel_id=1, source_target_pairs={{0,7},{1,0},{2,1},{3,2},{4,3},{5,4},{6,5},{7,6},{8,15},{9,8},{10,9... | collective-permute-start | bytes 645128 | tf_op jit(solution)/shard_map/ppermute | solution.py:161
  20.0 0.1 fusion.447
  20.1 0.1 add_multiply_fusion.14
  20.3 0.4 fusion.29
  20.7 0.4 fusion.10
  21.1 0.2 add_multiply_fusion.15
  21.3 0.4 fusion.25
  21.8 0.4 fusion.12
  22.3 0.6 %copy-done.1 = f32[19,14,14,128]{3,2,0,1:T(8,128)S(1)} copy-done((f32[19,14,14,128]{3,2,0,1:T(8,128)S(1)}, f32[19,14,14,128]{3,2,0,1:T(8,128)}, u32[]{:S(2)}) %copy-start.1) | copy-done | bytes 1906712
  22.9 0.2 pad_maximum_fusion.2
  23.1 1.9 %copy.553.band_ref = f32[19,18,14,128]{3,2,1,0:T(8,128)} copy(f32[19,18,14,128]{3,2,0,1:T(8,128)S(1)} %pad_maximum_fusion.2) | data formatting | bytes 4902912 | tf_op jit(solution)/shard_map/concatenate | solution.py:294
  25.0 0.1 fusion.450
  25.1 0.1 fusion.117
  25.2 0.1 fusion.118
  25.3 2.3 %collective-permute-done.2 = f32[21,20,128]{2,0,1:T(8,128)S(1)} collective-permute-done((f32[21,20,128]{2,0,1:T(8,128)S(1)}, f32[21,20,128]{2,0,1:T(8,128)S(1)}, u32[]{:S(2)}, u32[]{:S(2)}) %collective-permute-start.2) | collective-permute-done | bytes 215072 | tf_op jit(solution)/shard_map/ppermute | solution.py:161
  27.6 0.1 fusion.128
  27.7 0.1 fusion.129
  27.9 0.1 fusion.443
  28.0 0.1 fusion.442
  28.2 0.1 fusion.445
  28.3 0.1 fusion.444
  28.4 0.2 copy.550
  28.7 0.2 copy.479
  28.8 1.7 %pad_maximum_fusion.1 = (f32[19,18,17,128]{3,2,1,0:T(8,128)S(1)}, f32[19,18,17,128]{3,2,1,0:T(8,128)S(1)}) fusion(f32[19,18,1,128]{3,2,1,0:T(1,128)S(1)} %copy.550, f32[19,1,16,128]{3,2,1,0:T(8,128)S(1)} %get-tuple-element.108, f32[19,1,16,128]{3,2,1,0:T(8,128)S(1)} %get-tuple-element.102, f32[19,18,1,128]{3,2,1,0:T(1,128)S(1)} %copy.479, ...), kind=kLoop, calls=%fused_computation.38 | loop fusion | flops 4465152 | bytes 9105408 | tf_op jit(solution)/shard_map/concatenate | solution.py:283
  30.5 0.2 slice_reduce_fusion.1
  30.7 0.1 slice_reduce_fusion.2
  30.8 0.8 %add_multiply_fusion.6 = (f32[18,2,128]{2,1,0:T(2,128)S(1)}, f32[18,2,128]{2,1,0:T(2,128)S(1)}, f32[18,2,128]{2,1,0:T(2,128)S(1)}, f32[18,2,128]{2,1,0:T(2,128)S...) fusion(f32[18,2,128]{2,1,0:T(2,128)S(1)} %slice_reduce_fusion.1, ...), kind=kLoop, calls=%fused_computation.563 | loop fusion | flops 824832 | bytes 3421328 | tf_op jit(solution)/shard_map/mul | solution.py:180
  31.6 1.4 %fusion.21 = (f32[19,18,2,128]{3,2,1,0:T(2,128)S(1)}, f32[19,18,2,128]{3,2,1,0:T(2,128)S(1)}) fusion(f32[19,18,17,128]{3,2,1,0:T(8,128)S(1)} %get-tuple-element.53, f32[18,2,128]{2,1,0:T(2,128)S(1)} %get-tuple-element.14, f32[18,2,128]{2,1,0:T(2,128)S(1)} %slice_reduce_fusion.1, f32[19]{0:T(128)S(1)} %copy-done.3, f32[18,2,128]{2,1,0:T(2,128)S(1)} %get-tuple-element.19, ...), kind=kLoop, calls=%fused_computation.144 | loop fusion | flops 2188800 | bytes 1216816 | tf_op jit(solution)/shard_map/sub | solution.py:185
  33.1 0.3 pad_maximum_fusion.4
  33.4 0.3 fusion.6
  33.7 1.0 %copy_subtract_fusion.1.far_ref = f32[19,18,2,128]{3,2,1,0:T(2,128)} fusion(f32[19,18,2,128]{3,0,2,1:T(8,128)S(1)} %fusion.6, f32[19,18,17,128]{3,2,1,0:T(8,128)S(1)} %get-tuple-element.53), kind=kLoop, calls=%fused_computation.145 | loop fusion | flops 87552 | bytes 1050624 | tf_op jit(solution)/shard_map/sub | solution.py:186
  34.8 0.7 %add_multiply_fusion.10 = (f32[18,2,128]{2,1,0:T(2,128)S(1)}, f32[18,2,128]{2,1,0:T(2,128)S(1)}, f32[18,2,128]{2,1,0:T(2,128)S(1)}, f32[18,2,128]{2,1,0:T(2,128)...) fusion(f32[18,2,128]{2,1,0:T(2,128)S(1)} %slice_reduce_fusion.2, ...), kind=kLoop, calls=%fused_computation.568 | loop fusion | flops 843264 | bytes 3568496 | tf_op jit(solution)/shard_map/mul | solution.py:180
  35.5 1.3 %fusion.17 = (f32[19,18,2,128]{3,2,1,0:T(2,128)S(1)}, f32[19,18,2,128]{3,2,1,0:T(2,128)S(1)}) fusion(f32[19,18,17,128]{3,2,1,0:T(8,128)S(1)} %get-tuple-element.54, f32[18,2,128]{2,1,0:T(2,128)S(1)} %get-tuple-element.46, f32[18,2,128]{2,1,0:T(2,128)S(1)} %slice_reduce_fusion.2, f32[19]{0:T(128)S(1)} %copy-done.3, f32[18,2,128]{2,1,0:T(2,128)S(1)} %get-tuple-element.51, ...), kind=kLoop, calls=%fused_computation.140 | loop fusion | flops 2188800 | bytes 1216816 | tf_op jit(solution)/shard_map/sub | solution.py:185
  36.8 0.3 pad_maximum_fusion.3
  37.1 0.3 fusion.8
  37.5 1.0 %copy_subtract_fusion.2.near_ref = f32[19,18,2,128]{3,2,1,0:T(2,128)} fusion(f32[19,18,2,128]{3,0,2,1:T(8,128)S(1)} %fusion.8, f32[19,18,17,128]{3,2,1,0:T(8,128)S(1)} %get-tuple-element.54), kind=kLoop, calls=%fused_computation.146 | loop fusion | flops 87552 | bytes 1050624 | tf_op jit(solution)/shard_map/sub | solution.py:186
  38.5 4.3 %shard_map.302 = (f32[19,16,16,128]{3,2,1,0:T(8,128)}, f32[4,16,128]{2,1,0:T(8,128)}) custom-call(f32[19,18,2,128]{3,2,1,0:T(2,128)} %copy_subtract_fusion.2.near_ref, f32[19,18,14,128]{3,2,1,0:T(8,128)} %copy.553.band_ref, f32[19,18,2,128]{3,2,1,0:T(2,128)} %copy_subtract_fusion.1.far_ref), custom_call_target="tpu_custom_call" | custom-call | tf_op jit(solution)/shard_map/pallas_call | solution.py:234
  42.8 0.9 %reshape_reshape.3 = f32[4,16,2,2,32]{4,3,2,1,0:T(2,128)S(1)} reshape(f32[4,16,128]{2,1,0:T(8,128)} %get-tuple-element.5) | data formatting | bytes 65536 | tf_op jit(solution)/shard_map/reshape;reshape | solution.py:310
  43.7 0.1 fusion.451
  43.9 2.0 %collective-permute-start.4 = (f32[4,16,2,32]{3,1,0,2:T(8,128)S(1)}, f32[4,16,2,32]{3,1,0,2:T(8,128)S(1)}, u32[]{:S(2)}, u32[]{:S(2)}) collective-permute-start(f32[4,16,2,32]{3,1,0,2:T(8,128)S(1)} %select_bitcast_fusion), channel_id=1, source_target_pairs={{0,8},{8,0},{16,24},{24,16},{1,9},{9,1},{17,25},{25,17},{2,10},{10... | collective-permute-start | bytes 49160 | tf_op jit(solution)/shard_map/ppermute | solution.py:30
  45.9 2.3 %collective-permute-done.4 = f32[4,16,2,32]{3,1,0,2:T(8,128)S(1)} collective-permute-done((f32[4,16,2,32]{3,1,0,2:T(8,128)S(1)}, f32[4,16,2,32]{3,1,0,2:T(8,128)S(1)}, u32[]{:S(2)}, u32[]{:S(2)}) %collective-permute-start.4) | collective-permute-done | bytes 16416 | tf_op jit(solution)/shard_map/ppermute | solution.py:30
  48.3 1.5 %collective-permute-start.5 = (f32[4,16,1,32]{3,1,0,2:T(8,128)S(1)}, f32[4,16,1,32]{3,1,0,2:T(8,128)S(1)}, u32[]{:S(2)}, u32[]{:S(2)}) collective-permute-start(f32[4,16,1,32]{3,1,0,2:T(8,128)S(1)} %select_bitcast_fusion.1), channel_id=1, source_target_pairs={{0,16},{8,24},{16,0},{24,8},{1,17},{9,25},{17,1},{25,9},{2,18},{10... | collective-permute-start | bytes 24584 | tf_op jit(solution)/shard_map/ppermute | solution.py:30
  49.8 3.3 %copy.556 = f32[16,16,19,128]{3,1,2,0:T(8,128)} copy(f32[16,16,19,128]{3,1,0,2:T(8,128)} %bitcast.551) | data formatting | bytes 4980736
  53.1 0.6 %fusion.107 = f32[4,16,32]{2,1,0:T(8,128)} fusion(f32[4,16,1,32]{3,1,0,2:T(8,128)S(1)} %collective-permute-done.5, f32[16,32]{1,0:T(8,128)S(1)} %fusion.413, pred[]{:T(512)S(6)} %eq.19, f32[4,16,1,2,32]{4,1,0,3,2:T(8,128)S(1)} %fusion.104, pred[]{:T(512)S(6)} %eq.20), kind=kLoop, calls=%fused_computation.342 | loop fusion | flops 10240 | bytes 34818 | tf_op jit(solution)/shard_map/reshape | solution.py:319
  (57 shorter events, 0.9 us)
Async XLA Ops:
  0.6 2.5 %copy-start = (f32[16,16,19,128]{3,1,2,0:T(8,128)S(1)}, f32[16,16,19,128]{3,1,2,0:T(8,128)}, u32[]{:S(2)}) copy-start(f32[16,16,19,128]{3,1,2,0:T(8,128)} %param.31) | copy-start | bytes 7471108
  3.1 12.8 %collective-permute-start.1 = (f32[21,16,128]{2,1,0:T(8,128)S(1)}, f32[21,16,128]{2,1,0:T(8,128)S(1)}, u32[]{:S(2)}, u32[]{:S(2)}) collective-permute-start(f32[21,16,128]{2,1,0:T(8,128)S(1)} %pad_maximum_fusion.16), channel_id=1, source_target_pairs={{0,24},{8,0},{16,8},{24,16},{1,25},{9,1},{17,9},{25,17},{2,26},{10... | collective-permute-start | bytes 516104 | tf_op jit(solution)/shard_map/ppermute | solution.py:161
  7.1 9.0 %collective-permute-start = (f32[21,16,128]{2,1,0:T(8,128)S(1)}, f32[21,16,128]{2,1,0:T(8,128)S(1)}, u32[]{:S(2)}, u32[]{:S(2)}) collective-permute-start(f32[21,16,128]{2,1,0:T(8,128)S(1)} %pad_maximum_fusion.15), channel_id=1, source_target_pairs={{0,8},{8,16},{16,24},{24,0},{1,9},{9,17},{17,25},{25,1},{2,10},{10... | collective-permute-start | bytes 516104 | tf_op jit(solution)/shard_map/ppermute | solution.py:161
  7.9 1.0 %copy-start.3 = (f32[19]{0:T(128)S(1)}, f32[19]{0:T(128)}, u32[]{:S(2)}) copy-start(f32[19]{0:T(128)} %constant.112.clone) | copy-start | bytes 232
  7.9 1.0 %copy-start.4 = (f32[19]{0:T(128)S(1)}, f32[19]{0:T(128)}, u32[]{:S(2)}) copy-start(f32[19]{0:T(128)} %constant.57.clone) | copy-start | bytes 232
  7.9 1.0 %copy-start.5 = (f32[19]{0:T(128)S(1)}, f32[19]{0:T(128)}, u32[]{:S(2)}) copy-start(f32[19]{0:T(128)} %constant.56.clone) | copy-start | bytes 232
  7.9 1.0 %copy-start.6 = (f32[19]{0:T(128)S(1)}, f32[19]{0:T(128)}, u32[]{:S(2)}) copy-start(f32[19]{0:T(128)} %constant.53.clone) | copy-start | bytes 232
  11.0 0.7 %copy-start.2 = (f32[19,38,1,1]{1,0,3,2:T(8,128)S(1)}, f32[19,38,1,1]{1,0,3,2:T(8,128)}, u32[]{:S(2)}) copy-start(f32[19,38,1,1]{1,0,3,2:T(8,128)} %constant.117) | copy-start | bytes 8668
  17.1 7.9 %collective-permute-start.3 = (f32[21,20,128]{2,0,1:T(8,128)S(1)}, f32[21,20,128]{2,0,1:T(8,128)S(1)}, u32[]{:S(2)}, u32[]{:S(2)}) collective-permute-start(f32[21,20,128]{2,0,1:T(8,128)S(1)} %get-tuple-element.197), channel_id=1, source_target_pairs={{0,7},{1,0},{2,1},{3,2},{4,3},{5,4},{6,5},{7,6},{8,15},{9,8},{10,9... | collective-permute-start | bytes 645128 | tf_op jit(solution)/shard_map/ppermute | solution.py:161
  20.0 7.6 %collective-permute-start.2 = (f32[21,20,128]{2,0,1:T(8,128)S(1)}, f32[21,20,128]{2,0,1:T(8,128)S(1)}, u32[]{:S(2)}, u32[]{:S(2)}) collective-permute-start(f32[21,20,128]{2,0,1:T(8,128)S(1)} %get-tuple-element.198), channel_id=1, source_target_pairs={{0,1},{1,2},{2,3},{3,4},{4,5},{5,6},{6,7},{7,0},{8,9},{9,10},{10,1... | collective-permute-start | bytes 645128 | tf_op jit(solution)/shard_map/ppermute | solution.py:161
  21.3 1.6 %copy-start.1 = (f32[19,14,14,128]{3,2,0,1:T(8,128)S(1)}, f32[19,14,14,128]{3,2,0,1:T(8,128)}, u32[]{:S(2)}) copy-start(f32[19,14,14,128]{3,2,0,1:T(8,128)} %copy_subtract_fusion) | copy-start | bytes 5720068
  43.9 4.3 %collective-permute-start.4 = (f32[4,16,2,32]{3,1,0,2:T(8,128)S(1)}, f32[4,16,2,32]{3,1,0,2:T(8,128)S(1)}, u32[]{:S(2)}, u32[]{:S(2)}) collective-permute-start(f32[4,16,2,32]{3,1,0,2:T(8,128)S(1)} %select_bitcast_fusion), channel_id=1, source_target_pairs={{0,8},{8,0},{16,24},{24,16},{1,9},{9,1},{17,25},{25,17},{2,10},{10... | collective-permute-start | bytes 49160 | tf_op jit(solution)/shard_map/ppermute | solution.py:30
  48.3 4.8 %collective-permute-start.5 = (f32[4,16,1,32]{3,1,0,2:T(8,128)S(1)}, f32[4,16,1,32]{3,1,0,2:T(8,128)S(1)}, u32[]{:S(2)}, u32[]{:S(2)}) collective-permute-start(f32[4,16,1,32]{3,1,0,2:T(8,128)S(1)} %select_bitcast_fusion.1), channel_id=1, source_target_pairs={{0,16},{8,24},{16,0},{24,8},{1,17},{9,25},{17,1},{25,9},{2,18},{10... | collective-permute-start | bytes 24584 | tf_op jit(solution)/shard_map/ppermute | solution.py:30

commit v7 on v6

--- a/solution.py
+++ b/solution.py
@@ -245,18 +245,19 @@
 
 def collide_region(cells, pot, tables):
     velocities, weights, relaxing, forcing_map = tables
-    nx, ny = cells.shape[1], cells.shape[2]
-    centre = pot[1 : 1 + nx, 1 : 1 + ny]
+    nx, ny = cells.shape[-3], cells.shape[-2]
+    pot = pot.reshape((-1,) + pot.shape[-3:])
+    centre = pot[:, 1 : 1 + nx, 1 : 1 + ny]
     totals = [jnp.zeros_like(centre), jnp.zeros_like(centre), jnp.zeros_like(centre)]
     for q in range(1, 19):
         steps = [int(v) for v in velocities[q]]
-        neighbour = pot[1 + steps[0] : 1 + steps[0] + nx, 1 + steps[1] : 1 + steps[1] + ny]
-        neighbour = jnp.roll(neighbour, -steps[2], axis=2)
+        neighbour = pot[:, 1 + steps[0] : 1 + steps[0] + nx, 1 + steps[1] : 1 + steps[1] + ny]
+        neighbour = jnp.roll(neighbour, -steps[2], axis=3)
         for d in range(3):
             if steps[d] != 0:
                 totals[d] = totals[d] + weights[q] * steps[d] * neighbour
-    force = [-cohesion * centre * totals[d] for d in range(3)]
     rho = jnp.sum(cells, axis=0)
+    force = [(-cohesion * centre * totals[d]).reshape(rho.shape) for d in range(3)]
     return collide_major(cells, rho, force, velocities, weights, relaxing, forcing_map)
 
 
@@ -292,8 +293,13 @@
     near_x = collide_region(fx[:, 0:2, 1 : extent_y - 1], px[0:4], tables)
     far_x = collide_region(fx[:, extent_x : extent_x + 2, 1 : extent_y - 1], px[extent_x : extent_x + 4], tables)
     band = jnp.concatenate([near_x, inner, far_x], axis=1)
-    near_y = collide_region(fxy[:, :, 0:2], pxy[:, 0:4], tables)
-    far_y = collide_region(fxy[:, :, extent_y : extent_y + 2], pxy[:, extent_y : extent_y + 4], tables)
+    pair = collide_region(
+        jnp.stack([fxy[:, :, 0:2], fxy[:, :, extent_y : extent_y + 2]], axis=1),
+        jnp.stack([pxy[:, 0:4], pxy[:, extent_y : extent_y + 4]]),
+        tables,
+    )
+    near_y = pair[:, 0]
+    far_y = pair[:, 1]
     collided = (near_y, band, far_y)
     groups = lax.axis_size("gx")
     length_x = extent_x * groups

time: 54.1 us -> 89.8 us (1.66)
  local copies, waits for them, and re-layouts: 9.3 us -> 32 us
  other arithmetic: 20.1 us -> 34.5 us
  waiting for transfers between devices: 4.6 us -> 2.61 us
    transpose x0 -> x2, local copies, waits for them, and re-layouts: none -> 5.69 us  [body(): f = jnp.transpose(populations, (2, 0, 1, 3))]
    concatenate x0 -> x1, local copies, waits for them, and re-layouts: none -> 5.41 us  [body(): jnp.concatenate([from_prev[None, :19].transpose(1, 0, 2, 3), f, from_next...]
    mul x5 -> x2, other arithmetic: 2.61 us -> 7.11 us  [collide_major(): 1.5 * speed_squared]
    slice x12 -> x6, local copies, waits for them, and re-layouts: 1.27 us -> 5.6 us  [collide_region(): neighbour = jnp.roll(neighbour, -steps[2], axis=3)]
    sub x5 -> x4, other arithmetic: 5.65 us -> 9.6 us  [collide_major(): stacked = jnp.concatenate([f - balance, guo_term], axis=0)]
    sub x0 -> x4, other arithmetic: none -> 3.63 us  [the longest x2 3.58 us: collide_major(): 1.0 + 3.0 * along + 4.5 * along * along - 1.5 * speed_squared]
    concatenate x11 -> x0, other arithmetic: 2.48 us -> none  [the longest x1 1.67 us: body(): jnp.concatenate([from_below[:19, 1:-1, None], fx, from_above[:19, 1:-1, N...]
    ppermute x4, waiting for transfers between devices: 2.28 us -> 0.01 us  [shift_ring(): lax.ppermute(x, axis, [(i, (i - step) % count) for i in range(count)])]
  transfers between devices with their start and end apart: 6 -> 6, of which waited for: 2 -> 1; matrix products, arithmetic and copies ran while one was open for 31% -> 51% of each run, Pallas kernels for 0% -> 0%
where the time goes in v7:
time: 89.8 us; the launch traced here: 89.1 us
  other arithmetic  34.5 us (38%)
  local copies, waits for them, and re-layouts  32 us (36%)
  starting transfers between devices  9.92 us (11%)
  Pallas kernels  4.32 us (5%)
  matrix products  4.01 us (4%)
  waiting for transfers between devices  2.61 us (3%)
  between operations  1.71 us (2%)
    sub x4, other arithmetic, collide_major(): stacked = jnp.concatenate([f - balance, guo_term], axis=0)  9.6 us
    mul x2, other arithmetic, collide_major(): 1.5 * speed_squared  7.11 us
    ppermute x4, starting transfers between devices, shift_ring(): lax.ppermute(x, axis, [(i, (i - step) % count) for i in range(count)])  6.95 us
    unnamed x95, local copies, waits for them, and re-layouts  6.13 us
    transpose x2, local copies, waits for them, and re-layouts, body(): f = jnp.transpose(populations, (2, 0, 1, 3))  5.69 us
    slice x6, local copies, waits for them, and re-layouts, collide_region(): neighbour = jnp.roll(neighbour, -steps[2], axis=3)  5.6 us
    concatenate x1, local copies, waits for them, and re-layouts, body(): jnp.concatenate([from_prev[None, :19].transpose(1, 0, 2, 3), f, from_next...  5.41 us
    pallas_call x1, Pallas kernels, stream_and_render(): pl.pallas_call(kernel, out_shape=(jax.ShapeDtypeStruct((19, extent_x, ext...  4.32 us
  transfers between devices with their start and end apart: 6, of which 1 were waited for; matrix products, arithmetic and copies ran while one was open for 51% of the time, Pallas kernels for 0%

profile of v7, /device:TPU:0, one launch (start us, length us, event | category | flops | bytes accessed | tf_op | source)
XLA Modules:
  0.0 89.1 jit_solution(4183892748037576964)
XLA Ops:
  0.6 3.2 %fusion.36 = f32[16,16,128]{2,1,0:T(8,128)S(1)} fusion(f32[16,16,19,128]{3,1,2,0:T(8,128)} %param.25), kind=kLoop, calls=%fused_computation.175 | loop fusion | flops 589824 | bytes 2621440 | tf_op jit(solution)/shard_map/reduce_sum | solution.py:269
  3.9 0.9 copy.304
  4.9 3.9 %collective-permute-start.1 = (f32[21,16,128]{2,0,1:T(8,128)S(1)}, f32[21,16,128]{2,0,1:T(8,128)S(1)}, u32[]{:S(2)}, u32[]{:S(2)}) collective-permute-start(f32[21,16,128]{2,0,1:T(8,128)S(1)} %pad_maximum_fusion.17), channel_id=1, source_target_pairs={{0,24},{8,0},{16,8},{24,16},{1,25},{9,1},{17,9},{25,17},{2,26},{10... | collective-permute-start | bytes 516104 | tf_op jit(solution)/shard_map/ppermute | solution.py:161
  8.9 0.2 collective-permute-start
  9.2 1.3 %fusion.224 = (f32[1,14,14,127]{3,0,2,1:T(1,128)S(1)}, f32[1,14,14,127]{3,0,2,1:T(1,128)S(1)}, f32[1,14,14,127]{3,0,2,1:T(1,128)S(1)}, f32[1,14,14,127]{3,0,2,1:...) fusion(f32[1,16,16,128]{3,0,2,1:T(1,128)S(1)} %bitcast.404), kind=kLoop, calls=%fused_computation.523 | loop fusion | bytes 1991360 | tf_op jit(solution)/shard_map/jit(_roll_static)/slice | solution.py:255
  10.4 1.3 %fusion.225 = (f32[1,14,14,1]{3,0,2,1:T(1,128)S(1)}, f32[1,14,14,1]{3,0,2,1:T(1,128)S(1)}, f32[1,14,14,1]{3,0,2,1:T(1,128)S(1)}, f32[1,14,14,1]{3,0,2,1:T(1,128)...) fusion(f32[1,16,16,128]{3,0,2,1:T(1,128)S(1)} %bitcast.405), kind=kLoop, calls=%fused_computation.524 | loop fusion | bytes 15680 | tf_op jit(solution)/shard_map/jit(_roll_static)/slice | solution.py:255
  11.7 0.3 slice_reduce_fusion
  12.1 6.1 %add_multiply_fusion.4 = (f32[1,14,14,128]{3,0,2,1:T(1,128)S(1)}, f32[1,14,14,128]{3,0,2,1:T(1,128)S(1)}, f32[1,14,14,128]{3,0,2,1:T(1,128)S(1)}, f32[1,14,14,12...) fusion(f32[14,14,128]{2,1,0:T(8,128)S(1)} %slice_reduce_fusion,, ...), kind=kLoop, calls=%fused_computation.223 | loop fusion | flops 2985472 | bytes 4515840 | tf_op jit(solution)/shard_map/mul | solution.py:180
  18.3 0.2 multiply_add_fusion.4
  18.6 3.2 %fusion.221 = (f32[19,16,16,128]{3,1,2,0:T(8,128)}, f32[19,17,16,128]{3,1,2,0:T(8,128)}) fusion(f32[19,16,16,128]{3,2,0,1:T(8,128)S(1)} %bitcast.412), kind=kLoop, calls=%fused_computation.520 | loop fusion | bytes 7471104 | tf_op jit(solution)/shard_map/transpose | solution.py:268
  21.9 2.2 %fusion.7 = (f32[19,14,14,128]{3,0,2,1:T(8,128)S(1)}, f32[19,14,14,128]{3,0,2,1:T(8,128)S(1)}) fusion(f32[19,16,16,128]{3,0,2,1:T(8,128)S(1)} %bitcast.410, f32[14,14,128]{2,1,0:T(8,128)S(1)} %get-tuple-element.167, f32[14,14,128]{2,1,0:T(8,128)S(1)} %get-tuple-element.168, f32[19]{0:T(128)S(1)} %copy-done.38, f32[14,14,128]{2,1,0:T(8,128)S(1)} %get-tuple-element.169, ...), kind=kLoop, calls=%fused_computation.46 | loop fusion | flops 11916800 | bytes 6623536 | tf_op jit(solution)/shard_map/sub | solution.py:185
  24.1 2.9 %slice_subtract_fusion = f32[19,14,14,128]{3,0,2,1:T(8,128)} fusion(f32[19,16,16,128]{3,0,2,1:T(8,128)S(1)} %bitcast.411, f32[19,38,1,1]{1,0,3,2:T(8,128)S(1)} %copy-done.13, f32[19,14,14,128]{3,0,2,1:T(8,128)S(1)} %get-tuple-element.57, f32[19,14,14,128]{3,0,2,1:T(8,128)S(1)} %get-tuple-element.56), kind=kOutput, calls=%fused_computation.49 | convolution fusion | flops 110111232 | bytes 7629640 | tf_op jit(solution)/shard_map/pq,q...->p.../dot_general | solution.py:186
  26.9 2.5 %copy.156 = f32[19,16,16,128]{3,0,1,2:T(8,128)} copy(f32[19,16,16,128]{3,2,0,1:T(8,128)S(1)} %bitcast.413) | data formatting | bytes 4980736 | tf_op jit(solution)/shard_map/transpose | solution.py:268
  29.5 0.6 copy-done.5
  30.2 0.8 fusion.227
  30.9 0.8 fusion.228
  31.7 0.8 fusion.229
  32.5 0.8 fusion.230
  33.3 0.2 copy.188
  33.5 1.6 %fusion.147 = (f32[1,2,14,128]{3,1,2,0:T(2,128)}, f32[1,2,14,128]{3,1,2,0:T(2,128)}, f32[1,2,14,128]{3,1,2,0:T(2,128)}, f32[1,2,14,128]{3,1,2,0:T(2,128)}) fusion(f32[19,16,16,128]{3,1,2,0:T(8,128)} %get-tuple-element.52, f32[19,1,16,128]{3,1,2,0:T(1,128)S(1)} %copy.188), kind=kLoop, calls=%fused_computation.381 | loop fusion | flops 17920 | bytes 2703360 | tf_op jit(solution)/shard_map/concatenate | solution.py:274
  35.1 0.2 fusion.216
  35.3 0.8 copy.223
  36.2 0.9 copy-done.2
  37.2 0.9 fusion.34
  38.0 2.8 %collective-permute-start.3 = (f32[21,20,128]{2,0,1:T(8,128)}, f32[21,20,128]{2,0,1:T(8,128)}, u32[]{:S(2)}, u32[]{:S(2)}) collective-permute-start(f32[21,20,128]{2,0,1:T(8,128)} %get-tuple-element.162), channel_id=1, source_target_pairs={{0,7},{1,0},{2,1},{3,2},{4,3},{5,4},{6,5},{7,6},{8,15},{9,8},{10,9... | collective-permute-start | bytes 645128 | tf_op jit(solution)/shard_map/ppermute | solution.py:161
  40.8 5.4 %dynamic-update-slice.1 = f32[19,17,16,128]{3,1,2,0:T(8,128)} dynamic-update-slice(f32[19,17,16,128]{3,1,2,0:T(8,128)} %get-tuple-element.53, f32[19,1,16,128]{3,1,2,0:T(1,128)} %copy.223, s32[]{} %constant.132, s32[]{} %constant.133, s32[]{} %constant.132, s32[]{} %constant.132) | dynamic-update-slice | bytes 311300 | tf_op jit(solution)/shard_map/concatenate | solution.py:274
  46.2 1.8 %slice_reduce_fusion.1 = f32[2,14,128]{2,0,1:T(2,128)S(1)} fusion(f32[19,17,16,128]{3,1,2,0:T(8,128)} %dynamic-update-slice.1), kind=kLoop, calls=%fused_computation.174 | loop fusion | flops 64512 | bytes 286720 | tf_op jit(solution)/shard_map/reduce_sum | solution.py:259
  48.2 1.5 %multiply_bitcast_fusion.1 = (f32[2,14,128]{2,0,1:T(2,128)S(1)}, f32[1,2,14,128]{3,1,2,0:T(2,128)S(1)}, f32[1,2,14,128]{3,1,2,0:T(2,128)S(1)}, f32[1,2,14,128]{3...) fusion(f32[2,14,128]{2,0,1:T(2,128)S(1)} %get-tuple-element.19,, ...), kind=kLoop, calls=%fused_computation.497 | loop fusion | flops 508928 | bytes 3090432 | tf_op jit(solution)/shard_map/sub | solution.py:180
  49.7 1.7 %fusion.26 = (f32[19,2,14,128]{3,1,2,0:T(2,128)S(1)}, f32[19,2,14,128]{3,1,2,0:T(2,128)S(1)}) fusion(f32[19,2,14,128]{3,1,2,0:T(2,128)S(1)} %get-tuple-element.20, f32[2,14,128]{2,0,1:T(2,128)S(1)} %get-tuple-element.12, f32[2,14,128]{2,0,1:T(2,128)S(1)} %get-tuple-element.19, f32[19]{0:T(128)S(1)} %copy-done.37, f32[2,14,128]{2,0,1:T(2,128)S(1)} %bitcast.429, ...), kind=kLoop, calls=%fused_computation.146 | loop fusion | flops 1702400 | bytes 946480 | tf_op jit(solution)/shard_map/sub | solution.py:185
  51.4 0.2 pad_maximum_fusion.2
  51.7 0.3 fusion.18
  52.2 2.1 %multiply_bitcast_fusion = (f32[2,14,128]{2,0,1:T(2,128)S(1)}, f32[1,2,14,128]{3,1,2,0:T(2,128)S(1)}, f32[1,2,14,128]{3,1,2,0:T(2,128)S(1)}, f32[1,2,14,128]{3,1...) fusion(f32[2,14,128]{2,0,1:T(2,128)S(1)} %slice_reduce_fusion.1, ...), kind=kLoop, calls=%fused_computation.492 | loop fusion | flops 426496 | bytes 645120 | tf_op jit(solution)/shard_map/sub | solution.py:180
  54.4 2.8 %fusion.30 = (f32[19,2,14,128]{3,1,2,0:T(2,128)S(1)}, f32[19,2,14,128]{3,1,2,0:T(2,128)S(1)}) fusion(f32[19,17,16,128]{3,1,2,0:T(8,128)} %dynamic-update-slice.1, f32[2,14,128]{2,0,1:T(2,128)S(1)} %get-tuple-element.28, f32[2,14,128]{2,0,1:T(2,128)S(1)} %slice_reduce_fusion.1, f32[19]{0:T(128)S(1)} %copy-done.37, f32[2,14,128]{2,0,1:T(2,128)S(1)} %bitcast.423, ...), kind=kLoop, calls=%fused_computation.150 | loop fusion | flops 1702400 | bytes 946480 | tf_op jit(solution)/shard_map/sub | solution.py:185
  57.2 0.2 pad_maximum_fusion.3
  57.4 0.3 fusion.16
  57.7 2.0 %copy_subtract_fusion.1 = f32[19,2,14,128]{3,1,2,0:T(2,128)S(1)} fusion(f32[19,2,14,128]{3,0,2,1:T(8,128)S(1)} %fusion.16, f32[19,17,16,128]{3,1,2,0:T(8,128)} %dynamic-update-slice.1), kind=kLoop, calls=%fused_computation.151 | loop fusion | flops 68096 | bytes 817152 | tf_op jit(solution)/shard_map/sub | solution.py:186
  59.7 0.2 copy_subtract_fusion.2
  60.0 0.2 pad_maximum_fusion
  60.3 2.0 %copy.228.band_ref = f32[19,18,14,128]{3,2,1,0:T(8,128)} copy(f32[19,18,14,128]{3,0,2,1:T(8,128)S(1)} %pad_maximum_fusion) | data formatting | bytes 4902912 | tf_op jit(solution)/shard_map/concatenate | solution.py:295
  62.3 1.0 %slice_bitcast_fusion.23 = (f32[20,1,128]{2,1,0:T(1,128)S(1)}, f32[20,1,128]{2,1,0:T(1,128)S(1)}) fusion(f32[21,20,128]{2,0,1:T(8,128)} %collective-permute-done.3), kind=kLoop, calls=%fused_computation.505 | loop fusion | bytes 40960 | tf_op jit(solution)/shard_map/broadcast_in_dim;squeeze | solution.py:288
  63.3 1.0 %slice_bitcast_fusion.25 = (f32[20,1,128]{2,1,0:T(1,128)S(1)}, f32[20,1,128]{2,1,0:T(1,128)S(1)}) fusion(f32[21,20,128]{2,0,1:T(8,128)} %collective-permute-done.2), kind=kLoop, calls=%fused_computation.507 | loop fusion | bytes 40960 | tf_op jit(solution)/shard_map/broadcast_in_dim;squeeze | solution.py:288
  64.4 0.1 fusion.57
  64.5 0.3 fusion.96
  64.7 0.2 fusion.97
  65.0 1.0 %slice_bitcast_fusion.2 = f32[19,18,1,128]{3,0,1,2:T(8,128)S(1)} fusion(f32[21,20,128]{2,0,1:T(8,128)} %collective-permute-done.3), kind=kLoop, calls=%fused_computation.161 | loop fusion | bytes 350208 | tf_op jit(solution)/shard_map/broadcast_in_dim | solution.py:285
  65.9 1.0 %slice_bitcast_fusion.3 = f32[19,18,1,128]{3,0,1,2:T(8,128)S(1)} fusion(f32[21,20,128]{2,0,1:T(8,128)} %collective-permute-done.2), kind=kLoop, calls=%fused_computation.165 | loop fusion | bytes 350208 | tf_op jit(solution)/shard_map/broadcast_in_dim | solution.py:285
  66.9 0.1 fusion.20
  67.0 0.2 copy_dynamic-update-slice_fusion.1
  67.1 0.2 copy_dynamic-update-slice_fusion
  67.4 0.2 reduce_sum.52
  67.6 1.0 %add_multiply_fusion.8 = (f32[2,18,2,128]{3,2,1,0:T(2,128)S(1)}, f32[2,18,2,128]{3,2,1,0:T(2,128)S(1)}, f32[2,18,2,128]{3,2,1,0:T(2,128)S(1)}, f32[2,18,2,128]{3...) fusion(f32[2,18,2,128]{3,2,1,0:T(2,128)S(1)} %reduce_sum.52, ...), kind=kLoop, calls=%fused_computation.360 | loop fusion | flops 1281024 | bytes 1372448 | tf_op jit(solution)/shard_map/mul | solution.py:180
  68.6 2.9 %fusion.15 = (f32[19,2,18,2,128]{4,3,2,0,1:T(2,128)S(1)}, f32[19,2,18,2,128]{4,3,2,0,1:T(2,128)S(1)}) fusion(f32[19,2,18,2,128]{4,3,2,0,1:T(2,128)S(1)} %copy_dynamic-update-slice_fusion, f32[2,18,2,128]{3,2,1,0:T(2,128)S(1)} %get-tuple-element.35, f32[2,18,2,128]{3,2,1,0:T(2,128)S(1)} %reduce_sum.52, f32[19]{0:T(128)S(1)} %copy-done.37, ...), kind=kLoop, calls=%fused_computation.58 | loop fusion | flops 4377600 | bytes 2433328 | tf_op jit(solution)/shard_map/sub | solution.py:185
  71.6 0.6 pad_maximum_fusion.1
  72.2 0.6 fusion.10
  72.8 0.5 copy_subtract_fusion
  73.2 0.9 %slice_bitcast_fusion = (f32[19,18,2,128]{3,2,1,0:T(2,128)}, f32[19,18,2,128]{3,2,1,0:T(2,128)}) fusion(f32[19,2,18,2,128]{4,3,2,0,1:T(2,128)S(1)} %copy_subtract_fusion), kind=kLoop, calls=%fused_computation.138 | loop fusion | bytes 1400832 | tf_op jit(solution)/shard_map/squeeze | solution.py:302
  74.1 4.3 %shard_map.248 = (f32[19,16,16,128]{3,2,1,0:T(8,128)}, f32[4,16,128]{2,1,0:T(8,128)}) custom-call(f32[19,18,2,128]{3,2,1,0:T(2,128)} %get-tuple-element.55.near_ref, f32[19,18,14,128]{3,2,1,0:T(8,128)} %copy.228.band_ref, f32[19,18,2,128]{3,2,1,0:T(2,128)} %get-tuple-element.54.far_ref), custom_call_target="tpu_custom_call" | custom-call | tf_op jit(solution)/shard_map/pallas_call | solution.py:234
  78.5 0.9 %reshape_reshape.3 = f32[4,16,2,2,32]{4,3,2,1,0:T(2,128)S(1)} reshape(f32[4,16,128]{2,1,0:T(8,128)} %get-tuple-element.5) | data formatting | bytes 65536 | tf_op jit(solution)/shard_map/reshape;reshape | solution.py:316
  79.4 0.1 fusion.223
  79.5 1.7 %collective-permute-start.4 = (f32[4,16,2,32]{3,1,0,2:T(8,128)S(1)}, f32[4,16,2,32]{3,1,0,2:T(8,128)S(1)}, u32[]{:S(2)}, u32[]{:S(2)}) collective-permute-start(f32[4,16,2,32]{3,1,0,2:T(8,128)S(1)} %select_bitcast_fusion), channel_id=1, source_target_pairs={{0,8},{8,0},{16,24},{24,16},{1,9},{9,1},{17,25},{25,17},{2,10},{10... | collective-permute-start | bytes 49160 | tf_op jit(solution)/shard_map/ppermute | solution.py:30
  81.2 2.6 %collective-permute-done.4 = f32[4,16,2,32]{3,1,0,2:T(8,128)S(1)} collective-permute-done((f32[4,16,2,32]{3,1,0,2:T(8,128)S(1)}, f32[4,16,2,32]{3,1,0,2:T(8,128)S(1)}, u32[]{:S(2)}, u32[]{:S(2)}) %collective-permute-start.4) | collective-permute-done | bytes 16416 | tf_op jit(solution)/shard_map/ppermute | solution.py:30
  83.9 1.2 %collective-permute-start.5 = (f32[4,16,1,32]{3,1,0,2:T(8,128)S(1)}, f32[4,16,1,32]{3,1,0,2:T(8,128)S(1)}, u32[]{:S(2)}, u32[]{:S(2)}) collective-permute-start(f32[4,16,1,32]{3,1,0,2:T(8,128)S(1)} %select_bitcast_fusion.1), channel_id=1, source_target_pairs={{0,16},{8,24},{16,0},{24,8},{1,17},{9,25},{17,1},{25,9},{2,18},{10... | collective-permute-start | bytes 24584 | tf_op jit(solution)/shard_map/ppermute | solution.py:30
  85.1 3.3 %copy.231 = f32[16,16,19,128]{3,1,2,0:T(8,128)} copy(f32[16,16,19,128]{3,1,0,2:T(8,128)} %bitcast.414) | data formatting | bytes 4980736
  88.5 0.6 fusion.142
  (125 shorter events, 1.0 us)
Async XLA Ops:
  0.6 3.2 %copy-start = (f32[16,16,19,128]{3,1,2,0:T(8,128)S(1)}, f32[16,16,19,128]{3,1,2,0:T(8,128)}, u32[]{:S(2)}) copy-start(f32[16,16,19,128]{3,1,2,0:T(8,128)} %param.25) | copy-start | bytes 7471108
  4.9 24.5 %collective-permute-start.1 = (f32[21,16,128]{2,0,1:T(8,128)S(1)}, f32[21,16,128]{2,0,1:T(8,128)S(1)}, u32[]{:S(2)}, u32[]{:S(2)}) collective-permute-start(f32[21,16,128]{2,0,1:T(8,128)S(1)} %pad_maximum_fusion.17), channel_id=1, source_target_pairs={{0,24},{8,0},{16,8},{24,16},{1,25},{9,1},{17,9},{25,17},{2,26},{10... | collective-permute-start | bytes 516104 | tf_op jit(solution)/shard_map/ppermute | solution.py:161
  8.9 20.6 %collective-permute-start = (f32[21,16,128]{2,0,1:T(8,128)S(1)}, f32[21,16,128]{2,0,1:T(8,128)S(1)}, u32[]{:S(2)}, u32[]{:S(2)}) collective-permute-start(f32[21,16,128]{2,0,1:T(8,128)S(1)} %pad_maximum_fusion.16), channel_id=1, source_target_pairs={{0,8},{8,16},{16,24},{24,0},{1,9},{9,17},{17,25},{25,1},{2,10},{10... | collective-permute-start | bytes 516104 | tf_op jit(solution)/shard_map/ppermute | solution.py:161
  18.6 3.3 %copy-start.37 = (f32[19]{0:T(128)S(1)}, f32[19]{0:T(128)}, u32[]{:S(2)}) copy-start(f32[19]{0:T(128)} %constant.112.clone) | copy-start | bytes 232
  18.6 3.3 %copy-start.38 = (f32[19]{0:T(128)S(1)}, f32[19]{0:T(128)}, u32[]{:S(2)}) copy-start(f32[19]{0:T(128)} %constant.57.clone) | copy-start | bytes 232
  18.6 3.3 %copy-start.40 = (f32[19]{0:T(128)S(1)}, f32[19]{0:T(128)}, u32[]{:S(2)}) copy-start(f32[19]{0:T(128)} %constant.56.clone) | copy-start | bytes 232
  18.6 3.2 %copy-start.42 = (f32[19]{0:T(128)S(1)}, f32[19]{0:T(128)}, u32[]{:S(2)}) copy-start(f32[19]{0:T(128)} %constant.53.clone) | copy-start | bytes 232
  21.9 2.2 %copy-start.13 = (f32[19,38,1,1]{1,0,3,2:T(8,128)S(1)}, f32[19,38,1,1]{1,0,3,2:T(8,128)}, u32[]{:S(2)}) copy-start(f32[19,38,1,1]{1,0,3,2:T(8,128)} %constant.118) | copy-start | bytes 8668
  29.4 0.7 copy-start.5
  29.4 7.6 %copy-start.7 = (f32[2,16,128]{2,1,0:T(8,128)}, f32[2,16,128]{2,1,0:T(8,128)S(1)}, u32[]{:S(2)}) copy-start(f32[2,16,128]{2,1,0:T(8,128)S(1)} %copy.160) | copy-start | bytes 49156
  29.5 7.6 %copy-start.9 = (f32[1,16,128]{2,0,1:T(1,128)}, f32[1,16,128]{2,0,1:T(1,128)S(1)}, u32[]{:S(2)}) copy-start(f32[1,16,128]{2,0,1:T(1,128)S(1)} %get-tuple-element.64) | copy-start | bytes 24580
  29.5 7.6 %copy-start.11 = (f32[1,16,128]{2,0,1:T(1,128)}, f32[1,16,128]{2,0,1:T(1,128)S(1)}, u32[]{:S(2)}) copy-start(f32[1,16,128]{2,0,1:T(1,128)S(1)} %get-tuple-element.65) | copy-start | bytes 24580
  30.1 4.9 %copy-start.1 = (f32[19,16,16,128]{3,1,2,0:T(8,128)S(1)}, f32[19,16,16,128]{3,1,2,0:T(8,128)}, u32[]{:S(2)}) copy-start(f32[19,16,16,128]{3,1,2,0:T(8,128)} %get-tuple-element.52) | copy-start | bytes 7471108
  33.4 1.9 %copy-start.6 = (f32[21,16,128]{2,0,1:T(8,128)S(1)}, f32[21,16,128]{2,0,1:T(8,128)}, u32[]{:S(2)}) copy-start(f32[21,16,128]{2,0,1:T(8,128)} %copy-done.5) | copy-start | bytes 516100
  35.1 1.9 %copy-start.2 = (f32[19,16,16,128]{3,0,1,2:T(8,128)S(1)}, f32[19,16,16,128]{3,0,1,2:T(8,128)}, u32[]{:S(2)}) copy-start(f32[19,16,16,128]{3,0,1,2:T(8,128)} %copy.156) | copy-start | bytes 7471108
  37.0 11.0 %copy-start.35 = (f32[1,2,14,127]{3,1,2,0:T(2,128)S(1)}, f32[1,2,14,127]{3,1,2,0:T(2,128)}, u32[]{:S(2)}) copy-start(f32[1,2,14,127]{3,1,2,0:T(2,128)} %get-tuple-element.122) | copy-start | bytes 42676
  37.1 12.6 %copy-start.39 = (f32[19]{0:T(128)S(1)}, f32[19]{0:T(128)}, u32[]{:S(2)}) copy-start(f32[19]{0:T(128)} %constant.57.clone) | copy-start | bytes 232
  37.1 12.6 %copy-start.41 = (f32[19]{0:T(128)S(1)}, f32[19]{0:T(128)}, u32[]{:S(2)}) copy-start(f32[19]{0:T(128)} %constant.56.clone) | copy-start | bytes 232
  38.0 24.3 %collective-permute-start.3 = (f32[21,20,128]{2,0,1:T(8,128)}, f32[21,20,128]{2,0,1:T(8,128)}, u32[]{:S(2)}, u32[]{:S(2)}) collective-permute-start(f32[21,20,128]{2,0,1:T(8,128)} %get-tuple-element.162), channel_id=1, source_target_pairs={{0,7},{1,0},{2,1},{3,2},{4,3},{5,4},{6,5},{7,6},{8,15},{9,8},{10,9... | collective-permute-start | bytes 645128 | tf_op jit(solution)/shard_map/ppermute | solution.py:161
  40.8 22.5 %collective-permute-start.2 = (f32[21,20,128]{2,0,1:T(8,128)}, f32[21,20,128]{2,0,1:T(8,128)}, u32[]{:S(2)}, u32[]{:S(2)}) collective-permute-start(f32[21,20,128]{2,0,1:T(8,128)} %get-tuple-element.163), channel_id=1, source_target_pairs={{0,1},{1,2},{2,3},{3,4},{4,5},{5,6},{6,7},{7,0},{8,9},{9,10},{10,1... | collective-permute-start | bytes 645128 | tf_op jit(solution)/shard_map/ppermute | solution.py:161
  48.0 3.7 %copy-start.14 = (f32[19,38,1,1]{1,0,3,2:T(8,128)S(1)}, f32[19,38,1,1]{1,0,3,2:T(8,128)}, u32[]{:S(2)}) copy-start(f32[19,38,1,1]{1,0,3,2:T(8,128)} %constant.118) | copy-start | bytes 8668
  48.0 4.0 %copy-start.15 = (f32[1,2,14,127]{3,1,2,0:T(2,128)S(1)}, f32[1,2,14,127]{3,1,2,0:T(2,128)}, u32[]{:S(2)}) copy-start(f32[1,2,14,127]{3,1,2,0:T(2,128)} %get-tuple-element.142) | copy-start | bytes 42676
  48.0 4.0 %copy-start.16 = (f32[1,2,14,127]{3,1,2,0:T(2,128)S(1)}, f32[1,2,14,127]{3,1,2,0:T(2,128)}, u32[]{:S(2)}) copy-start(f32[1,2,14,127]{3,1,2,0:T(2,128)} %get-tuple-element.143) | copy-start | bytes 42676
  48.0 4.0 %copy-start.17 = (f32[1,2,14,127]{3,1,2,0:T(2,128)S(1)}, f32[1,2,14,127]{3,1,2,0:T(2,128)}, u32[]{:S(2)}) copy-start(f32[1,2,14,127]{3,1,2,0:T(2,128)} %get-tuple-element.144) | copy-start | bytes 42676
  48.0 4.0 %copy-start.18 = (f32[1,2,14,127]{3,1,2,0:T(2,128)S(1)}, f32[1,2,14,127]{3,1,2,0:T(2,128)}, u32[]{:S(2)}) copy-start(f32[1,2,14,127]{3,1,2,0:T(2,128)} %get-tuple-element.145) | copy-start | bytes 42676
  48.1 4.0 %copy-start.19 = (f32[1,2,14,127]{3,1,2,0:T(2,128)S(1)}, f32[1,2,14,127]{3,1,2,0:T(2,128)}, u32[]{:S(2)}) copy-start(f32[1,2,14,127]{3,1,2,0:T(2,128)} %get-tuple-element.146) | copy-start | bytes 42676
  48.1 4.0 %copy-start.20 = (f32[1,2,14,127]{3,1,2,0:T(2,128)S(1)}, f32[1,2,14,127]{3,1,2,0:T(2,128)}, u32[]{:S(2)}) copy-start(f32[1,2,14,127]{3,1,2,0:T(2,128)} %get-tuple-element.147) | copy-start | bytes 42676
  48.1 4.0 %copy-start.21 = (f32[1,2,14,127]{3,1,2,0:T(2,128)S(1)}, f32[1,2,14,127]{3,1,2,0:T(2,128)}, u32[]{:S(2)}) copy-start(f32[1,2,14,127]{3,1,2,0:T(2,128)} %get-tuple-element.148) | copy-start | bytes 42676
  48.1 4.0 %copy-start.22 = (f32[1,2,14,127]{3,1,2,0:T(2,128)S(1)}, f32[1,2,14,127]{3,1,2,0:T(2,128)}, u32[]{:S(2)}) copy-start(f32[1,2,14,127]{3,1,2,0:T(2,128)} %get-tuple-element.149) | copy-start | bytes 42676
  48.1 4.0 %copy-start.23 = (f32[1,2,14,127]{3,1,2,0:T(2,128)S(1)}, f32[1,2,14,127]{3,1,2,0:T(2,128)}, u32[]{:S(2)}) copy-start(f32[1,2,14,127]{3,1,2,0:T(2,128)} %get-tuple-element.150) | copy-start | bytes 42676
  48.1 4.0 %copy-start.24 = (f32[1,2,14,127]{3,1,2,0:T(2,128)S(1)}, f32[1,2,14,127]{3,1,2,0:T(2,128)}, u32[]{:S(2)}) copy-start(f32[1,2,14,127]{3,1,2,0:T(2,128)} %get-tuple-element.151) | copy-start | bytes 42676
  48.1 4.0 %copy-start.25 = (f32[1,2,14,1]{3,1,2,0:T(2,128)S(1)}, f32[1,2,14,1]{3,1,2,0:T(2,128)}, u32[]{:S(2)}) copy-start(f32[1,2,14,1]{3,1,2,0:T(2,128)} %get-tuple-element.152) | copy-start | bytes 340
  48.1 4.0 %copy-start.26 = (f32[1,2,14,1]{3,1,2,0:T(2,128)S(1)}, f32[1,2,14,1]{3,1,2,0:T(2,128)}, u32[]{:S(2)}) copy-start(f32[1,2,14,1]{3,1,2,0:T(2,128)} %get-tuple-element.153) | copy-start | bytes 340
  48.1 4.0 %copy-start.27 = (f32[1,2,14,1]{3,1,2,0:T(2,128)S(1)}, f32[1,2,14,1]{3,1,2,0:T(2,128)}, u32[]{:S(2)}) copy-start(f32[1,2,14,1]{3,1,2,0:T(2,128)} %get-tuple-element.154) | copy-start | bytes 340
  48.1 4.0 %copy-start.28 = (f32[1,2,14,1]{3,1,2,0:T(2,128)S(1)}, f32[1,2,14,1]{3,1,2,0:T(2,128)}, u32[]{:S(2)}) copy-start(f32[1,2,14,1]{3,1,2,0:T(2,128)} %get-tuple-element.155) | copy-start | bytes 340
  48.2 4.0 %copy-start.29 = (f32[1,2,14,1]{3,1,2,0:T(2,128)S(1)}, f32[1,2,14,1]{3,1,2,0:T(2,128)}, u32[]{:S(2)}) copy-start(f32[1,2,14,1]{3,1,2,0:T(2,128)} %get-tuple-element.156) | copy-start | bytes 340
  48.2 4.0 %copy-start.30 = (f32[1,2,14,1]{3,1,2,0:T(2,128)S(1)}, f32[1,2,14,1]{3,1,2,0:T(2,128)}, u32[]{:S(2)}) copy-start(f32[1,2,14,1]{3,1,2,0:T(2,128)} %get-tuple-element.157) | copy-start | bytes 340
  48.2 4.0 %copy-start.31 = (f32[1,2,14,1]{3,1,2,0:T(2,128)S(1)}, f32[1,2,14,1]{3,1,2,0:T(2,128)}, u32[]{:S(2)}) copy-start(f32[1,2,14,1]{3,1,2,0:T(2,128)} %get-tuple-element.158) | copy-start | bytes 340
  48.2 4.0 %copy-start.32 = (f32[1,2,14,1]{3,1,2,0:T(2,128)S(1)}, f32[1,2,14,1]{3,1,2,0:T(2,128)}, u32[]{:S(2)}) copy-start(f32[1,2,14,1]{3,1,2,0:T(2,128)} %get-tuple-element.159) | copy-start | bytes 340
  48.2 4.0 %copy-start.33 = (f32[1,2,14,1]{3,1,2,0:T(2,128)S(1)}, f32[1,2,14,1]{3,1,2,0:T(2,128)}, u32[]{:S(2)}) copy-start(f32[1,2,14,1]{3,1,2,0:T(2,128)} %get-tuple-element.160) | copy-start | bytes 340
  48.2 4.0 %copy-start.34 = (f32[1,2,14,1]{3,1,2,0:T(2,128)S(1)}, f32[1,2,14,1]{3,1,2,0:T(2,128)}, u32[]{:S(2)}) copy-start(f32[1,2,14,1]{3,1,2,0:T(2,128)} %get-tuple-element.161) | copy-start | bytes 340
  49.7 4.7 %copy-start.43 = (f32[19]{0:T(128)S(1)}, f32[19]{0:T(128)}, u32[]{:S(2)}) copy-start(f32[19]{0:T(128)} %constant.53.clone) | copy-start | bytes 232
  57.1 2.9 %copy-start.4 = (f32[19,14,14,128]{3,0,2,1:T(8,128)S(1)}, f32[19,14,14,128]{3,0,2,1:T(8,128)}, u32[]{:S(2)}) copy-start(f32[19,14,14,128]{3,0,2,1:T(8,128)} %slice_subtract_fusion) | copy-start | bytes 5720068
  60.2 4.0 %copy-start.8 = (f32[2,16,128]{2,1,0:T(8,128)S(1)}, f32[2,16,128]{2,1,0:T(8,128)}, u32[]{:S(2)}) copy-start(f32[2,16,128]{2,1,0:T(8,128)} %copy-done.7) | copy-start | bytes 49156
  60.2 4.0 %copy-start.10 = (f32[1,16,128]{2,0,1:T(1,128)S(1)}, f32[1,16,128]{2,0,1:T(1,128)}, u32[]{:S(2)}) copy-start(f32[1,16,128]{2,0,1:T(1,128)} %copy-done.9) | copy-start | bytes 24580
  60.2 4.0 %copy-start.12 = (f32[1,16,128]{2,0,1:T(1,128)S(1)}, f32[1,16,128]{2,0,1:T(1,128)}, u32[]{:S(2)}) copy-start(f32[1,16,128]{2,0,1:T(1,128)} %copy-done.11) | copy-start | bytes 24580
  60.3 6.6 %copy-start.3 = (f32[19,16,16,128]{3,0,1,2:T(8,128)S(1)}, f32[19,16,16,128]{3,0,1,2:T(8,128)}, u32[]{:S(2)}) copy-start(f32[19,16,16,128]{3,0,1,2:T(8,128)} %copy.156) | copy-start | bytes 7471108
  68.6 3.6 %copy-start.36 = (f32[19,38,1,1,1]{1,0,4,3,2:T(8,128)S(1)}, f32[19,38,1,1,1]{1,0,4,3,2:T(8,128)}, u32[]{:S(2)}) copy-start(f32[19,38,1,1,1]{1,0,4,3,2:T(8,128)} %constant.117) | copy-start | bytes 8668
  79.5 4.3 %collective-permute-start.4 = (f32[4,16,2,32]{3,1,0,2:T(8,128)S(1)}, f32[4,16,2,32]{3,1,0,2:T(8,128)S(1)}, u32[]{:S(2)}, u32[]{:S(2)}) collective-permute-start(f32[4,16,2,32]{3,1,0,2:T(8,128)S(1)} %select_bitcast_fusion), channel_id=1, source_target_pairs={{0,8},{8,0},{16,24},{24,16},{1,9},{9,1},{17,25},{25,17},{2,10},{10... | collective-permute-start | bytes 49160 | tf_op jit(solution)/shard_map/ppermute | solution.py:30
  83.9 4.6 %collective-permute-start.5 = (f32[4,16,1,32]{3,1,0,2:T(8,128)S(1)}, f32[4,16,1,32]{3,1,0,2:T(8,128)S(1)}, u32[]{:S(2)}, u32[]{:S(2)}) collective-permute-start(f32[4,16,1,32]{3,1,0,2:T(8,128)S(1)} %select_bitcast_fusion.1), channel_id=1, source_target_pairs={{0,16},{8,24},{16,0},{24,8},{1,17},{9,25},{17,1},{25,9},{2,18},{10... | collective-permute-start | bytes 24584 | tf_op jit(solution)/shard_map/ppermute | solution.py:30

commit v8 on v6

--- a/solution.py
+++ b/solution.py
@@ -266,8 +266,15 @@
     extent_y = populations.shape[1]
     f = jnp.transpose(populations, (2, 0, 1, 3))
     potential = 1.0 - jnp.exp(-jnp.sum(f, axis=0))
-    to_next = jnp.concatenate([f[:, extent_x - 1], potential[extent_x - 1 : extent_x], potential[extent_x - 2 : extent_x - 1]])
-    to_prev = jnp.concatenate([f[:, 0], potential[0:1], potential[1:2]])
+
+    def edge(row):
+        cells = jnp.transpose(populations[row], (1, 0, 2))
+        return cells, 1.0 - jnp.exp(-jnp.sum(cells, axis=0, keepdims=True))
+
+    last, last_pot = edge(extent_x - 1)
+    first, first_pot = edge(0)
+    to_next = jnp.concatenate([last, last_pot, edge(extent_x - 2)[1]])
+    to_prev = jnp.concatenate([first, first_pot, edge(1)[1]])
     from_prev = shift_ring(to_next, "gx", -1)
     from_next = shift_ring(to_prev, "gx", 1)
     fx = jnp.concatenate([from_prev[None, :19].transpose(1, 0, 2, 3), f, from_next[None, :19].transpose(1, 0, 2, 3)], axis=1)

time: 54.1 us -> 58.5 us (1.081)
  other arithmetic: 20.1 us -> 23.7 us
  matrix products: 3.79 us -> 5.12 us
  local copies, waits for them, and re-layouts: 9.3 us -> 8.52 us
    reduce_sum x0 -> x2, other arithmetic: none -> 2.2 us  [edge(): return (cells, 1.0 - jnp.exp(-jnp.sum(cells, axis=0, keepdims=True)))]
    concatenate x1 -> x0, local copies, waits for them, and re-layouts: 1.86 us -> none  [body(): band = jnp.concatenate([near_x, inner, far_x], axis=1)]
    concatenate x1, other arithmetic: 0.2 us -> 1.73 us  [body(): band = jnp.concatenate([near_x, inner, far_x], axis=1)]
    dot_general x5, matrix products: 3.79 us -> 5.12 us  [collide_major(): jnp.einsum('pq,q...->p...', table, stacked, precision=lax.Precision.HIGH)]
    unnamed x15 -> x16, local copies, waits for them, and re-layouts: 4.6 us -> 5.75 us
    sub x4 -> x5, other arithmetic: 4.12 us -> 4.17 us  [collide_major(): f - jnp.einsum('pq,q...->p...', table, stacked, precision=lax.Precision.H...]
  transfers between devices with their start and end apart: 6 -> 6, of which waited for: 2 -> 2; matrix products, arithmetic and copies ran while one was open for 31% -> 34% of each run, Pallas kernels for 0% -> 0%
where the time goes in v8:
time: 58.5 us; the launch traced here: 58.1 us
  other arithmetic  23.7 us (41%)
  starting transfers between devices  10.4 us (18%)
  local copies, waits for them, and re-layouts  8.52 us (15%)
  matrix products  5.12 us (9%)
  waiting for transfers between devices  4.71 us (8%)
  Pallas kernels  4.38 us (7%)
  between operations  1.27 us (2%)
    ppermute x4, starting transfers between devices, shift_ring(): lax.ppermute(x, axis, [(i, (i - step) % count) for i in range(count)])  6.83 us
    unnamed x16, local copies, waits for them, and re-layouts  5.75 us
    sub x5, other arithmetic, collide_major(): stacked = jnp.concatenate([f - balance, guo_term], axis=0)  5.61 us
    dot_general x5, matrix products, collide_major(): jnp.einsum('pq,q...->p...', table, stacked, precision=lax.Precision.HIGH)  5.12 us
    pallas_call x1, Pallas kernels, stream_and_render(): pl.pallas_call(kernel, out_shape=(jax.ShapeDtypeStruct((19, extent_x, ext...  4.38 us
    sub x5, other arithmetic, collide_major(): f - jnp.einsum('pq,q...->p...', table, stacked, precision=lax.Precision.H...  4.17 us
    ppermute x2, starting transfers between devices, from_partner(): lax.ppermute(x, axis, [(i, i ^ 1 << distance) for i in range(lax.axis_siz...  3.54 us
    mul x5, other arithmetic, collide_major(): 1.5 * speed_squared  2.63 us
  transfers between devices with their start and end apart: 6, of which 2 were waited for; matrix products, arithmetic and copies ran while one was open for 34% of the time, Pallas kernels for 0%

profile of v8, /device:TPU:0, one launch (start us, length us, event | category | flops | bytes accessed | tf_op | source)
XLA Modules:
  0.0 58.1 jit_solution(12266653945610738276)
XLA Ops:
  0.6 1.0 %fusion.380 = (f32[16,128]{1,0:T(8,128)S(1)}, f32[16,128]{1,0:T(8,128)S(1)}) fusion(f32[16,16,19,128]{3,1,2,0:T(8,128)} %param.31), kind=kLoop, calls=%fused_computation.781 | loop fusion | flops 73728 | bytes 327680 | tf_op jit(solution)/shard_map/reduce_sum | solution.py:272
  1.6 1.2 %slice_reduce_fusion.4 = (f32[16,128]{1,0:T(8,128)S(1)}, f32[16,128]{1,0:T(8,128)S(1)}, f32[19,16,128]{2,1,0:T(8,128)S(1)}, f32[19,16,128]{2,1,0:T(8,128)S(1)}) fusion(f32[16,16,19,128]{3,1,2,0:T(8,128)} %param.31), kind=kLoop, calls=%fused_computation.190 | loop fusion | flops 73728 | bytes 950272 | tf_op jit(solution)/shard_map/reduce_sum | solution.py:272
  2.9 3.9 %collective-permute-start.1 = (f32[21,16,128]{2,1,0:T(8,128)S(1)}, f32[21,16,128]{2,1,0:T(8,128)S(1)}, u32[]{:S(2)}, u32[]{:S(2)}) collective-permute-start(f32[21,16,128]{2,1,0:T(8,128)S(1)} %pad_maximum_fusion.16), channel_id=1, source_target_pairs={{0,24},{8,0},{16,8},{24,16},{1,25},{9,1},{17,9},{25,17},{2,26},{10... | collective-permute-start | bytes 516104 | tf_op jit(solution)/shard_map/ppermute | solution.py:161
  6.9 1.9 %fusion.382 = f32[16,16,128]{2,1,0:T(8,128)S(1)} fusion(f32[16,16,19,128]{3,1,2,0:T(8,128)} %param.31), kind=kLoop, calls=%fused_computation.783 | loop fusion | flops 589824 | bytes 2621440 | tf_op jit(solution)/shard_map/reduce_sum | solution.py:268
  8.8 0.2 fusion.421
  9.1 0.2 fusion.422
  9.3 1.2 %copy-done = f32[16,16,19,128]{3,1,2,0:T(8,128)S(1)} copy-done((f32[16,16,19,128]{3,1,2,0:T(8,128)S(1)}, f32[16,16,19,128]{3,1,2,0:T(8,128)}, u32[]{:S(2)}) %copy-start) | copy-done | bytes 2490392
  10.5 0.3 copy.252
  10.8 0.3 slice_reduce_fusion
  11.1 0.9 %add_multiply_fusion.5 = (f32[14,14,128]{2,1,0:T(8,128)S(1)}, f32[14,14,128]{2,1,0:T(8,128)S(1)}, f32[14,14,128]{2,1,0:T(8,128)S(1)}, f32[14,14,128]{2,1,0:T(8,1...) fusion(f32[14,14,128]{2,1,0:T(8,128)S(1)} %slice_reduce_fusion, ...), kind=kLoop, calls=%fused_computation.300 | loop fusion | flops 2985472 | bytes 4515840 | tf_op jit(solution)/shard_map/mul | solution.py:180
  12.1 2.1 %fusion.5 = (f32[19,14,14,128]{3,2,1,0:T(8,128)S(1)}, f32[19,14,14,128]{3,2,1,0:T(8,128)S(1)}) fusion(f32[19,16,16,128]{3,2,1,0:T(8,128)S(1)} %bitcast.267, f32[14,14,128]{2,1,0:T(8,128)S(1)} %get-tuple-element.34, f32[14,14,128]{2,1,0:T(8,128)S(1)} %get-tuple-element.39, f32[19]{0:T(128)S(1)} %copy-done.4, f32[14,14,128]{2,1,0:T(8,128)S(1)} %get-tuple-element.37, ...), kind=kLoop, calls=%fused_computation.47 | loop fusion | flops 11916800 | bytes 6623536 | tf_op jit(solution)/shard_map/sub | solution.py:185
  14.2 0.3 pad_maximum_fusion
  14.5 0.4 copy-done.2
  14.9 3.3 %fusion = f32[19,14,14,128]{3,0,2,1:T(8,128)S(1)} fusion(f32[19,38,1,1]{1,0,3,2:T(8,128)S(1)} %copy-done.2, f32[38,14,14,128]{3,2,1,0:T(8,128)S(1)} %pad_maximum_fusion), kind=kOutput, calls=%fused_computation.39 | convolution fusion | flops 108681216 | bytes 5722952 | tf_op jit(solution)/shard_map/pq,q...->p.../dot_general | solution.py:186
  18.2 2.0 %copy_subtract_fusion = f32[19,14,14,128]{3,2,1,0:T(8,128)} fusion(f32[19,14,14,128]{3,0,2,1:T(8,128)S(1)} %fusion, f32[19,16,16,128]{3,2,1,0:T(8,128)S(1)} %bitcast.268), kind=kLoop, calls=%fused_computation.48 | loop fusion | flops 476672 | bytes 5720064 | tf_op jit(solution)/shard_map/sub | solution.py:186
  20.2 0.1 fusion.320
  20.5 0.1 fusion.293
  20.6 0.1 fusion.292
  20.7 0.2 pad_maximum_fusion.12
  21.0 0.1 fusion.392
  21.1 0.1 fusion.418
  21.2 0.1 fusion.35
  21.3 2.8 %collective-permute-start.3 = (f32[21,20,128]{2,0,1:T(8,128)S(1)}, f32[21,20,128]{2,0,1:T(8,128)S(1)}, u32[]{:S(2)}, u32[]{:S(2)}) collective-permute-start(f32[21,20,128]{2,0,1:T(8,128)S(1)} %get-tuple-element.197), channel_id=1, source_target_pairs={{0,7},{1,0},{2,1},{3,2},{4,3},{5,4},{6,5},{7,6},{8,15},{9,8},{10,9... | collective-permute-start | bytes 645128 | tf_op jit(solution)/shard_map/ppermute | solution.py:161
  24.3 0.1 add_multiply_fusion.14
  24.5 0.4 fusion.29
  24.9 0.6 fusion.10
  25.5 0.2 add_multiply_fusion.15
  25.7 0.4 fusion.25
  26.1 0.6 fusion.12
  26.8 0.5 copy-done.1
  27.3 1.7 %pad_maximum_fusion.2.band_ref = f32[19,18,14,128]{3,2,1,0:T(8,128)} fusion(f32[19,2,14,128]{3,2,1,0:T(8,128)S(1)} %copy_subtract_fusion.3, f32[19,14,14,128]{3,2,1,0:T(8,128)S(1)} %copy-done.1, f32[19,2,14,128]{3,2,1,0:T(8,128)S(1)} %copy_subtract_fusion.4), kind=kLoop, calls=%fused_computation.42 | loop fusion | flops 1225728 | bytes 4902912 | tf_op jit(solution)/shard_map/concatenate | solution.py:301
  29.0 0.1 fusion.419
  29.2 0.1 fusion.117
  29.3 0.1 fusion.118
  29.4 2.4 %collective-permute-done.2 = f32[21,20,128]{2,0,1:T(8,128)S(1)} collective-permute-done((f32[21,20,128]{2,0,1:T(8,128)S(1)}, f32[21,20,128]{2,0,1:T(8,128)S(1)}, u32[]{:S(2)}, u32[]{:S(2)}) %collective-permute-start.2) | collective-permute-done | bytes 215072 | tf_op jit(solution)/shard_map/ppermute | solution.py:161
  31.8 0.1 fusion.128
  31.9 0.1 fusion.129
  32.1 0.1 fusion.412
  32.2 0.1 fusion.411
  32.3 0.1 fusion.414
  32.5 0.1 fusion.413
  32.6 0.2 copy.211
  32.8 0.2 copy.200
  33.0 1.7 %pad_maximum_fusion.1 = (f32[19,18,17,128]{3,2,1,0:T(8,128)S(1)}, f32[19,18,17,128]{3,2,1,0:T(8,128)S(1)}) fusion(f32[19,18,1,128]{3,2,1,0:T(1,128)S(1)} %copy.211, f32[19,1,16,128]{3,2,1,0:T(8,128)S(1)} %slice_bitcast_fusion.2, f32[19,16,16,128]{3,2,1,0:T(8,128)S(1)} %bitcast.274, f32[19,1,16,128]{3,2,1,0:T(8,128)S(1)} %slice_bitcast_fusion.3, ...), kind=kLoop, calls=%fused_computation.38 | loop fusion | flops 4465152 | bytes 9105408 | tf_op jit(solution)/shard_map/concatenate | solution.py:290
  34.8 0.2 slice_reduce_fusion.1
  35.0 0.1 slice_reduce_fusion.2
  35.0 0.8 %add_multiply_fusion.6 = (f32[18,2,128]{2,1,0:T(2,128)S(1)}, f32[18,2,128]{2,1,0:T(2,128)S(1)}, f32[18,2,128]{2,1,0:T(2,128)S(1)}, f32[18,2,128]{2,1,0:T(2,128)S...) fusion(f32[18,2,128]{2,1,0:T(2,128)S(1)} %slice_reduce_fusion.1, ...), kind=kLoop, calls=%fused_computation.547 | loop fusion | flops 824832 | bytes 3421328 | tf_op jit(solution)/shard_map/mul | solution.py:180
  35.9 1.4 %fusion.21 = (f32[19,18,2,128]{3,2,1,0:T(2,128)S(1)}, f32[19,18,2,128]{3,2,1,0:T(2,128)S(1)}) fusion(f32[19,18,17,128]{3,2,1,0:T(8,128)S(1)} %get-tuple-element.57, f32[18,2,128]{2,1,0:T(2,128)S(1)} %get-tuple-element.18, f32[18,2,128]{2,1,0:T(2,128)S(1)} %slice_reduce_fusion.1, f32[19]{0:T(128)S(1)} %copy-done.3, f32[18,2,128]{2,1,0:T(2,128)S(1)} %get-tuple-element.23, ...), kind=kLoop, calls=%fused_computation.145 | loop fusion | flops 2188800 | bytes 1216816 | tf_op jit(solution)/shard_map/sub | solution.py:185
  37.3 0.3 pad_maximum_fusion.4
  37.6 0.3 fusion.6
  38.0 1.0 %copy_subtract_fusion.1.far_ref = f32[19,18,2,128]{3,2,1,0:T(2,128)} fusion(f32[19,18,2,128]{3,0,2,1:T(8,128)S(1)} %fusion.6, f32[19,18,17,128]{3,2,1,0:T(8,128)S(1)} %get-tuple-element.57), kind=kLoop, calls=%fused_computation.146 | loop fusion | flops 87552 | bytes 1050624 | tf_op jit(solution)/shard_map/sub | solution.py:186
  39.0 0.7 %add_multiply_fusion.10 = (f32[18,2,128]{2,1,0:T(2,128)S(1)}, f32[18,2,128]{2,1,0:T(2,128)S(1)}, f32[18,2,128]{2,1,0:T(2,128)S(1)}, f32[18,2,128]{2,1,0:T(2,128)...) fusion(f32[18,2,128]{2,1,0:T(2,128)S(1)} %slice_reduce_fusion.2, ...), kind=kLoop, calls=%fused_computation.552 | loop fusion | flops 843264 | bytes 3568496 | tf_op jit(solution)/shard_map/mul | solution.py:180
  39.7 1.3 %fusion.17 = (f32[19,18,2,128]{3,2,1,0:T(2,128)S(1)}, f32[19,18,2,128]{3,2,1,0:T(2,128)S(1)}) fusion(f32[19,18,17,128]{3,2,1,0:T(8,128)S(1)} %get-tuple-element.58, f32[18,2,128]{2,1,0:T(2,128)S(1)} %get-tuple-element.50, f32[18,2,128]{2,1,0:T(2,128)S(1)} %slice_reduce_fusion.2, f32[19]{0:T(128)S(1)} %copy-done.3, f32[18,2,128]{2,1,0:T(2,128)S(1)} %get-tuple-element.55, ...), kind=kLoop, calls=%fused_computation.141 | loop fusion | flops 2188800 | bytes 1216816 | tf_op jit(solution)/shard_map/sub | solution.py:185
  41.0 0.3 pad_maximum_fusion.3
  41.4 0.3 fusion.8
  41.7 1.0 %copy_subtract_fusion.2.near_ref = f32[19,18,2,128]{3,2,1,0:T(2,128)} fusion(f32[19,18,2,128]{3,0,2,1:T(8,128)S(1)} %fusion.8, f32[19,18,17,128]{3,2,1,0:T(8,128)S(1)} %get-tuple-element.58), kind=kLoop, calls=%fused_computation.147 | loop fusion | flops 87552 | bytes 1050624 | tf_op jit(solution)/shard_map/sub | solution.py:186
  42.7 4.4 %shard_map.302 = (f32[19,16,16,128]{3,2,1,0:T(8,128)}, f32[4,16,128]{2,1,0:T(8,128)}) custom-call(f32[19,18,2,128]{3,2,1,0:T(2,128)} %copy_subtract_fusion.2.near_ref, f32[19,18,14,128]{3,2,1,0:T(8,128)} %pad_maximum_fusion.2.band_ref, f32[19,18,2,128]{3,2,1,0:T(2,128)} %copy_subtract_fusion.1.far_ref), custom_call_target="tpu_custom_call" | custom-call | tf_op jit(solution)/shard_map/pallas_call | solution.py:234
  47.1 0.9 %reshape_reshape.3 = f32[4,16,2,2,32]{4,3,2,1,0:T(2,128)S(1)} reshape(f32[4,16,128]{2,1,0:T(8,128)} %get-tuple-element.5) | data formatting | bytes 65536 | tf_op jit(solution)/shard_map/reshape;reshape | solution.py:317
  48.0 0.1 fusion.420
  48.2 2.0 %collective-permute-start.4 = (f32[4,16,2,32]{3,1,0,2:T(8,128)S(1)}, f32[4,16,2,32]{3,1,0,2:T(8,128)S(1)}, u32[]{:S(2)}, u32[]{:S(2)}) collective-permute-start(f32[4,16,2,32]{3,1,0,2:T(8,128)S(1)} %select_bitcast_fusion), channel_id=1, source_target_pairs={{0,8},{8,0},{16,24},{24,16},{1,9},{9,1},{17,25},{25,17},{2,10},{10... | collective-permute-start | bytes 49160 | tf_op jit(solution)/shard_map/ppermute | solution.py:30
  50.2 2.3 %collective-permute-done.4 = f32[4,16,2,32]{3,1,0,2:T(8,128)S(1)} collective-permute-done((f32[4,16,2,32]{3,1,0,2:T(8,128)S(1)}, f32[4,16,2,32]{3,1,0,2:T(8,128)S(1)}, u32[]{:S(2)}, u32[]{:S(2)}) %collective-permute-start.4) | collective-permute-done | bytes 16416 | tf_op jit(solution)/shard_map/ppermute | solution.py:30
  52.6 1.5 %collective-permute-start.5 = (f32[4,16,1,32]{3,1,0,2:T(8,128)S(1)}, f32[4,16,1,32]{3,1,0,2:T(8,128)S(1)}, u32[]{:S(2)}, u32[]{:S(2)}) collective-permute-start(f32[4,16,1,32]{3,1,0,2:T(8,128)S(1)} %select_bitcast_fusion.1), channel_id=1, source_target_pairs={{0,16},{8,24},{16,0},{24,8},{1,17},{9,25},{17,1},{25,9},{2,18},{10... | collective-permute-start | bytes 24584 | tf_op jit(solution)/shard_map/ppermute | solution.py:30
  54.1 3.3 %copy.216 = f32[16,16,19,128]{3,1,2,0:T(8,128)} copy(f32[16,16,19,128]{3,1,0,2:T(8,128)} %bitcast.277) | data formatting | bytes 4980736
  57.4 0.6 %fusion.107 = f32[4,16,32]{2,1,0:T(8,128)} fusion(f32[4,16,1,32]{3,1,0,2:T(8,128)S(1)} %collective-permute-done.5, f32[16,32]{1,0:T(8,128)S(1)} %fusion.379, pred[]{:T(512)S(6)} %eq.19, f32[4,16,1,2,32]{4,1,0,3,2:T(8,128)S(1)} %fusion.104, pred[]{:T(512)S(6)} %eq.20), kind=kLoop, calls=%fused_computation.326 | loop fusion | flops 10240 | bytes 34818 | tf_op jit(solution)/shard_map/reshape | solution.py:326
  (57 shorter events, 1.1 us)
Async XLA Ops:
  2.9 17.3 %collective-permute-start.1 = (f32[21,16,128]{2,1,0:T(8,128)S(1)}, f32[21,16,128]{2,1,0:T(8,128)S(1)}, u32[]{:S(2)}, u32[]{:S(2)}) collective-permute-start(f32[21,16,128]{2,1,0:T(8,128)S(1)} %pad_maximum_fusion.16), channel_id=1, source_target_pairs={{0,24},{8,0},{16,8},{24,16},{1,25},{9,1},{17,9},{25,17},{2,26},{10... | collective-permute-start | bytes 516104 | tf_op jit(solution)/shard_map/ppermute | solution.py:161
  6.9 13.5 %collective-permute-start = (f32[21,16,128]{2,1,0:T(8,128)S(1)}, f32[21,16,128]{2,1,0:T(8,128)S(1)}, u32[]{:S(2)}, u32[]{:S(2)}) collective-permute-start(f32[21,16,128]{2,1,0:T(8,128)S(1)} %pad_maximum_fusion.15), channel_id=1, source_target_pairs={{0,8},{8,16},{16,24},{24,0},{1,9},{9,17},{17,25},{25,1},{2,10},{10... | collective-permute-start | bytes 516104 | tf_op jit(solution)/shard_map/ppermute | solution.py:161
  8.8 1.7 %copy-start = (f32[16,16,19,128]{3,1,2,0:T(8,128)S(1)}, f32[16,16,19,128]{3,1,2,0:T(8,128)}, u32[]{:S(2)}) copy-start(f32[16,16,19,128]{3,1,2,0:T(8,128)} %param.31) | copy-start | bytes 7471108
  11.0 1.0 %copy-start.3 = (f32[19]{0:T(128)S(1)}, f32[19]{0:T(128)}, u32[]{:S(2)}) copy-start(f32[19]{0:T(128)} %constant.58.clone) | copy-start | bytes 232
  11.1 1.0 %copy-start.4 = (f32[19]{0:T(128)S(1)}, f32[19]{0:T(128)}, u32[]{:S(2)}) copy-start(f32[19]{0:T(128)} %constant.57.clone) | copy-start | bytes 232
  11.1 1.0 %copy-start.5 = (f32[19]{0:T(128)S(1)}, f32[19]{0:T(128)}, u32[]{:S(2)}) copy-start(f32[19]{0:T(128)} %constant.54.clone) | copy-start | bytes 232
  11.1 1.0 %copy-start.6 = (f32[19]{0:T(128)S(1)}, f32[19]{0:T(128)}, u32[]{:S(2)}) copy-start(f32[19]{0:T(128)} %constant.53.clone) | copy-start | bytes 232
  14.2 0.7 %copy-start.2 = (f32[19,38,1,1]{1,0,3,2:T(8,128)S(1)}, f32[19,38,1,1]{1,0,3,2:T(8,128)}, u32[]{:S(2)}) copy-start(f32[19,38,1,1]{1,0,3,2:T(8,128)} %constant.118) | copy-start | bytes 8668
  21.3 7.8 %collective-permute-start.3 = (f32[21,20,128]{2,0,1:T(8,128)S(1)}, f32[21,20,128]{2,0,1:T(8,128)S(1)}, u32[]{:S(2)}, u32[]{:S(2)}) collective-permute-start(f32[21,20,128]{2,0,1:T(8,128)S(1)} %get-tuple-element.197), channel_id=1, source_target_pairs={{0,7},{1,0},{2,1},{3,2},{4,3},{5,4},{6,5},{7,6},{8,15},{9,8},{10,9... | collective-permute-start | bytes 645128 | tf_op jit(solution)/shard_map/ppermute | solution.py:161
  24.2 7.6 %collective-permute-start.2 = (f32[21,20,128]{2,0,1:T(8,128)S(1)}, f32[21,20,128]{2,0,1:T(8,128)S(1)}, u32[]{:S(2)}, u32[]{:S(2)}) collective-permute-start(f32[21,20,128]{2,0,1:T(8,128)S(1)} %get-tuple-element.198), channel_id=1, source_target_pairs={{0,1},{1,2},{2,3},{3,4},{4,5},{5,6},{6,7},{7,0},{8,9},{9,10},{10,1... | collective-permute-start | bytes 645128 | tf_op jit(solution)/shard_map/ppermute | solution.py:161
  25.7 1.6 %copy-start.1 = (f32[19,14,14,128]{3,2,1,0:T(8,128)S(1)}, f32[19,14,14,128]{3,2,1,0:T(8,128)}, u32[]{:S(2)}) copy-start(f32[19,14,14,128]{3,2,1,0:T(8,128)} %copy_subtract_fusion) | copy-start | bytes 5720068
  48.2 4.3 %collective-permute-start.4 = (f32[4,16,2,32]{3,1,0,2:T(8,128)S(1)}, f32[4,16,2,32]{3,1,0,2:T(8,128)S(1)}, u32[]{:S(2)}, u32[]{:S(2)}) collective-permute-start(f32[4,16,2,32]{3,1,0,2:T(8,128)S(1)} %select_bitcast_fusion), channel_id=1, source_target_pairs={{0,8},{8,0},{16,24},{24,16},{1,9},{9,1},{17,25},{25,17},{2,10},{10... | collective-permute-start | bytes 49160 | tf_op jit(solution)/shard_map/ppermute | solution.py:30
  52.6 4.8 %collective-permute-start.5 = (f32[4,16,1,32]{3,1,0,2:T(8,128)S(1)}, f32[4,16,1,32]{3,1,0,2:T(8,128)S(1)}, u32[]{:S(2)}, u32[]{:S(2)}) collective-permute-start(f32[4,16,1,32]{3,1,0,2:T(8,128)S(1)} %select_bitcast_fusion.1), channel_id=1, source_target_pairs={{0,16},{8,24},{16,0},{24,8},{1,17},{9,25},{17,1},{25,9},{2,18},{10... | collective-permute-start | bytes 24584 | tf_op jit(solution)/shard_map/ppermute | solution.py:30

commit v9 on v6

--- a/solution.py
+++ b/solution.py
@@ -243,14 +243,15 @@
     )(near_y, band, far_y)
 
 
-def collide_region(cells, pot, tables):
+def collide_region(cells, pot, tables, swapped=False):
     velocities, weights, relaxing, forcing_map = tables
     nx, ny = cells.shape[1], cells.shape[2]
     centre = pot[1 : 1 + nx, 1 : 1 + ny]
     totals = [jnp.zeros_like(centre), jnp.zeros_like(centre), jnp.zeros_like(centre)]
     for q in range(1, 19):
         steps = [int(v) for v in velocities[q]]
-        neighbour = pot[1 + steps[0] : 1 + steps[0] + nx, 1 + steps[1] : 1 + steps[1] + ny]
+        first, second = (steps[1], steps[0]) if swapped else (steps[0], steps[1])
+        neighbour = pot[1 + first : 1 + first + nx, 1 + second : 1 + second + ny]
         neighbour = jnp.roll(neighbour, -steps[2], axis=2)
         for d in range(3):
             if steps[d] != 0:
@@ -292,8 +293,14 @@
     near_x = collide_region(fx[:, 0:2, 1 : extent_y - 1], px[0:4], tables)
     far_x = collide_region(fx[:, extent_x : extent_x + 2, 1 : extent_y - 1], px[extent_x : extent_x + 4], tables)
     band = jnp.concatenate([near_x, inner, far_x], axis=1)
-    near_y = collide_region(fxy[:, :, 0:2], pxy[:, 0:4], tables)
-    far_y = collide_region(fxy[:, :, extent_y : extent_y + 2], pxy[:, extent_y : extent_y + 4], tables)
+
+    def strip(lo, hi):
+        cells = jnp.swapaxes(fxy[:, :, lo:hi], 1, 2)
+        pot = jnp.swapaxes(pxy[:, lo : hi + 2], 0, 1)
+        return jnp.swapaxes(collide_region(cells, pot, tables, swapped=True), 1, 2)
+
+    near_y = strip(0, 2)
+    far_y = strip(extent_y, extent_y + 2)
     collided = (near_y, band, far_y)
     groups = lax.axis_size("gx")
     length_x = extent_x * groups

time: 54.1 us -> 63.3 us (1.17)
  local copies, waits for them, and re-layouts: 9.3 us -> 13.5 us
  waiting for transfers between devices: 4.6 us -> 8.78 us
  matrix products: 3.79 us -> 5.07 us
  starting transfers between devices: 10.4 us -> 9.31 us
  other arithmetic: 20.1 us -> 20.8 us
    ppermute x4, waiting for transfers between devices: 2.28 us -> 5.1 us  [shift_ring(): lax.ppermute(x, axis, [(i, (i - step) % count) for i in range(count)])]
    transpose x0 -> x1, local copies, waits for them, and re-layouts: none -> 2.58 us  [body(): f = jnp.transpose(populations, (2, 0, 1, 3))]
    concatenate x1, other arithmetic: 1.67 us -> 0.08 us  [body(): jnp.concatenate([from_below[:19, 1:-1, None], fx, from_above[:19, 1:-1, N...]
    sub x5, other arithmetic: 5.65 us -> 7.09 us  [collide_major(): stacked = jnp.concatenate([f - balance, guo_term], axis=0)]
    ppermute x2, waiting for transfers between devices: 2.32 us -> 3.67 us  [from_partner(): lax.ppermute(x, axis, [(i, i ^ 1 << distance) for i in range(lax.axis_siz...]
    ppermute x2, starting transfers between devices: 3.53 us -> 2.24 us  [from_partner(): lax.ppermute(x, axis, [(i, i ^ 1 << distance) for i in range(lax.axis_siz...]
    dot_general x5, matrix products: 3.79 us -> 5.07 us  [collide_major(): jnp.einsum('pq,q...->p...', table, stacked, precision=lax.Precision.HIGH)]
    sub x0 -> x2, local copies, waits for them, and re-layouts: none -> 0.96 us  [the longest x1 0.91 us: collide_major(): f - jnp.einsum('pq,q...->p...', table, stacked, precision=lax.Precision.H...]
  transfers between devices with their start and end apart: 6 -> 6, of which waited for: 2 -> 3; matrix products, arithmetic and copies ran while one was open for 31% -> 30% of each run, Pallas kernels for 0% -> 0%
where the time goes in v9:
time: 63.3 us; the launch traced here: 63 us
  other arithmetic  20.8 us (33%)
  local copies, waits for them, and re-layouts  13.5 us (21%)
  starting transfers between devices  9.31 us (15%)
  waiting for transfers between devices  8.78 us (14%)
  matrix products  5.07 us (8%)
  Pallas kernels  4.37 us (7%)
  between operations  1.21 us (2%)
    sub x5, other arithmetic, collide_major(): stacked = jnp.concatenate([f - balance, guo_term], axis=0)  7.09 us
    ppermute x4, starting transfers between devices, shift_ring(): lax.ppermute(x, axis, [(i, (i - step) % count) for i in range(count)])  7.07 us
    ppermute x4, waiting for transfers between devices, shift_ring(): lax.ppermute(x, axis, [(i, (i - step) % count) for i in range(count)])  5.1 us
    dot_general x5, matrix products, collide_major(): jnp.einsum('pq,q...->p...', table, stacked, precision=lax.Precision.HIGH)  5.07 us
    unnamed x16, local copies, waits for them, and re-layouts  5.02 us
    pallas_call x1, Pallas kernels, stream_and_render(): pl.pallas_call(kernel, out_shape=(jax.ShapeDtypeStruct((19, extent_x, ext...  4.37 us
    ppermute x2, waiting for transfers between devices, from_partner(): lax.ppermute(x, axis, [(i, i ^ 1 << distance) for i in range(lax.axis_siz...  3.67 us
    sub x3, other arithmetic, collide_major(): f - jnp.einsum('pq,q...->p...', table, stacked, precision=lax.Precision.H...  3.61 us
  transfers between devices with their start and end apart: 6, of which 3 were waited for; matrix products, arithmetic and copies ran while one was open for 30% of the time, Pallas kernels for 0%

profile of v9, /device:TPU:0, one launch (start us, length us, event | category | flops | bytes accessed | tf_op | source)
XLA Modules:
  0.0 63.0 jit_solution(5724846961955076978)
XLA Ops:
  0.6 2.0 %bitcast_reduce_fusion = f32[16,16,128]{2,1,0:T(8,128)S(1)} fusion(f32[16,16,19,128]{3,1,2,0:T(8,128)} %param.31), kind=kLoop, calls=%fused_computation.687 | loop fusion | flops 589824 | bytes 2621440 | tf_op jit(solution)/shard_map/reduce_sum | solution.py:269
  2.7 0.4 copy-done
  3.1 0.9 %copy.468 = f32[16,16,19,128]{3,0,1,2:T(8,128)S(1)} copy(f32[16,16,19,128]{3,1,2,0:T(8,128)S(1)} %copy-done) | data formatting | bytes 4980736 | tf_op args[0]
  4.1 0.2 fusion.346
  4.3 3.0 %collective-permute-start = (f32[21,16,128]{2,1,0:T(8,128)S(1)}, f32[21,16,128]{2,1,0:T(8,128)S(1)}, u32[]{:S(2)}, u32[]{:S(2)}) collective-permute-start(f32[21,16,128]{2,1,0:T(8,128)S(1)} %pad_maximum_fusion.18), channel_id=1, source_target_pairs={{0,8},{8,16},{16,24},{24,0},{1,9},{9,17},{17,25},{25,1},{2,10},{10... | collective-permute-start | bytes 516104 | tf_op jit(solution)/shard_map/ppermute | solution.py:161
  7.4 1.0 %collective-permute-start.1 = (f32[21,16,128]{2,0,1:T(8,128)S(1)}, f32[21,16,128]{2,0,1:T(8,128)S(1)}, u32[]{:S(2)}, u32[]{:S(2)}) collective-permute-start(f32[21,16,128]{2,0,1:T(8,128)S(1)} %copy.281), channel_id=1, source_target_pairs={{0,24},{8,0},{16,8},{24,16},{1,25},{9,1},{17,9},{25,17},{2,26},{10... | collective-permute-start | bytes 516104 | tf_op jit(solution)/shard_map/ppermute | solution.py:161
  8.4 0.2 fusion.353
  8.7 0.2 fusion.352
  8.9 0.3 slice_reduce_fusion
  9.2 0.9 %add_multiply_fusion.5 = (f32[14,14,128]{2,0,1:T(8,128)S(1)}, f32[14,14,128]{2,0,1:T(8,128)S(1)}, f32[14,14,128]{2,0,1:T(8,128)S(1)}, f32[14,14,128]{2,0,1:T(8,1...) fusion(f32[14,14,128]{2,0,1:T(8,128)S(1)} %slice_reduce_fusion, ...), kind=kLoop, calls=%fused_computation.293 | loop fusion | flops 2985472 | bytes 4515840 | tf_op jit(solution)/shard_map/mul | solution.py:180
  10.2 2.1 %fusion.5 = (f32[19,14,14,128]{3,1,2,0:T(8,128)S(1)}, f32[19,14,14,128]{3,1,2,0:T(8,128)S(1)}) fusion(f32[19,16,16,128]{3,1,2,0:T(8,128)S(1)} %bitcast.264, f32[14,14,128]{2,0,1:T(8,128)S(1)} %get-tuple-element.36, f32[14,14,128]{2,0,1:T(8,128)S(1)} %get-tuple-element.41, f32[19]{0:T(128)S(1)} %copy-done.4, f32[14,14,128]{2,0,1:T(8,128)S(1)} %get-tuple-element.39, ...), kind=kLoop, calls=%fused_computation.81 | loop fusion | flops 11916800 | bytes 6623536 | tf_op jit(solution)/shard_map/sub | solution.py:185
  12.3 0.3 pad_maximum_fusion
  12.7 0.4 copy-done.2
  13.0 3.8 %fusion = f32[19,14,14,128]{3,0,2,1:T(8,128)S(1)} fusion(f32[19,38,1,1]{1,0,3,2:T(8,128)S(1)} %copy-done.2, f32[38,14,14,128]{3,1,2,0:T(8,128)S(1)} %pad_maximum_fusion), kind=kOutput, calls=%fused_computation.73 | convolution fusion | flops 108681216 | bytes 5722952 | tf_op jit(solution)/shard_map/pq,q...->p.../dot_general | solution.py:186
  16.8 2.4 %copy_subtract_fusion = f32[19,14,14,128]{3,1,2,0:T(8,128)} fusion(f32[19,14,14,128]{3,0,2,1:T(8,128)S(1)} %fusion, f32[19,16,16,128]{3,1,2,0:T(8,128)S(1)} %bitcast.265), kind=kLoop, calls=%fused_computation.82 | loop fusion | flops 476672 | bytes 5720064 | tf_op jit(solution)/shard_map/sub | solution.py:186
  19.2 2.6 %copy.283 = f32[19,16,16,128]{3,0,1,2:T(8,128)S(1)} copy(f32[19,16,16,128]{3,2,0,1:T(8,128)} %bitcast.270) | data formatting | bytes 4980736 | tf_op jit(solution)/shard_map/transpose | solution.py:268
  21.8 0.1 fusion.228
  21.9 0.1 fusion.227
  22.1 0.2 fusion.278
  22.3 0.2 fusion.279
  22.5 0.2 copy.344
  22.7 0.1 fusion.252
  22.8 0.6 fusion.329
  23.5 0.1 fusion.347
  23.5 0.1 fusion.348
  23.6 0.6 add_multiply_fusion.14
  24.2 1.2 %fusion.31 = (f32[19,2,14,128]{3,1,2,0:T(2,128)S(1)}, f32[19,2,14,128]{3,1,2,0:T(2,128)S(1)}) fusion(f32[19,2,14,128]{3,1,2,0:T(2,128)S(1)} %get-tuple-element.78, f32[2,14,128]{2,0,1:T(2,128)S(1)} %get-tuple-element.43, f32[2,14,128]{2,0,1:T(2,128)S(1)} %get-tuple-element.77, f32[19]{0:T(128)S(1)} %copy-done.3, f32[2,14,128]{2,0,1:T(2,128)S(1)} %get-tuple-element.48, ...), kind=kLoop, calls=%fused_computation.178 | loop fusion | flops 1702400 | bytes 946480 | tf_op jit(solution)/shard_map/sub | solution.py:185
  25.5 0.2 pad_maximum_fusion.5
  25.7 0.3 fusion.10
  26.2 0.1 fusion.216
  26.3 0.1 fusion.197
  26.4 0.3 add_multiply_fusion.18
  26.7 1.1 %fusion.27 = (f32[19,2,14,128]{3,1,2,0:T(2,128)S(1)}, f32[19,2,14,128]{3,1,2,0:T(2,128)S(1)}, f32[19,2,14,128]{3,1,2,0:T(2,128)S(1)}) fusion(f32[19,2,14,128]{3,1,2,0:T(2,128)S(1)} %get-tuple-element.35, f32[2,14,128]{2,0,1:T(2,128)S(1)} %get-tuple-element.21, f32[2,14,128]{2,0,1:T(2,128)S(1)} %get-tuple-element.34, f32[19]{0:T(128)S(1)} %copy-done.3, ...), kind=kLoop, calls=%fused_computation.174 | loop fusion | flops 1770496 | bytes 1763632 | tf_op jit(solution)/shard_map/sub | solution.py:185
  27.8 0.2 pad_maximum_fusion.4
  28.1 0.3 fusion.12
  28.5 3.0 %collective-permute-start.3 = (f32[21,20,128]{2,0,1:T(8,128)S(1)}, f32[21,20,128]{2,0,1:T(8,128)S(1)}, u32[]{:S(2)}, u32[]{:S(2)}) collective-permute-start(f32[21,20,128]{2,0,1:T(8,128)S(1)} %get-tuple-element.209), channel_id=1, source_target_pairs={{0,7},{1,0},{2,1},{3,2},{4,3},{5,4},{6,5},{7,6},{8,15},{9,8},{10,9... | collective-permute-start | bytes 645128 | tf_op jit(solution)/shard_map/ppermute | solution.py:161
  31.5 0.2 copy_subtract_fusion.2
  31.8 0.5 pad_maximum_fusion.1
  32.3 2.0 %copy.360.band_ref = f32[19,18,14,128]{3,2,1,0:T(8,128)} copy(f32[19,18,14,128]{3,1,2,0:T(8,128)S(1)} %pad_maximum_fusion.1) | data formatting | bytes 4902912 | tf_op jit(solution)/shard_map/concatenate | solution.py:295
  34.3 2.4 %collective-permute-done.3 = f32[21,20,128]{2,0,1:T(8,128)S(1)} collective-permute-done((f32[21,20,128]{2,0,1:T(8,128)S(1)}, f32[21,20,128]{2,0,1:T(8,128)S(1)}, u32[]{:S(2)}, u32[]{:S(2)}) %collective-permute-start.3) | collective-permute-done | bytes 215072 | tf_op jit(solution)/shard_map/ppermute | solution.py:161
  36.7 2.7 %collective-permute-done.2 = f32[21,20,128]{2,0,1:T(8,128)S(1)} collective-permute-done((f32[21,20,128]{2,0,1:T(8,128)S(1)}, f32[21,20,128]{2,0,1:T(8,128)S(1)}, u32[]{:S(2)}, u32[]{:S(2)}) %collective-permute-start.2) | collective-permute-done | bytes 215072 | tf_op jit(solution)/shard_map/ppermute | solution.py:161
  39.5 0.2 fusion.355
  39.7 0.2 fusion.356
  39.9 0.2 fusion.357
  40.0 0.2 fusion.358
  40.3 0.4 fusion.324
  40.7 0.5 add_multiply_fusion.10
  41.2 1.3 %fusion.17 = (f32[19,2,18,128]{3,1,2,0:T(2,128)S(1)}, f32[19,2,18,128]{3,1,2,0:T(2,128)S(1)}) fusion(f32[19,2,18,128]{3,1,2,0:T(2,128)S(1)} %get-tuple-element.215, f32[2,18,128]{2,0,1:T(2,128)S(1)} %get-tuple-element.52, f32[2,18,128]{2,0,1:T(2,128)S(1)} %get-tuple-element.214, f32[19]{0:T(128)S(1)} %copy-done.3, f32[2,18,128]{2,0,1:T(2,128)S(1)} %get-tuple-element.57, ...), kind=kLoop, calls=%fused_computation.158 | loop fusion | flops 2188800 | bytes 1216816 | tf_op jit(solution)/shard_map/sub | solution.py:185
  42.6 0.3 pad_maximum_fusion.2
  42.9 0.4 fusion.6
  43.3 0.9 %copy.359.near_ref = f32[19,18,2,128]{3,2,1,0:T(2,128)} copy(f32[19,18,2,128]{3,0,1,2:T(8,128)S(1)} %fusion.6) | data formatting | bytes 700416 | tf_op jit(solution)/shard_map/sub | solution.py:186
  44.2 0.5 add_multiply_fusion.6
  44.7 1.3 %fusion.21 = (f32[19,2,18,128]{3,1,2,0:T(2,128)S(1)}, f32[19,2,18,128]{3,1,2,0:T(2,128)S(1)}) fusion(f32[19,2,18,128]{3,1,2,0:T(2,128)S(1)} %get-tuple-element.20, f32[2,18,128]{2,0,1:T(2,128)S(1)} %get-tuple-element.12, f32[2,18,128]{2,0,1:T(2,128)S(1)} %get-tuple-element.19, f32[19]{0:T(128)S(1)} %copy-done.3, f32[2,18,128]{2,0,1:T(2,128)S(1)} %get-tuple-element.17, ...), kind=kLoop, calls=%fused_computation.162 | loop fusion | flops 2188800 | bytes 1216816 | tf_op jit(solution)/shard_map/sub | solution.py:185
  46.0 0.3 pad_maximum_fusion.3
  46.3 0.3 fusion.7
  46.7 1.0 %bitcast_subtract_fusion.far_ref = f32[19,18,2,128]{3,2,1,0:T(2,128)} fusion(f32[19,2,18,128]{3,0,2,1:T(8,128)S(1)} %fusion.7, f32[19,18,2,128]{3,0,1,2:T(8,128)S(1)} %get-tuple-element.61), kind=kLoop, calls=%fused_computation.163 | loop fusion | flops 87552 | bytes 1050624 | tf_op jit(solution)/shard_map/sub | solution.py:186
  47.7 4.4 %shard_map.302 = (f32[19,16,16,128]{3,2,1,0:T(8,128)}, f32[4,16,128]{2,1,0:T(8,128)}) custom-call(f32[19,18,2,128]{3,2,1,0:T(2,128)} %copy.359.near_ref, f32[19,18,14,128]{3,2,1,0:T(8,128)} %copy.360.band_ref, f32[19,18,2,128]{3,2,1,0:T(2,128)} %bitcast_subtract_fusion.far_ref), custom_call_target="tpu_custom_call" | custom-call | tf_op jit(solution)/shard_map/pallas_call | solution.py:234
  52.0 0.9 %reshape_reshape.3 = f32[4,16,2,2,32]{4,3,2,1,0:T(2,128)S(1)} reshape(f32[4,16,128]{2,1,0:T(8,128)} %get-tuple-element.5) | data formatting | bytes 65536 | tf_op jit(solution)/shard_map/reshape;reshape | solution.py:317
  53.0 0.1 fusion.351
  53.1 0.7 %collective-permute-start.4 = (f32[4,16,2,32]{3,1,0,2:T(8,128)S(1)}, f32[4,16,2,32]{3,1,0,2:T(8,128)S(1)}, u32[]{:S(2)}, u32[]{:S(2)}) collective-permute-start(f32[4,16,2,32]{3,1,0,2:T(8,128)S(1)} %select_bitcast_fusion), channel_id=1, source_target_pairs={{0,8},{8,0},{16,24},{24,16},{1,9},{9,1},{17,25},{25,17},{2,10},{10... | collective-permute-start | bytes 49160 | tf_op jit(solution)/shard_map/ppermute | solution.py:30
  53.7 3.7 %collective-permute-done.4 = f32[4,16,2,32]{3,1,0,2:T(8,128)S(1)} collective-permute-done((f32[4,16,2,32]{3,1,0,2:T(8,128)S(1)}, f32[4,16,2,32]{3,1,0,2:T(8,128)S(1)}, u32[]{:S(2)}, u32[]{:S(2)}) %collective-permute-start.4) | collective-permute-done | bytes 16416 | tf_op jit(solution)/shard_map/ppermute | solution.py:30
  57.5 1.6 %collective-permute-start.5 = (f32[4,16,1,32]{3,1,0,2:T(8,128)S(1)}, f32[4,16,1,32]{3,1,0,2:T(8,128)S(1)}, u32[]{:S(2)}, u32[]{:S(2)}) collective-permute-start(f32[4,16,1,32]{3,1,0,2:T(8,128)S(1)} %select_bitcast_fusion.1), channel_id=1, source_target_pairs={{0,16},{8,24},{16,0},{24,8},{1,17},{9,25},{17,1},{25,9},{2,18},{10... | collective-permute-start | bytes 24584 | tf_op jit(solution)/shard_map/ppermute | solution.py:30
  59.1 3.3 %copy.363 = f32[16,16,19,128]{3,1,2,0:T(8,128)} copy(f32[16,16,19,128]{3,1,0,2:T(8,128)} %bitcast.274) | data formatting | bytes 4980736
  62.4 0.6 fusion.113
  (56 shorter events, 1.2 us)
Async XLA Ops:
  0.6 2.5 %copy-start = (f32[16,16,19,128]{3,1,2,0:T(8,128)S(1)}, f32[16,16,19,128]{3,1,2,0:T(8,128)}, u32[]{:S(2)}) copy-start(f32[16,16,19,128]{3,1,2,0:T(8,128)} %param.31) | copy-start | bytes 7471108
  4.3 17.5 %collective-permute-start = (f32[21,16,128]{2,1,0:T(8,128)S(1)}, f32[21,16,128]{2,1,0:T(8,128)S(1)}, u32[]{:S(2)}, u32[]{:S(2)}) collective-permute-start(f32[21,16,128]{2,1,0:T(8,128)S(1)} %pad_maximum_fusion.18), channel_id=1, source_target_pairs={{0,8},{8,16},{16,24},{24,0},{1,9},{9,17},{17,25},{25,1},{2,10},{10... | collective-permute-start | bytes 516104 | tf_op jit(solution)/shard_map/ppermute | solution.py:161
  7.4 14.6 %collective-permute-start.1 = (f32[21,16,128]{2,0,1:T(8,128)S(1)}, f32[21,16,128]{2,0,1:T(8,128)S(1)}, u32[]{:S(2)}, u32[]{:S(2)}) collective-permute-start(f32[21,16,128]{2,0,1:T(8,128)S(1)} %copy.281), channel_id=1, source_target_pairs={{0,24},{8,0},{16,8},{24,16},{1,25},{9,1},{17,9},{25,17},{2,26},{10... | collective-permute-start | bytes 516104 | tf_op jit(solution)/shard_map/ppermute | solution.py:161
  9.1 1.0 %copy-start.3 = (f32[19]{0:T(128)S(1)}, f32[19]{0:T(128)}, u32[]{:S(2)}) copy-start(f32[19]{0:T(128)} %constant.112.clone) | copy-start | bytes 232
  9.2 1.0 %copy-start.4 = (f32[19]{0:T(128)S(1)}, f32[19]{0:T(128)}, u32[]{:S(2)}) copy-start(f32[19]{0:T(128)} %constant.57.clone) | copy-start | bytes 232
  9.2 1.0 %copy-start.5 = (f32[19]{0:T(128)S(1)}, f32[19]{0:T(128)}, u32[]{:S(2)}) copy-start(f32[19]{0:T(128)} %constant.56.clone) | copy-start | bytes 232
  9.2 1.0 %copy-start.6 = (f32[19]{0:T(128)S(1)}, f32[19]{0:T(128)}, u32[]{:S(2)}) copy-start(f32[19]{0:T(128)} %constant.53.clone) | copy-start | bytes 232
  12.3 0.7 %copy-start.2 = (f32[19,38,1,1]{1,0,3,2:T(8,128)S(1)}, f32[19,38,1,1]{1,0,3,2:T(8,128)}, u32[]{:S(2)}) copy-start(f32[19,38,1,1]{1,0,3,2:T(8,128)} %constant.117) | copy-start | bytes 8668
  28.4 3.4 %copy-start.1 = (f32[19,14,14,128]{3,1,2,0:T(8,128)S(1)}, f32[19,14,14,128]{3,1,2,0:T(8,128)}, u32[]{:S(2)}) copy-start(f32[19,14,14,128]{3,1,2,0:T(8,128)} %copy_subtract_fusion) | copy-start | bytes 5720068
  28.5 8.2 %collective-permute-start.3 = (f32[21,20,128]{2,0,1:T(8,128)S(1)}, f32[21,20,128]{2,0,1:T(8,128)S(1)}, u32[]{:S(2)}, u32[]{:S(2)}) collective-permute-start(f32[21,20,128]{2,0,1:T(8,128)S(1)} %get-tuple-element.209), channel_id=1, source_target_pairs={{0,7},{1,0},{2,1},{3,2},{4,3},{5,4},{6,5},{7,6},{8,15},{9,8},{10,9... | collective-permute-start | bytes 645128 | tf_op jit(solution)/shard_map/ppermute | solution.py:161
  31.7 7.7 %collective-permute-start.2 = (f32[21,20,128]{2,0,1:T(8,128)S(1)}, f32[21,20,128]{2,0,1:T(8,128)S(1)}, u32[]{:S(2)}, u32[]{:S(2)}) collective-permute-start(f32[21,20,128]{2,0,1:T(8,128)S(1)} %get-tuple-element.210), channel_id=1, source_target_pairs={{0,1},{1,2},{2,3},{3,4},{4,5},{5,6},{6,7},{7,0},{8,9},{9,10},{10,1... | collective-permute-start | bytes 645128 | tf_op jit(solution)/shard_map/ppermute | solution.py:161
  53.1 4.3 %collective-permute-start.4 = (f32[4,16,2,32]{3,1,0,2:T(8,128)S(1)}, f32[4,16,2,32]{3,1,0,2:T(8,128)S(1)}, u32[]{:S(2)}, u32[]{:S(2)}) collective-permute-start(f32[4,16,2,32]{3,1,0,2:T(8,128)S(1)} %select_bitcast_fusion), channel_id=1, source_target_pairs={{0,8},{8,0},{16,24},{24,16},{1,9},{9,1},{17,25},{25,17},{2,10},{10... | collective-permute-start | bytes 49160 | tf_op jit(solution)/shard_map/ppermute | solution.py:30
  57.5 4.9 %collective-permute-start.5 = (f32[4,16,1,32]{3,1,0,2:T(8,128)S(1)}, f32[4,16,1,32]{3,1,0,2:T(8,128)S(1)}, u32[]{:S(2)}, u32[]{:S(2)}) collective-permute-start(f32[4,16,1,32]{3,1,0,2:T(8,128)S(1)} %select_bitcast_fusion.1), channel_id=1, source_target_pairs={{0,16},{8,24},{16,0},{24,8},{1,17},{9,25},{17,1},{25,9},{2,18},{10... | collective-permute-start | bytes 24584 | tf_op jit(solution)/shard_map/ppermute | solution.py:30

commit v10 on v6

--- a/solution.py
+++ b/solution.py
@@ -302,21 +302,11 @@
     depth_z = layered.shape[2]
     block_len = depth_z // groups
     blocked = layered.reshape(4, extent_y, groups, block_len)
-    position = lax.axis_index("gx")
-    current = blocked
-    for level in range(groups.bit_length() - 1):
-        parity = position // (1 << level) % 2
-        halves = current.shape[2] // 2
-        paired = current.reshape(4, extent_y, halves, 2, block_len)
-        lower = paired[:, :, :, 0]
-        upper = paired[:, :, :, 1]
-        kept = jnp.where(parity == 1, upper, lower)
-        handed = jnp.where(parity == 1, lower, upper)
-        partner = from_partner(handed, "gx", level)
-        nearer = jnp.where(parity == 0, kept, partner)
-        farther = jnp.where(parity == 0, partner, kept)
-        current = nearer + (1.0 - nearer[3:4]) * farther
-    picture = current.reshape(4, extent_y, block_len)
+    gathered = lax.all_to_all(blocked, "gx", 2, 2, tiled=True)
+    current = gathered[:, :, 0]
+    for source in range(1, groups):
+        current = current + (1.0 - current[3:4]) * gathered[:, :, source]
+    picture = current
     return (fresh, picture)
 
 

time: 54.1 us -> 54.4 us (level)
  waiting for transfers between devices: 4.6 us -> 5.34 us
  other arithmetic: 20.1 us -> 19.4 us
  local copies, waits for them, and re-layouts: 9.3 us -> 9.87 us
    all_to_all x0 -> x1, starting transfers between devices: none -> 3.69 us  [body(): gathered = lax.all_to_all(blocked, 'gx', 2, 2, tiled=True)]
    ppermute x2 -> x0, starting transfers between devices: 3.53 us -> none  [from_partner(): lax.ppermute(x, axis, [(i, i ^ 1 << distance) for i in range(lax.axis_siz...]
    ppermute x2 -> x0, waiting for transfers between devices: 2.32 us -> none  [from_partner(): lax.ppermute(x, axis, [(i, i ^ 1 << distance) for i in range(lax.axis_siz...]
    ppermute x4, waiting for transfers between devices: 2.28 us -> 3.91 us  [shift_ring(): lax.ppermute(x, axis, [(i, (i - step) % count) for i in range(count)])]
    all_to_all x0 -> x1, waiting for transfers between devices: none -> 1.44 us  [body(): gathered = lax.all_to_all(blocked, 'gx', 2, 2, tiled=True)]
    sub x4, other arithmetic: 4.12 us -> 2.78 us  [collide_major(): f - jnp.einsum('pq,q...->p...', table, stacked, precision=lax.Precision.H...]
    another operation x1 -> x0, local copies, waits for them, and re-layouts: 0.91 us -> none  [body(): paired = current.reshape(4, extent_y, halves, 2, block_len)]
    reshape x0 -> x2, local copies, waits for them, and re-layouts: none -> 0.88 us  [body(): blocked = layered.reshape(4, extent_y, groups, block_len)]
  transfers between devices with their start and end apart: 6 -> 5, of which waited for: 2 -> 4; matrix products, arithmetic and copies ran while one was open for 31% -> 28% of each run, Pallas kernels for 0% -> 0%
where the time goes in v10:
time: 54.4 us; the launch traced here: 54.1 us
  other arithmetic  19.4 us (36%)
  starting transfers between devices  10 us (18%)
  local copies, waits for them, and re-layouts  9.87 us (18%)
  waiting for transfers between devices  5.34 us (10%)
  Pallas kernels  4.37 us (8%)
  matrix products  3.79 us (7%)
  between operations  1.24 us (2%)
    ppermute x4, starting transfers between devices, shift_ring(): lax.ppermute(x, axis, [(i, (i - step) % count) for i in range(count)])  6.33 us
    sub x5, other arithmetic, collide_major(): stacked = jnp.concatenate([f - balance, guo_term], axis=0)  5.72 us
    unnamed x15, local copies, waits for them, and re-layouts  4.81 us
    pallas_call x1, Pallas kernels, stream_and_render(): pl.pallas_call(kernel, out_shape=(jax.ShapeDtypeStruct((19, extent_x, ext...  4.37 us
    ppermute x4, waiting for transfers between devices, shift_ring(): lax.ppermute(x, axis, [(i, (i - step) % count) for i in range(count)])  3.91 us
    dot_general x5, matrix products, collide_major(): jnp.einsum('pq,q...->p...', table, stacked, precision=lax.Precision.HIGH)  3.79 us
    all_to_all x1, starting transfers between devices, body(): gathered = lax.all_to_all(blocked, 'gx', 2, 2, tiled=True)  3.69 us
    sub x4, other arithmetic, collide_major(): f - jnp.einsum('pq,q...->p...', table, stacked, precision=lax.Precision.H...  2.78 us
  transfers between devices with their start and end apart: 5, of which 4 were waited for; matrix products, arithmetic and copies ran while one was open for 28% of the time, Pallas kernels for 0%

profile of v10, /device:TPU:0, one launch (start us, length us, event | category | flops | bytes accessed | tf_op | source)
XLA Modules:
  0.0 54.1 jit_solution(4147039106370011739)
XLA Ops:
  0.6 2.0 %bitcast_reduce_fusion = f32[16,16,128]{2,1,0:T(8,128)S(1)} fusion(f32[16,16,19,128]{3,1,2,0:T(8,128)} %param.31), kind=kLoop, calls=%fused_computation.830 | loop fusion | flops 589824 | bytes 2621440 | tf_op jit(solution)/shard_map/reduce_sum | solution.py:268
  2.7 0.4 copy-done
  3.1 3.9 %collective-permute-start.1 = (f32[21,16,128]{2,1,0:T(8,128)S(1)}, f32[21,16,128]{2,1,0:T(8,128)S(1)}, u32[]{:S(2)}, u32[]{:S(2)}) collective-permute-start(f32[21,16,128]{2,1,0:T(8,128)S(1)} %pad_maximum_fusion.16), channel_id=1, source_target_pairs={{0,24},{8,0},{16,8},{24,16},{1,25},{9,1},{17,9},{25,17},{2,26},{10... | collective-permute-start | bytes 516104 | tf_op jit(solution)/shard_map/ppermute | solution.py:161
  7.2 0.2 slice_reduce_fusion
  7.4 0.2 fusion.452
  7.6 0.2 fusion.453
  7.9 0.9 %add_multiply_fusion.5 = (f32[14,14,128]{2,1,0:T(8,128)S(1)}, f32[14,14,128]{2,1,0:T(8,128)S(1)}, f32[14,14,128]{2,1,0:T(8,128)S(1)}, f32[14,14,128]{2,1,0:T(8,1...) fusion(f32[14,14,128]{2,1,0:T(8,128)S(1)} %slice_reduce_fusion, ...), kind=kLoop, calls=%fused_computation.316 | loop fusion | flops 2985472 | bytes 6207488 | tf_op jit(solution)/shard_map/mul | solution.py:180
  8.9 2.2 %fusion.5 = (f32[19,14,14,128]{3,2,0,1:T(8,128)S(1)}, f32[19,14,14,128]{3,2,0,1:T(8,128)S(1)}) fusion(f32[19,16,16,128]{3,2,0,1:T(8,128)S(1)} %bitcast.546, f32[14,14,128]{2,1,0:T(8,128)S(1)} %get-tuple-element.30, f32[14,14,128]{2,1,0:T(8,128)S(1)} %get-tuple-element.35, f32[19]{0:T(128)S(1)} %copy-done.3, f32[14,14,128]{2,1,0:T(8,128)S(1)} %get-tuple-element.33, ...), kind=kLoop, calls=%fused_computation.46 | loop fusion | flops 11916800 | bytes 6623536 | tf_op jit(solution)/shard_map/sub | solution.py:185
  11.1 0.4 pad_maximum_fusion
  11.5 0.3 copy-done.1
  11.8 2.2 %fusion = f32[19,14,14,128]{3,0,2,1:T(8,128)S(1)} fusion(f32[19,38,1,1]{1,0,3,2:T(8,128)S(1)} %copy-done.1, f32[38,14,14,128]{3,2,0,1:T(8,128)S(1)} %pad_maximum_fusion), kind=kOutput, calls=%fused_computation.39 | convolution fusion | flops 108681216 | bytes 5722952 | tf_op jit(solution)/shard_map/pq,q...->p.../dot_general | solution.py:186
  14.0 0.7 %copy_subtract_fusion = f32[19,14,14,128]{3,2,0,1:T(8,128)S(1)} fusion(f32[19,14,14,128]{3,0,2,1:T(8,128)S(1)} %fusion, f32[19,16,16,128]{3,2,0,1:T(8,128)S(1)} %bitcast.547), kind=kLoop, calls=%fused_computation.47 | loop fusion | flops 476672 | bytes 5720064 | tf_op jit(solution)/shard_map/sub | solution.py:186
  14.9 0.5 collective-permute-done
  15.5 0.1 fusion.303
  15.6 0.1 fusion.302
  15.8 0.1 fusion.424
  15.9 0.1 fusion.450
  16.0 0.2 pad_maximum_fusion.12
  16.4 2.3 %collective-permute-start.3 = (f32[21,20,128]{2,0,1:T(8,128)S(1)}, f32[21,20,128]{2,0,1:T(8,128)S(1)}, u32[]{:S(2)}, u32[]{:S(2)}) collective-permute-start(f32[21,20,128]{2,0,1:T(8,128)S(1)} %get-tuple-element.195), channel_id=1, source_target_pairs={{0,7},{1,0},{2,1},{3,2},{4,3},{5,4},{6,5},{7,6},{8,15},{9,8},{10,9... | collective-permute-start | bytes 645128 | tf_op jit(solution)/shard_map/ppermute | solution.py:161
  18.9 0.1 add_multiply_fusion.14
  19.0 0.4 fusion.29
  19.4 0.4 fusion.10
  19.9 0.2 add_multiply_fusion.15
  20.1 0.4 fusion.25
  20.5 0.4 fusion.12
  21.0 0.1 copy_subtract_fusion.4
  21.1 0.2 pad_maximum_fusion.2
  21.3 1.9 %copy.550.band_ref = f32[19,18,14,128]{3,2,1,0:T(8,128)} copy(f32[19,18,14,128]{3,2,0,1:T(8,128)S(1)} %pad_maximum_fusion.2) | data formatting | bytes 4902912 | tf_op jit(solution)/shard_map/concatenate | solution.py:294
  23.1 0.1 fusion.451
  23.2 0.8 %collective-permute-done.3 = f32[21,20,128]{2,0,1:T(8,128)S(1)} collective-permute-done((f32[21,20,128]{2,0,1:T(8,128)S(1)}, f32[21,20,128]{2,0,1:T(8,128)S(1)}, u32[]{:S(2)}, u32[]{:S(2)}) %collective-permute-start.3) | collective-permute-done | bytes 215072 | tf_op jit(solution)/shard_map/ppermute | solution.py:161
  24.1 0.1 fusion.117
  24.2 0.1 fusion.118
  24.3 2.6 %collective-permute-done.2 = f32[21,20,128]{2,0,1:T(8,128)S(1)} collective-permute-done((f32[21,20,128]{2,0,1:T(8,128)S(1)}, f32[21,20,128]{2,0,1:T(8,128)S(1)}, u32[]{:S(2)}, u32[]{:S(2)}) %collective-permute-start.2) | collective-permute-done | bytes 215072 | tf_op jit(solution)/shard_map/ppermute | solution.py:161
  26.9 0.1 fusion.128
  27.0 0.1 fusion.129
  27.1 0.1 fusion.444
  27.3 0.1 fusion.443
  27.4 0.1 fusion.446
  27.5 0.1 fusion.445
  27.7 0.2 copy.547
  27.9 0.2 copy.476
  28.1 1.6 %pad_maximum_fusion.1 = (f32[19,18,17,128]{3,2,1,0:T(8,128)S(1)}, f32[19,18,17,128]{3,2,1,0:T(8,128)S(1)}) fusion(f32[19,18,1,128]{3,2,1,0:T(1,128)S(1)} %copy.547, f32[19,1,16,128]{3,2,1,0:T(8,128)S(1)} %get-tuple-element.108, f32[19,1,16,128]{3,2,1,0:T(8,128)S(1)} %get-tuple-element.102, f32[19,18,1,128]{3,2,1,0:T(1,128)S(1)} %copy.476, ...), kind=kLoop, calls=%fused_computation.38 | loop fusion | flops 4465152 | bytes 9105408 | tf_op jit(solution)/shard_map/concatenate | solution.py:283
  29.7 0.2 slice_reduce_fusion.1
  29.9 0.1 slice_reduce_fusion.2
  29.9 0.8 %add_multiply_fusion.6 = (f32[18,2,128]{2,1,0:T(2,128)S(1)}, f32[18,2,128]{2,1,0:T(2,128)S(1)}, f32[18,2,128]{2,1,0:T(2,128)S(1)}, f32[18,2,128]{2,1,0:T(2,128)S...) fusion(f32[18,2,128]{2,1,0:T(2,128)S(1)} %slice_reduce_fusion.1, ...), kind=kLoop, calls=%fused_computation.559 | loop fusion | flops 824832 | bytes 3421328 | tf_op jit(solution)/shard_map/mul | solution.py:180
  30.8 1.4 %fusion.21 = (f32[19,18,2,128]{3,2,1,0:T(2,128)S(1)}, f32[19,18,2,128]{3,2,1,0:T(2,128)S(1)}) fusion(f32[19,18,17,128]{3,2,1,0:T(8,128)S(1)} %get-tuple-element.53, f32[18,2,128]{2,1,0:T(2,128)S(1)} %get-tuple-element.14, f32[18,2,128]{2,1,0:T(2,128)S(1)} %slice_reduce_fusion.1, f32[19]{0:T(128)S(1)} %copy-done.2, f32[18,2,128]{2,1,0:T(2,128)S(1)} %get-tuple-element.19, ...), kind=kLoop, calls=%fused_computation.144 | loop fusion | flops 2188800 | bytes 1216816 | tf_op jit(solution)/shard_map/sub | solution.py:185
  32.2 0.3 pad_maximum_fusion.4
  32.5 0.3 fusion.6
  32.9 1.0 %copy_subtract_fusion.1.far_ref = f32[19,18,2,128]{3,2,1,0:T(2,128)} fusion(f32[19,18,2,128]{3,0,2,1:T(8,128)S(1)} %fusion.6, f32[19,18,17,128]{3,2,1,0:T(8,128)S(1)} %get-tuple-element.53), kind=kLoop, calls=%fused_computation.145 | loop fusion | flops 87552 | bytes 1050624 | tf_op jit(solution)/shard_map/sub | solution.py:186
  33.9 0.7 %add_multiply_fusion.10 = (f32[18,2,128]{2,1,0:T(2,128)S(1)}, f32[18,2,128]{2,1,0:T(2,128)S(1)}, f32[18,2,128]{2,1,0:T(2,128)S(1)}, f32[18,2,128]{2,1,0:T(2,128)...) fusion(f32[18,2,128]{2,1,0:T(2,128)S(1)} %slice_reduce_fusion.2, ...), kind=kLoop, calls=%fused_computation.564 | loop fusion | flops 843264 | bytes 3568496 | tf_op jit(solution)/shard_map/mul | solution.py:180
  34.6 1.3 %fusion.17 = (f32[19,18,2,128]{3,2,1,0:T(2,128)S(1)}, f32[19,18,2,128]{3,2,1,0:T(2,128)S(1)}) fusion(f32[19,18,17,128]{3,2,1,0:T(8,128)S(1)} %get-tuple-element.54, f32[18,2,128]{2,1,0:T(2,128)S(1)} %get-tuple-element.46, f32[18,2,128]{2,1,0:T(2,128)S(1)} %slice_reduce_fusion.2, f32[19]{0:T(128)S(1)} %copy-done.2, f32[18,2,128]{2,1,0:T(2,128)S(1)} %get-tuple-element.51, ...), kind=kLoop, calls=%fused_computation.140 | loop fusion | flops 2188800 | bytes 1216816 | tf_op jit(solution)/shard_map/sub | solution.py:185
  35.9 0.3 pad_maximum_fusion.3
  36.2 0.3 fusion.8
  36.6 1.0 %copy_subtract_fusion.2.near_ref = f32[19,18,2,128]{3,2,1,0:T(2,128)} fusion(f32[19,18,2,128]{3,0,2,1:T(8,128)S(1)} %fusion.8, f32[19,18,17,128]{3,2,1,0:T(8,128)S(1)} %get-tuple-element.54), kind=kLoop, calls=%fused_computation.146 | loop fusion | flops 87552 | bytes 1050624 | tf_op jit(solution)/shard_map/sub | solution.py:186
  37.6 4.4 %shard_map.302 = (f32[19,16,16,128]{3,2,1,0:T(8,128)}, f32[4,16,128]{2,1,0:T(8,128)}) custom-call(f32[19,18,2,128]{3,2,1,0:T(2,128)} %copy_subtract_fusion.2.near_ref, f32[19,18,14,128]{3,2,1,0:T(8,128)} %copy.550.band_ref, f32[19,18,2,128]{3,2,1,0:T(2,128)} %copy_subtract_fusion.1.far_ref), custom_call_target="tpu_custom_call" | custom-call | tf_op jit(solution)/shard_map/pallas_call | solution.py:234
  42.0 0.9 %reshape.197 = f32[4,16,4,32]{3,2,1,0:T(4,128)S(1)} reshape(f32[4,16,128]{2,1,0:T(8,128)} %get-tuple-element.5) | data formatting | bytes 65536 | tf_op jit(solution)/shard_map/reshape | solution.py:304
  42.9 0.7 %reshape.334 = f32[4,1,2048]{2,1,0:T(1,128)} reshape(f32[4,4,16,32]{3,2,1,0:T(8,128)S(1)} %bitcast.558) | data formatting | bytes 65536
  43.6 3.7 %all-to-all-start = ((f32[4,1,2048]{2,1,0:T(1,128)}), f32[4,1,2048]{2,1,0:T(1,128)S(1)}, u32[]{:S(2)}, u32[]{:S(2)}) async-start(f32[4,1,2048]{2,1,0:T(1,128)} %reshape.334), calls=%async_computation | async-start | bytes 65536 | tf_op jit(solution)/shard_map/all_to_all | solution.py:305
  47.3 3.3 %copy.552 = f32[16,16,19,128]{3,1,2,0:T(8,128)} copy(f32[16,16,19,128]{3,1,0,2:T(8,128)} %bitcast.553) | data formatting | bytes 4980736
  50.6 1.4 %all-to-all-done = f32[4,1,2048]{2,1,0:T(1,128)S(1)} async-done(((f32[4,1,2048]{2,1,0:T(1,128)}), f32[4,1,2048]{2,1,0:T(1,128)S(1)}, u32[]{:S(2)}, u32[]{:S(2)}) %all-to-all-start) | async-done | bytes 32800 | tf_op jit(solution)/shard_map/all_to_all | solution.py:305
  52.0 0.5 broadcast.707
  52.5 0.7 %reduce = f32[4,2048]{1,0:T(4,128)S(1)} reduce(f32[4,1,2048]{2,1,0:T(1,128)S(1)} %all-to-all-done, f32[]{:T(128)} %broadcast.707), dimensions={1}, to_apply=%all_to_all.3.reduce_sub_computation | reduce | bytes 65540 | tf_op jit(solution)/shard_map/all_to_all | solution.py:305
  53.3 0.1 reshape.335
  53.4 0.6 %fusion.103 = f32[4,16,32]{2,1,0:T(8,128)} fusion(f32[4,16,32]{2,1,0:T(8,128)S(1)} %fusion.105, f32[4,16,4,32]{3,1,0,2:T(8,128)S(1)} %bitcast.557, f32[16,32]{1,0:T(8,128)S(1)} %fusion.412), kind=kLoop, calls=%fused_computation.333 | loop fusion | flops 4096 | bytes 26624 | tf_op jit(solution)/shard_map/add | solution.py:308
  (55 shorter events, 1.1 us)
Async XLA Ops:
  0.6 2.5 %copy-start = (f32[16,16,19,128]{3,1,2,0:T(8,128)S(1)}, f32[16,16,19,128]{3,1,2,0:T(8,128)}, u32[]{:S(2)}) copy-start(f32[16,16,19,128]{3,1,2,0:T(8,128)} %param.31) | copy-start | bytes 7471108
  3.1 11.6 %collective-permute-start.1 = (f32[21,16,128]{2,1,0:T(8,128)S(1)}, f32[21,16,128]{2,1,0:T(8,128)S(1)}, u32[]{:S(2)}, u32[]{:S(2)}) collective-permute-start(f32[21,16,128]{2,1,0:T(8,128)S(1)} %pad_maximum_fusion.16), channel_id=1, source_target_pairs={{0,24},{8,0},{16,8},{24,16},{1,25},{9,1},{17,9},{25,17},{2,26},{10... | collective-permute-start | bytes 516104 | tf_op jit(solution)/shard_map/ppermute | solution.py:161
  7.1 8.3 %collective-permute-start = (f32[21,16,128]{2,1,0:T(8,128)S(1)}, f32[21,16,128]{2,1,0:T(8,128)S(1)}, u32[]{:S(2)}, u32[]{:S(2)}) collective-permute-start(f32[21,16,128]{2,1,0:T(8,128)S(1)} %pad_maximum_fusion.15), channel_id=1, source_target_pairs={{0,8},{8,16},{16,24},{24,0},{1,9},{9,17},{17,25},{25,1},{2,10},{10... | collective-permute-start | bytes 516104 | tf_op jit(solution)/shard_map/ppermute | solution.py:161
  7.9 1.0 %copy-start.2 = (f32[19]{0:T(128)S(1)}, f32[19]{0:T(128)}, u32[]{:S(2)}) copy-start(f32[19]{0:T(128)} %constant.35.clone) | copy-start | bytes 232
  7.9 1.0 %copy-start.3 = (f32[19]{0:T(128)S(1)}, f32[19]{0:T(128)}, u32[]{:S(2)}) copy-start(f32[19]{0:T(128)} %constant.34.clone) | copy-start | bytes 232
  7.9 1.0 %copy-start.4 = (f32[19]{0:T(128)S(1)}, f32[19]{0:T(128)}, u32[]{:S(2)}) copy-start(f32[19]{0:T(128)} %constant.33.clone) | copy-start | bytes 232
  7.9 1.0 %copy-start.5 = (f32[19]{0:T(128)S(1)}, f32[19]{0:T(128)}, u32[]{:S(2)}) copy-start(f32[19]{0:T(128)} %constant.32.clone) | copy-start | bytes 232
  11.1 0.7 %copy-start.1 = (f32[19,38,1,1]{1,0,3,2:T(8,128)S(1)}, f32[19,38,1,1]{1,0,3,2:T(8,128)}, u32[]{:S(2)}) copy-start(f32[19,38,1,1]{1,0,3,2:T(8,128)} %constant.8) | copy-start | bytes 8668
  16.4 7.6 %collective-permute-start.3 = (f32[21,20,128]{2,0,1:T(8,128)S(1)}, f32[21,20,128]{2,0,1:T(8,128)S(1)}, u32[]{:S(2)}, u32[]{:S(2)}) collective-permute-start(f32[21,20,128]{2,0,1:T(8,128)S(1)} %get-tuple-element.195), channel_id=1, source_target_pairs={{0,7},{1,0},{2,1},{3,2},{4,3},{5,4},{6,5},{7,6},{8,15},{9,8},{10,9... | collective-permute-start | bytes 645128 | tf_op jit(solution)/shard_map/ppermute | solution.py:161
  18.7 8.1 %collective-permute-start.2 = (f32[21,20,128]{2,0,1:T(8,128)S(1)}, f32[21,20,128]{2,0,1:T(8,128)S(1)}, u32[]{:S(2)}, u32[]{:S(2)}) collective-permute-start(f32[21,20,128]{2,0,1:T(8,128)S(1)} %get-tuple-element.196), channel_id=1, source_target_pairs={{0,1},{1,2},{2,3},{3,4},{4,5},{5,6},{6,7},{7,0},{8,9},{9,10},{10,1... | collective-permute-start | bytes 645128 | tf_op jit(solution)/shard_map/ppermute | solution.py:161
  43.6 8.4 %all-to-all-start = ((f32[4,1,2048]{2,1,0:T(1,128)}), f32[4,1,2048]{2,1,0:T(1,128)S(1)}, u32[]{:S(2)}, u32[]{:S(2)}) async-start(f32[4,1,2048]{2,1,0:T(1,128)} %reshape.334), calls=%async_computation | async-start | bytes 65536 | tf_op jit(solution)/shard_map/all_to_all | solution.py:305

commit v11 on v10

--- a/solution.py
+++ b/solution.py
@@ -186,7 +186,7 @@
     return f - jnp.einsum("pq,q...->p...", table, stacked, precision=lax.Precision.HIGH)
 
 
-def stream_and_render(collided, velocities, extent_x, extent_y, length_x):
+def stream_and_render(collided, velocities, extent_x, extent_y, length_x, groups):
     near_y, band, far_y = collided
     depth_z = band.shape[3]
     edge = near_y.shape[2]
@@ -226,16 +226,16 @@
 
         zero = jnp.zeros((extent_y, depth_z), jnp.float32)
         depth, red, green, blue = lax.fori_loop(0, extent_x, render, (zero, zero, zero, zero), unroll=True)
-        pic_ref[0] = red
-        pic_ref[1] = green
-        pic_ref[2] = blue
-        pic_ref[3] = 1.0 - jnp.exp(-depth)
+        block_len = depth_z // groups
+        for channel, value in enumerate((red, green, blue, 1.0 - jnp.exp(-depth))):
+            for block in range(groups):
+                pic_ref[block, channel] = value[:, block * block_len : (block + 1) * block_len]
 
     return pl.pallas_call(
         kernel,
         out_shape=(
             jax.ShapeDtypeStruct((19, extent_x, extent_y, depth_z), jnp.float32),
-            jax.ShapeDtypeStruct((4, extent_y, depth_z), jnp.float32),
+            jax.ShapeDtypeStruct((groups, 4, extent_y, depth_z // groups), jnp.float32),
         ),
         in_specs=[pl.BlockSpec(memory_space=pltpu.VMEM)] * 3,
         out_specs=(pl.BlockSpec(memory_space=pltpu.VMEM), pl.BlockSpec(memory_space=pltpu.VMEM)),
@@ -297,15 +297,12 @@
     collided = (near_y, band, far_y)
     groups = lax.axis_size("gx")
     length_x = extent_x * groups
-    fresh_major, layered = stream_and_render(collided, velocities, extent_x, extent_y, length_x)
+    fresh_major, blocked = stream_and_render(collided, velocities, extent_x, extent_y, length_x, groups)
     fresh = jnp.transpose(fresh_major, (1, 2, 0, 3))
-    depth_z = layered.shape[2]
-    block_len = depth_z // groups
-    blocked = layered.reshape(4, extent_y, groups, block_len)
-    gathered = lax.all_to_all(blocked, "gx", 2, 2, tiled=True)
-    current = gathered[:, :, 0]
+    gathered = lax.all_to_all(blocked, "gx", 0, 0, tiled=True)
+    current = gathered[0]
     for source in range(1, groups):
-        current = current + (1.0 - current[3:4]) * gathered[:, :, source]
+        current = current + (1.0 - current[3:4]) * gathered[source]
     picture = current
     return (fresh, picture)
 

time: 54.4 us -> 54.4 us (level)
    unnamed x15, local copies, waits for them, and re-layouts: 4.81 us -> 5.71 us
    reshape x2 -> x0, local copies, waits for them, and re-layouts: 0.88 us -> none  [body(): blocked = layered.reshape(4, extent_y, groups, block_len)]
where the time goes in v11:
time: 54.4 us; the launch traced here: 54.1 us
  other arithmetic  19.4 us (36%)
  starting transfers between devices  10 us (18%)
  local copies, waits for them, and re-layouts  9.89 us (18%)
  waiting for transfers between devices  5.34 us (10%)
  Pallas kernels  4.43 us (8%)
  matrix products  3.79 us (7%)
  between operations  1.23 us (2%)
    ppermute x4, starting transfers between devices, shift_ring(): lax.ppermute(x, axis, [(i, (i - step) % count) for i in range(count)])  6.33 us
    sub x5, other arithmetic, collide_major(): stacked = jnp.concatenate([f - balance, guo_term], axis=0)  5.72 us
    unnamed x15, local copies, waits for them, and re-layouts  5.71 us
    pallas_call x1, Pallas kernels, stream_and_render(): pl.pallas_call(kernel, out_shape=(jax.ShapeDtypeStruct((19, extent_x, ext...  4.43 us
    ppermute x4, waiting for transfers between devices, shift_ring(): lax.ppermute(x, axis, [(i, (i - step) % count) for i in range(count)])  3.91 us
    dot_general x5, matrix products, collide_major(): jnp.einsum('pq,q...->p...', table, stacked, precision=lax.Precision.HIGH)  3.79 us
    all_to_all x1, starting transfers between devices, body(): gathered = lax.all_to_all(blocked, 'gx', 0, 0, tiled=True)  3.69 us
    sub x4, other arithmetic, collide_major(): f - jnp.einsum('pq,q...->p...', table, stacked, precision=lax.Precision.H...  2.78 us
  transfers between devices with their start and end apart: 5, of which 4 were waited for; matrix products, arithmetic and copies ran while one was open for 28% of the time, Pallas kernels for 0%

profile of v11, /device:TPU:0, one launch (start us, length us, event | category | flops | bytes accessed | tf_op | source)
XLA Modules:
  0.0 54.1 jit_solution(13891479209564216739)
XLA Ops:
  0.6 2.0 %bitcast_reduce_fusion = f32[16,16,128]{2,1,0:T(8,128)S(1)} fusion(f32[16,16,19,128]{3,1,2,0:T(8,128)} %param.31), kind=kLoop, calls=%fused_computation.830 | loop fusion | flops 589824 | bytes 2621440 | tf_op jit(solution)/shard_map/reduce_sum | solution.py:268
  2.7 0.4 copy-done
  3.1 3.9 %collective-permute-start.1 = (f32[21,16,128]{2,1,0:T(8,128)S(1)}, f32[21,16,128]{2,1,0:T(8,128)S(1)}, u32[]{:S(2)}, u32[]{:S(2)}) collective-permute-start(f32[21,16,128]{2,1,0:T(8,128)S(1)} %pad_maximum_fusion.16), channel_id=1, source_target_pairs={{0,24},{8,0},{16,8},{24,16},{1,25},{9,1},{17,9},{25,17},{2,26},{10... | collective-permute-start | bytes 516104 | tf_op jit(solution)/shard_map/ppermute | solution.py:161
  7.2 0.2 slice_reduce_fusion
  7.4 0.2 fusion.452
  7.6 0.2 fusion.453
  7.9 0.9 %add_multiply_fusion.5 = (f32[14,14,128]{2,1,0:T(8,128)S(1)}, f32[14,14,128]{2,1,0:T(8,128)S(1)}, f32[14,14,128]{2,1,0:T(8,128)S(1)}, f32[14,14,128]{2,1,0:T(8,1...) fusion(f32[14,14,128]{2,1,0:T(8,128)S(1)} %slice_reduce_fusion, ...), kind=kLoop, calls=%fused_computation.316 | loop fusion | flops 2985472 | bytes 6207488 | tf_op jit(solution)/shard_map/mul | solution.py:180
  8.9 2.2 %fusion.5 = (f32[19,14,14,128]{3,2,0,1:T(8,128)S(1)}, f32[19,14,14,128]{3,2,0,1:T(8,128)S(1)}) fusion(f32[19,16,16,128]{3,2,0,1:T(8,128)S(1)} %bitcast.542, f32[14,14,128]{2,1,0:T(8,128)S(1)} %get-tuple-element.30, f32[14,14,128]{2,1,0:T(8,128)S(1)} %get-tuple-element.35, f32[19]{0:T(128)S(1)} %copy-done.3, f32[14,14,128]{2,1,0:T(8,128)S(1)} %get-tuple-element.33, ...), kind=kLoop, calls=%fused_computation.46 | loop fusion | flops 11916800 | bytes 6623536 | tf_op jit(solution)/shard_map/sub | solution.py:185
  11.1 0.4 pad_maximum_fusion
  11.5 0.3 copy-done.1
  11.8 2.2 %fusion = f32[19,14,14,128]{3,0,2,1:T(8,128)S(1)} fusion(f32[19,38,1,1]{1,0,3,2:T(8,128)S(1)} %copy-done.1, f32[38,14,14,128]{3,2,0,1:T(8,128)S(1)} %pad_maximum_fusion), kind=kOutput, calls=%fused_computation.39 | convolution fusion | flops 108681216 | bytes 5722952 | tf_op jit(solution)/shard_map/pq,q...->p.../dot_general | solution.py:186
  14.0 0.7 %copy_subtract_fusion = f32[19,14,14,128]{3,2,0,1:T(8,128)S(1)} fusion(f32[19,14,14,128]{3,0,2,1:T(8,128)S(1)} %fusion, f32[19,16,16,128]{3,2,0,1:T(8,128)S(1)} %bitcast.543), kind=kLoop, calls=%fused_computation.47 | loop fusion | flops 476672 | bytes 5720064 | tf_op jit(solution)/shard_map/sub | solution.py:186
  14.7 0.1 fusion.330
  14.9 0.5 collective-permute-done
  15.5 0.1 fusion.303
  15.6 0.1 fusion.302
  15.8 0.1 fusion.424
  15.9 0.1 fusion.450
  16.0 0.2 pad_maximum_fusion.12
  16.4 2.3 %collective-permute-start.3 = (f32[21,20,128]{2,0,1:T(8,128)S(1)}, f32[21,20,128]{2,0,1:T(8,128)S(1)}, u32[]{:S(2)}, u32[]{:S(2)}) collective-permute-start(f32[21,20,128]{2,0,1:T(8,128)S(1)} %get-tuple-element.195), channel_id=1, source_target_pairs={{0,7},{1,0},{2,1},{3,2},{4,3},{5,4},{6,5},{7,6},{8,15},{9,8},{10,9... | collective-permute-start | bytes 645128 | tf_op jit(solution)/shard_map/ppermute | solution.py:161
  18.9 0.1 add_multiply_fusion.14
  19.0 0.4 fusion.29
  19.4 0.4 fusion.10
  19.9 0.2 add_multiply_fusion.15
  20.1 0.4 fusion.25
  20.5 0.4 fusion.12
  21.0 0.1 copy_subtract_fusion.4
  21.1 0.2 pad_maximum_fusion.2
  21.3 1.9 %copy.547.band_ref = f32[19,18,14,128]{3,2,1,0:T(8,128)} copy(f32[19,18,14,128]{3,2,0,1:T(8,128)S(1)} %pad_maximum_fusion.2) | data formatting | bytes 4902912 | tf_op jit(solution)/shard_map/concatenate | solution.py:294
  23.1 0.1 fusion.451
  23.2 0.8 %collective-permute-done.3 = f32[21,20,128]{2,0,1:T(8,128)S(1)} collective-permute-done((f32[21,20,128]{2,0,1:T(8,128)S(1)}, f32[21,20,128]{2,0,1:T(8,128)S(1)}, u32[]{:S(2)}, u32[]{:S(2)}) %collective-permute-start.3) | collective-permute-done | bytes 215072 | tf_op jit(solution)/shard_map/ppermute | solution.py:161
  24.1 0.1 fusion.117
  24.2 0.1 fusion.118
  24.3 2.6 %collective-permute-done.2 = f32[21,20,128]{2,0,1:T(8,128)S(1)} collective-permute-done((f32[21,20,128]{2,0,1:T(8,128)S(1)}, f32[21,20,128]{2,0,1:T(8,128)S(1)}, u32[]{:S(2)}, u32[]{:S(2)}) %collective-permute-start.2) | collective-permute-done | bytes 215072 | tf_op jit(solution)/shard_map/ppermute | solution.py:161
  26.9 0.1 fusion.128
  27.0 0.1 fusion.129
  27.1 0.1 fusion.444
  27.3 0.1 fusion.443
  27.4 0.1 fusion.446
  27.5 0.1 fusion.445
  27.7 0.2 copy.544
  27.9 0.2 copy.473
  28.1 1.6 %pad_maximum_fusion.1 = (f32[19,18,17,128]{3,2,1,0:T(8,128)S(1)}, f32[19,18,17,128]{3,2,1,0:T(8,128)S(1)}) fusion(f32[19,18,1,128]{3,2,1,0:T(1,128)S(1)} %copy.544, f32[19,1,16,128]{3,2,1,0:T(8,128)S(1)} %get-tuple-element.108, f32[19,1,16,128]{3,2,1,0:T(8,128)S(1)} %get-tuple-element.102, f32[19,18,1,128]{3,2,1,0:T(1,128)S(1)} %copy.473, ...), kind=kLoop, calls=%fused_computation.38 | loop fusion | flops 4465152 | bytes 9105408 | tf_op jit(solution)/shard_map/concatenate | solution.py:283
  29.7 0.2 slice_reduce_fusion.1
  29.9 0.1 slice_reduce_fusion.2
  29.9 0.8 %add_multiply_fusion.6 = (f32[18,2,128]{2,1,0:T(2,128)S(1)}, f32[18,2,128]{2,1,0:T(2,128)S(1)}, f32[18,2,128]{2,1,0:T(2,128)S(1)}, f32[18,2,128]{2,1,0:T(2,128)S...) fusion(f32[18,2,128]{2,1,0:T(2,128)S(1)} %slice_reduce_fusion.1, ...), kind=kLoop, calls=%fused_computation.559 | loop fusion | flops 824832 | bytes 3421328 | tf_op jit(solution)/shard_map/mul | solution.py:180
  30.8 1.4 %fusion.21 = (f32[19,18,2,128]{3,2,1,0:T(2,128)S(1)}, f32[19,18,2,128]{3,2,1,0:T(2,128)S(1)}) fusion(f32[19,18,17,128]{3,2,1,0:T(8,128)S(1)} %get-tuple-element.53, f32[18,2,128]{2,1,0:T(2,128)S(1)} %get-tuple-element.14, f32[18,2,128]{2,1,0:T(2,128)S(1)} %slice_reduce_fusion.1, f32[19]{0:T(128)S(1)} %copy-done.2, f32[18,2,128]{2,1,0:T(2,128)S(1)} %get-tuple-element.19, ...), kind=kLoop, calls=%fused_computation.144 | loop fusion | flops 2188800 | bytes 1216816 | tf_op jit(solution)/shard_map/sub | solution.py:185
  32.2 0.3 pad_maximum_fusion.4
  32.5 0.3 fusion.6
  32.9 1.0 %copy_subtract_fusion.1.far_ref = f32[19,18,2,128]{3,2,1,0:T(2,128)} fusion(f32[19,18,2,128]{3,0,2,1:T(8,128)S(1)} %fusion.6, f32[19,18,17,128]{3,2,1,0:T(8,128)S(1)} %get-tuple-element.53), kind=kLoop, calls=%fused_computation.145 | loop fusion | flops 87552 | bytes 1050624 | tf_op jit(solution)/shard_map/sub | solution.py:186
  33.9 0.7 %add_multiply_fusion.10 = (f32[18,2,128]{2,1,0:T(2,128)S(1)}, f32[18,2,128]{2,1,0:T(2,128)S(1)}, f32[18,2,128]{2,1,0:T(2,128)S(1)}, f32[18,2,128]{2,1,0:T(2,128)...) fusion(f32[18,2,128]{2,1,0:T(2,128)S(1)} %slice_reduce_fusion.2, ...), kind=kLoop, calls=%fused_computation.564 | loop fusion | flops 843264 | bytes 3568496 | tf_op jit(solution)/shard_map/mul | solution.py:180
  34.6 1.3 %fusion.17 = (f32[19,18,2,128]{3,2,1,0:T(2,128)S(1)}, f32[19,18,2,128]{3,2,1,0:T(2,128)S(1)}) fusion(f32[19,18,17,128]{3,2,1,0:T(8,128)S(1)} %get-tuple-element.54, f32[18,2,128]{2,1,0:T(2,128)S(1)} %get-tuple-element.46, f32[18,2,128]{2,1,0:T(2,128)S(1)} %slice_reduce_fusion.2, f32[19]{0:T(128)S(1)} %copy-done.2, f32[18,2,128]{2,1,0:T(2,128)S(1)} %get-tuple-element.51, ...), kind=kLoop, calls=%fused_computation.140 | loop fusion | flops 2188800 | bytes 1216816 | tf_op jit(solution)/shard_map/sub | solution.py:185
  35.9 0.3 pad_maximum_fusion.3
  36.2 0.3 fusion.8
  36.6 1.0 %copy_subtract_fusion.2.near_ref = f32[19,18,2,128]{3,2,1,0:T(2,128)} fusion(f32[19,18,2,128]{3,0,2,1:T(8,128)S(1)} %fusion.8, f32[19,18,17,128]{3,2,1,0:T(8,128)S(1)} %get-tuple-element.54), kind=kLoop, calls=%fused_computation.146 | loop fusion | flops 87552 | bytes 1050624 | tf_op jit(solution)/shard_map/sub | solution.py:186
  37.6 4.4 %shard_map.302 = (f32[19,16,16,128]{3,2,1,0:T(8,128)}, f32[4,4,16,32]{3,2,1,0:T(8,128)}) custom-call(f32[19,18,2,128]{3,2,1,0:T(2,128)} %copy_subtract_fusion.2.near_ref, f32[19,18,14,128]{3,2,1,0:T(8,128)} %copy.547.band_ref, f32[19,18,2,128]{3,2,1,0:T(2,128)} %copy_subtract_fusion.1.far_ref), custom_call_target="tpu_custom_call" | custom-call | tf_op jit(solution)/shard_map/pallas_call | solution.py:234
  42.0 1.6 %reshape.330 = f32[4,1,2048]{2,1,0:T(1,128)} reshape(f32[4,4,16,32]{3,2,1,0:T(8,128)} %get-tuple-element.5) | data formatting | bytes 65536
  43.6 3.7 %all-to-all-start = ((f32[4,1,2048]{2,1,0:T(1,128)}), f32[4,1,2048]{2,1,0:T(1,128)S(1)}, u32[]{:S(2)}, u32[]{:S(2)}) async-start(f32[4,1,2048]{2,1,0:T(1,128)} %reshape.330), calls=%async_computation | async-start | bytes 65536 | tf_op jit(solution)/shard_map/all_to_all | solution.py:302
  47.3 3.3 %copy.548 = f32[16,16,19,128]{3,1,2,0:T(8,128)} copy(f32[16,16,19,128]{3,1,0,2:T(8,128)} %bitcast.549) | data formatting | bytes 4980736
  50.7 1.4 %all-to-all-done = f32[4,1,2048]{2,1,0:T(1,128)S(1)} async-done(((f32[4,1,2048]{2,1,0:T(1,128)}), f32[4,1,2048]{2,1,0:T(1,128)S(1)}, u32[]{:S(2)}, u32[]{:S(2)}) %all-to-all-start) | async-done | bytes 32800 | tf_op jit(solution)/shard_map/all_to_all | solution.py:302
  52.1 0.5 broadcast.707
  52.6 0.7 %reduce = f32[4,2048]{1,0:T(4,128)S(1)} reduce(f32[4,1,2048]{2,1,0:T(1,128)S(1)} %all-to-all-done, f32[]{:T(128)} %broadcast.707), dimensions={1}, to_apply=%all_to_all.3.reduce_sub_computation | reduce | bytes 65540 | tf_op jit(solution)/shard_map/all_to_all | solution.py:302
  53.3 0.1 reshape.331
  53.5 0.6 %fusion.103 = f32[4,16,32]{2,1,0:T(8,128)} fusion(f32[4,16,32]{2,1,0:T(8,128)S(1)} %fusion.105, f32[4,4,16,32]{3,2,1,0:T(8,128)S(1)} %reshape.331, f32[16,32]{1,0:T(8,128)S(1)} %fusion.412), kind=kLoop, calls=%fused_computation.333 | loop fusion | flops 4096 | bytes 26624 | tf_op jit(solution)/shard_map/add | solution.py:305
  (53 shorter events, 1.0 us)
Async XLA Ops:
  0.6 2.5 %copy-start = (f32[16,16,19,128]{3,1,2,0:T(8,128)S(1)}, f32[16,16,19,128]{3,1,2,0:T(8,128)}, u32[]{:S(2)}) copy-start(f32[16,16,19,128]{3,1,2,0:T(8,128)} %param.31) | copy-start | bytes 7471108
  3.1 11.6 %collective-permute-start.1 = (f32[21,16,128]{2,1,0:T(8,128)S(1)}, f32[21,16,128]{2,1,0:T(8,128)S(1)}, u32[]{:S(2)}, u32[]{:S(2)}) collective-permute-start(f32[21,16,128]{2,1,0:T(8,128)S(1)} %pad_maximum_fusion.16), channel_id=1, source_target_pairs={{0,24},{8,0},{16,8},{24,16},{1,25},{9,1},{17,9},{25,17},{2,26},{10... | collective-permute-start | bytes 516104 | tf_op jit(solution)/shard_map/ppermute | solution.py:161
  7.1 8.3 %collective-permute-start = (f32[21,16,128]{2,1,0:T(8,128)S(1)}, f32[21,16,128]{2,1,0:T(8,128)S(1)}, u32[]{:S(2)}, u32[]{:S(2)}) collective-permute-start(f32[21,16,128]{2,1,0:T(8,128)S(1)} %pad_maximum_fusion.15), channel_id=1, source_target_pairs={{0,8},{8,16},{16,24},{24,0},{1,9},{9,17},{17,25},{25,1},{2,10},{10... | collective-permute-start | bytes 516104 | tf_op jit(solution)/shard_map/ppermute | solution.py:161
  7.9 1.0 %copy-start.2 = (f32[19]{0:T(128)S(1)}, f32[19]{0:T(128)}, u32[]{:S(2)}) copy-start(f32[19]{0:T(128)} %constant.35.clone) | copy-start | bytes 232
  7.9 1.0 %copy-start.3 = (f32[19]{0:T(128)S(1)}, f32[19]{0:T(128)}, u32[]{:S(2)}) copy-start(f32[19]{0:T(128)} %constant.34.clone) | copy-start | bytes 232
  7.9 1.0 %copy-start.4 = (f32[19]{0:T(128)S(1)}, f32[19]{0:T(128)}, u32[]{:S(2)}) copy-start(f32[19]{0:T(128)} %constant.33.clone) | copy-start | bytes 232
  7.9 1.0 %copy-start.5 = (f32[19]{0:T(128)S(1)}, f32[19]{0:T(128)}, u32[]{:S(2)}) copy-start(f32[19]{0:T(128)} %constant.32.clone) | copy-start | bytes 232
  11.1 0.7 %copy-start.1 = (f32[19,38,1,1]{1,0,3,2:T(8,128)S(1)}, f32[19,38,1,1]{1,0,3,2:T(8,128)}, u32[]{:S(2)}) copy-start(f32[19,38,1,1]{1,0,3,2:T(8,128)} %constant.8) | copy-start | bytes 8668
  16.4 7.6 %collective-permute-start.3 = (f32[21,20,128]{2,0,1:T(8,128)S(1)}, f32[21,20,128]{2,0,1:T(8,128)S(1)}, u32[]{:S(2)}, u32[]{:S(2)}) collective-permute-start(f32[21,20,128]{2,0,1:T(8,128)S(1)} %get-tuple-element.195), channel_id=1, source_target_pairs={{0,7},{1,0},{2,1},{3,2},{4,3},{5,4},{6,5},{7,6},{8,15},{9,8},{10,9... | collective-permute-start | bytes 645128 | tf_op jit(solution)/shard_map/ppermute | solution.py:161
  18.7 8.1 %collective-permute-start.2 = (f32[21,20,128]{2,0,1:T(8,128)S(1)}, f32[21,20,128]{2,0,1:T(8,128)S(1)}, u32[]{:S(2)}, u32[]{:S(2)}) collective-permute-start(f32[21,20,128]{2,0,1:T(8,128)S(1)} %get-tuple-element.196), channel_id=1, source_target_pairs={{0,1},{1,2},{2,3},{3,4},{4,5},{5,6},{6,7},{7,0},{8,9},{9,10},{10,1... | collective-permute-start | bytes 645128 | tf_op jit(solution)/shard_map/ppermute | solution.py:161
  43.6 8.4 %all-to-all-start = ((f32[4,1,2048]{2,1,0:T(1,128)}), f32[4,1,2048]{2,1,0:T(1,128)S(1)}, u32[]{:S(2)}, u32[]{:S(2)}) async-start(f32[4,1,2048]{2,1,0:T(1,128)} %reshape.330), calls=%async_computation | async-start | bytes 65536 | tf_op jit(solution)/shard_map/all_to_all | solution.py:302

commit v12 on v6

--- a/solution.py
+++ b/solution.py
@@ -190,27 +190,45 @@
     near_y, band, far_y = collided
     depth_z = band.shape[3]
     edge = near_y.shape[2]
+    inner_rows = extent_y - 2 * edge
     steps = [[int(v) for v in velocities[q]] for q in range(19)]
-
-    def kernel(near_ref, band_ref, far_ref, o_ref, pic_ref, c_ref):
+    fresh_shape = jax.ShapeDtypeStruct((19, extent_x, extent_y, depth_z), jnp.float32)
+
+    def shifted(v, cz):
+        return pltpu.roll(v, shift=cz % depth_z, axis=1) if cz != 0 else v
+
+    def band_kernel(band_ref, o_ref):
+        for q in range(19):
+            cx, cy, cz = steps[q]
+            for x in range(extent_x):
+                v = band_ref[q, x + 1 - cx, pl.ds(1 - cy, inner_rows), :]
+                o_ref[q, x, pl.ds(edge, inner_rows), :] = shifted(v, cz)
+
+    partial = pl.pallas_call(
+        band_kernel,
+        out_shape=fresh_shape,
+        in_specs=[pl.BlockSpec(memory_space=pltpu.VMEM)],
+        out_specs=pl.BlockSpec(memory_space=pltpu.VMEM),
+        cost_estimate=pl.CostEstimate(flops=0, transcendentals=0, bytes_accessed=2 * band.size * 4),
+    )(band)
+
+    def edge_kernel(near_ref, band_ref, far_ref, fresh_ref, o_ref, pic_ref, low_ref, high_ref):
         def gather(q, carry):
-            c_ref[q, :, 0:edge] = near_ref[q]
-            c_ref[q, :, edge : edge + extent_y - 2] = band_ref[q]
-            c_ref[q, :, edge + extent_y - 2 :] = far_ref[q]
+            o_ref[q] = fresh_ref[q]
+            low_ref[q, :, 0:edge] = near_ref[q]
+            low_ref[q, :, edge : 2 * edge] = band_ref[q, :, 0:edge]
+            high_ref[q, :, 0:edge] = band_ref[q, :, inner_rows : inner_rows + edge]
+            high_ref[q, :, edge : 2 * edge] = far_ref[q]
             return carry
 
         lax.fori_loop(0, 19, gather, 0)
         for q in range(19):
             cx, cy, cz = steps[q]
-
-            def move(x, carry):
-                v = c_ref[q, x + 1 - cx, pl.ds(1 - cy, extent_y), :]
-                if cz != 0:
-                    v = pltpu.roll(v, shift=cz % depth_z, axis=1)
-                o_ref[q, x] = v
-                return carry
-
-            lax.fori_loop(0, extent_x, move, 0, unroll=True)
+            for x in range(extent_x):
+                v = low_ref[q, x + 1 - cx, pl.ds(1 - cy, edge), :]
+                o_ref[q, x, pl.ds(0, edge), :] = shifted(v, cz)
+                v = high_ref[q, x + 1 - cx, pl.ds(1 - cy, edge), :]
+                o_ref[q, x, pl.ds(extent_y - edge, edge), :] = shifted(v, cz)
 
         def render(x, carry):
             depth, red, green, blue = carry
@@ -232,15 +250,16 @@
         pic_ref[3] = 1.0 - jnp.exp(-depth)
 
     return pl.pallas_call(
-        kernel,
-        out_shape=(
-            jax.ShapeDtypeStruct((19, extent_x, extent_y, depth_z), jnp.float32),
-            jax.ShapeDtypeStruct((4, extent_y, depth_z), jnp.float32),
-        ),
-        in_specs=[pl.BlockSpec(memory_space=pltpu.VMEM)] * 3,
+        edge_kernel,
+        out_shape=(fresh_shape, jax.ShapeDtypeStruct((4, extent_y, depth_z), jnp.float32)),
+        in_specs=[pl.BlockSpec(memory_space=pltpu.VMEM)] * 4,
         out_specs=(pl.BlockSpec(memory_space=pltpu.VMEM), pl.BlockSpec(memory_space=pltpu.VMEM)),
-        scratch_shapes=[pltpu.VMEM((19, extent_x + 2, extent_y + 2, depth_z), jnp.float32)],
-    )(near_y, band, far_y)
+        scratch_shapes=[
+            pltpu.VMEM((19, extent_x + 2, 2 * edge, depth_z), jnp.float32),
+            pltpu.VMEM((19, extent_x + 2, 2 * edge, depth_z), jnp.float32),
+        ],
+        input_output_aliases={3: 0},
+    )(near_y, band, far_y, partial)
 
 
 def collide_region(cells, pot, tables):

time: 54.1 us -> 65.1 us (1.20)
  Pallas kernels: 4.34 us -> 9.02 us
  local copies, waits for them, and re-layouts: 9.3 us -> 13.8 us
  other arithmetic: 20.1 us -> 22.8 us
  waiting for transfers between devices: 4.6 us -> 3.21 us
    pallas_call x1 -> x2, Pallas kernels: 4.34 us -> 9.02 us  [the longest x1 5.37 us: stream_and_render(): pl.pallas_call(edge_kernel, out_shape=(fresh_shape, jax.ShapeDtypeStruct(...]
    ppermute x4, waiting for transfers between devices: 2.28 us -> 0.01 us  [shift_ring(): lax.ppermute(x, axis, [(i, (i - step) % count) for i in range(count)])]
    another operation x1, local copies, waits for them, and re-layouts: 0.02 us -> 0.98 us  [body(): from_below[20][:, None]]
    another operation x1, local copies, waits for them, and re-layouts: 0.02 us -> 0.98 us  [body(): from_above[20][:, None]]
    broadcast_in_dim x2, local copies, waits for them, and re-layouts: 0.2 us -> 1.13 us  [body(): from_below[:19, 1:-1, None]]
    broadcast_in_dim x2, local copies, waits for them, and re-layouts: 0.2 us -> 1.13 us  [body(): from_above[:19, 1:-1, None]]
    ppermute x2, waiting for transfers between devices: 2.32 us -> 3.2 us  [from_partner(): lax.ppermute(x, axis, [(i, i ^ 1 << distance) for i in range(lax.axis_siz...]
    concatenate x1, other arithmetic: 0.08 us -> 0.77 us  [y_message(): jnp.concatenate([pops, px[None, :, row_near], px[None, :, row_far]], axis=0)]
  transfers between devices with their start and end apart: 6 -> 6, of which waited for: 2 -> 1; matrix products, arithmetic and copies ran while one was open for 31% -> 29% of each run, Pallas kernels for 0% -> 6%
where the time goes in v12:
time: 65.1 us; the launch traced here: 64.6 us
  other arithmetic  22.8 us (35%)
  local copies, waits for them, and re-layouts  13.8 us (21%)
  starting transfers between devices  10.6 us (16%)
  Pallas kernels  9.02 us (14%)
  matrix products  3.79 us (6%)
  waiting for transfers between devices  3.21 us (5%)
  between operations  1.43 us (2%)
    ppermute x4, starting transfers between devices, shift_ring(): lax.ppermute(x, axis, [(i, (i - step) % count) for i in range(count)])  7.44 us
    sub x5, other arithmetic, collide_major(): stacked = jnp.concatenate([f - balance, guo_term], axis=0)  5.66 us
    pallas_call x1, Pallas kernels, stream_and_render(): pl.pallas_call(edge_kernel, out_shape=(fresh_shape, jax.ShapeDtypeStruct(...  5.37 us
    unnamed x41, local copies, waits for them, and re-layouts  4.65 us
    sub x4, other arithmetic, collide_major(): f - jnp.einsum('pq,q...->p...', table, stacked, precision=lax.Precision.H...  4.13 us
    dot_general x5, matrix products, collide_major(): jnp.einsum('pq,q...->p...', table, stacked, precision=lax.Precision.HIGH)  3.79 us
    pallas_call x1, Pallas kernels, stream_and_render(): pl.pallas_call(band_kernel, out_shape=fresh_shape, in_specs=[pl.BlockSpec...  3.65 us
    ppermute x2, waiting for transfers between devices, from_partner(): lax.ppermute(x, axis, [(i, i ^ 1 << distance) for i in range(lax.axis_siz...  3.2 us
  transfers between devices with their start and end apart: 6, of which 1 were waited for; matrix products, arithmetic and copies ran while one was open for 29% of the time, Pallas kernels for 6%

profile of v12, /device:TPU:0, one launch (start us, length us, event | category | flops | bytes accessed | tf_op | source)
XLA Modules:
  0.0 64.6 jit_solution(13756004921981898317)
XLA Ops:
  0.6 2.0 %bitcast_reduce_fusion = f32[16,16,128]{2,1,0:T(8,128)S(1)} fusion(f32[16,16,19,128]{3,1,2,0:T(8,128)} %param.31), kind=kLoop, calls=%fused_computation.832 | loop fusion | flops 589824 | bytes 2621440 | tf_op jit(solution)/shard_map/reduce_sum | solution.py:287
  2.7 0.4 copy-done
  3.1 0.7 %pad_maximum_fusion.15 = f32[21,16,128]{2,1,0:T(8,128)} fusion(f32[1,16,128]{2,1,0:T(8,128)S(1)} %get-tuple-element.182, f32[1,16,128]{2,1,0:T(8,128)S(1)} %get-tuple-element.181, f32[19,16,128]{2,1,0:T(8,128)S(1)} %get-tuple-element.69), kind=kLoop, calls=%fused_computation.182 | loop fusion | flops 86016 | bytes 344064 | tf_op jit(solution)/shard_map/concatenate | solution.py:288
  3.8 2.9 %collective-permute-start = (f32[21,16,128]{2,1,0:T(8,128)}, f32[21,16,128]{2,1,0:T(8,128)S(1)}, u32[]{:S(2)}, u32[]{:S(2)}) collective-permute-start(f32[21,16,128]{2,1,0:T(8,128)} %pad_maximum_fusion.15), channel_id=1, source_target_pairs={{0,8},{8,16},{16,24},{24,0},{1,9},{9,17},{17,25},{25,1},{2,10},{10... | collective-permute-start | bytes 516104 | tf_op jit(solution)/shard_map/ppermute | solution.py:161
  6.7 0.7 %pad_maximum_fusion.16 = f32[21,16,128]{2,1,0:T(8,128)} fusion(f32[2,16,128]{2,1,0:T(8,128)S(1)} %slice.1486, f32[19,16,128]{2,1,0:T(8,128)S(1)} %get-tuple-element.70), kind=kLoop, calls=%fused_computation.183 | loop fusion | flops 43008 | bytes 344064 | tf_op jit(solution)/shard_map/concatenate | solution.py:289
  7.4 1.0 %collective-permute-start.1 = (f32[21,16,128]{2,1,0:T(8,128)}, f32[21,16,128]{2,1,0:T(8,128)S(1)}, u32[]{:S(2)}, u32[]{:S(2)}) collective-permute-start(f32[21,16,128]{2,1,0:T(8,128)} %pad_maximum_fusion.16), channel_id=1, source_target_pairs={{0,24},{8,0},{16,8},{24,16},{1,25},{9,1},{17,9},{25,17},{2,26},{10... | collective-permute-start | bytes 516104 | tf_op jit(solution)/shard_map/ppermute | solution.py:161
  8.4 0.2 fusion.452
  8.6 0.2 fusion.453
  8.8 0.2 slice_reduce_fusion
  9.1 0.9 %add_multiply_fusion.5 = (f32[14,14,128]{2,1,0:T(8,128)S(1)}, f32[14,14,128]{2,1,0:T(8,128)S(1)}, f32[14,14,128]{2,1,0:T(8,128)S(1)}, f32[14,14,128]{2,1,0:T(8,1...) fusion(f32[14,14,128]{2,1,0:T(8,128)S(1)} %slice_reduce_fusion, ...), kind=kLoop, calls=%fused_computation.316 | loop fusion | flops 2985472 | bytes 6207488 | tf_op jit(solution)/shard_map/mul | solution.py:180
  10.1 2.1 %fusion.5 = (f32[19,14,14,128]{3,2,0,1:T(8,128)S(1)}, f32[19,14,14,128]{3,2,0,1:T(8,128)S(1)}) fusion(f32[19,16,16,128]{3,2,0,1:T(8,128)S(1)} %bitcast.544, f32[14,14,128]{2,1,0:T(8,128)S(1)} %get-tuple-element.30, f32[14,14,128]{2,1,0:T(8,128)S(1)} %get-tuple-element.35, f32[19]{0:T(128)S(1)} %copy-done.17, f32[14,14,128]{2,1,0:T(8,128)S(1)} %get-tuple-element.33, ...), kind=kLoop, calls=%fused_computation.46 | loop fusion | flops 11916800 | bytes 6623536 | tf_op jit(solution)/shard_map/sub | solution.py:185
  12.2 0.4 pad_maximum_fusion
  12.7 0.3 copy-done.2
  12.9 2.2 %fusion = f32[19,14,14,128]{3,0,2,1:T(8,128)S(1)} fusion(f32[19,38,1,1]{1,0,3,2:T(8,128)S(1)} %copy-done.2, f32[38,14,14,128]{3,2,0,1:T(8,128)S(1)} %pad_maximum_fusion), kind=kOutput, calls=%fused_computation.39 | convolution fusion | flops 108681216 | bytes 5722952 | tf_op jit(solution)/shard_map/pq,q...->p.../dot_general | solution.py:186
  15.2 2.0 %copy_subtract_fusion = f32[19,14,14,128]{3,2,0,1:T(8,128)} fusion(f32[19,14,14,128]{3,0,2,1:T(8,128)S(1)} %fusion, f32[19,16,16,128]{3,2,0,1:T(8,128)S(1)} %bitcast.545), kind=kLoop, calls=%fused_computation.47 | loop fusion | flops 476672 | bytes 5720064 | tf_op jit(solution)/shard_map/sub | solution.py:186
  17.2 0.6 fusion.143
  18.4 0.2 pad_maximum_fusion.12
  18.8 0.8 %fusion.35 = (f32[21,20,128]{2,0,1:T(8,128)S(1)}, f32[21,20,128]{2,0,1:T(8,128)}) fusion(f32[19,1,128]{2,0,1:T(8,128)S(1)} %broadcast_in_dim.6, f32[1,20,128]{2,0,1:T(1,128)S(1)} %get-tuple-element.114, f32[1,20,128]{2,0,1:T(1,128)S(1)} %get-tuple-element.113, f32[19,18,128]{2,0,1:T(8,128)S(1)} %get-tuple-element.202, ...), kind=kLoop, calls=%fused_computation.170 | loop fusion | flops 430080 | bytes 830976 | tf_op jit(solution)/shard_map/concatenate | solution.py:298
  19.5 3.5 %collective-permute-start.3 = (f32[21,20,128]{2,0,1:T(8,128)S(1)}, f32[21,20,128]{2,0,1:T(8,128)}, u32[]{:S(2)}, u32[]{:S(2)}) collective-permute-start(f32[21,20,128]{2,0,1:T(8,128)S(1)} %get-tuple-element.197), channel_id=1, source_target_pairs={{0,7},{1,0},{2,1},{3,2},{4,3},{5,4},{6,5},{7,6},{8,15},{9,8},{10,9... | collective-permute-start | bytes 645128 | tf_op jit(solution)/shard_map/ppermute | solution.py:161
  23.1 0.7 %fusion.449 = (f32[18,2,1]{2,1,0:T(2,128)}, f32[18,2,1]{2,1,0:T(2,128)}, f32[18,2,1]{2,1,0:T(2,128)}, f32[18,2,1]{2,1,0:T(2,128)}) fusion(f32[19,16,128]{2,1,0:T(8,128)S(1)} %pad_maximum_fusion.17), kind=kLoop, calls=%fused_computation.842 | loop fusion | bytes 1152 | tf_op jit(solution)/shard_map/jit(_roll_static)/slice | solution.py:273
  24.0 0.1 add_multiply_fusion.14
  24.2 0.4 fusion.29
  24.6 0.4 fusion.10
  25.0 0.2 add_multiply_fusion.15
  25.2 0.4 fusion.25
  25.7 0.4 fusion.12
  26.2 0.6 copy-done.1
  26.8 0.2 pad_maximum_fusion.2
  27.1 1.9 %copy.558.band_ref = f32[19,18,14,128]{3,2,1,0:T(8,128)} copy(f32[19,18,14,128]{3,2,0,1:T(8,128)S(1)} %pad_maximum_fusion.2) | data formatting | bytes 4902912 | tf_op jit(solution)/shard_map/concatenate | solution.py:313
  28.9 3.6 %shard_map.302.fresh_ref = f32[19,16,16,128]{3,2,1,0:T(8,128)} custom-call(f32[19,18,14,128]{3,2,1,0:T(8,128)} %copy.558.band_ref), custom_call_target="tpu_custom_call" | custom-call | bytes 4902912 | tf_op jit(solution)/shard_map/pallas_call | solution.py:207
  32.7 1.0 %slice_bitcast_fusion.11 = (f32[20,1,128]{2,1,0:T(1,128)S(1)}, f32[20,1,128]{2,1,0:T(1,128)S(1)}) fusion(f32[21,20,128]{2,0,1:T(8,128)} %collective-permute-done.2), kind=kLoop, calls=%fused_computation.826 | loop fusion | bytes 40960 | tf_op jit(solution)/shard_map/broadcast_in_dim;squeeze | solution.py:306
  33.7 1.0 %slice_bitcast_fusion.9 = (f32[20,1,128]{2,1,0:T(1,128)S(1)}, f32[20,1,128]{2,1,0:T(1,128)S(1)}) fusion(f32[21,20,128]{2,0,1:T(8,128)} %collective-permute-done.3), kind=kLoop, calls=%fused_computation.819 | loop fusion | bytes 40960 | tf_op jit(solution)/shard_map/broadcast_in_dim;squeeze | solution.py:306
  34.7 0.1 fusion.442
  34.8 0.1 fusion.443
  35.0 0.1 fusion.118
  35.1 0.1 fusion.117
  35.2 0.1 fusion.444
  35.3 0.1 fusion.445
  35.4 0.1 fusion.129
  35.6 0.1 fusion.128
  35.7 1.0 %slice_bitcast_fusion.1 = f32[19,18,1,128]{3,0,1,2:T(8,128)S(1)} fusion(f32[21,20,128]{2,0,1:T(8,128)} %collective-permute-done.2), kind=kLoop, calls=%fused_computation.174 | loop fusion | bytes 350208 | tf_op jit(solution)/shard_map/broadcast_in_dim | solution.py:303
  36.6 0.2 copy.483
  36.8 1.0 %slice_bitcast_fusion = f32[19,18,1,128]{3,0,2,1:T(8,128)S(1)} fusion(f32[21,20,128]{2,0,1:T(8,128)} %collective-permute-done.3), kind=kLoop, calls=%fused_computation.173 | loop fusion | bytes 350208 | tf_op jit(solution)/shard_map/broadcast_in_dim | solution.py:303
  37.8 0.2 copy.554
  38.0 1.6 %pad_maximum_fusion.1 = (f32[19,18,17,128]{3,2,1,0:T(8,128)S(1)}, f32[19,18,17,128]{3,2,1,0:T(8,128)S(1)}) fusion(f32[19,18,1,128]{3,2,1,0:T(1,128)S(1)} %copy.554, f32[19,1,16,128]{3,2,1,0:T(8,128)S(1)} %get-tuple-element.108, f32[19,1,16,128]{3,2,1,0:T(8,128)S(1)} %get-tuple-element.102, f32[19,18,1,128]{3,2,1,0:T(1,128)S(1)} %copy.483, ...), kind=kLoop, calls=%fused_computation.38 | loop fusion | flops 4465152 | bytes 9105408 | tf_op jit(solution)/shard_map/concatenate | solution.py:302
  39.7 0.2 slice_reduce_fusion.1
  39.9 0.8 %add_multiply_fusion.6 = (f32[18,2,128]{2,1,0:T(2,128)S(1)}, f32[18,2,128]{2,1,0:T(2,128)S(1)}, f32[18,2,128]{2,1,0:T(2,128)S(1)}, f32[18,2,128]{2,1,0:T(2,128)S...) fusion(f32[18,2,128]{2,1,0:T(2,128)S(1)} %slice_reduce_fusion.1, ...), kind=kLoop, calls=%fused_computation.563 | loop fusion | flops 824832 | bytes 3421328 | tf_op jit(solution)/shard_map/mul | solution.py:180
  40.8 1.4 %fusion.21 = (f32[19,18,2,128]{3,2,1,0:T(2,128)S(1)}, f32[19,18,2,128]{3,2,1,0:T(2,128)S(1)}) fusion(f32[19,18,17,128]{3,2,1,0:T(8,128)S(1)} %get-tuple-element.53, f32[18,2,128]{2,1,0:T(2,128)S(1)} %get-tuple-element.14, f32[18,2,128]{2,1,0:T(2,128)S(1)} %slice_reduce_fusion.1, f32[19]{0:T(128)S(1)} %copy-done.10, f32[18,2,128]{2,1,0:T(2,128)S(1)} %get-tuple-element.19, ...), kind=kLoop, calls=%fused_computation.144 | loop fusion | flops 2188800 | bytes 1216816 | tf_op jit(solution)/shard_map/sub | solution.py:185
  42.3 0.3 pad_maximum_fusion.4
  42.6 0.3 fusion.6
  42.9 1.0 %copy_subtract_fusion.1.far_ref = f32[19,18,2,128]{3,2,1,0:T(2,128)} fusion(f32[19,18,2,128]{3,0,2,1:T(8,128)S(1)} %fusion.6, f32[19,18,17,128]{3,2,1,0:T(8,128)S(1)} %get-tuple-element.53), kind=kLoop, calls=%fused_computation.145 | loop fusion | flops 87552 | bytes 1050624 | tf_op jit(solution)/shard_map/sub | solution.py:186
  44.1 0.7 %add_multiply_fusion.10 = (f32[18,2,128]{2,1,0:T(2,128)S(1)}, f32[18,2,128]{2,1,0:T(2,128)S(1)}, f32[18,2,128]{2,1,0:T(2,128)S(1)}, f32[18,2,128]{2,1,0:T(2,128)...) fusion(f32[18,2,128]{2,1,0:T(2,128)S(1)} %slice_reduce_fusion.2, ...), kind=kLoop, calls=%fused_computation.568 | loop fusion | flops 843264 | bytes 3568496 | tf_op jit(solution)/shard_map/mul | solution.py:180
  44.8 1.3 %fusion.17 = (f32[19,18,2,128]{3,2,1,0:T(2,128)S(1)}, f32[19,18,2,128]{3,2,1,0:T(2,128)S(1)}) fusion(f32[19,18,17,128]{3,2,1,0:T(8,128)S(1)} %get-tuple-element.54, f32[18,2,128]{2,1,0:T(2,128)S(1)} %get-tuple-element.46, f32[18,2,128]{2,1,0:T(2,128)S(1)} %slice_reduce_fusion.2, f32[19]{0:T(128)S(1)} %copy-done.10, f32[18,2,128]{2,1,0:T(2,128)S(1)} %get-tuple-element.51, ...), kind=kLoop, calls=%fused_computation.140 | loop fusion | flops 2188800 | bytes 1216816 | tf_op jit(solution)/shard_map/sub | solution.py:185
  46.1 0.3 pad_maximum_fusion.3
  46.4 0.3 fusion.8
  46.8 1.0 %copy_subtract_fusion.2.near_ref = f32[19,18,2,128]{3,2,1,0:T(2,128)} fusion(f32[19,18,2,128]{3,0,2,1:T(8,128)S(1)} %fusion.8, f32[19,18,17,128]{3,2,1,0:T(8,128)S(1)} %get-tuple-element.54), kind=kLoop, calls=%fused_computation.146 | loop fusion | flops 87552 | bytes 1050624 | tf_op jit(solution)/shard_map/sub | solution.py:186
  47.8 5.4 %shard_map.303 = (f32[19,16,16,128]{3,2,1,0:T(8,128)}, f32[4,16,128]{2,1,0:T(8,128)}) custom-call(f32[19,18,2,128]{3,2,1,0:T(2,128)} %copy_subtract_fusion.2.near_ref, f32[19,18,14,128]{3,2,1,0:T(8,128)} %copy.558.band_ref, f32[19,18,2,128]{3,2,1,0:T(2,128)} %copy_subtract_fusion.1.far_ref, ...), custom_call_target="tpu_custom_call", output_to_operand_aliasing={{0}: (3, {})} | custom-call | tf_op jit(solution)/shard_map/pallas_call | solution.py:252
  53.2 0.9 %reshape_reshape.3 = f32[4,16,2,2,32]{4,3,2,1,0:T(2,128)S(1)} reshape(f32[4,16,128]{2,1,0:T(8,128)} %get-tuple-element.5) | data formatting | bytes 65536 | tf_op jit(solution)/shard_map/reshape;reshape | solution.py:329
  54.1 0.1 fusion.451
  54.2 1.1 %collective-permute-start.4 = (f32[4,16,2,32]{3,1,0,2:T(8,128)S(1)}, f32[4,16,2,32]{3,1,0,2:T(8,128)S(1)}, u32[]{:S(2)}, u32[]{:S(2)}) collective-permute-start(f32[4,16,2,32]{3,1,0,2:T(8,128)S(1)} %select_bitcast_fusion), channel_id=1, source_target_pairs={{0,8},{8,0},{16,24},{24,16},{1,9},{9,1},{17,25},{25,17},{2,10},{10... | collective-permute-start | bytes 49160 | tf_op jit(solution)/shard_map/ppermute | solution.py:30
  55.3 3.2 %collective-permute-done.4 = f32[4,16,2,32]{3,1,0,2:T(8,128)S(1)} collective-permute-done((f32[4,16,2,32]{3,1,0,2:T(8,128)S(1)}, f32[4,16,2,32]{3,1,0,2:T(8,128)S(1)}, u32[]{:S(2)}, u32[]{:S(2)}) %collective-permute-start.4) | collective-permute-done | bytes 16416 | tf_op jit(solution)/shard_map/ppermute | solution.py:30
  58.6 2.1 %collective-permute-start.5 = (f32[4,16,1,32]{3,1,0,2:T(8,128)S(1)}, f32[4,16,1,32]{3,1,0,2:T(8,128)S(1)}, u32[]{:S(2)}, u32[]{:S(2)}) collective-permute-start(f32[4,16,1,32]{3,1,0,2:T(8,128)S(1)} %select_bitcast_fusion.1), channel_id=1, source_target_pairs={{0,16},{8,24},{16,0},{24,8},{1,17},{9,25},{17,1},{25,9},{2,18},{10... | collective-permute-start | bytes 24584 | tf_op jit(solution)/shard_map/ppermute | solution.py:30
  60.7 3.3 %copy.561 = f32[16,16,19,128]{3,1,2,0:T(8,128)} copy(f32[16,16,19,128]{3,1,0,2:T(8,128)} %bitcast.551) | data formatting | bytes 4980736
  64.0 0.6 fusion.107
  (84 shorter events, 1.5 us)
Async XLA Ops:
  0.6 2.5 %copy-start = (f32[16,16,19,128]{3,1,2,0:T(8,128)S(1)}, f32[16,16,19,128]{3,1,2,0:T(8,128)}, u32[]{:S(2)}) copy-start(f32[16,16,19,128]{3,1,2,0:T(8,128)} %param.31) | copy-start | bytes 7471108
  3.8 13.4 %collective-permute-start = (f32[21,16,128]{2,1,0:T(8,128)}, f32[21,16,128]{2,1,0:T(8,128)S(1)}, u32[]{:S(2)}, u32[]{:S(2)}) collective-permute-start(f32[21,16,128]{2,1,0:T(8,128)} %pad_maximum_fusion.15), channel_id=1, source_target_pairs={{0,8},{8,16},{16,24},{24,0},{1,9},{9,17},{17,25},{25,1},{2,10},{10... | collective-permute-start | bytes 516104 | tf_op jit(solution)/shard_map/ppermute | solution.py:161
  7.4 9.8 %collective-permute-start.1 = (f32[21,16,128]{2,1,0:T(8,128)}, f32[21,16,128]{2,1,0:T(8,128)S(1)}, u32[]{:S(2)}, u32[]{:S(2)}) collective-permute-start(f32[21,16,128]{2,1,0:T(8,128)} %pad_maximum_fusion.16), channel_id=1, source_target_pairs={{0,24},{8,0},{16,8},{24,16},{1,25},{9,1},{17,9},{25,17},{2,26},{10... | collective-permute-start | bytes 516104 | tf_op jit(solution)/shard_map/ppermute | solution.py:161
  9.1 1.0 %copy-start.10 = (f32[19]{0:T(128)S(1)}, f32[19]{0:T(128)}, u32[]{:S(2)}) copy-start(f32[19]{0:T(128)} %constant.112.clone) | copy-start | bytes 232
  9.1 1.0 %copy-start.11 = (f32[19]{0:T(128)S(1)}, f32[19]{0:T(128)}, u32[]{:S(2)}) copy-start(f32[19]{0:T(128)} %constant.53.clone) | copy-start | bytes 232
  9.1 1.0 %copy-start.14 = (f32[19]{0:T(128)S(1)}, f32[19]{0:T(128)}, u32[]{:S(2)}) copy-start(f32[19]{0:T(128)} %constant.56.clone) | copy-start | bytes 232
  9.1 1.0 %copy-start.17 = (f32[19]{0:T(128)S(1)}, f32[19]{0:T(128)}, u32[]{:S(2)}) copy-start(f32[19]{0:T(128)} %constant.57.clone) | copy-start | bytes 232
  12.2 0.7 %copy-start.2 = (f32[19,38,1,1]{1,0,3,2:T(8,128)S(1)}, f32[19,38,1,1]{1,0,3,2:T(8,128)}, u32[]{:S(2)}) copy-start(f32[19,38,1,1]{1,0,3,2:T(8,128)} %constant.117) | copy-start | bytes 8668
  18.7 5.4 %copy-start.12 = (f32[19]{0:T(128)S(1)}, f32[19]{0:T(128)}, u32[]{:S(2)}) copy-start(f32[19]{0:T(128)} %constant.53.clone) | copy-start | bytes 232
  18.7 5.4 %copy-start.15 = (f32[19]{0:T(128)S(1)}, f32[19]{0:T(128)}, u32[]{:S(2)}) copy-start(f32[19]{0:T(128)} %constant.56.clone) | copy-start | bytes 232
  18.8 5.4 %copy-start.18 = (f32[19]{0:T(128)S(1)}, f32[19]{0:T(128)}, u32[]{:S(2)}) copy-start(f32[19]{0:T(128)} %constant.57.clone) | copy-start | bytes 232
  19.5 13.1 %collective-permute-start.2 = (f32[21,20,128]{2,0,1:T(8,128)}, f32[21,20,128]{2,0,1:T(8,128)}, u32[]{:S(2)}, u32[]{:S(2)}) collective-permute-start(f32[21,20,128]{2,0,1:T(8,128)} %get-tuple-element.198), channel_id=1, source_target_pairs={{0,1},{1,2},{2,3},{3,4},{4,5},{5,6},{6,7},{7,0},{8,9},{9,10},{10,1... | collective-permute-start | bytes 645128 | tf_op jit(solution)/shard_map/ppermute | solution.py:161
  19.5 14.1 %collective-permute-start.3 = (f32[21,20,128]{2,0,1:T(8,128)S(1)}, f32[21,20,128]{2,0,1:T(8,128)}, u32[]{:S(2)}, u32[]{:S(2)}) collective-permute-start(f32[21,20,128]{2,0,1:T(8,128)S(1)} %get-tuple-element.197), channel_id=1, source_target_pairs={{0,7},{1,0},{2,1},{3,2},{4,3},{5,4},{6,5},{7,6},{8,15},{9,8},{10,9... | collective-permute-start | bytes 645128 | tf_op jit(solution)/shard_map/ppermute | solution.py:161
  25.2 1.6 %copy-start.1 = (f32[19,14,14,128]{3,2,0,1:T(8,128)S(1)}, f32[19,14,14,128]{3,2,0,1:T(8,128)}, u32[]{:S(2)}) copy-start(f32[19,14,14,128]{3,2,0,1:T(8,128)} %copy_subtract_fusion) | copy-start | bytes 5720068
  38.0 1.9 %copy-start.5 = (f32[18,2,1]{2,1,0:T(2,128)S(1)}, f32[18,2,1]{2,1,0:T(2,128)}, u32[]{:S(2)}) copy-start(f32[18,2,1]{2,1,0:T(2,128)} %get-tuple-element.117) | copy-start | bytes 436
  38.0 1.9 %copy-start.6 = (f32[18,2,1]{2,1,0:T(2,128)S(1)}, f32[18,2,1]{2,1,0:T(2,128)}, u32[]{:S(2)}) copy-start(f32[18,2,1]{2,1,0:T(2,128)} %get-tuple-element.118) | copy-start | bytes 436
  38.0 1.9 %copy-start.8 = (f32[18,2,128]{2,1,0:T(2,128)S(1)}, f32[18,2,128]{2,1,0:T(2,128)}, u32[]{:S(2)}) copy-start(f32[18,2,128]{2,1,0:T(2,128)} %get-tuple-element.125) | copy-start | bytes 55300
  38.0 1.9 %copy-start.9 = (f32[18,2,128]{2,1,0:T(2,128)S(1)}, f32[18,2,128]{2,1,0:T(2,128)}, u32[]{:S(2)}) copy-start(f32[18,2,128]{2,1,0:T(2,128)} %get-tuple-element.152) | copy-start | bytes 55300
  39.7 1.1 %copy-start.13 = (f32[19]{0:T(128)S(1)}, f32[19]{0:T(128)}, u32[]{:S(2)}) copy-start(f32[19]{0:T(128)} %constant.53.clone) | copy-start | bytes 232
  39.7 1.1 %copy-start.16 = (f32[19]{0:T(128)S(1)}, f32[19]{0:T(128)}, u32[]{:S(2)}) copy-start(f32[19]{0:T(128)} %constant.56.clone) | copy-start | bytes 232
  39.7 1.1 %copy-start.19 = (f32[19]{0:T(128)S(1)}, f32[19]{0:T(128)}, u32[]{:S(2)}) copy-start(f32[19]{0:T(128)} %constant.57.clone) | copy-start | bytes 232
  40.8 3.3 %copy-start.3 = (f32[18,2,1]{2,1,0:T(2,128)S(1)}, f32[18,2,1]{2,1,0:T(2,128)}, u32[]{:S(2)}) copy-start(f32[18,2,1]{2,1,0:T(2,128)} %get-tuple-element.119) | copy-start | bytes 436
  40.8 3.3 %copy-start.4 = (f32[18,2,1]{2,1,0:T(2,128)S(1)}, f32[18,2,1]{2,1,0:T(2,128)}, u32[]{:S(2)}) copy-start(f32[18,2,1]{2,1,0:T(2,128)} %get-tuple-element.120) | copy-start | bytes 436
  40.8 3.3 %copy-start.7 = (f32[18,2,128]{2,1,0:T(2,128)S(1)}, f32[18,2,128]{2,1,0:T(2,128)}, u32[]{:S(2)}) copy-start(f32[18,2,128]{2,1,0:T(2,128)} %get-tuple-element.126) | copy-start | bytes 55300
  54.2 4.3 %collective-permute-start.4 = (f32[4,16,2,32]{3,1,0,2:T(8,128)S(1)}, f32[4,16,2,32]{3,1,0,2:T(8,128)S(1)}, u32[]{:S(2)}, u32[]{:S(2)}) collective-permute-start(f32[4,16,2,32]{3,1,0,2:T(8,128)S(1)} %select_bitcast_fusion), channel_id=1, source_target_pairs={{0,8},{8,0},{16,24},{24,16},{1,9},{9,1},{17,25},{25,17},{2,10},{10... | collective-permute-start | bytes 49160 | tf_op jit(solution)/shard_map/ppermute | solution.py:30
  58.6 5.4 %collective-permute-start.5 = (f32[4,16,1,32]{3,1,0,2:T(8,128)S(1)}, f32[4,16,1,32]{3,1,0,2:T(8,128)S(1)}, u32[]{:S(2)}, u32[]{:S(2)}) collective-permute-start(f32[4,16,1,32]{3,1,0,2:T(8,128)S(1)} %select_bitcast_fusion.1), channel_id=1, source_target_pairs={{0,16},{8,24},{16,0},{24,8},{1,17},{9,25},{17,1},{25,9},{2,18},{10... | collective-permute-start | bytes 24584 | tf_op jit(solution)/shard_map/ppermute | solution.py:30

commit v13 on v6

--- a/solution.py
+++ b/solution.py
@@ -243,7 +243,7 @@
     )(near_y, band, far_y)
 
 
-def collide_region(cells, pot, tables):
+def collide_region(cells, pot, tables, force_only=False):
     velocities, weights, relaxing, forcing_map = tables
     nx, ny = cells.shape[1], cells.shape[2]
     centre = pot[1 : 1 + nx, 1 : 1 + ny]
@@ -256,6 +256,8 @@
             if steps[d] != 0:
                 totals[d] = totals[d] + weights[q] * steps[d] * neighbour
     force = [-cohesion * centre * totals[d] for d in range(3)]
+    if force_only:
+        return force
     rho = jnp.sum(cells, axis=0)
     return collide_major(cells, rho, force, velocities, weights, relaxing, forcing_map)
 
@@ -292,8 +294,15 @@
     near_x = collide_region(fx[:, 0:2, 1 : extent_y - 1], px[0:4], tables)
     far_x = collide_region(fx[:, extent_x : extent_x + 2, 1 : extent_y - 1], px[extent_x : extent_x + 4], tables)
     band = jnp.concatenate([near_x, inner, far_x], axis=1)
-    near_y = collide_region(fxy[:, :, 0:2], pxy[:, 0:4], tables)
-    far_y = collide_region(fxy[:, :, extent_y : extent_y + 2], pxy[:, extent_y : extent_y + 4], tables)
+    low_cells = fxy[:, :, 0:2]
+    high_cells = fxy[:, :, extent_y : extent_y + 2]
+    low_force = collide_region(low_cells, pxy[:, 0:4], tables, force_only=True)
+    high_force = collide_region(high_cells, pxy[:, extent_y : extent_y + 4], tables, force_only=True)
+    strips = jnp.concatenate([low_cells, high_cells], axis=1)
+    strip_force = [jnp.concatenate([low_force[d], high_force[d]], axis=0) for d in range(3)]
+    both = collide_major(strips, jnp.sum(strips, axis=0), strip_force, velocities, weights, relaxing, forcing_map)
+    near_y = both[:, : extent_x + 2]
+    far_y = both[:, extent_x + 2 :]
     collided = (near_y, band, far_y)
     groups = lax.axis_size("gx")
     length_x = extent_x * groups

time: 54.1 us -> 55.3 us (1.022)
  other arithmetic: 20.1 us -> 17.4 us
  waiting for transfers between devices: 4.6 us -> 7.22 us
  local copies, waits for them, and re-layouts: 9.3 us -> 10 us
    ppermute x4, waiting for transfers between devices: 2.28 us -> 4.07 us  [shift_ring(): lax.ppermute(x, axis, [(i, (i - step) % count) for i in range(count)])]
    concatenate x1 -> x3, other arithmetic: 1.67 us -> 0.06 us  [body(): jnp.concatenate([low_force[d], high_force[d]], axis=0)]
    sub x4 -> x3, other arithmetic: 4.12 us -> 2.56 us  [collide_major(): f - jnp.einsum('pq,q...->p...', table, stacked, precision=lax.Precision.H...]
    mul x5 -> x3, other arithmetic: 2.61 us -> 1.15 us  [collide_major(): 1.5 * speed_squared]
    mul x1 -> x6, other arithmetic: 0.02 us -> 1.27 us  [collide_region(): force = [-cohesion * centre * totals[d] for d in range(3)]]
    slice x2 -> x3, local copies, waits for them, and re-layouts: 0.02 us -> 0.95 us  [the longest x1 0.92 us: body(): far_y = both[:, extent_x + 2:]]
    ppermute x2, waiting for transfers between devices: 2.32 us -> 3.14 us  [from_partner(): lax.ppermute(x, axis, [(i, i ^ 1 << distance) for i in range(lax.axis_siz...]
    ppermute x4, starting transfers between devices: 6.82 us -> 7.62 us  [shift_ring(): lax.ppermute(x, axis, [(i, (i - step) % count) for i in range(count)])]
  transfers between devices with their start and end apart: 6 -> 6, of which waited for: 2 -> 3; matrix products, arithmetic and copies ran while one was open for 31% -> 22% of each run, Pallas kernels for 0% -> 0%
where the time goes in v13:
time: 55.3 us; the launch traced here: 54.9 us
  other arithmetic  17.4 us (31%)
  starting transfers between devices  10.9 us (20%)
  local copies, waits for them, and re-layouts  10 us (18%)
  waiting for transfers between devices  7.22 us (13%)
  Pallas kernels  4.34 us (8%)
  matrix products  3.76 us (7%)
  between operations  1.25 us (2%)
    ppermute x4, starting transfers between devices, shift_ring(): lax.ppermute(x, axis, [(i, (i - step) % count) for i in range(count)])  7.62 us
    sub x4, other arithmetic, collide_major(): stacked = jnp.concatenate([f - balance, guo_term], axis=0)  5.58 us
    unnamed x15, local copies, waits for them, and re-layouts  4.58 us
    pallas_call x1, Pallas kernels, stream_and_render(): pl.pallas_call(kernel, out_shape=(jax.ShapeDtypeStruct((19, extent_x, ext...  4.34 us
    ppermute x4, waiting for transfers between devices, shift_ring(): lax.ppermute(x, axis, [(i, (i - step) % count) for i in range(count)])  4.07 us
    dot_general x4, matrix products, collide_major(): jnp.einsum('pq,q...->p...', table, stacked, precision=lax.Precision.HIGH)  3.76 us
    ppermute x2, starting transfers between devices, from_partner(): lax.ppermute(x, axis, [(i, i ^ 1 << distance) for i in range(lax.axis_siz...  3.3 us
    ppermute x2, waiting for transfers between devices, from_partner(): lax.ppermute(x, axis, [(i, i ^ 1 << distance) for i in range(lax.axis_siz...  3.14 us
  transfers between devices with their start and end apart: 6, of which 3 were waited for; matrix products, arithmetic and copies ran while one was open for 22% of the time, Pallas kernels for 0%

profile of v13, /device:TPU:0, one launch (start us, length us, event | category | flops | bytes accessed | tf_op | source)
XLA Modules:
  0.0 54.9 jit_solution(16393160915829727701)
XLA Ops:
  0.6 2.0 %bitcast_reduce_fusion = f32[16,16,128]{2,1,0:T(8,128)S(1)} fusion(f32[16,16,19,128]{3,1,2,0:T(8,128)} %param.25), kind=kLoop, calls=%fused_computation.758 | loop fusion | flops 589824 | bytes 2621440 | tf_op jit(solution)/shard_map/reduce_sum | solution.py:270
  2.7 0.4 copy-done
  3.1 3.0 %collective-permute-start = (f32[21,16,128]{2,1,0:T(8,128)S(1)}, f32[21,16,128]{2,1,0:T(8,128)S(1)}, u32[]{:S(2)}, u32[]{:S(2)}) collective-permute-start(f32[21,16,128]{2,1,0:T(8,128)S(1)} %pad_maximum_fusion.19), channel_id=1, source_target_pairs={{0,8},{8,16},{16,24},{24,0},{1,9},{9,17},{17,25},{25,1},{2,10},{10... | collective-permute-start | bytes 516104 | tf_op jit(solution)/shard_map/ppermute | solution.py:161
  6.1 1.0 %collective-permute-start.1 = (f32[21,16,128]{2,1,0:T(8,128)S(1)}, f32[21,16,128]{2,1,0:T(8,128)S(1)}, u32[]{:S(2)}, u32[]{:S(2)}) collective-permute-start(f32[21,16,128]{2,1,0:T(8,128)S(1)} %pad_maximum_fusion.20), channel_id=1, source_target_pairs={{0,24},{8,0},{16,8},{24,16},{1,25},{9,1},{17,9},{25,17},{2,26},{10... | collective-permute-start | bytes 516104 | tf_op jit(solution)/shard_map/ppermute | solution.py:161
  7.2 0.2 fusion.415
  7.4 0.2 fusion.416
  7.6 0.2 slice_reduce_fusion
  7.9 0.9 %add_multiply_fusion.4 = (f32[14,14,128]{2,1,0:T(8,128)S(1)}, f32[14,14,128]{2,1,0:T(8,128)S(1)}, f32[14,14,128]{2,1,0:T(8,128)S(1)}, f32[14,14,128]{2,1,0:T(8,1...) fusion(f32[14,14,128]{2,1,0:T(8,128)S(1)} %slice_reduce_fusion, ...), kind=kLoop, calls=%fused_computation.317 | loop fusion | flops 2985472 | bytes 4515840 | tf_op jit(solution)/shard_map/mul | solution.py:180
  8.9 2.1 %fusion.5 = (f32[19,14,14,128]{3,2,0,1:T(8,128)S(1)}, f32[19,14,14,128]{3,2,0,1:T(8,128)S(1)}) fusion(f32[19,16,16,128]{3,2,0,1:T(8,128)S(1)} %bitcast.681, f32[14,14,128]{2,1,0:T(8,128)S(1)} %get-tuple-element.17, f32[14,14,128]{2,1,0:T(8,128)S(1)} %get-tuple-element.22, f32[19]{0:T(128)S(1)} %copy-done.6, f32[14,14,128]{2,1,0:T(8,128)S(1)} %get-tuple-element.20, ...), kind=kLoop, calls=%fused_computation.44 | loop fusion | flops 11916800 | bytes 6623536 | tf_op jit(solution)/shard_map/sub | solution.py:185
  11.0 0.4 pad_maximum_fusion
  11.5 0.3 copy-done.2
  11.7 2.2 %fusion = f32[19,14,14,128]{3,0,2,1:T(8,128)S(1)} fusion(f32[19,38,1,1]{1,0,3,2:T(8,128)S(1)} %copy-done.2, f32[38,14,14,128]{3,2,0,1:T(8,128)S(1)} %pad_maximum_fusion), kind=kOutput, calls=%fused_computation.37 | convolution fusion | flops 108681216 | bytes 5722952 | tf_op jit(solution)/shard_map/pq,q...->p.../dot_general | solution.py:186
  14.0 2.0 %copy_subtract_fusion = f32[19,14,14,128]{3,2,0,1:T(8,128)} fusion(f32[19,14,14,128]{3,0,2,1:T(8,128)S(1)} %fusion, f32[19,16,16,128]{3,2,0,1:T(8,128)S(1)} %bitcast.682), kind=kLoop, calls=%fused_computation.45 | loop fusion | flops 476672 | bytes 5720064 | tf_op jit(solution)/shard_map/sub | solution.py:186
  16.0 0.1 fusion.254
  16.1 0.1 fusion.255
  16.2 0.1 fusion.385
  16.5 0.2 pad_maximum_fusion.18
  17.0 0.1 add_multiply_fusion.11
  17.1 0.4 fusion.24
  17.5 0.4 fusion.13
  18.0 0.1 add_multiply_fusion.12
  18.2 0.4 fusion.20
  18.6 0.4 fusion.15
  19.1 0.1 copy_subtract_fusion.3
  19.2 0.6 %copy-done.1 = f32[19,14,14,128]{3,2,0,1:T(8,128)S(1)} copy-done((f32[19,14,14,128]{3,2,0,1:T(8,128)S(1)}, f32[19,14,14,128]{3,2,0,1:T(8,128)}, u32[]{:S(2)}) %copy-start.1) | copy-done | bytes 1906712
  19.8 0.2 pad_maximum_fusion.1
  20.0 1.9 %copy.91.band_ref = f32[19,18,14,128]{3,2,1,0:T(8,128)} copy(f32[19,18,14,128]{3,2,0,1:T(8,128)S(1)} %pad_maximum_fusion.1) | data formatting | bytes 4902912 | tf_op jit(solution)/shard_map/concatenate | solution.py:296
  21.9 0.1 fusion.28
  22.1 3.5 %collective-permute-start.3 = (f32[21,20,128]{2,0,1:T(8,128)S(1)}, f32[21,20,128]{2,0,1:T(8,128)S(1)}, u32[]{:S(2)}, u32[]{:S(2)}) collective-permute-start(f32[21,20,128]{2,0,1:T(8,128)S(1)} %get-tuple-element.180), channel_id=1, source_target_pairs={{0,7},{1,0},{2,1},{3,2},{4,3},{5,4},{6,5},{7,6},{8,15},{9,8},{10,9... | collective-permute-start | bytes 645128 | tf_op jit(solution)/shard_map/ppermute | solution.py:161
  25.6 0.1 fusion.412
  25.7 0.1 fusion.413
  25.8 3.8 %collective-permute-done.2 = f32[21,20,128]{2,0,1:T(8,128)S(1)} collective-permute-done((f32[21,20,128]{2,0,1:T(8,128)S(1)}, f32[21,20,128]{2,0,1:T(8,128)S(1)}, u32[]{:S(2)}, u32[]{:S(2)}) %collective-permute-start.2) | collective-permute-done | bytes 215072 | tf_op jit(solution)/shard_map/ppermute | solution.py:161
  29.6 0.2 collective-permute-done.3
  30.0 0.1 fusion.405
  30.1 0.1 fusion.406
  30.2 0.1 fusion.407
  30.3 0.1 fusion.408
  30.5 0.1 fusion.143
  30.6 0.1 fusion.134
  30.7 0.1 fusion.132
  30.8 0.1 fusion.123
  30.9 0.1 broadcast_in_dim.7
  31.1 0.1 broadcast_in_dim.8
  31.2 0.2 add_multiply_fusion.10
  31.4 0.2 add_multiply_fusion.9
  31.6 0.2 add_multiply_fusion.8
  31.8 0.2 add_multiply_fusion.7
  32.0 0.3 add_multiply_fusion.6
  32.3 0.3 add_multiply_fusion.5
  32.6 0.7 %fusion.402 = (f32[36,2,128]{2,1,0:T(2,128)S(1)}, f32[19,36,2,128]{3,2,0,1:T(2,128)S(1)}) fusion(f32[19,18,1,128]{3,2,0,1:T(1,128)S(1)} %broadcast_in_dim.8, f32[19,1,16,128]{3,2,0,1:T(8,128)S(1)} %slice_bitcast_fusion, f32[19,16,16,128]{3,2,0,1:T(8,128)S(1)} %bitcast.688, f32[19,1,16,128]{3,2,0,1:T(8,128)S(1)} %slice_bitcast_fusion.2, ...), kind=kLoop, calls=%fused_computation.761 | loop fusion | flops 1391616 | bytes 3889152 | tf_op jit(solution)/shard_map/reduce_sum | solution.py:303
  33.3 0.3 multiply_bitcast_fusion
  33.6 2.7 %fusion.11 = (f32[19,36,2,128]{3,2,1,0:T(2,128)S(1)}, f32[19,36,2,128]{3,2,1,0:T(2,128)S(1)}) fusion(f32[36,2,128]{2,1,0:T(2,128)S(1)} %get-tuple-element.33, f32[36,2,128]{2,1,0:T(2,128)S(1)} %get-tuple-element.41, f32[19]{0:T(128)S(1)} %copy-done.3, f32[36,2,128]{2,1,0:T(2,128)S(1)} %bitcast.692, f32[19]{0:T(128)S(1)} %copy-done.6, ...), kind=kLoop, calls=%fused_computation.122 | loop fusion | flops 4377600 | bytes 2433328 | tf_op jit(solution)/shard_map/sub | solution.py:185
  36.3 0.6 %pad_maximum_fusion.2 = f32[38,36,2,128]{3,2,1,0:T(2,128)S(1)} fusion(f32[19,36,2,128]{3,2,1,0:T(2,128)S(1)} %get-tuple-element.168, f32[19,36,2,128]{3,2,1,0:T(2,128)S(1)} %get-tuple-element.167), kind=kLoop, calls=%fused_computation.51 | loop fusion | flops 350208 | bytes 2801664 | tf_op jit(solution)/shard_map/concatenate | solution.py:185
  36.9 0.7 %fusion.6 = f32[19,36,2,128]{3,0,2,1:T(8,128)S(1)} fusion(f32[19,38,1,1]{1,0,3,2:T(8,128)S(1)} %copy-done.2, f32[38,36,2,128]{3,2,1,0:T(2,128)S(1)} %pad_maximum_fusion.2), kind=kOutput, calls=%fused_computation.49 | convolution fusion | flops 39923712 | bytes 2104136 | tf_op jit(solution)/shard_map/pq,q...->p.../dot_general | solution.py:186
  37.6 0.5 copy_subtract_fusion.1
  38.1 0.9 %fusion.404 = (f32[19,18,2,128]{3,2,1,0:T(2,128)}, f32[19,18,2,128]{3,2,1,0:T(2,128)}) fusion(f32[19,36,2,128]{3,2,1,0:T(2,128)S(1)} %copy_subtract_fusion.1), kind=kLoop, calls=%fused_computation.762 | loop fusion | bytes 1400832 | tf_op jit(solution)/shard_map/slice | solution.py:305
  39.0 4.3 %shard_map.248 = (f32[19,16,16,128]{3,2,1,0:T(8,128)}, f32[4,16,128]{2,1,0:T(8,128)}) custom-call(f32[19,18,2,128]{3,2,1,0:T(2,128)} %get-tuple-element.62.near_ref, f32[19,18,14,128]{3,2,1,0:T(8,128)} %copy.91.band_ref, f32[19,18,2,128]{3,2,1,0:T(2,128)} %get-tuple-element.61.far_ref), custom_call_target="tpu_custom_call" | custom-call | tf_op jit(solution)/shard_map/pallas_call | solution.py:234
  43.4 0.9 %reshape_reshape.3 = f32[4,16,2,2,32]{4,3,2,1,0:T(2,128)S(1)} reshape(f32[4,16,128]{2,1,0:T(8,128)} %get-tuple-element.5) | data formatting | bytes 65536 | tf_op jit(solution)/shard_map/reshape;reshape | solution.py:319
  44.3 0.1 fusion.414
  44.4 1.2 %collective-permute-start.4 = (f32[4,16,2,32]{3,1,0,2:T(8,128)S(1)}, f32[4,16,2,32]{3,1,0,2:T(8,128)S(1)}, u32[]{:S(2)}, u32[]{:S(2)}) collective-permute-start(f32[4,16,2,32]{3,1,0,2:T(8,128)S(1)} %select_bitcast_fusion), channel_id=1, source_target_pairs={{0,8},{8,0},{16,24},{24,16},{1,9},{9,1},{17,25},{25,17},{2,10},{10... | collective-permute-start | bytes 49160 | tf_op jit(solution)/shard_map/ppermute | solution.py:30
  45.6 3.1 %collective-permute-done.4 = f32[4,16,2,32]{3,1,0,2:T(8,128)S(1)} collective-permute-done((f32[4,16,2,32]{3,1,0,2:T(8,128)S(1)}, f32[4,16,2,32]{3,1,0,2:T(8,128)S(1)}, u32[]{:S(2)}, u32[]{:S(2)}) %collective-permute-start.4) | collective-permute-done | bytes 16416 | tf_op jit(solution)/shard_map/ppermute | solution.py:30
  48.8 2.1 %collective-permute-start.5 = (f32[4,16,1,32]{3,1,0,2:T(8,128)S(1)}, f32[4,16,1,32]{3,1,0,2:T(8,128)S(1)}, u32[]{:S(2)}, u32[]{:S(2)}) collective-permute-start(f32[4,16,1,32]{3,1,0,2:T(8,128)S(1)} %select_bitcast_fusion.1), channel_id=1, source_target_pairs={{0,16},{8,24},{16,0},{24,8},{1,17},{9,25},{17,1},{25,9},{2,18},{10... | collective-permute-start | bytes 24584 | tf_op jit(solution)/shard_map/ppermute | solution.py:30
  50.9 3.3 %copy.94 = f32[16,16,19,128]{3,1,2,0:T(8,128)} copy(f32[16,16,19,128]{3,1,0,2:T(8,128)} %bitcast.689) | data formatting | bytes 4980736
  54.3 0.6 %fusion.122 = f32[4,16,32]{2,1,0:T(8,128)} fusion(f32[4,16,1,32]{3,1,0,2:T(8,128)S(1)} %collective-permute-done.5, f32[16,32]{1,0:T(8,128)S(1)} %fusion.378, pred[]{:T(512)S(6)} %eq.19, f32[4,16,1,2,32]{4,1,0,3,2:T(8,128)S(1)} %fusion.104, pred[]{:T(512)S(6)} %eq.20), kind=kLoop, calls=%fused_computation.375 | loop fusion | flops 10240 | bytes 34818 | tf_op jit(solution)/shard_map/reshape | solution.py:328
  (55 shorter events, 1.1 us)
Async XLA Ops:
  0.6 2.5 %copy-start = (f32[16,16,19,128]{3,1,2,0:T(8,128)S(1)}, f32[16,16,19,128]{3,1,2,0:T(8,128)}, u32[]{:S(2)}) copy-start(f32[16,16,19,128]{3,1,2,0:T(8,128)} %param.25) | copy-start | bytes 7471108
  3.1 12.8 %collective-permute-start = (f32[21,16,128]{2,1,0:T(8,128)S(1)}, f32[21,16,128]{2,1,0:T(8,128)S(1)}, u32[]{:S(2)}, u32[]{:S(2)}) collective-permute-start(f32[21,16,128]{2,1,0:T(8,128)S(1)} %pad_maximum_fusion.19), channel_id=1, source_target_pairs={{0,8},{8,16},{16,24},{24,0},{1,9},{9,17},{17,25},{25,1},{2,10},{10... | collective-permute-start | bytes 516104 | tf_op jit(solution)/shard_map/ppermute | solution.py:161
  6.1 10.1 %collective-permute-start.1 = (f32[21,16,128]{2,1,0:T(8,128)S(1)}, f32[21,16,128]{2,1,0:T(8,128)S(1)}, u32[]{:S(2)}, u32[]{:S(2)}) collective-permute-start(f32[21,16,128]{2,1,0:T(8,128)S(1)} %pad_maximum_fusion.20), channel_id=1, source_target_pairs={{0,24},{8,0},{16,8},{24,16},{1,25},{9,1},{17,9},{25,17},{2,26},{10... | collective-permute-start | bytes 516104 | tf_op jit(solution)/shard_map/ppermute | solution.py:161
  7.9 1.0 %copy-start.3 = (f32[19]{0:T(128)S(1)}, f32[19]{0:T(128)}, u32[]{:S(2)}) copy-start(f32[19]{0:T(128)} %constant.112.clone) | copy-start | bytes 232
  7.9 1.0 %copy-start.4 = (f32[19]{0:T(128)S(1)}, f32[19]{0:T(128)}, u32[]{:S(2)}) copy-start(f32[19]{0:T(128)} %constant.53.clone) | copy-start | bytes 232
  7.9 1.0 %copy-start.5 = (f32[19]{0:T(128)S(1)}, f32[19]{0:T(128)}, u32[]{:S(2)}) copy-start(f32[19]{0:T(128)} %constant.56.clone) | copy-start | bytes 232
  7.9 1.0 %copy-start.6 = (f32[19]{0:T(128)S(1)}, f32[19]{0:T(128)}, u32[]{:S(2)}) copy-start(f32[19]{0:T(128)} %constant.57.clone) | copy-start | bytes 232
  11.0 0.7 %copy-start.2 = (f32[19,38,1,1]{1,0,3,2:T(8,128)S(1)}, f32[19,38,1,1]{1,0,3,2:T(8,128)}, u32[]{:S(2)}) copy-start(f32[19,38,1,1]{1,0,3,2:T(8,128)} %constant.117) | copy-start | bytes 8668
  18.1 1.6 %copy-start.1 = (f32[19,14,14,128]{3,2,0,1:T(8,128)S(1)}, f32[19,14,14,128]{3,2,0,1:T(8,128)}, u32[]{:S(2)}) copy-start(f32[19,14,14,128]{3,2,0,1:T(8,128)} %copy_subtract_fusion) | copy-start | bytes 5720068
  22.0 7.6 %collective-permute-start.2 = (f32[21,20,128]{2,0,1:T(8,128)S(1)}, f32[21,20,128]{2,0,1:T(8,128)S(1)}, u32[]{:S(2)}, u32[]{:S(2)}) collective-permute-start(f32[21,20,128]{2,0,1:T(8,128)S(1)} %get-tuple-element.179), channel_id=1, source_target_pairs={{0,1},{1,2},{2,3},{3,4},{4,5},{5,6},{6,7},{7,0},{8,9},{9,10},{10,1... | collective-permute-start | bytes 645128 | tf_op jit(solution)/shard_map/ppermute | solution.py:161
  22.1 7.8 %collective-permute-start.3 = (f32[21,20,128]{2,0,1:T(8,128)S(1)}, f32[21,20,128]{2,0,1:T(8,128)S(1)}, u32[]{:S(2)}, u32[]{:S(2)}) collective-permute-start(f32[21,20,128]{2,0,1:T(8,128)S(1)} %get-tuple-element.180), channel_id=1, source_target_pairs={{0,7},{1,0},{2,1},{3,2},{4,3},{5,4},{6,5},{7,6},{8,15},{9,8},{10,9... | collective-permute-start | bytes 645128 | tf_op jit(solution)/shard_map/ppermute | solution.py:161
  44.4 4.3 %collective-permute-start.4 = (f32[4,16,2,32]{3,1,0,2:T(8,128)S(1)}, f32[4,16,2,32]{3,1,0,2:T(8,128)S(1)}, u32[]{:S(2)}, u32[]{:S(2)}) collective-permute-start(f32[4,16,2,32]{3,1,0,2:T(8,128)S(1)} %select_bitcast_fusion), channel_id=1, source_target_pairs={{0,8},{8,0},{16,24},{24,16},{1,9},{9,1},{17,25},{25,17},{2,10},{10... | collective-permute-start | bytes 49160 | tf_op jit(solution)/shard_map/ppermute | solution.py:30
  48.8 5.4 %collective-permute-start.5 = (f32[4,16,1,32]{3,1,0,2:T(8,128)S(1)}, f32[4,16,1,32]{3,1,0,2:T(8,128)S(1)}, u32[]{:S(2)}, u32[]{:S(2)}) collective-permute-start(f32[4,16,1,32]{3,1,0,2:T(8,128)S(1)} %select_bitcast_fusion.1), channel_id=1, source_target_pairs={{0,16},{8,24},{16,0},{24,8},{1,17},{9,25},{17,1},{25,9},{2,18},{10... | collective-permute-start | bytes 24584 | tf_op jit(solution)/shard_map/ppermute | solution.py:30

commit v14 on v6

--- a/solution.py
+++ b/solution.py
@@ -192,22 +192,24 @@
     edge = near_y.shape[2]
     steps = [[int(v) for v in velocities[q]] for q in range(19)]
 
-    def kernel(near_ref, band_ref, far_ref, o_ref, pic_ref, c_ref):
-        def gather(q, carry):
-            c_ref[q, :, 0:edge] = near_ref[q]
-            c_ref[q, :, edge : edge + extent_y - 2] = band_ref[q]
-            c_ref[q, :, edge + extent_y - 2 :] = far_ref[q]
-            return carry
-
-        lax.fori_loop(0, 19, gather, 0)
+    pieces = ((0, 0, edge), (1, edge, extent_y - 2), (2, edge + extent_y - 2, edge))
+
+    def kernel(near_ref, band_ref, far_ref, o_ref, pic_ref):
+        refs = (near_ref, band_ref, far_ref)
         for q in range(19):
             cx, cy, cz = steps[q]
+            first = 1 - cy
 
             def move(x, carry):
-                v = c_ref[q, x + 1 - cx, pl.ds(1 - cy, extent_y), :]
-                if cz != 0:
-                    v = pltpu.roll(v, shift=cz % depth_z, axis=1)
-                o_ref[q, x] = v
+                for which, start, count in pieces:
+                    lo = max(first, start)
+                    hi = min(first + extent_y, start + count)
+                    if hi <= lo:
+                        continue
+                    v = refs[which][q, x + 1 - cx, lo - start : hi - start, :]
+                    if cz != 0:
+                        v = pltpu.roll(v, shift=cz % depth_z, axis=1)
+                    o_ref[q, x, lo - first : hi - first, :] = v
                 return carry
 
             lax.fori_loop(0, extent_x, move, 0, unroll=True)
@@ -239,7 +241,6 @@
         ),
         in_specs=[pl.BlockSpec(memory_space=pltpu.VMEM)] * 3,
         out_specs=(pl.BlockSpec(memory_space=pltpu.VMEM), pl.BlockSpec(memory_space=pltpu.VMEM)),
-        scratch_shapes=[pltpu.VMEM((19, extent_x + 2, extent_y + 2, depth_z), jnp.float32)],
     )(near_y, band, far_y)
 
 

time: 54.1 us -> 53.8 us (level)
  no operation moved by 1% of the time
where the time goes in v14:
time: 53.8 us; the launch traced here: 53.5 us
  other arithmetic  20.1 us (37%)
  starting transfers between devices  10.4 us (19%)
  local copies, waits for them, and re-layouts  9.3 us (17%)
  waiting for transfers between devices  4.6 us (9%)
  Pallas kernels  4.12 us (8%)
  matrix products  3.79 us (7%)
  between operations  1.28 us (2%)
    ppermute x4, starting transfers between devices, shift_ring(): lax.ppermute(x, axis, [(i, (i - step) % count) for i in range(count)])  6.82 us
    sub x5, other arithmetic, collide_major(): stacked = jnp.concatenate([f - balance, guo_term], axis=0)  5.65 us
    unnamed x15, local copies, waits for them, and re-layouts  4.6 us
    sub x4, other arithmetic, collide_major(): f - jnp.einsum('pq,q...->p...', table, stacked, precision=lax.Precision.H...  4.12 us
    pallas_call x1, Pallas kernels, stream_and_render(): pl.pallas_call(kernel, out_shape=(jax.ShapeDtypeStruct((19, extent_x, ext...  4.12 us
    dot_general x5, matrix products, collide_major(): jnp.einsum('pq,q...->p...', table, stacked, precision=lax.Precision.HIGH)  3.79 us
    ppermute x2, starting transfers between devices, from_partner(): lax.ppermute(x, axis, [(i, i ^ 1 << distance) for i in range(lax.axis_siz...  3.53 us
    mul x5, other arithmetic, collide_major(): 1.5 * speed_squared  2.61 us
  transfers between devices with their start and end apart: 6, of which 2 were waited for; matrix products, arithmetic and copies ran while one was open for 31% of the time, Pallas kernels for 0%

profile of v14, /device:TPU:0, one launch (start us, length us, event | category | flops | bytes accessed | tf_op | source)
XLA Modules:
  0.0 53.5 jit_solution(5994268920890000007)
XLA Ops:
  0.6 2.0 %bitcast_reduce_fusion = f32[16,16,128]{2,1,0:T(8,128)S(1)} fusion(f32[16,16,19,128]{3,1,2,0:T(8,128)} %param.31), kind=kLoop, calls=%fused_computation.832 | loop fusion | flops 589824 | bytes 2621440 | tf_op jit(solution)/shard_map/reduce_sum | solution.py:269
  2.7 0.4 copy-done
  3.1 3.9 %collective-permute-start.1 = (f32[21,16,128]{2,1,0:T(8,128)S(1)}, f32[21,16,128]{2,1,0:T(8,128)S(1)}, u32[]{:S(2)}, u32[]{:S(2)}) collective-permute-start(f32[21,16,128]{2,1,0:T(8,128)S(1)} %pad_maximum_fusion.16), channel_id=1, source_target_pairs={{0,24},{8,0},{16,8},{24,16},{1,25},{9,1},{17,9},{25,17},{2,26},{10... | collective-permute-start | bytes 516104 | tf_op jit(solution)/shard_map/ppermute | solution.py:161
  7.2 0.2 slice_reduce_fusion
  7.4 0.2 fusion.452
  7.6 0.2 fusion.453
  7.9 0.9 %add_multiply_fusion.5 = (f32[14,14,128]{2,1,0:T(8,128)S(1)}, f32[14,14,128]{2,1,0:T(8,128)S(1)}, f32[14,14,128]{2,1,0:T(8,128)S(1)}, f32[14,14,128]{2,1,0:T(8,1...) fusion(f32[14,14,128]{2,1,0:T(8,128)S(1)} %slice_reduce_fusion, ...), kind=kLoop, calls=%fused_computation.316 | loop fusion | flops 2985472 | bytes 6207488 | tf_op jit(solution)/shard_map/mul | solution.py:180
  8.9 2.1 %fusion.5 = (f32[19,14,14,128]{3,2,0,1:T(8,128)S(1)}, f32[19,14,14,128]{3,2,0,1:T(8,128)S(1)}) fusion(f32[19,16,16,128]{3,2,0,1:T(8,128)S(1)} %bitcast.544, f32[14,14,128]{2,1,0:T(8,128)S(1)} %get-tuple-element.30, f32[14,14,128]{2,1,0:T(8,128)S(1)} %get-tuple-element.35, f32[19]{0:T(128)S(1)} %copy-done.4, f32[14,14,128]{2,1,0:T(8,128)S(1)} %get-tuple-element.33, ...), kind=kLoop, calls=%fused_computation.46 | loop fusion | flops 11916800 | bytes 6623536 | tf_op jit(solution)/shard_map/sub | solution.py:185
  11.0 0.4 pad_maximum_fusion
  11.5 0.3 copy-done.2
  11.7 2.2 %fusion = f32[19,14,14,128]{3,0,2,1:T(8,128)S(1)} fusion(f32[19,38,1,1]{1,0,3,2:T(8,128)S(1)} %copy-done.2, f32[38,14,14,128]{3,2,0,1:T(8,128)S(1)} %pad_maximum_fusion), kind=kOutput, calls=%fused_computation.39 | convolution fusion | flops 108681216 | bytes 5722952 | tf_op jit(solution)/shard_map/pq,q...->p.../dot_general | solution.py:186
  14.0 2.0 %copy_subtract_fusion = f32[19,14,14,128]{3,2,0,1:T(8,128)} fusion(f32[19,14,14,128]{3,0,2,1:T(8,128)S(1)} %fusion, f32[19,16,16,128]{3,2,0,1:T(8,128)S(1)} %bitcast.545), kind=kLoop, calls=%fused_computation.47 | loop fusion | flops 476672 | bytes 5720064 | tf_op jit(solution)/shard_map/sub | solution.py:186
  16.0 0.1 fusion.330
  16.1 0.1 fusion.329
  16.2 0.1 fusion.303
  16.3 0.1 fusion.302
  16.5 0.1 fusion.423
  16.6 0.1 fusion.449
  16.8 0.2 pad_maximum_fusion.12
  17.1 0.1 fusion.35
  17.1 2.8 %collective-permute-start.3 = (f32[21,20,128]{2,0,1:T(8,128)S(1)}, f32[21,20,128]{2,0,1:T(8,128)S(1)}, u32[]{:S(2)}, u32[]{:S(2)}) collective-permute-start(f32[21,20,128]{2,0,1:T(8,128)S(1)} %get-tuple-element.197), channel_id=1, source_target_pairs={{0,7},{1,0},{2,1},{3,2},{4,3},{5,4},{6,5},{7,6},{8,15},{9,8},{10,9... | collective-permute-start | bytes 645128 | tf_op jit(solution)/shard_map/ppermute | solution.py:161
  20.0 0.1 fusion.447
  20.1 0.1 add_multiply_fusion.14
  20.3 0.4 fusion.29
  20.7 0.4 fusion.10
  21.1 0.2 add_multiply_fusion.15
  21.3 0.4 fusion.25
  21.8 0.4 fusion.12
  22.3 0.6 %copy-done.1 = f32[19,14,14,128]{3,2,0,1:T(8,128)S(1)} copy-done((f32[19,14,14,128]{3,2,0,1:T(8,128)S(1)}, f32[19,14,14,128]{3,2,0,1:T(8,128)}, u32[]{:S(2)}) %copy-start.1) | copy-done | bytes 1906712
  22.9 0.2 pad_maximum_fusion.2
  23.1 1.9 %copy.553.band_ref = f32[19,18,14,128]{3,2,1,0:T(8,128)} copy(f32[19,18,14,128]{3,2,0,1:T(8,128)S(1)} %pad_maximum_fusion.2) | data formatting | bytes 4902912 | tf_op jit(solution)/shard_map/concatenate | solution.py:295
  25.0 0.1 fusion.450
  25.1 0.1 fusion.117
  25.2 0.1 fusion.118
  25.3 2.3 %collective-permute-done.2 = f32[21,20,128]{2,0,1:T(8,128)S(1)} collective-permute-done((f32[21,20,128]{2,0,1:T(8,128)S(1)}, f32[21,20,128]{2,0,1:T(8,128)S(1)}, u32[]{:S(2)}, u32[]{:S(2)}) %collective-permute-start.2) | collective-permute-done | bytes 215072 | tf_op jit(solution)/shard_map/ppermute | solution.py:161
  27.6 0.1 fusion.128
  27.7 0.1 fusion.129
  27.9 0.1 fusion.443
  28.0 0.1 fusion.442
  28.2 0.1 fusion.445
  28.3 0.1 fusion.444
  28.4 0.2 copy.550
  28.7 0.2 copy.479
  28.8 1.7 %pad_maximum_fusion.1 = (f32[19,18,17,128]{3,2,1,0:T(8,128)S(1)}, f32[19,18,17,128]{3,2,1,0:T(8,128)S(1)}) fusion(f32[19,18,1,128]{3,2,1,0:T(1,128)S(1)} %copy.550, f32[19,1,16,128]{3,2,1,0:T(8,128)S(1)} %get-tuple-element.108, f32[19,1,16,128]{3,2,1,0:T(8,128)S(1)} %get-tuple-element.102, f32[19,18,1,128]{3,2,1,0:T(1,128)S(1)} %copy.479, ...), kind=kLoop, calls=%fused_computation.38 | loop fusion | flops 4465152 | bytes 9105408 | tf_op jit(solution)/shard_map/concatenate | solution.py:284
  30.5 0.2 slice_reduce_fusion.1
  30.7 0.1 slice_reduce_fusion.2
  30.8 0.8 %add_multiply_fusion.6 = (f32[18,2,128]{2,1,0:T(2,128)S(1)}, f32[18,2,128]{2,1,0:T(2,128)S(1)}, f32[18,2,128]{2,1,0:T(2,128)S(1)}, f32[18,2,128]{2,1,0:T(2,128)S...) fusion(f32[18,2,128]{2,1,0:T(2,128)S(1)} %slice_reduce_fusion.1, ...), kind=kLoop, calls=%fused_computation.563 | loop fusion | flops 824832 | bytes 3421328 | tf_op jit(solution)/shard_map/mul | solution.py:180
  31.6 1.4 %fusion.21 = (f32[19,18,2,128]{3,2,1,0:T(2,128)S(1)}, f32[19,18,2,128]{3,2,1,0:T(2,128)S(1)}) fusion(f32[19,18,17,128]{3,2,1,0:T(8,128)S(1)} %get-tuple-element.53, f32[18,2,128]{2,1,0:T(2,128)S(1)} %get-tuple-element.14, f32[18,2,128]{2,1,0:T(2,128)S(1)} %slice_reduce_fusion.1, f32[19]{0:T(128)S(1)} %copy-done.3, f32[18,2,128]{2,1,0:T(2,128)S(1)} %get-tuple-element.19, ...), kind=kLoop, calls=%fused_computation.144 | loop fusion | flops 2188800 | bytes 1216816 | tf_op jit(solution)/shard_map/sub | solution.py:185
  33.1 0.3 pad_maximum_fusion.4
  33.4 0.3 fusion.6
  33.7 1.0 %copy_subtract_fusion.1.far_ref = f32[19,18,2,128]{3,2,1,0:T(2,128)} fusion(f32[19,18,2,128]{3,0,2,1:T(8,128)S(1)} %fusion.6, f32[19,18,17,128]{3,2,1,0:T(8,128)S(1)} %get-tuple-element.53), kind=kLoop, calls=%fused_computation.145 | loop fusion | flops 87552 | bytes 1050624 | tf_op jit(solution)/shard_map/sub | solution.py:186
  34.8 0.7 %add_multiply_fusion.10 = (f32[18,2,128]{2,1,0:T(2,128)S(1)}, f32[18,2,128]{2,1,0:T(2,128)S(1)}, f32[18,2,128]{2,1,0:T(2,128)S(1)}, f32[18,2,128]{2,1,0:T(2,128)...) fusion(f32[18,2,128]{2,1,0:T(2,128)S(1)} %slice_reduce_fusion.2, ...), kind=kLoop, calls=%fused_computation.568 | loop fusion | flops 843264 | bytes 3568496 | tf_op jit(solution)/shard_map/mul | solution.py:180
  35.5 1.3 %fusion.17 = (f32[19,18,2,128]{3,2,1,0:T(2,128)S(1)}, f32[19,18,2,128]{3,2,1,0:T(2,128)S(1)}) fusion(f32[19,18,17,128]{3,2,1,0:T(8,128)S(1)} %get-tuple-element.54, f32[18,2,128]{2,1,0:T(2,128)S(1)} %get-tuple-element.46, f32[18,2,128]{2,1,0:T(2,128)S(1)} %slice_reduce_fusion.2, f32[19]{0:T(128)S(1)} %copy-done.3, f32[18,2,128]{2,1,0:T(2,128)S(1)} %get-tuple-element.51, ...), kind=kLoop, calls=%fused_computation.140 | loop fusion | flops 2188800 | bytes 1216816 | tf_op jit(solution)/shard_map/sub | solution.py:185
  36.8 0.3 pad_maximum_fusion.3
  37.1 0.3 fusion.8
  37.5 1.0 %copy_subtract_fusion.2.near_ref = f32[19,18,2,128]{3,2,1,0:T(2,128)} fusion(f32[19,18,2,128]{3,0,2,1:T(8,128)S(1)} %fusion.8, f32[19,18,17,128]{3,2,1,0:T(8,128)S(1)} %get-tuple-element.54), kind=kLoop, calls=%fused_computation.146 | loop fusion | flops 87552 | bytes 1050624 | tf_op jit(solution)/shard_map/sub | solution.py:186
  38.5 4.1 %shard_map.302 = (f32[19,16,16,128]{3,2,1,0:T(8,128)}, f32[4,16,128]{2,1,0:T(8,128)}) custom-call(f32[19,18,2,128]{3,2,1,0:T(2,128)} %copy_subtract_fusion.2.near_ref, f32[19,18,14,128]{3,2,1,0:T(8,128)} %copy.553.band_ref, f32[19,18,2,128]{3,2,1,0:T(2,128)} %copy_subtract_fusion.1.far_ref), custom_call_target="tpu_custom_call" | custom-call | tf_op jit(solution)/shard_map/pallas_call | solution.py:236
  42.6 0.9 %reshape_reshape.3 = f32[4,16,2,2,32]{4,3,2,1,0:T(2,128)S(1)} reshape(f32[4,16,128]{2,1,0:T(8,128)} %get-tuple-element.5) | data formatting | bytes 65536 | tf_op jit(solution)/shard_map/reshape;reshape | solution.py:311
  43.5 0.1 fusion.451
  43.7 2.0 %collective-permute-start.4 = (f32[4,16,2,32]{3,1,0,2:T(8,128)S(1)}, f32[4,16,2,32]{3,1,0,2:T(8,128)S(1)}, u32[]{:S(2)}, u32[]{:S(2)}) collective-permute-start(f32[4,16,2,32]{3,1,0,2:T(8,128)S(1)} %select_bitcast_fusion), channel_id=1, source_target_pairs={{0,8},{8,0},{16,24},{24,16},{1,9},{9,1},{17,25},{25,17},{2,10},{10... | collective-permute-start | bytes 49160 | tf_op jit(solution)/shard_map/ppermute | solution.py:30
  45.7 2.3 %collective-permute-done.4 = f32[4,16,2,32]{3,1,0,2:T(8,128)S(1)} collective-permute-done((f32[4,16,2,32]{3,1,0,2:T(8,128)S(1)}, f32[4,16,2,32]{3,1,0,2:T(8,128)S(1)}, u32[]{:S(2)}, u32[]{:S(2)}) %collective-permute-start.4) | collective-permute-done | bytes 16416 | tf_op jit(solution)/shard_map/ppermute | solution.py:30
  48.1 1.5 %collective-permute-start.5 = (f32[4,16,1,32]{3,1,0,2:T(8,128)S(1)}, f32[4,16,1,32]{3,1,0,2:T(8,128)S(1)}, u32[]{:S(2)}, u32[]{:S(2)}) collective-permute-start(f32[4,16,1,32]{3,1,0,2:T(8,128)S(1)} %select_bitcast_fusion.1), channel_id=1, source_target_pairs={{0,16},{8,24},{16,0},{24,8},{1,17},{9,25},{17,1},{25,9},{2,18},{10... | collective-permute-start | bytes 24584 | tf_op jit(solution)/shard_map/ppermute | solution.py:30
  49.6 3.3 %copy.556 = f32[16,16,19,128]{3,1,2,0:T(8,128)} copy(f32[16,16,19,128]{3,1,0,2:T(8,128)} %bitcast.551) | data formatting | bytes 4980736
  52.9 0.6 %fusion.107 = f32[4,16,32]{2,1,0:T(8,128)} fusion(f32[4,16,1,32]{3,1,0,2:T(8,128)S(1)} %collective-permute-done.5, f32[16,32]{1,0:T(8,128)S(1)} %fusion.413, pred[]{:T(512)S(6)} %eq.19, f32[4,16,1,2,32]{4,1,0,3,2:T(8,128)S(1)} %fusion.104, pred[]{:T(512)S(6)} %eq.20), kind=kLoop, calls=%fused_computation.342 | loop fusion | flops 10240 | bytes 34818 | tf_op jit(solution)/shard_map/reshape | solution.py:320
  (57 shorter events, 0.9 us)
Async XLA Ops:
  0.6 2.5 %copy-start = (f32[16,16,19,128]{3,1,2,0:T(8,128)S(1)}, f32[16,16,19,128]{3,1,2,0:T(8,128)}, u32[]{:S(2)}) copy-start(f32[16,16,19,128]{3,1,2,0:T(8,128)} %param.31) | copy-start | bytes 7471108
  3.1 12.8 %collective-permute-start.1 = (f32[21,16,128]{2,1,0:T(8,128)S(1)}, f32[21,16,128]{2,1,0:T(8,128)S(1)}, u32[]{:S(2)}, u32[]{:S(2)}) collective-permute-start(f32[21,16,128]{2,1,0:T(8,128)S(1)} %pad_maximum_fusion.16), channel_id=1, source_target_pairs={{0,24},{8,0},{16,8},{24,16},{1,25},{9,1},{17,9},{25,17},{2,26},{10... | collective-permute-start | bytes 516104 | tf_op jit(solution)/shard_map/ppermute | solution.py:161
  7.1 9.0 %collective-permute-start = (f32[21,16,128]{2,1,0:T(8,128)S(1)}, f32[21,16,128]{2,1,0:T(8,128)S(1)}, u32[]{:S(2)}, u32[]{:S(2)}) collective-permute-start(f32[21,16,128]{2,1,0:T(8,128)S(1)} %pad_maximum_fusion.15), channel_id=1, source_target_pairs={{0,8},{8,16},{16,24},{24,0},{1,9},{9,17},{17,25},{25,1},{2,10},{10... | collective-permute-start | bytes 516104 | tf_op jit(solution)/shard_map/ppermute | solution.py:161
  7.9 1.0 %copy-start.3 = (f32[19]{0:T(128)S(1)}, f32[19]{0:T(128)}, u32[]{:S(2)}) copy-start(f32[19]{0:T(128)} %constant.112.clone) | copy-start | bytes 232
  7.9 1.0 %copy-start.4 = (f32[19]{0:T(128)S(1)}, f32[19]{0:T(128)}, u32[]{:S(2)}) copy-start(f32[19]{0:T(128)} %constant.57.clone) | copy-start | bytes 232
  7.9 1.0 %copy-start.5 = (f32[19]{0:T(128)S(1)}, f32[19]{0:T(128)}, u32[]{:S(2)}) copy-start(f32[19]{0:T(128)} %constant.56.clone) | copy-start | bytes 232
  7.9 1.0 %copy-start.6 = (f32[19]{0:T(128)S(1)}, f32[19]{0:T(128)}, u32[]{:S(2)}) copy-start(f32[19]{0:T(128)} %constant.53.clone) | copy-start | bytes 232
  11.0 0.7 %copy-start.2 = (f32[19,38,1,1]{1,0,3,2:T(8,128)S(1)}, f32[19,38,1,1]{1,0,3,2:T(8,128)}, u32[]{:S(2)}) copy-start(f32[19,38,1,1]{1,0,3,2:T(8,128)} %constant.117) | copy-start | bytes 8668
  17.1 7.9 %collective-permute-start.3 = (f32[21,20,128]{2,0,1:T(8,128)S(1)}, f32[21,20,128]{2,0,1:T(8,128)S(1)}, u32[]{:S(2)}, u32[]{:S(2)}) collective-permute-start(f32[21,20,128]{2,0,1:T(8,128)S(1)} %get-tuple-element.197), channel_id=1, source_target_pairs={{0,7},{1,0},{2,1},{3,2},{4,3},{5,4},{6,5},{7,6},{8,15},{9,8},{10,9... | collective-permute-start | bytes 645128 | tf_op jit(solution)/shard_map/ppermute | solution.py:161
  20.0 7.6 %collective-permute-start.2 = (f32[21,20,128]{2,0,1:T(8,128)S(1)}, f32[21,20,128]{2,0,1:T(8,128)S(1)}, u32[]{:S(2)}, u32[]{:S(2)}) collective-permute-start(f32[21,20,128]{2,0,1:T(8,128)S(1)} %get-tuple-element.198), channel_id=1, source_target_pairs={{0,1},{1,2},{2,3},{3,4},{4,5},{5,6},{6,7},{7,0},{8,9},{9,10},{10,1... | collective-permute-start | bytes 645128 | tf_op jit(solution)/shard_map/ppermute | solution.py:161
  21.3 1.6 %copy-start.1 = (f32[19,14,14,128]{3,2,0,1:T(8,128)S(1)}, f32[19,14,14,128]{3,2,0,1:T(8,128)}, u32[]{:S(2)}) copy-start(f32[19,14,14,128]{3,2,0,1:T(8,128)} %copy_subtract_fusion) | copy-start | bytes 5720068
  43.7 4.3 %collective-permute-start.4 = (f32[4,16,2,32]{3,1,0,2:T(8,128)S(1)}, f32[4,16,2,32]{3,1,0,2:T(8,128)S(1)}, u32[]{:S(2)}, u32[]{:S(2)}) collective-permute-start(f32[4,16,2,32]{3,1,0,2:T(8,128)S(1)} %select_bitcast_fusion), channel_id=1, source_target_pairs={{0,8},{8,0},{16,24},{24,16},{1,9},{9,1},{17,25},{25,17},{2,10},{10... | collective-permute-start | bytes 49160 | tf_op jit(solution)/shard_map/ppermute | solution.py:30
  48.1 4.8 %collective-permute-start.5 = (f32[4,16,1,32]{3,1,0,2:T(8,128)S(1)}, f32[4,16,1,32]{3,1,0,2:T(8,128)S(1)}, u32[]{:S(2)}, u32[]{:S(2)}) collective-permute-start(f32[4,16,1,32]{3,1,0,2:T(8,128)S(1)} %select_bitcast_fusion.1), channel_id=1, source_target_pairs={{0,16},{8,24},{16,0},{24,8},{1,17},{9,25},{17,1},{25,9},{2,18},{10... | collective-permute-start | bytes 24584 | tf_op jit(solution)/shard_map/ppermute | solution.py:30

commit v15 on v14

--- a/solution.py
+++ b/solution.py
@@ -303,21 +303,11 @@
     depth_z = layered.shape[2]
     block_len = depth_z // groups
     blocked = layered.reshape(4, extent_y, groups, block_len)
-    position = lax.axis_index("gx")
-    current = blocked
-    for level in range(groups.bit_length() - 1):
-        parity = position // (1 << level) % 2
-        halves = current.shape[2] // 2
-        paired = current.reshape(4, extent_y, halves, 2, block_len)
-        lower = paired[:, :, :, 0]
-        upper = paired[:, :, :, 1]
-        kept = jnp.where(parity == 1, upper, lower)
-        handed = jnp.where(parity == 1, lower, upper)
-        partner = from_partner(handed, "gx", level)
-        nearer = jnp.where(parity == 0, kept, partner)
-        farther = jnp.where(parity == 0, partner, kept)
-        current = nearer + (1.0 - nearer[3:4]) * farther
-    picture = current.reshape(4, extent_y, block_len)
+    gathered = lax.all_to_all(blocked, "gx", 2, 2, tiled=True)
+    current = gathered[:, :, 0]
+    for source in range(1, groups):
+        current = current + (1.0 - current[3:4]) * gathered[:, :, source]
+    picture = current
     return (fresh, picture)
 
 

time: 53.8 us -> 54.2 us (level)
  waiting for transfers between devices: 4.6 us -> 5.34 us
  other arithmetic: 20.1 us -> 19.4 us
  local copies, waits for them, and re-layouts: 9.3 us -> 9.87 us
    all_to_all x0 -> x1, starting transfers between devices: none -> 3.69 us  [body(): gathered = lax.all_to_all(blocked, 'gx', 2, 2, tiled=True)]
    ppermute x2 -> x0, starting transfers between devices: 3.53 us -> none  [from_partner(): lax.ppermute(x, axis, [(i, i ^ 1 << distance) for i in range(lax.axis_siz...]
    ppermute x2 -> x0, waiting for transfers between devices: 2.32 us -> none  [from_partner(): lax.ppermute(x, axis, [(i, i ^ 1 << distance) for i in range(lax.axis_siz...]
    ppermute x4, waiting for transfers between devices: 2.28 us -> 3.91 us  [shift_ring(): lax.ppermute(x, axis, [(i, (i - step) % count) for i in range(count)])]
    all_to_all x0 -> x1, waiting for transfers between devices: none -> 1.44 us  [body(): gathered = lax.all_to_all(blocked, 'gx', 2, 2, tiled=True)]
    sub x4, other arithmetic: 4.12 us -> 2.78 us  [collide_major(): f - jnp.einsum('pq,q...->p...', table, stacked, precision=lax.Precision.H...]
    another operation x1 -> x0, local copies, waits for them, and re-layouts: 0.91 us -> none  [body(): paired = current.reshape(4, extent_y, halves, 2, block_len)]
    reshape x0 -> x2, local copies, waits for them, and re-layouts: none -> 0.88 us  [body(): blocked = layered.reshape(4, extent_y, groups, block_len)]
  transfers between devices with their start and end apart: 6 -> 5, of which waited for: 2 -> 4; matrix products, arithmetic and copies ran while one was open for 31% -> 28% of each run, Pallas kernels for 0% -> 0%
where the time goes in v15:
time: 54.2 us; the launch traced here: 53.8 us
  other arithmetic  19.4 us (36%)
  starting transfers between devices  10 us (18%)
  local copies, waits for them, and re-layouts  9.87 us (18%)
  waiting for transfers between devices  5.34 us (10%)
  Pallas kernels  4.15 us (8%)
  matrix products  3.79 us (7%)
  between operations  1.24 us (2%)
    ppermute x4, starting transfers between devices, shift_ring(): lax.ppermute(x, axis, [(i, (i - step) % count) for i in range(count)])  6.33 us
    sub x5, other arithmetic, collide_major(): stacked = jnp.concatenate([f - balance, guo_term], axis=0)  5.72 us
    unnamed x15, local copies, waits for them, and re-layouts  4.81 us
    pallas_call x1, Pallas kernels, stream_and_render(): pl.pallas_call(kernel, out_shape=(jax.ShapeDtypeStruct((19, extent_x, ext...  4.15 us
    ppermute x4, waiting for transfers between devices, shift_ring(): lax.ppermute(x, axis, [(i, (i - step) % count) for i in range(count)])  3.91 us
    dot_general x5, matrix products, collide_major(): jnp.einsum('pq,q...->p...', table, stacked, precision=lax.Precision.HIGH)  3.79 us
    all_to_all x1, starting transfers between devices, body(): gathered = lax.all_to_all(blocked, 'gx', 2, 2, tiled=True)  3.69 us
    sub x4, other arithmetic, collide_major(): f - jnp.einsum('pq,q...->p...', table, stacked, precision=lax.Precision.H...  2.78 us
  transfers between devices with their start and end apart: 5, of which 4 were waited for; matrix products, arithmetic and copies ran while one was open for 28% of the time, Pallas kernels for 0%

profile of v15, /device:TPU:0, one launch (start us, length us, event | category | flops | bytes accessed | tf_op | source)
XLA Modules:
  0.0 53.8 jit_solution(16631791411856965756)
XLA Ops:
  0.6 2.0 %bitcast_reduce_fusion = f32[16,16,128]{2,1,0:T(8,128)S(1)} fusion(f32[16,16,19,128]{3,1,2,0:T(8,128)} %param.31), kind=kLoop, calls=%fused_computation.830 | loop fusion | flops 589824 | bytes 2621440 | tf_op jit(solution)/shard_map/reduce_sum | solution.py:269
  2.7 0.4 copy-done
  3.1 3.9 %collective-permute-start.1 = (f32[21,16,128]{2,1,0:T(8,128)S(1)}, f32[21,16,128]{2,1,0:T(8,128)S(1)}, u32[]{:S(2)}, u32[]{:S(2)}) collective-permute-start(f32[21,16,128]{2,1,0:T(8,128)S(1)} %pad_maximum_fusion.16), channel_id=1, source_target_pairs={{0,24},{8,0},{16,8},{24,16},{1,25},{9,1},{17,9},{25,17},{2,26},{10... | collective-permute-start | bytes 516104 | tf_op jit(solution)/shard_map/ppermute | solution.py:161
  7.2 0.2 slice_reduce_fusion
  7.4 0.2 fusion.452
  7.6 0.2 fusion.453
  7.9 0.9 %add_multiply_fusion.5 = (f32[14,14,128]{2,1,0:T(8,128)S(1)}, f32[14,14,128]{2,1,0:T(8,128)S(1)}, f32[14,14,128]{2,1,0:T(8,128)S(1)}, f32[14,14,128]{2,1,0:T(8,1...) fusion(f32[14,14,128]{2,1,0:T(8,128)S(1)} %slice_reduce_fusion, ...), kind=kLoop, calls=%fused_computation.316 | loop fusion | flops 2985472 | bytes 6207488 | tf_op jit(solution)/shard_map/mul | solution.py:180
  8.9 2.2 %fusion.5 = (f32[19,14,14,128]{3,2,0,1:T(8,128)S(1)}, f32[19,14,14,128]{3,2,0,1:T(8,128)S(1)}) fusion(f32[19,16,16,128]{3,2,0,1:T(8,128)S(1)} %bitcast.546, f32[14,14,128]{2,1,0:T(8,128)S(1)} %get-tuple-element.30, f32[14,14,128]{2,1,0:T(8,128)S(1)} %get-tuple-element.35, f32[19]{0:T(128)S(1)} %copy-done.3, f32[14,14,128]{2,1,0:T(8,128)S(1)} %get-tuple-element.33, ...), kind=kLoop, calls=%fused_computation.46 | loop fusion | flops 11916800 | bytes 6623536 | tf_op jit(solution)/shard_map/sub | solution.py:185
  11.1 0.4 pad_maximum_fusion
  11.5 0.3 copy-done.1
  11.8 2.2 %fusion = f32[19,14,14,128]{3,0,2,1:T(8,128)S(1)} fusion(f32[19,38,1,1]{1,0,3,2:T(8,128)S(1)} %copy-done.1, f32[38,14,14,128]{3,2,0,1:T(8,128)S(1)} %pad_maximum_fusion), kind=kOutput, calls=%fused_computation.39 | convolution fusion | flops 108681216 | bytes 5722952 | tf_op jit(solution)/shard_map/pq,q...->p.../dot_general | solution.py:186
  14.0 0.7 %copy_subtract_fusion = f32[19,14,14,128]{3,2,0,1:T(8,128)S(1)} fusion(f32[19,14,14,128]{3,0,2,1:T(8,128)S(1)} %fusion, f32[19,16,16,128]{3,2,0,1:T(8,128)S(1)} %bitcast.547), kind=kLoop, calls=%fused_computation.47 | loop fusion | flops 476672 | bytes 5720064 | tf_op jit(solution)/shard_map/sub | solution.py:186
  14.9 0.5 collective-permute-done
  15.5 0.1 fusion.303
  15.6 0.1 fusion.302
  15.8 0.1 fusion.424
  15.9 0.1 fusion.450
  16.0 0.2 pad_maximum_fusion.12
  16.4 2.3 %collective-permute-start.3 = (f32[21,20,128]{2,0,1:T(8,128)S(1)}, f32[21,20,128]{2,0,1:T(8,128)S(1)}, u32[]{:S(2)}, u32[]{:S(2)}) collective-permute-start(f32[21,20,128]{2,0,1:T(8,128)S(1)} %get-tuple-element.195), channel_id=1, source_target_pairs={{0,7},{1,0},{2,1},{3,2},{4,3},{5,4},{6,5},{7,6},{8,15},{9,8},{10,9... | collective-permute-start | bytes 645128 | tf_op jit(solution)/shard_map/ppermute | solution.py:161
  18.9 0.1 add_multiply_fusion.14
  19.0 0.4 fusion.29
  19.4 0.4 fusion.10
  19.9 0.2 add_multiply_fusion.15
  20.1 0.4 fusion.25
  20.5 0.4 fusion.12
  21.0 0.1 copy_subtract_fusion.4
  21.1 0.2 pad_maximum_fusion.2
  21.3 1.9 %copy.550.band_ref = f32[19,18,14,128]{3,2,1,0:T(8,128)} copy(f32[19,18,14,128]{3,2,0,1:T(8,128)S(1)} %pad_maximum_fusion.2) | data formatting | bytes 4902912 | tf_op jit(solution)/shard_map/concatenate | solution.py:295
  23.1 0.1 fusion.451
  23.2 0.8 %collective-permute-done.3 = f32[21,20,128]{2,0,1:T(8,128)S(1)} collective-permute-done((f32[21,20,128]{2,0,1:T(8,128)S(1)}, f32[21,20,128]{2,0,1:T(8,128)S(1)}, u32[]{:S(2)}, u32[]{:S(2)}) %collective-permute-start.3) | collective-permute-done | bytes 215072 | tf_op jit(solution)/shard_map/ppermute | solution.py:161
  24.1 0.1 fusion.117
  24.2 0.1 fusion.118
  24.3 2.6 %collective-permute-done.2 = f32[21,20,128]{2,0,1:T(8,128)S(1)} collective-permute-done((f32[21,20,128]{2,0,1:T(8,128)S(1)}, f32[21,20,128]{2,0,1:T(8,128)S(1)}, u32[]{:S(2)}, u32[]{:S(2)}) %collective-permute-start.2) | collective-permute-done | bytes 215072 | tf_op jit(solution)/shard_map/ppermute | solution.py:161
  26.9 0.1 fusion.128
  27.0 0.1 fusion.129
  27.1 0.1 fusion.444
  27.3 0.1 fusion.443
  27.4 0.1 fusion.446
  27.5 0.1 fusion.445
  27.7 0.2 copy.547
  27.9 0.2 copy.476
  28.1 1.6 %pad_maximum_fusion.1 = (f32[19,18,17,128]{3,2,1,0:T(8,128)S(1)}, f32[19,18,17,128]{3,2,1,0:T(8,128)S(1)}) fusion(f32[19,18,1,128]{3,2,1,0:T(1,128)S(1)} %copy.547, f32[19,1,16,128]{3,2,1,0:T(8,128)S(1)} %get-tuple-element.108, f32[19,1,16,128]{3,2,1,0:T(8,128)S(1)} %get-tuple-element.102, f32[19,18,1,128]{3,2,1,0:T(1,128)S(1)} %copy.476, ...), kind=kLoop, calls=%fused_computation.38 | loop fusion | flops 4465152 | bytes 9105408 | tf_op jit(solution)/shard_map/concatenate | solution.py:284
  29.7 0.2 slice_reduce_fusion.1
  29.9 0.1 slice_reduce_fusion.2
  29.9 0.8 %add_multiply_fusion.6 = (f32[18,2,128]{2,1,0:T(2,128)S(1)}, f32[18,2,128]{2,1,0:T(2,128)S(1)}, f32[18,2,128]{2,1,0:T(2,128)S(1)}, f32[18,2,128]{2,1,0:T(2,128)S...) fusion(f32[18,2,128]{2,1,0:T(2,128)S(1)} %slice_reduce_fusion.1, ...), kind=kLoop, calls=%fused_computation.559 | loop fusion | flops 824832 | bytes 3421328 | tf_op jit(solution)/shard_map/mul | solution.py:180
  30.8 1.4 %fusion.21 = (f32[19,18,2,128]{3,2,1,0:T(2,128)S(1)}, f32[19,18,2,128]{3,2,1,0:T(2,128)S(1)}) fusion(f32[19,18,17,128]{3,2,1,0:T(8,128)S(1)} %get-tuple-element.53, f32[18,2,128]{2,1,0:T(2,128)S(1)} %get-tuple-element.14, f32[18,2,128]{2,1,0:T(2,128)S(1)} %slice_reduce_fusion.1, f32[19]{0:T(128)S(1)} %copy-done.2, f32[18,2,128]{2,1,0:T(2,128)S(1)} %get-tuple-element.19, ...), kind=kLoop, calls=%fused_computation.144 | loop fusion | flops 2188800 | bytes 1216816 | tf_op jit(solution)/shard_map/sub | solution.py:185
  32.2 0.3 pad_maximum_fusion.4
  32.5 0.3 fusion.6
  32.9 1.0 %copy_subtract_fusion.1.far_ref = f32[19,18,2,128]{3,2,1,0:T(2,128)} fusion(f32[19,18,2,128]{3,0,2,1:T(8,128)S(1)} %fusion.6, f32[19,18,17,128]{3,2,1,0:T(8,128)S(1)} %get-tuple-element.53), kind=kLoop, calls=%fused_computation.145 | loop fusion | flops 87552 | bytes 1050624 | tf_op jit(solution)/shard_map/sub | solution.py:186
  33.9 0.7 %add_multiply_fusion.10 = (f32[18,2,128]{2,1,0:T(2,128)S(1)}, f32[18,2,128]{2,1,0:T(2,128)S(1)}, f32[18,2,128]{2,1,0:T(2,128)S(1)}, f32[18,2,128]{2,1,0:T(2,128)...) fusion(f32[18,2,128]{2,1,0:T(2,128)S(1)} %slice_reduce_fusion.2, ...), kind=kLoop, calls=%fused_computation.564 | loop fusion | flops 843264 | bytes 3568496 | tf_op jit(solution)/shard_map/mul | solution.py:180
  34.6 1.3 %fusion.17 = (f32[19,18,2,128]{3,2,1,0:T(2,128)S(1)}, f32[19,18,2,128]{3,2,1,0:T(2,128)S(1)}) fusion(f32[19,18,17,128]{3,2,1,0:T(8,128)S(1)} %get-tuple-element.54, f32[18,2,128]{2,1,0:T(2,128)S(1)} %get-tuple-element.46, f32[18,2,128]{2,1,0:T(2,128)S(1)} %slice_reduce_fusion.2, f32[19]{0:T(128)S(1)} %copy-done.2, f32[18,2,128]{2,1,0:T(2,128)S(1)} %get-tuple-element.51, ...), kind=kLoop, calls=%fused_computation.140 | loop fusion | flops 2188800 | bytes 1216816 | tf_op jit(solution)/shard_map/sub | solution.py:185
  35.9 0.3 pad_maximum_fusion.3
  36.2 0.3 fusion.8
  36.6 1.0 %copy_subtract_fusion.2.near_ref = f32[19,18,2,128]{3,2,1,0:T(2,128)} fusion(f32[19,18,2,128]{3,0,2,1:T(8,128)S(1)} %fusion.8, f32[19,18,17,128]{3,2,1,0:T(8,128)S(1)} %get-tuple-element.54), kind=kLoop, calls=%fused_computation.146 | loop fusion | flops 87552 | bytes 1050624 | tf_op jit(solution)/shard_map/sub | solution.py:186
  37.6 4.1 %shard_map.302 = (f32[19,16,16,128]{3,2,1,0:T(8,128)}, f32[4,16,128]{2,1,0:T(8,128)}) custom-call(f32[19,18,2,128]{3,2,1,0:T(2,128)} %copy_subtract_fusion.2.near_ref, f32[19,18,14,128]{3,2,1,0:T(8,128)} %copy.550.band_ref, f32[19,18,2,128]{3,2,1,0:T(2,128)} %copy_subtract_fusion.1.far_ref), custom_call_target="tpu_custom_call" | custom-call | tf_op jit(solution)/shard_map/pallas_call | solution.py:236
  41.7 0.9 %reshape.197 = f32[4,16,4,32]{3,2,1,0:T(4,128)S(1)} reshape(f32[4,16,128]{2,1,0:T(8,128)} %get-tuple-element.5) | data formatting | bytes 65536 | tf_op jit(solution)/shard_map/reshape | solution.py:305
  42.6 0.7 %reshape.334 = f32[4,1,2048]{2,1,0:T(1,128)} reshape(f32[4,4,16,32]{3,2,1,0:T(8,128)S(1)} %bitcast.558) | data formatting | bytes 65536
  43.4 3.7 %all-to-all-start = ((f32[4,1,2048]{2,1,0:T(1,128)}), f32[4,1,2048]{2,1,0:T(1,128)S(1)}, u32[]{:S(2)}, u32[]{:S(2)}) async-start(f32[4,1,2048]{2,1,0:T(1,128)} %reshape.334), calls=%async_computation | async-start | bytes 65536 | tf_op jit(solution)/shard_map/all_to_all | solution.py:306
  47.1 3.3 %copy.552 = f32[16,16,19,128]{3,1,2,0:T(8,128)} copy(f32[16,16,19,128]{3,1,0,2:T(8,128)} %bitcast.553) | data formatting | bytes 4980736
  50.4 1.4 %all-to-all-done = f32[4,1,2048]{2,1,0:T(1,128)S(1)} async-done(((f32[4,1,2048]{2,1,0:T(1,128)}), f32[4,1,2048]{2,1,0:T(1,128)S(1)}, u32[]{:S(2)}, u32[]{:S(2)}) %all-to-all-start) | async-done | bytes 32800 | tf_op jit(solution)/shard_map/all_to_all | solution.py:306
  51.8 0.5 broadcast.707
  52.3 0.7 %reduce = f32[4,2048]{1,0:T(4,128)S(1)} reduce(f32[4,1,2048]{2,1,0:T(1,128)S(1)} %all-to-all-done, f32[]{:T(128)} %broadcast.707), dimensions={1}, to_apply=%all_to_all.3.reduce_sub_computation | reduce | bytes 65540 | tf_op jit(solution)/shard_map/all_to_all | solution.py:306
  53.1 0.1 reshape.335
  53.2 0.6 %fusion.103 = f32[4,16,32]{2,1,0:T(8,128)} fusion(f32[4,16,32]{2,1,0:T(8,128)S(1)} %fusion.105, f32[4,16,4,32]{3,1,0,2:T(8,128)S(1)} %bitcast.557, f32[16,32]{1,0:T(8,128)S(1)} %fusion.412), kind=kLoop, calls=%fused_computation.333 | loop fusion | flops 4096 | bytes 26624 | tf_op jit(solution)/shard_map/add | solution.py:309
  (55 shorter events, 1.1 us)
Async XLA Ops:
  0.6 2.5 %copy-start = (f32[16,16,19,128]{3,1,2,0:T(8,128)S(1)}, f32[16,16,19,128]{3,1,2,0:T(8,128)}, u32[]{:S(2)}) copy-start(f32[16,16,19,128]{3,1,2,0:T(8,128)} %param.31) | copy-start | bytes 7471108
  3.1 11.6 %collective-permute-start.1 = (f32[21,16,128]{2,1,0:T(8,128)S(1)}, f32[21,16,128]{2,1,0:T(8,128)S(1)}, u32[]{:S(2)}, u32[]{:S(2)}) collective-permute-start(f32[21,16,128]{2,1,0:T(8,128)S(1)} %pad_maximum_fusion.16), channel_id=1, source_target_pairs={{0,24},{8,0},{16,8},{24,16},{1,25},{9,1},{17,9},{25,17},{2,26},{10... | collective-permute-start | bytes 516104 | tf_op jit(solution)/shard_map/ppermute | solution.py:161
  7.1 8.3 %collective-permute-start = (f32[21,16,128]{2,1,0:T(8,128)S(1)}, f32[21,16,128]{2,1,0:T(8,128)S(1)}, u32[]{:S(2)}, u32[]{:S(2)}) collective-permute-start(f32[21,16,128]{2,1,0:T(8,128)S(1)} %pad_maximum_fusion.15), channel_id=1, source_target_pairs={{0,8},{8,16},{16,24},{24,0},{1,9},{9,17},{17,25},{25,1},{2,10},{10... | collective-permute-start | bytes 516104 | tf_op jit(solution)/shard_map/ppermute | solution.py:161
  7.9 1.0 %copy-start.2 = (f32[19]{0:T(128)S(1)}, f32[19]{0:T(128)}, u32[]{:S(2)}) copy-start(f32[19]{0:T(128)} %constant.35.clone) | copy-start | bytes 232
  7.9 1.0 %copy-start.3 = (f32[19]{0:T(128)S(1)}, f32[19]{0:T(128)}, u32[]{:S(2)}) copy-start(f32[19]{0:T(128)} %constant.34.clone) | copy-start | bytes 232
  7.9 1.0 %copy-start.4 = (f32[19]{0:T(128)S(1)}, f32[19]{0:T(128)}, u32[]{:S(2)}) copy-start(f32[19]{0:T(128)} %constant.33.clone) | copy-start | bytes 232
  7.9 1.0 %copy-start.5 = (f32[19]{0:T(128)S(1)}, f32[19]{0:T(128)}, u32[]{:S(2)}) copy-start(f32[19]{0:T(128)} %constant.32.clone) | copy-start | bytes 232
  11.1 0.7 %copy-start.1 = (f32[19,38,1,1]{1,0,3,2:T(8,128)S(1)}, f32[19,38,1,1]{1,0,3,2:T(8,128)}, u32[]{:S(2)}) copy-start(f32[19,38,1,1]{1,0,3,2:T(8,128)} %constant.8) | copy-start | bytes 8668
  16.4 7.6 %collective-permute-start.3 = (f32[21,20,128]{2,0,1:T(8,128)S(1)}, f32[21,20,128]{2,0,1:T(8,128)S(1)}, u32[]{:S(2)}, u32[]{:S(2)}) collective-permute-start(f32[21,20,128]{2,0,1:T(8,128)S(1)} %get-tuple-element.195), channel_id=1, source_target_pairs={{0,7},{1,0},{2,1},{3,2},{4,3},{5,4},{6,5},{7,6},{8,15},{9,8},{10,9... | collective-permute-start | bytes 645128 | tf_op jit(solution)/shard_map/ppermute | solution.py:161
  18.7 8.1 %collective-permute-start.2 = (f32[21,20,128]{2,0,1:T(8,128)S(1)}, f32[21,20,128]{2,0,1:T(8,128)S(1)}, u32[]{:S(2)}, u32[]{:S(2)}) collective-permute-start(f32[21,20,128]{2,0,1:T(8,128)S(1)} %get-tuple-element.196), channel_id=1, source_target_pairs={{0,1},{1,2},{2,3},{3,4},{4,5},{5,6},{6,7},{7,0},{8,9},{9,10},{10,1... | collective-permute-start | bytes 645128 | tf_op jit(solution)/shard_map/ppermute | solution.py:161
  43.4 8.4 %all-to-all-start = ((f32[4,1,2048]{2,1,0:T(1,128)}), f32[4,1,2048]{2,1,0:T(1,128)S(1)}, u32[]{:S(2)}, u32[]{:S(2)}) async-start(f32[4,1,2048]{2,1,0:T(1,128)} %reshape.334), calls=%async_computation | async-start | bytes 65536 | tf_op jit(solution)/shard_map/all_to_all | solution.py:306
